TPU v7x, 32 devices: a whole 2x2x4 slice. The times are simulated.
32 devices in a mesh: az: 4 (over x, core), rad: 4 (over z), ax: 2 (over y).
Axes of the slice: x: 2, y: 2, z: 4, core: 2. Of those that a mesh axis runs over, the one named last changes fastest.
Arguments:
- flow_state: float32 [5, 2, 512, 1024], P(None, 'ax', 'az', 'rad'), may hold values from -6 to 6
- source: float32 [5, 2, 512, 1024], P(None, 'ax', 'az', 'rad'), may hold values from -6 to 6
- cell_az: float32 [2, 512, 1024], P('ax', 'az', 'rad'), may hold values from 0.5 to 2
- cell_rad: float32 [2, 512, 1024], P('ax', 'az', 'rad'), may hold values from 0.5 to 2
- visc_az: float32 [5, 1024], P(None, 'rad'), may hold values from 1 to 20000
- beta_az: float32 [5, 1024], P(None, 'rad'), may hold values from -0.6 to 0.6
- visc_rad: float32 [5, 1024], replicated, may hold values from 1 to 20000
- axial_diff: float32 [5, 1024], P(None, 'rad'), may hold values from 0.1 to 0.45
- mix_in: float32 [5, 5, 1024], P(None, None, 'rad'), may hold values from -1.2 to 1.2
- mix_mid: float32 [5, 5, 1024], P(None, None, 'rad'), may hold values from -1.2 to 1.2
- mix_out: float32 [5, 5, 1024], P(None, None, 'rad'), may hold values from -1.2 to 1.2
Outputs:
- update: float32 [5, 2, 512, 1024], P(None, 'ax', 'az', 'rad')
All inputs are finite; a program needn't handle non-finite values.
Results may differ from a plain program's by a relative error of at most 0.00045.
Values sent between devices are 32-bit elements; how exact they have to be, the bound alone decides.
No kernel may reach another device: no remote copies, remote signals or barrier semaphores. Data moves between devices by JAX's collectives and lax.ppermute only.
A program may use at most 128 MiB of HBM per device.

v0:
```python
import jax
import jax.numpy as jnp
from jax import lax
from jax.sharding import PartitionSpec as P


def with_halo(block, sides, width, periodic):
    for axis, dim in sides:
        count = lax.axis_size(axis)
        forward = [(i, i + 1) for i in range(count - 1)]
        if periodic:
            forward.append((count - 1, 0))
        backward = [(target, source) for source, target in forward]
        low = lax.ppermute(
            lax.slice_in_dim(block, block.shape[dim] - width, None, axis=dim), axis, forward
        )
        high = lax.ppermute(lax.slice_in_dim(block, 0, width, axis=dim), axis, backward)
        block = jnp.concatenate([low, block, high], axis=dim)
    return block


def from_behind(block, axis, distance):
    devices = range(lax.axis_size(axis))
    route = [((i - distance) % len(devices), i) for i in devices]
    return lax.ppermute(block, axis, route)


def passed_along(value, axis, by):
    devices = lax.axis_size(axis)
    pairs = [(i, i + by) for i in range(devices) if 0 <= i + by < devices]
    return lax.ppermute(value, axis, pairs)


def eliminate(stack, left, right):
    lower, upper, target = (stack[0], stack[1], stack[2])
    pivots = 1.0 - lower * left[1] - upper * right[0]
    return jnp.stack(
        [
            -lower * left[0] / pivots,
            -upper * right[1] / pivots,
            (target - lower * left[2] - upper * right[2]) / pivots,
        ]
    )


def reduce_lines(stack, length, fetch):
    stride = 1
    while stride < length:
        left, right = fetch(stack, stride)
        stack = eliminate(stack, left, right)
        stride = stride * 2
    return stack[2] / (1.0 + stack[0] + stack[1])


def mix(matrix, values):
    mixed_rows = []
    for out_var in range(values.shape[0]):
        summed = values[out_var]
        for in_var in range(values.shape[0]):
            summed = summed + matrix[out_var, in_var][None, None, :] * values[in_var]
        mixed_rows.append(summed)
    return jnp.stack(mixed_rows)


def az_pair(stack, stride):
    length = stack.shape[3]
    if stride < length:
        padded = with_halo(stack, (("az", 3),), stride, True)
        return (padded[:, :, :, :length], padded[:, :, :, 2 * stride : 2 * stride + length])
    reach = stride // length
    fetched = [from_behind(stack, "az", offset) for offset in (reach, -reach)]
    return (fetched[0], fetched[1])


def rad_pair(stack, stride):
    length = stack.shape[4]
    if stride < length:
        padded = with_halo(stack, (("rad", 4),), stride, False)
        return (padded[:, :, :, :, :length], padded[:, :, :, :, 2 * stride : 2 * stride + length])
    reach = stride // length
    fetched = [passed_along(stack, "rad", offset) for offset in (reach, -reach)]
    return (fetched[0], fetched[1])


def az_coeffs(visc_rows, tilt_rows, cells, values):
    coupling = visc_rows[:, None, None, :] * cells[None]
    centre = 1.0 + 2.0 * coupling
    tilt = tilt_rows[:, None, None, :]
    lower = -coupling * (1.0 + tilt) / centre
    upper = -coupling * (1.0 - tilt) / centre
    return jnp.stack([lower, upper, values / centre])


def rad_coeffs(visc_rows, cells, values):
    coupling = visc_rows[:, None, None, :] * cells[None]
    centre = 1.0 + 2.0 * coupling
    side = -coupling / centre
    return jnp.stack([side, side, values / centre])


def per_device(
    flow_state,
    source,
    cell_az,
    cell_rad,
    visc_az,
    beta_az,
    visc_rad,
    axial_diff,
    mix_in,
    mix_mid,
    mix_out,
):
    az_cells = flow_state.shape[2]
    rad_cells = flow_state.shape[3]
    padded = with_halo(flow_state, (("ax", 1),), 1, False)
    explicit = source + axial_diff[:, None, None, :] * (
        padded[:, :-2] - 2.0 * flow_state + padded[:, 2:]
    )
    section_one = mix(mix_in, explicit)
    stack = az_coeffs(visc_az, beta_az, cell_az, section_one)
    section_two = reduce_lines(stack, az_cells * lax.axis_size("az"), az_pair)
    section_three = mix(mix_mid, section_two)
    visc_local = lax.dynamic_slice_in_dim(visc_rad, lax.axis_index("rad") * rad_cells, rad_cells, 1)
    stack = rad_coeffs(visc_local, cell_rad, section_three)
    section_four = reduce_lines(stack, rad_cells * lax.axis_size("rad"), rad_pair)
    return mix(mix_out, section_four)


def solution(mesh):
    in_specs = (
        P(None, "ax", "az", "rad"),
        P(None, "ax", "az", "rad"),
        P("ax", "az", "rad"),
        P("ax", "az", "rad"),
        P(None, "rad"),
        P(None, "rad"),
        P(),
        P(None, "rad"),
        P(None, None, "rad"),
        P(None, None, "rad"),
        P(None, None, "rad"),
    )
    out_specs = P(None, "ax", "az", "rad")
    return jax.shard_map(
        per_device, mesh=mesh, in_specs=in_specs, out_specs=out_specs, check_vma=False
    )
```

profile of v0, /device:TPU:0, one launch (start us, length us, event | category | flops | bytes accessed | tf_op | source)
XLA Modules:
  0.0 521.4 jit_solution(3025860337091176618)
XLA Ops:
  0.0 5.0 collective-permute-start
  8.9 10.4 %collective-permute-done = f32[5,1,128,256]{3,2,1,0:T(8,128)S(1)} collective-permute-done((f32[5,1,128,256]{3,2,1,0:T(8,128)}, f32[5,1,128,256]{3,2,1,0:T(8,128)S(1)}, u32[]{:S(2)}, u32[]{:S(2)}) %collective-permute-start) | collective-permute-done | bytes 655392 | tf_op jit(solution)/shard_map/ppermute | solution.py:14
  19.3 4.1 collective-permute-done.1
  46.7 2.5 collective-permute-done.8
  52.3 4.8 collective-permute-done.10
  60.5 10.0 %collective-permute-done.12 = f32[3,5,1,32,256]{4,3,2,1,0:T(8,128)S(1)} collective-permute-done((f32[3,5,1,32,256]{4,3,2,1,0:T(8,128)S(1)}, f32[3,5,1,32,256]{4,3,2,1,0:T(8,128)S(1)}, u32[]{:S(2)}, u32[]{:S(2)}) %collective-permute-start.12) | collective-permute-done | bytes 491552 | tf_op jit(solution)/shard_map/ppermute | solution.py:14
  74.6 20.4 %collective-permute-done.14 = f32[3,5,1,64,256]{4,3,2,1,0:T(8,128)S(1)} collective-permute-done((f32[3,5,1,64,256]{4,3,2,1,0:T(8,128)S(1)}, f32[3,5,1,64,256]{4,3,2,1,0:T(8,128)S(1)}, u32[]{:S(2)}, u32[]{:S(2)}) %collective-permute-start.14) | collective-permute-done | bytes 983072 | tf_op jit(solution)/shard_map/ppermute | solution.py:14
  99.6 40.9 %collective-permute-done.16 = f32[3,5,1,128,256]{4,3,1,2,0:T(8,128)S(1)} collective-permute-done((f32[3,5,1,128,256]{4,3,1,2,0:T(8,128)S(1)}, f32[3,5,1,128,256]{4,3,1,2,0:T(8,128)S(1)}, u32[]{:S(2)}, u32[]{:S(2)}) %collective-permute-start.16) | collective-permute-done | bytes 1966112 | tf_op jit(solution)/shard_map/ppermute | solution.py:25
  144.7 2.3 collective-permute-start.18
  153.8 36.5 %collective-permute-done.18 = f32[3,5,1,128,256]{4,3,1,2,0:T(8,128)} collective-permute-done((f32[3,5,1,128,256]{4,3,1,2,0:T(8,128)}, f32[3,5,1,128,256]{4,3,1,2,0:T(8,128)}, u32[]{:S(2)}, u32[]{:S(2)}) %collective-permute-start.18) | collective-permute-done | bytes 1966112 | tf_op jit(solution)/shard_map/ppermute | solution.py:25
  190.4 11.2 %fusion.110 = f32[5,1,128,256]{3,2,0,1:T(8,128)S(1)} fusion(f32[5,1,128,256]{3,2,0,1:T(8,128)S(1)} %constant_dynamic-update-slice_fusion, f32[1,5,1,128,256]{4,3,1,2,0:T(8,128)} %get-tuple-element.50, f32[3,5,1,128,256]{4,3,1,2,0:T(8,128)} %collective-permute-done.18, f32[1,5,1,128,256]{4,3,1,2,0:T(8,128)} %copy-done.96, ...), kind=kLoop, calls=%fused_computation.372 | loop fusion | flops 40796160 | bytes 28265472 | tf_op jit(solution)/shard_map/div | solution.py:52
  205.9 3.5 collective-permute-start.19
  212.4 2.9 collective-permute-done.20
  216.6 2.7 multiply_divide_fusion.15
  221.7 3.2 bitcast_divide_fusion.8
  227.8 3.5 collective-permute-start.21
  234.3 3.0 collective-permute-done.22
  237.6 2.1 multiply_divide_fusion.13
  246.7 3.5 collective-permute-start.23
  253.5 2.9 collective-permute-done.24
  256.7 2.1 multiply_divide_fusion.11
  264.9 1.9 collective-permute-start.25
  269.9 3.3 collective-permute-done.26
  273.6 2.7 multiply_divide_fusion.9
  287.9 4.3 collective-permute-done.28
  293.5 3.1 multiply_divide_fusion.7
  302.1 2.2 copy.286
  304.3 2.7 collective-permute-start.29
  307.1 2.2 copy.288
  310.6 2.2 copy.287
  312.8 4.9 collective-permute-done.30
  317.7 2.2 copy.289
  319.9 2.5 multiply_divide_fusion.5
  327.3 2.3 copy.294
  329.6 2.3 collective-permute-start.31
  331.9 2.3 copy.296
  335.7 2.0 collective-permute-done.31
  337.7 2.3 copy.295
  340.0 5.2 collective-permute-done.32
  345.2 2.4 copy.297
  347.6 3.1 multiply_divide_fusion.3
  356.4 12.4 %collective-permute-done.33 = f32[3,5,1,128,128]{4,3,1,2,0:T(8,128)S(1)} collective-permute-done((f32[3,5,1,128,128]{4,3,1,2,0:T(8,128)S(1)}, f32[3,5,1,128,128]{4,3,1,2,0:T(8,128)S(1)}, u32[]{:S(2)}, u32[]{:S(2)}) %collective-permute-start.33) | collective-permute-done | bytes 983072 | tf_op jit(solution)/shard_map/ppermute | solution.py:14
  368.8 4.1 collective-permute-done.34
  377.7 32.5 %collective-permute-done.35 = f32[3,5,1,128,256]{4,3,1,2,0:T(8,128)S(1)} collective-permute-done((f32[3,5,1,128,256]{4,3,1,2,0:T(8,128)S(1)}, f32[3,5,1,128,256]{4,3,1,2,0:T(8,128)S(1)}, u32[]{:S(2)}, u32[]{:S(2)}) %collective-permute-start.35) | collective-permute-done | bytes 1966112 | tf_op jit(solution)/shard_map/ppermute | solution.py:31
  410.2 4.8 collective-permute-done.36
  418.5 23.5 %collective-permute-start.37 = (f32[3,5,1,128,256]{4,3,1,2,0:T(8,128)S(1)}, f32[3,5,1,128,256]{4,3,1,2,0:T(8,128)S(1)}, u32[]{:S(2)}, u32[]{:S(2)}) collective-permute-start(f32[3,5,1,128,256]{4,3,1,2,0:T(8,128)S(1)} %get-tuple-element.73), channel_id=1, source_target_pairs={{0,4},{2,6},{1,5},{3,7},{8,12},{10,14},{9,13},{11,15},{16,20},{18,... | collective-permute-start | bytes 5898248 | tf_op jit(solution)/shard_map/ppermute | solution.py:31
  442.1 56.3 %collective-permute-done.38 = f32[3,5,1,128,256]{4,3,2,1,0:T(8,128)S(1)} collective-permute-done((f32[3,5,1,128,256]{4,3,2,1,0:T(8,128)S(1)}, f32[3,5,1,128,256]{4,3,2,1,0:T(8,128)S(1)}, u32[]{:S(2)}, u32[]{:S(2)}) %collective-permute-start.38) | collective-permute-done | bytes 1966112 | tf_op jit(solution)/shard_map/ppermute | solution.py:31
  500.3 17.1 %fusion.31 = f32[5,1,128,256]{3,2,0,1:T(8,128)} fusion(f32[3,5,1,128,256]{4,3,2,1,0:T(8,128)} %copy-done.109, f32[3,5,1,128,256]{4,3,1,2,0:T(8,128)} %copy-done.108, f32[3,5,1,128,256]{4,3,1,2,0:T(8,128)} %bitcast.1176, f32[5,1,128,256]{3,2,0,1:T(8,128)} %copy-done.112, f32[1,5,1,128,256]{4,3,1,2,0:T(8,128)} %get-tuple-element.44, ...), kind=kLoop, calls=%fused_computation.57 | loop fusion | flops 39649280 | bytes 40082432 | tf_op jit(solution)/shard_map/div | solution.py:52
  (409 shorter events, 134.9 us)
Async XLA Ops:
  0.0 147.0 %copy-start = (f32[5,1024]{1,0:T(8,128)S(1)}, f32[5,1024]{1,0:T(8,128)}, u32[]{:S(2)}) copy-start(f32[5,1024]{1,0:T(8,128)} %param.17) | copy-start | bytes 61444
  0.0 19.3 %collective-permute-start = (f32[5,1,128,256]{3,2,1,0:T(8,128)}, f32[5,1,128,256]{3,2,1,0:T(8,128)S(1)}, u32[]{:S(2)}, u32[]{:S(2)}) collective-permute-start(f32[5,1,128,256]{3,2,1,0:T(8,128)} %param.11), channel_id=1, source_target_pairs={{0,1},{2,3},{4,5},{6,7},{8,9},{10,11},{12,13},{14,15},{16,17},{18,... | collective-permute-start | bytes 1966088 | tf_op jit(solution)/shard_map/ppermute | solution.py:14
  5.0 18.3 %collective-permute-start.1 = (f32[5,1,128,256]{3,2,1,0:T(8,128)}, f32[5,1,128,256]{3,2,1,0:T(8,128)S(1)}, u32[]{:S(2)}, u32[]{:S(2)}) collective-permute-start(f32[5,1,128,256]{3,2,1,0:T(8,128)} %param.11), channel_id=1, source_target_pairs={{1,0},{3,2},{5,4},{7,6},{9,8},{11,10},{13,12},{15,14},{17,16},{19,... | collective-permute-start | bytes 1966088 | tf_op jit(solution)/shard_map/ppermute | solution.py:17
  29.2 1.5 collective-permute-start.3
  29.2 3.4 collective-permute-start.2
  35.6 3.4 collective-permute-start.4
  36.8 2.2 collective-permute-start.5
  40.1 3.7 collective-permute-start.6
  41.6 2.2 collective-permute-start.7
  44.8 4.4 collective-permute-start.8
  46.4 3.0 collective-permute-start.9
  50.3 6.8 %collective-permute-start.10 = (f32[3,5,1,16,256]{4,3,2,1,0:T(8,128)S(1)}, f32[3,5,1,16,256]{4,3,2,1,0:T(8,128)S(1)}, u32[]{:S(2)}, u32[]{:S(2)}) collective-permute-start(f32[3,5,1,16,256]{4,3,2,1,0:T(8,128)S(1)} %get-tuple-element.95), channel_id=1, source_target_pairs={{0,8},{8,16},{16,24},{24,0},{1,9},{9,17},{17,25},{25,1},{2,10},{10... | collective-permute-start | bytes 737288 | tf_op jit(solution)/shard_map/ppermute | solution.py:14
  51.7 5.9 %collective-permute-start.11 = (f32[3,5,1,16,256]{4,3,2,1,0:T(8,128)S(1)}, f32[3,5,1,16,256]{4,3,2,1,0:T(8,128)S(1)}, u32[]{:S(2)}, u32[]{:S(2)}) collective-permute-start(f32[3,5,1,16,256]{4,3,2,1,0:T(8,128)S(1)} %get-tuple-element.96), channel_id=1, source_target_pairs={{8,0},{16,8},{24,16},{0,24},{9,1},{17,9},{25,17},{1,25},{10,2},{18... | collective-permute-start | bytes 737288 | tf_op jit(solution)/shard_map/ppermute | solution.py:17
  58.5 12.0 %collective-permute-start.12 = (f32[3,5,1,32,256]{4,3,2,1,0:T(8,128)S(1)}, f32[3,5,1,32,256]{4,3,2,1,0:T(8,128)S(1)}, u32[]{:S(2)}, u32[]{:S(2)}) collective-permute-start(f32[3,5,1,32,256]{4,3,2,1,0:T(8,128)S(1)} %get-tuple-element.93), channel_id=1, source_target_pairs={{0,8},{8,16},{16,24},{24,0},{1,9},{9,17},{17,25},{25,1},{2,10},{10... | collective-permute-start | bytes 1474568 | tf_op jit(solution)/shard_map/ppermute | solution.py:14
  59.6 11.6 %collective-permute-start.13 = (f32[3,5,1,32,256]{4,3,2,1,0:T(8,128)S(1)}, f32[3,5,1,32,256]{4,3,2,1,0:T(8,128)S(1)}, u32[]{:S(2)}, u32[]{:S(2)}) collective-permute-start(f32[3,5,1,32,256]{4,3,2,1,0:T(8,128)S(1)} %get-tuple-element.94), channel_id=1, source_target_pairs={{8,0},{16,8},{24,16},{0,24},{9,1},{17,9},{25,17},{1,25},{10,2},{18... | collective-permute-start | bytes 1474568 | tf_op jit(solution)/shard_map/ppermute | solution.py:17
  72.6 22.5 %collective-permute-start.14 = (f32[3,5,1,64,256]{4,3,2,1,0:T(8,128)S(1)}, f32[3,5,1,64,256]{4,3,2,1,0:T(8,128)S(1)}, u32[]{:S(2)}, u32[]{:S(2)}) collective-permute-start(f32[3,5,1,64,256]{4,3,2,1,0:T(8,128)S(1)} %get-tuple-element.92), channel_id=1, source_target_pairs={{0,8},{8,16},{16,24},{24,0},{1,9},{9,17},{17,25},{25,1},{2,10},{10... | collective-permute-start | bytes 2949128 | tf_op jit(solution)/shard_map/ppermute | solution.py:14
  73.6 22.2 %collective-permute-start.15 = (f32[3,5,1,64,256]{4,3,2,1,0:T(8,128)S(1)}, f32[3,5,1,64,256]{4,3,2,1,0:T(8,128)S(1)}, u32[]{:S(2)}, u32[]{:S(2)}) collective-permute-start(f32[3,5,1,64,256]{4,3,2,1,0:T(8,128)S(1)} %get-tuple-element.91), channel_id=1, source_target_pairs={{8,0},{16,8},{24,16},{0,24},{9,1},{17,9},{25,17},{1,25},{10,2},{18... | collective-permute-start | bytes 2949128 | tf_op jit(solution)/shard_map/ppermute | solution.py:17
  97.4 43.1 %collective-permute-start.16 = (f32[3,5,1,128,256]{4,3,1,2,0:T(8,128)S(1)}, f32[3,5,1,128,256]{4,3,1,2,0:T(8,128)S(1)}, u32[]{:S(2)}, u32[]{:S(2)}) collective-permute-start(f32[3,5,1,128,256]{4,3,1,2,0:T(8,128)S(1)} %pad_maximum_fusion.3), channel_id=1, source_target_pairs={{24,0},{0,8},{8,16},{16,24},{25,1},{1,9},{9,17},{17,25},{26,2},{2,... | collective-permute-start | bytes 5898248 | tf_op jit(solution)/shard_map/ppermute | solution.py:25
  98.3 43.6 %collective-permute-start.17 = (f32[3,5,1,128,256]{4,3,1,2,0:T(8,128)S(1)}, f32[3,5,1,128,256]{4,3,1,2,0:T(8,128)S(1)}, u32[]{:S(2)}, u32[]{:S(2)}) collective-permute-start(f32[3,5,1,128,256]{4,3,1,2,0:T(8,128)S(1)} %pad_maximum_fusion.3), channel_id=1, source_target_pairs={{8,0},{16,8},{24,16},{0,24},{9,1},{17,9},{25,17},{1,25},{10,2},{18... | collective-permute-start | bytes 5898248 | tf_op jit(solution)/shard_map/ppermute | solution.py:25
  144.7 45.7 %collective-permute-start.18 = (f32[3,5,1,128,256]{4,3,1,2,0:T(8,128)}, f32[3,5,1,128,256]{4,3,1,2,0:T(8,128)}, u32[]{:S(2)}, u32[]{:S(2)}) collective-permute-start(f32[3,5,1,128,256]{4,3,1,2,0:T(8,128)} %pad_maximum_fusion.4), channel_id=1, source_target_pairs={{16,0},{24,8},{0,16},{8,24},{17,1},{25,9},{1,17},{9,25},{18,2},{26... | collective-permute-start | bytes 5898248 | tf_op jit(solution)/shard_map/ppermute | solution.py:25
  147.0 43.4 %copy-start.16 = (f32[1,5,1,128,256]{4,3,1,2,0:T(8,128)S(1)}, f32[1,5,1,128,256]{4,3,1,2,0:T(8,128)}, u32[]{:S(2)}) copy-start(f32[1,5,1,128,256]{4,3,1,2,0:T(8,128)} %copy-done.15) | copy-start | bytes 1966084
  147.0 43.4 %copy-start.18 = (f32[1,5,1,128,256]{4,3,1,2,0:T(8,128)S(1)}, f32[1,5,1,128,256]{4,3,1,2,0:T(8,128)}, u32[]{:S(2)}) copy-start(f32[1,5,1,128,256]{4,3,1,2,0:T(8,128)} %copy-done.17) | copy-start | bytes 1966084
  147.0 43.4 %copy-start.105 = (f32[1,128,256]{2,1,0:T(8,128)S(1)}, f32[1,128,256]{2,1,0:T(8,128)}, u32[]{:S(2)}) copy-start(f32[1,128,256]{2,1,0:T(8,128)} %param.13) | copy-start | bytes 393220
  149.1 53.1 %copy-start.54 = (f32[1,5,1,128,256]{4,3,1,2,0:T(8,128)}, f32[1,5,1,128,256]{4,3,1,2,0:T(8,128)S(1)}, u32[]{:S(2)}) copy-start(f32[1,5,1,128,256]{4,3,1,2,0:T(8,128)S(1)} %fusion.23) | copy-start | bytes 1966084
  205.9 5.1 collective-permute-start.19
  209.8 5.6 %collective-permute-start.20 = (f32[3,5,1,128,1]{3,4,2,1,0:T(1,128)S(1)}, f32[3,5,1,128,1]{3,4,2,1,0:T(1,128)S(1)}, u32[]{:S(2)}, u32[]{:S(2)}) collective-permute-start(f32[3,5,1,128,1]{3,4,2,1,0:T(1,128)S(1)} %copy.248), channel_id=1, source_target_pairs={{2,0},{4,2},{6,4},{3,1},{5,3},{7,5},{10,8},{12,10},{14,12},{11,9},... | collective-permute-start | bytes 23048 | tf_op jit(solution)/shard_map/ppermute | solution.py:17
  227.8 5.2 collective-permute-start.21
  231.6 5.6 %collective-permute-start.22 = (f32[3,5,1,128,2]{3,4,2,1,0:T(2,128)S(1)}, f32[3,5,1,128,2]{3,4,2,1,0:T(2,128)S(1)}, u32[]{:S(2)}, u32[]{:S(2)}) collective-permute-start(f32[3,5,1,128,2]{3,4,2,1,0:T(2,128)S(1)} %copy.256), channel_id=1, source_target_pairs={{2,0},{4,2},{6,4},{3,1},{5,3},{7,5},{10,8},{12,10},{14,12},{11,9},... | collective-permute-start | bytes 46088 | tf_op jit(solution)/shard_map/ppermute | solution.py:17
  246.7 5.4 %collective-permute-start.23 = (f32[3,5,1,128,4]{3,4,2,1,0:T(4,128)S(1)}, f32[3,5,1,128,4]{3,4,2,1,0:T(4,128)S(1)}, u32[]{:S(2)}, u32[]{:S(2)}) collective-permute-start(f32[3,5,1,128,4]{3,4,2,1,0:T(4,128)S(1)} %copy.262), channel_id=1, source_target_pairs={{0,2},{2,4},{4,6},{1,3},{3,5},{5,7},{8,10},{10,12},{12,14},{9,11},... | collective-permute-start | bytes 92168 | tf_op jit(solution)/shard_map/ppermute | solution.py:14
  250.6 5.8 %collective-permute-start.24 = (f32[3,5,1,128,4]{3,4,2,1,0:T(4,128)S(1)}, f32[3,5,1,128,4]{3,4,2,1,0:T(4,128)S(1)}, u32[]{:S(2)}, u32[]{:S(2)}) collective-permute-start(f32[3,5,1,128,4]{3,4,2,1,0:T(4,128)S(1)} %copy.264), channel_id=1, source_target_pairs={{2,0},{4,2},{6,4},{3,1},{5,3},{7,5},{10,8},{12,10},{14,12},{11,9},... | collective-permute-start | bytes 92168 | tf_op jit(solution)/shard_map/ppermute | solution.py:17
  264.9 3.8 collective-permute-start.25
  267.1 6.1 %collective-permute-start.26 = (f32[3,5,1,128,8]{3,4,2,1,0:T(8,128)S(1)}, f32[3,5,1,128,8]{3,4,2,1,0:T(8,128)S(1)}, u32[]{:S(2)}, u32[]{:S(2)}) collective-permute-start(f32[3,5,1,128,8]{3,4,2,1,0:T(8,128)S(1)} %copy.272), channel_id=1, source_target_pairs={{2,0},{4,2},{6,4},{3,1},{5,3},{7,5},{10,8},{12,10},{14,12},{11,9},... | collective-permute-start | bytes 184328 | tf_op jit(solution)/shard_map/ppermute | solution.py:17
  282.3 4.4 collective-permute-start.27
  285.2 7.1 %collective-permute-start.28 = (f32[3,5,1,128,16]{3,4,2,1,0:T(8,128)}, f32[3,5,1,128,16]{3,4,2,1,0:T(8,128)}, u32[]{:S(2)}, u32[]{:S(2)}) collective-permute-start(f32[3,5,1,128,16]{3,4,2,1,0:T(8,128)} %copy.280), channel_id=1, source_target_pairs={{2,0},{4,2},{6,4},{3,1},{5,3},{7,5},{10,8},{12,10},{14,12},{11,9},... | collective-permute-start | bytes 368648 | tf_op jit(solution)/shard_map/ppermute | solution.py:17
  304.3 6.3 %collective-permute-start.29 = (f32[3,5,1,128,32]{3,4,2,1,0:T(8,128)}, f32[3,5,1,128,32]{3,4,2,1,0:T(8,128)}, u32[]{:S(2)}, u32[]{:S(2)}) collective-permute-start(f32[3,5,1,128,32]{3,4,2,1,0:T(8,128)} %copy.286), channel_id=1, source_target_pairs={{0,2},{2,4},{4,6},{1,3},{3,5},{5,7},{8,10},{10,12},{12,14},{9,11},... | collective-permute-start | bytes 737288 | tf_op jit(solution)/shard_map/ppermute | solution.py:14
  309.3 8.4 %collective-permute-start.30 = (f32[3,5,1,128,32]{3,4,2,1,0:T(8,128)}, f32[3,5,1,128,32]{3,4,2,1,0:T(8,128)}, u32[]{:S(2)}, u32[]{:S(2)}) collective-permute-start(f32[3,5,1,128,32]{3,4,2,1,0:T(8,128)} %copy.288), channel_id=1, source_target_pairs={{2,0},{4,2},{6,4},{3,1},{5,3},{7,5},{10,8},{12,10},{14,12},{11,9},... | collective-permute-start | bytes 737288 | tf_op jit(solution)/shard_map/ppermute | solution.py:17
  329.6 8.1 %collective-permute-start.31 = (f32[3,5,1,128,64]{3,4,2,1,0:T(8,128)}, f32[3,5,1,128,64]{3,4,2,1,0:T(8,128)}, u32[]{:S(2)}, u32[]{:S(2)}) collective-permute-start(f32[3,5,1,128,64]{3,4,2,1,0:T(8,128)} %copy.294), channel_id=1, source_target_pairs={{0,2},{2,4},{4,6},{1,3},{3,5},{5,7},{8,10},{10,12},{12,14},{9,11},... | collective-permute-start | bytes 1474568 | tf_op jit(solution)/shard_map/ppermute | solution.py:14
  334.2 11.0 %collective-permute-start.32 = (f32[3,5,1,128,64]{3,4,2,1,0:T(8,128)}, f32[3,5,1,128,64]{3,4,2,1,0:T(8,128)}, u32[]{:S(2)}, u32[]{:S(2)}) collective-permute-start(f32[3,5,1,128,64]{3,4,2,1,0:T(8,128)} %copy.296), channel_id=1, source_target_pairs={{2,0},{4,2},{6,4},{3,1},{5,3},{7,5},{10,8},{12,10},{14,12},{11,9},... | collective-permute-start | bytes 1474568 | tf_op jit(solution)/shard_map/ppermute | solution.py:17
  353.6 15.2 %collective-permute-start.33 = (f32[3,5,1,128,128]{4,3,1,2,0:T(8,128)S(1)}, f32[3,5,1,128,128]{4,3,1,2,0:T(8,128)S(1)}, u32[]{:S(2)}, u32[]{:S(2)}) collective-permute-start(f32[3,5,1,128,128]{4,3,1,2,0:T(8,128)S(1)} %get-tuple-element.76), channel_id=1, source_target_pairs={{0,2},{2,4},{4,6},{1,3},{3,5},{5,7},{8,10},{10,12},{12,14},{9,11},... | collective-permute-start | bytes 2949128 | tf_op jit(solution)/shard_map/ppermute | solution.py:14
  355.1 17.8 %collective-permute-start.34 = (f32[3,5,1,128,128]{4,3,1,2,0:T(8,128)S(1)}, f32[3,5,1,128,128]{4,3,1,2,0:T(8,128)S(1)}, u32[]{:S(2)}, u32[]{:S(2)}) collective-permute-start(f32[3,5,1,128,128]{4,3,1,2,0:T(8,128)S(1)} %get-tuple-element.75), channel_id=1, source_target_pairs={{2,0},{4,2},{6,4},{3,1},{5,3},{7,5},{10,8},{12,10},{14,12},{11,9},... | collective-permute-start | bytes 2949128 | tf_op jit(solution)/shard_map/ppermute | solution.py:17
  374.7 35.5 %collective-permute-start.35 = (f32[3,5,1,128,256]{4,3,1,2,0:T(8,128)S(1)}, f32[3,5,1,128,256]{4,3,1,2,0:T(8,128)S(1)}, u32[]{:S(2)}, u32[]{:S(2)}) collective-permute-start(f32[3,5,1,128,256]{4,3,1,2,0:T(8,128)S(1)} %pad_maximum_fusion.13), channel_id=1, source_target_pairs={{0,2},{2,4},{4,6},{1,3},{3,5},{5,7},{8,10},{10,12},{12,14},{9,11},... | collective-permute-start | bytes 5898248 | tf_op jit(solution)/shard_map/ppermute | solution.py:31
  376.4 38.6 %collective-permute-start.36 = (f32[3,5,1,128,256]{4,3,1,2,0:T(8,128)S(1)}, f32[3,5,1,128,256]{4,3,1,2,0:T(8,128)S(1)}, u32[]{:S(2)}, u32[]{:S(2)}) collective-permute-start(f32[3,5,1,128,256]{4,3,1,2,0:T(8,128)S(1)} %pad_maximum_fusion.13), channel_id=1, source_target_pairs={{2,0},{4,2},{6,4},{3,1},{5,3},{7,5},{10,8},{12,10},{14,12},{11,9},... | collective-permute-start | bytes 5898248 | tf_op jit(solution)/shard_map/ppermute | solution.py:31
  416.6 83.6 %copy-start.3 = (f32[1,5,1,128,256]{4,3,2,1,0:T(8,128)S(1)}, f32[1,5,1,128,256]{4,3,2,1,0:T(8,128)}, u32[]{:S(2)}) copy-start(f32[1,5,1,128,256]{4,3,2,1,0:T(8,128)} %copy-done.2) | copy-start | bytes 1966084
  416.7 83.6 %copy-start.5 = (f32[3,5,1,128,2]{4,3,1,2,0:T(8,128)S(1)}, f32[3,5,1,128,2]{4,3,1,2,0:T(8,128)}, u32[]{:S(2)}) copy-start(f32[3,5,1,128,2]{4,3,1,2,0:T(8,128)} %copy-done.4) | copy-start | bytes 46084
  416.7 83.6 %copy-start.7 = (f32[3,5,1,128,4]{4,3,1,2,0:T(8,128)S(1)}, f32[3,5,1,128,4]{4,3,1,2,0:T(8,128)}, u32[]{:S(2)}) copy-start(f32[3,5,1,128,4]{4,3,1,2,0:T(8,128)} %copy-done.6) | copy-start | bytes 92164
  416.7 83.6 %copy-start.9 = (f32[3,5,1,128,8]{4,3,1,2,0:T(8,128)S(1)}, f32[3,5,1,128,8]{4,3,1,2,0:T(8,128)}, u32[]{:S(2)}) copy-start(f32[3,5,1,128,8]{4,3,1,2,0:T(8,128)} %copy-done.8) | copy-start | bytes 184324
  417.0 81.4 %collective-permute-start.38 = (f32[3,5,1,128,256]{4,3,2,1,0:T(8,128)S(1)}, f32[3,5,1,128,256]{4,3,2,1,0:T(8,128)S(1)}, u32[]{:S(2)}, u32[]{:S(2)}) collective-permute-start(f32[3,5,1,128,256]{4,3,2,1,0:T(8,128)S(1)} %get-tuple-element.74), channel_id=1, source_target_pairs={{4,0},{6,2},{5,1},{7,3},{12,8},{14,10},{13,9},{15,11},{20,16},{22,... | collective-permute-start | bytes 5898248 | tf_op jit(solution)/shard_map/ppermute | solution.py:31
  418.5 79.9 %collective-permute-start.37 = (f32[3,5,1,128,256]{4,3,1,2,0:T(8,128)S(1)}, f32[3,5,1,128,256]{4,3,1,2,0:T(8,128)S(1)}, u32[]{:S(2)}, u32[]{:S(2)}) collective-permute-start(f32[3,5,1,128,256]{4,3,1,2,0:T(8,128)S(1)} %get-tuple-element.73), channel_id=1, source_target_pairs={{0,4},{2,6},{1,5},{3,7},{8,12},{10,14},{9,13},{11,15},{16,20},{18,... | collective-permute-start | bytes 5898248 | tf_op jit(solution)/shard_map/ppermute | solution.py:31
  (109 other events, 599.4 us)
where the time goes:
time: 531 us; the launch traced here: 521 us
  waiting for transfers between devices  278 us (52%)
  starting transfers between devices  82.7 us (16%)
  other arithmetic  82.4 us (16%)
  local copies, waits for them, and re-layouts  76.2 us (14%)
    ppermute x4, waiting for transfers between devices, passed_along(): return lax.ppermute(value, axis, pairs)  93.6 us
    ppermute x3, waiting for transfers between devices, from_behind(): return lax.ppermute(block, axis, route)  78.9 us
    ppermute x16, waiting for transfers between devices, with_halo(): lax.ppermute(lax.slice_in_dim(block, block.shape[dim] - width, None, axis...  67.8 us
    ppermute x16, waiting for transfers between devices, with_halo(): lax.ppermute(lax.slice_in_dim(block, 0, width, axis=dim), axis, backward)  37.6 us
    ppermute x16, starting transfers between devices, with_halo(): lax.ppermute(lax.slice_in_dim(block, block.shape[dim] - width, None, axis...  34.1 us
    div x2, other arithmetic, reduce_lines(): return stack[2] / (1.0 + stack[0] + stack[1])  28.3 us
    ppermute x4, starting transfers between devices, passed_along(): return lax.ppermute(value, axis, pairs)  28 us
    unnamed x244, local copies, waits for them, and re-layouts  22.9 us
  transfers between devices with their start and end apart: 39, of which 32 were waited for; matrix products, arithmetic and copies ran while one was open for 5% of the time, Pallas kernels for 0%

commit v1 on v0

v1 whole, which is shorter than its diff:
```python
import jax
import jax.numpy as jnp
from jax import lax
from jax.sharding import PartitionSpec as P


def with_halo(block, sides, width, periodic):
    for axis, dim in sides:
        count = lax.axis_size(axis)
        forward = [(i, i + 1) for i in range(count - 1)]
        if periodic:
            forward.append((count - 1, 0))
        backward = [(target, source) for source, target in forward]
        low = lax.ppermute(
            lax.slice_in_dim(block, block.shape[dim] - width, None, axis=dim), axis, forward
        )
        high = lax.ppermute(lax.slice_in_dim(block, 0, width, axis=dim), axis, backward)
        block = jnp.concatenate([low, block, high], axis=dim)
    return block


def shifted(values, offset, axis, periodic):
    if periodic:
        return jnp.roll(values, offset, axis)
    length = values.shape[axis]
    zero_shape = list(values.shape)
    zero_shape[axis] = abs(offset)
    zeros = jnp.zeros(zero_shape, values.dtype)
    if offset > 0:
        kept = lax.slice_in_dim(values, 0, length - offset, axis=axis)
        return jnp.concatenate([zeros, kept], axis=axis)
    kept = lax.slice_in_dim(values, -offset, length, axis=axis)
    return jnp.concatenate([kept, zeros], axis=axis)


def cyclic_reduce(lower, upper, rhs, axis, periodic, steps_below):
    stride = 1
    while stride < steps_below:
        ll, ul = shifted(lower, stride, axis, periodic), shifted(upper, stride, axis, periodic)
        lr, ur = shifted(lower, -stride, axis, periodic), shifted(upper, -stride, axis, periodic)
        inv = 1.0 / (1.0 - lower * ul - upper * lr)
        rhs = [
            (r - lower * shifted(r, stride, axis, periodic) - upper * shifted(r, -stride, axis, periodic)) * inv
            for r in rhs
        ]
        lower, upper = -lower * ll * inv, -upper * ur * inv
        stride = stride * 2
    return lower, upper, rhs


def row(values, index, axis):
    return lax.slice_in_dim(values, index, index + 1, axis=axis)


def solve_lines(lower, upper, target, axis, axis_name, periodic):
    length = lower.shape[axis]
    idx = lax.broadcasted_iota(jnp.int32, lower.shape, axis)
    edge = (idx == 0) | (idx == length - 1)
    second = idx == 1
    penult = idx == length - 2
    zero = jnp.zeros_like(lower)
    il = jnp.where(edge | second, zero, lower)
    iu = jnp.where(edge | penult, zero, upper)
    it = jnp.where(edge, zero, target)
    ia = jnp.where(second, lower, zero)
    ib = jnp.where(penult, upper, zero)
    _, _, (it, ia, ib) = cyclic_reduce(il, iu, [it, ia, ib], axis, False, length - 2)
    l0, u0, t0 = row(lower, 0, axis), row(upper, 0, axis), row(target, 0, axis)
    le, ue, te = (row(v, length - 1, axis) for v in (lower, upper, target))
    a1, b1, t1 = row(ia, 1, axis), row(ib, 1, axis), row(it, 1, axis)
    a2, b2, t2 = (row(v, length - 2, axis) for v in (ia, ib, it))
    inv_f = 1.0 / (1.0 - u0 * a1)
    inv_e = 1.0 / (1.0 - le * b2)
    red = jnp.stack(
        [
            jnp.concatenate([l0 * inv_f, -le * a2 * inv_e], axis=axis),
            jnp.concatenate([-u0 * b1 * inv_f, ue * inv_e], axis=axis),
            jnp.concatenate([(t0 - u0 * t1) * inv_f, (te - le * t2) * inv_e], axis=axis),
        ]
    )
    red = lax.all_gather(red, axis_name, axis=axis + 1, tiled=True)
    count = red.shape[axis + 1]
    rl, ru, (rt,) = cyclic_reduce(red[0], red[1], [red[2]], axis, periodic, count)
    ends = rt / (1.0 + rl + ru)
    mine = lax.dynamic_slice_in_dim(ends, 2 * lax.axis_index(axis_name), 2, axis)
    first, last = row(mine, 0, axis), row(mine, 1, axis)
    inner = it - ia * first - ib * last
    return jnp.where(idx == 0, first, jnp.where(idx == length - 1, last, inner))


def mix(matrix, values):
    mixed_rows = []
    for out_var in range(values.shape[0]):
        summed = values[out_var]
        for in_var in range(values.shape[0]):
            summed = summed + matrix[out_var, in_var][None, None, :] * values[in_var]
        mixed_rows.append(summed)
    return jnp.stack(mixed_rows)


def per_device(
    flow_state,
    source,
    cell_az,
    cell_rad,
    visc_az,
    beta_az,
    visc_rad,
    axial_diff,
    mix_in,
    mix_mid,
    mix_out,
):
    rad_cells = flow_state.shape[3]
    padded = with_halo(flow_state, (("ax", 1),), 1, False)
    explicit = source + axial_diff[:, None, None, :] * (
        padded[:, :-2] - 2.0 * flow_state + padded[:, 2:]
    )
    section_one = mix(mix_in, explicit)
    coupling = visc_az[:, None, None, :] * cell_az[None]
    centre = 1.0 + 2.0 * coupling
    tilt = beta_az[:, None, None, :]
    lower = -coupling * (1.0 + tilt) / centre
    upper = -coupling * (1.0 - tilt) / centre
    section_two = solve_lines(lower, upper, section_one / centre, 2, "az", True)
    section_three = mix(mix_mid, section_two)
    visc_local = lax.dynamic_slice_in_dim(visc_rad, lax.axis_index("rad") * rad_cells, rad_cells, 1)
    coupling = visc_local[:, None, None, :] * cell_rad[None]
    centre = 1.0 + 2.0 * coupling
    side = -coupling / centre
    section_four = solve_lines(side, side, section_three / centre, 3, "rad", False)
    return mix(mix_out, section_four)


def solution(mesh):
    in_specs = (
        P(None, "ax", "az", "rad"),
        P(None, "ax", "az", "rad"),
        P("ax", "az", "rad"),
        P("ax", "az", "rad"),
        P(None, "rad"),
        P(None, "rad"),
        P(),
        P(None, "rad"),
        P(None, None, "rad"),
        P(None, None, "rad"),
        P(None, None, "rad"),
    )
    out_specs = P(None, "ax", "az", "rad")
    return jax.shard_map(
        per_device, mesh=mesh, in_specs=in_specs, out_specs=out_specs, check_vma=False
    )
```

time: 531 us -> 133 us (0.25); the launches traced: 521 us -> 133 us
  waiting for transfers between devices: 278 us -> 0.01 us
  starting transfers between devices: 82.7 us -> 7.13 us
  other arithmetic: 82.4 us -> 32.1 us
  blocking collectives: 0 us -> 18.8 us
    ppermute x7 -> x0, waiting for transfers between devices: 172 us -> none  [the longest x4 93.6 us: passed_along(): return lax.ppermute(value, axis, pairs)]
    div x51 -> x2, other arithmetic: 69.2 us -> 0.08 us  [solve_lines(): ends = rt / (1.0 + rl + ru)]
    ppermute x16 -> x1, waiting for transfers between devices: 67.8 us -> 0.01 us  [with_halo(): lax.ppermute(lax.slice_in_dim(block, block.shape[dim] - width, None, axis...]
    ppermute x16 -> x1, waiting for transfers between devices: 37.6 us -> 0.01 us  [with_halo(): lax.ppermute(lax.slice_in_dim(block, 0, width, axis=dim), axis, backward)]
    ppermute x7 -> x0, starting transfers between devices: 32.4 us -> none  [the longest x4 28 us: passed_along(): return lax.ppermute(value, axis, pairs)]
    ppermute x16 -> x1, starting transfers between devices: 34.1 us -> 5.85 us  [with_halo(): lax.ppermute(lax.slice_in_dim(block, block.shape[dim] - width, None, axis...]
    all_gather x0 -> x2, blocking collectives: none -> 18.8 us  [solve_lines(): red = lax.all_gather(red, axis_name, axis=axis + 1, tiled=True)]
    mul x0 -> x39, other arithmetic: none -> 17.8 us  [the longest x27 17.3 us: cyclic_reduce(): (r - lower * shifted(r, stride, axis, periodic) - upper * shifted(r, -str...]
  transfers between devices with their start and end apart: 39 -> 2, of which waited for: 32 -> 0; matrix products, arithmetic and copies ran while one was open for 5% -> 16% of each run, Pallas kernels for 0% -> 0%
where the time goes in v1:
time: 133 us
  local copies, waits for them, and re-layouts  72.3 us (54%)
  other arithmetic  32.1 us (24%)
  blocking collectives  18.8 us (14%)
  starting transfers between devices  7.13 us (5%)
  between operations  2.46 us (2%)
    all_gather x2, blocking collectives, solve_lines(): red = lax.all_gather(red, axis_name, axis=axis + 1, tiled=True)  18.8 us
    mul x27, other arithmetic, cyclic_reduce(): (r - lower * shifted(r, stride, axis, periodic) - upper * shifted(r, -str...  17.3 us
    slice x18, local copies, waits for them, and re-layouts, shifted(): kept = lax.slice_in_dim(values, -offset, length, axis=axis)  17.1 us
    unnamed x250, local copies, waits for them, and re-layouts  16 us
    slice x65, local copies, waits for them, and re-layouts, shifted(): kept = lax.slice_in_dim(values, 0, length - offset, axis=axis)  13 us
    slice x10, local copies, waits for them, and re-layouts, row(): return lax.slice_in_dim(values, index, index + 1, axis=axis)  11.2 us
    ppermute x1, starting transfers between devices, with_halo(): lax.ppermute(lax.slice_in_dim(block, block.shape[dim] - width, None, axis...  5.85 us
    slice x6, local copies, waits for them, and re-layouts, mix(): summed = summed + matrix[out_var, in_var][None, None, :] * values[in_var]  5.65 us
  transfers between devices with their start and end apart: 2, of which 0 were waited for; matrix products, arithmetic and copies ran while one was open for 16% of the time, Pallas kernels for 0%

profile of v1, /device:TPU:0, one launch (start us, length us, event | category | flops | bytes accessed | tf_op | source)
XLA Modules:
  0.0 132.8 jit_solution(3103718862489715797)
XLA Ops:
  0.0 5.9 %collective-permute-start = (f32[5,1,128,256]{3,2,1,0:T(8,128)}, f32[5,1,128,256]{3,2,1,0:T(8,128)}, u32[]{:S(2)}, u32[]{:S(2)}) collective-permute-start(f32[5,1,128,256]{3,2,1,0:T(8,128)} %param.11), channel_id=1, source_target_pairs={{0,1},{2,3},{4,5},{6,7},{8,9},{10,11},{12,13},{14,15},{16,17},{18,... | collective-permute-start | bytes 1966088 | tf_op jit(solution)/shard_map/ppermute | solution.py:14
  5.9 1.3 collective-permute-start.1
  7.1 1.7 %fusion.189 = (f32[1,1,256]{2,1,0:T(1,128)}, f32[1,1,256]{2,1,0:T(1,128)}, f32[1,1,256]{2,1,0:T(1,128)}, f32[1,1,256]{2,1,0:T(1,128)}, f32[1,1,256]{2,1,0:T(1,12...) fusion(f32[5,5,256]{2,1,0:T(8,128)} %param.19), kind=kLoop, calls=%fused_computation.382 | loop fusion | bytes 38912 | tf_op jit(solution)/shard_map/slice | solution.py:96
  8.8 1.4 %fusion.190 = (f32[1,1,256]{2,1,0:T(1,128)}, f32[1,1,256]{2,1,0:T(1,128)}, f32[1,1,256]{2,1,0:T(1,128)}, f32[1,1,256]{2,1,0:T(1,128)}, f32[1,1,256]{2,1,0:T(1,128)}, /*index=5*/f32[1,1,256]{2,1,0:T(1,128)}) fusion(f32[5,5,256]{2,1,0:T(8,128)} %param.19), kind=kLoop, calls=%fused_computation.383 | loop fusion | bytes 12288 | tf_op jit(solution)/shard_map/slice | solution.py:96
  10.3 1.4 %copy.384 = f32[5,1,128,256]{2,3,1,0:T(8,128)S(1)} copy(f32[5,1,128,256]{3,2,1,0:T(8,128)} %param.11) | data formatting | bytes 1310720 | tf_op args[0]
  13.4 0.7 fusion.187
  15.7 0.7 fusion.185
  17.0 1.1 copy.387
  19.4 1.1 fusion.137
  20.5 1.3 fusion.138
  21.8 1.2 fusion.139
  23.6 0.9 fusion.165
  25.1 1.2 fusion.166
  26.2 1.2 fusion.167
  27.5 1.3 copy.385
  28.8 2.2 %copy.386 = f32[5,1,128,256]{2,3,1,0:T(8,128)} copy(f32[5,1,128,256]{3,2,1,0:T(8,128)} %collective-permute-done.1) | data formatting | bytes 1310720 | tf_op jit(solution)/shard_map/ppermute | solution.py:17
  31.1 1.3 multiply_add_fusion
  37.2 1.1 subtract_multiply_fusion.28
  38.8 0.8 copy-done.3
  39.6 1.5 %subtract_multiply_fusion.14 = (f32[5,1,128,256]{2,3,1,0:T(8,128)S(1)}, f32[5,1,128,256]{2,3,1,0:T(8,128)S(1)}, f32[5,1,128,256]{2,3,1,0:T(8,128)S(1)}, f32[5,1,128,256]{2,3,1,0:T(8,128)S(1)}) fusion(f32[5,1,128,256]{2,3,1,0:T(8,128)S(1)} %get-tuple-element.38, f32[5,1,127,256]{2,3,1,0:T(8,128)S(1)} %get-tuple-element.151, ...), kind=kLoop, calls=%fused_computation.37 | loop fusion | flops 4423680 | bytes 7980416 | tf_op jit(solution)/shard_map/mul | solution.py:43
  42.8 0.9 subtract_multiply_fusion.13
  45.4 0.9 subtract_multiply_fusion.12
  48.0 0.9 subtract_multiply_fusion.11
  50.6 0.9 subtract_multiply_fusion.10
  53.2 0.9 subtract_multiply_fusion.9
  54.6 13.0 %slice.1468 = f32[5,1,64,256]{2,3,1,0:T(8,128)S(1)} slice(f32[5,1,128,256]{2,3,1,0:T(8,128)S(1)} %get-tuple-element.86), slice={[0:5], [0:1], [64:128], [0:256]} | slice | bytes 655360 | tf_op jit(solution)/shard_map/slice | solution.py:32
  67.8 0.9 subtract_multiply_fusion.22
  68.7 3.4 %fusion.104 = (f32[5,1,1,256]{2,3,1,0:T(8,128)}, f32[5,1,1,256]{2,3,1,0:T(8,128)}, f32[5,1,1,256]{2,3,1,0:T(8,128)}, f32[5,1,1,256]{2,3,1,0:T(8,128)}, f32[5,1,1...) fusion(f32[5,1,128,256]{2,3,1,0:T(8,128)S(1)} %get-tuple-element.262, ...), kind=kLoop, calls=%fused_computation.297 | loop fusion | flops 12800 | bytes 81920 | tf_op jit(solution)/shard_map/slice | solution.py:52
  72.1 1.3 copy.376
  73.4 1.3 copy.377
  74.7 1.3 copy.380
  76.0 1.3 copy.393
  77.4 1.5 %fusion.105 = (f32[5,1,1,256]{2,3,1,0:T(8,128)}, f32[5,1,1,256]{2,3,1,0:T(8,128)}) fusion(f32[5,1,128,256]{2,3,1,0:T(8,128)S(1)} %get-tuple-element.43), kind=kLoop, calls=%fused_computation.298 | loop fusion | bytes 20480 | tf_op jit(solution)/shard_map/slice | solution.py:52
  78.8 1.3 copy.394
  80.1 1.3 fusion.106
  81.4 1.4 %copy.395 = f32[5,1,1,256]{3,2,1,0:T(1,128)S(1)} copy(f32[5,1,1,256]{2,3,1,0:T(8,128)} %get-tuple-element.134) | data formatting | bytes 10240 | tf_op jit(solution)/shard_map/slice | solution.py:52
  83.0 1.4 %copy.379 = f32[5,1,1,256]{3,2,1,0:T(1,128)S(1)} copy(f32[5,1,1,256]{2,3,1,0:T(8,128)} %get-tuple-element.128) | data formatting | bytes 10240 | tf_op jit(solution)/shard_map/div | solution.py:73
  84.4 1.3 copy.382
  86.0 1.4 %copy.398 = f32[5,1,1,256]{3,2,1,0:T(1,128)S(1)} copy(f32[5,1,1,256]{2,3,1,0:T(8,128)} %get-tuple-element.133) | data formatting | bytes 10240 | tf_op jit(solution)/shard_map/slice | solution.py:52
  87.8 5.4 %all_gather.6 = f32[3,5,1,8,256]{4,2,1,0,3:T(1,128)S(1)} all-gather(f32[3,5,1,2,256]{4,2,1,0,3:T(1,128)S(1)} %copy.401), channel_id=1, replica_groups=mesh['az'=4,'rad'=4,'ax'=2] {'az'}, dimensions={3}, use_global_device_ids=true | all-gather | bytes 153600 | tf_op jit(solution)/shard_map/all_gather | solution.py:81
  93.8 0.6 copy-done.118
  99.8 1.0 broadcast_select_fusion
  101.0 1.0 copy-done.2
  102.0 1.1 subtract_multiply_fusion.7
  104.0 0.7 subtract_multiply_fusion.6
  105.6 0.7 subtract_multiply_fusion.5
  112.4 13.3 %all_gather.7 = f32[3,5,1,128,8]{3,2,1,0,4:T(1,128)S(1)} all-gather(f32[3,5,1,128,2]{3,2,1,0,4:T(1,128)S(1)} %copy.410), channel_id=1, replica_groups=mesh['az'=4,'rad'=4,'ax'=2] {'rad'}, dimensions={4}, use_global_device_ids=true | all-gather | bytes 76800 | tf_op jit(solution)/shard_map/all_gather | solution.py:81
  131.5 1.1 copy.419
  (420 shorter events, 39.5 us)
Async XLA Ops:
  0.0 23.2 %copy-start = (f32[5,1024]{1,0:T(8,128)S(1)}, f32[5,1024]{1,0:T(8,128)}, u32[]{:S(2)}) copy-start(f32[5,1024]{1,0:T(8,128)} %param.17) | copy-start | bytes 61444
  0.0 27.5 %collective-permute-start = (f32[5,1,128,256]{3,2,1,0:T(8,128)}, f32[5,1,128,256]{3,2,1,0:T(8,128)}, u32[]{:S(2)}, u32[]{:S(2)}) collective-permute-start(f32[5,1,128,256]{3,2,1,0:T(8,128)} %param.11), channel_id=1, source_target_pairs={{0,1},{2,3},{4,5},{6,7},{8,9},{10,11},{12,13},{14,15},{16,17},{18,... | collective-permute-start | bytes 1966088 | tf_op jit(solution)/shard_map/ppermute | solution.py:14
  5.9 23.0 %collective-permute-start.1 = (f32[5,1,128,256]{3,2,1,0:T(8,128)}, f32[5,1,128,256]{3,2,1,0:T(8,128)}, u32[]{:S(2)}, u32[]{:S(2)}) collective-permute-start(f32[5,1,128,256]{3,2,1,0:T(8,128)} %param.11), channel_id=1, source_target_pairs={{1,0},{3,2},{5,4},{7,6},{9,8},{11,10},{13,12},{15,14},{17,16},{19,... | collective-permute-start | bytes 1966088 | tf_op jit(solution)/shard_map/ppermute | solution.py:17
  10.3 3.1 %copy-start.23 = (f32[5,5,256]{2,1,0:T(8,128)S(1)}, f32[5,5,256]{2,1,0:T(8,128)}, u32[]{:S(2)}) copy-start(f32[5,5,256]{2,1,0:T(8,128)} %param.20) | copy-start | bytes 76804
  10.3 6.7 %copy-start.16 = (f32[5,1,128,256]{3,2,1,0:T(8,128)S(1)}, f32[5,1,128,256]{3,2,1,0:T(8,128)}, u32[]{:S(2)}) copy-start(f32[5,1,128,256]{3,2,1,0:T(8,128)} %param.12) | copy-start | bytes 1966084
  11.7 6.5 %copy-start.30 = (pred[128]{0:T(512)(128)(4,1)}, pred[128]{0:T(512)(128)(4,1)S(1)}, u32[]{:S(2)}) copy-start(pred[128]{0:T(512)(128)(4,1)S(1)} %get-tuple-element.426) | copy-start | bytes 388
  11.7 6.5 %copy-start.32 = (pred[128]{0:T(512)(128)(4,1)}, pred[128]{0:T(512)(128)(4,1)S(1)}, u32[]{:S(2)}) copy-start(pred[128]{0:T(512)(128)(4,1)S(1)} %get-tuple-element.427) | copy-start | bytes 388
  12.2 6.0 %copy-start.113 = (pred[128]{0:T(512)(128)(4,1)}, pred[128]{0:T(512)(128)(4,1)S(1)}, u32[]{:S(2)}) copy-start(pred[128]{0:T(512)(128)(4,1)S(1)} %get-tuple-element.431) | copy-start | bytes 388
  12.8 2.9 %copy-start.24 = (f32[5,5,256]{2,1,0:T(8,128)S(1)}, f32[5,5,256]{2,1,0:T(8,128)}, u32[]{:S(2)}) copy-start(f32[5,5,256]{2,1,0:T(8,128)} %param.21) | copy-start | bytes 76804
  14.7 8.5 %copy-start.26 = (pred[256]{0:T(512)(128)(4,1)}, pred[256]{0:T(512)(128)(4,1)S(1)}, u32[]{:S(2)}) copy-start(pred[256]{0:T(512)(128)(4,1)S(1)} %get-tuple-element.428) | copy-start | bytes 772
  14.7 8.5 %copy-start.28 = (pred[256]{0:T(512)(128)(4,1)}, pred[256]{0:T(512)(128)(4,1)S(1)}, u32[]{:S(2)}) copy-start(pred[256]{0:T(512)(128)(4,1)S(1)} %get-tuple-element.429) | copy-start | bytes 772
  15.2 8.0 %copy-start.110 = (pred[256]{0:T(512)(128)(4,1)}, pred[256]{0:T(512)(128)(4,1)S(1)}, u32[]{:S(2)}) copy-start(pred[256]{0:T(512)(128)(4,1)S(1)} %get-tuple-element.433) | copy-start | bytes 772
  28.8 2.3 %copy-start.11 = (f32[5,1,128,256]{2,3,1,0:T(8,128)S(1)}, f32[5,1,128,256]{2,3,1,0:T(8,128)}, u32[]{:S(2)}) copy-start(f32[5,1,128,256]{2,3,1,0:T(8,128)} %copy.387) | copy-start | bytes 1966084
  34.0 2.5 %copy-start.15 = (f32[5,1,127,256]{2,3,1,0:T(8,128)S(1)}, f32[5,1,127,256]{2,3,1,0:T(8,128)}, u32[]{:S(2)}) copy-start(f32[5,1,127,256]{2,3,1,0:T(8,128)} %get-tuple-element.201) | copy-start | bytes 1950724
  34.9 1.6 %copy-start.14 = (f32[5,1,127,256]{2,3,1,0:T(8,128)S(1)}, f32[5,1,127,256]{2,3,1,0:T(8,128)}, u32[]{:S(2)}) copy-start(f32[5,1,127,256]{2,3,1,0:T(8,128)} %get-tuple-element.200) | copy-start | bytes 1950724
  83.0 2.7 %copy-start.4 = (f32[5,1,1,256]{2,3,1,0:T(8,128)S(1)}, f32[5,1,1,256]{2,3,1,0:T(8,128)}, u32[]{:S(2)}) copy-start(f32[5,1,1,256]{2,3,1,0:T(8,128)} %get-tuple-element.131) | copy-start | bytes 15364
  94.5 2.3 %copy-start.68 = (f32[1,1,256]{2,1,0:T(1,128)S(1)}, f32[1,1,256]{2,1,0:T(1,128)}, u32[]{:S(2)}) copy-start(f32[1,1,256]{2,1,0:T(1,128)} %get-tuple-element.351) | copy-start | bytes 3076
  94.6 2.3 %copy-start.69 = (f32[1,1,256]{2,1,0:T(1,128)S(1)}, f32[1,1,256]{2,1,0:T(1,128)}, u32[]{:S(2)}) copy-start(f32[1,1,256]{2,1,0:T(1,128)} %get-tuple-element.352) | copy-start | bytes 3076
  94.6 2.3 %copy-start.70 = (f32[1,1,256]{2,1,0:T(1,128)S(1)}, f32[1,1,256]{2,1,0:T(1,128)}, u32[]{:S(2)}) copy-start(f32[1,1,256]{2,1,0:T(1,128)} %get-tuple-element.353) | copy-start | bytes 3076
  94.6 2.3 %copy-start.71 = (f32[1,1,256]{2,1,0:T(1,128)S(1)}, f32[1,1,256]{2,1,0:T(1,128)}, u32[]{:S(2)}) copy-start(f32[1,1,256]{2,1,0:T(1,128)} %get-tuple-element.354) | copy-start | bytes 3076
  95.7 2.1 %copy-start.63 = (f32[1,1,256]{2,1,0:T(1,128)S(1)}, f32[1,1,256]{2,1,0:T(1,128)}, u32[]{:S(2)}) copy-start(f32[1,1,256]{2,1,0:T(1,128)} %get-tuple-element.346) | copy-start | bytes 3076
  95.7 2.1 %copy-start.64 = (f32[1,1,256]{2,1,0:T(1,128)S(1)}, f32[1,1,256]{2,1,0:T(1,128)}, u32[]{:S(2)}) copy-start(f32[1,1,256]{2,1,0:T(1,128)} %get-tuple-element.347) | copy-start | bytes 3076
  95.7 2.1 %copy-start.65 = (f32[1,1,256]{2,1,0:T(1,128)S(1)}, f32[1,1,256]{2,1,0:T(1,128)}, u32[]{:S(2)}) copy-start(f32[1,1,256]{2,1,0:T(1,128)} %get-tuple-element.348) | copy-start | bytes 3076
  95.7 2.1 %copy-start.66 = (f32[1,1,256]{2,1,0:T(1,128)S(1)}, f32[1,1,256]{2,1,0:T(1,128)}, u32[]{:S(2)}) copy-start(f32[1,1,256]{2,1,0:T(1,128)} %get-tuple-element.349) | copy-start | bytes 3076
  96.6 2.1 %copy-start.59 = (f32[1,1,256]{2,1,0:T(1,128)S(1)}, f32[1,1,256]{2,1,0:T(1,128)}, u32[]{:S(2)}) copy-start(f32[1,1,256]{2,1,0:T(1,128)} %get-tuple-element.342) | copy-start | bytes 3076
  96.6 2.1 %copy-start.60 = (f32[1,1,256]{2,1,0:T(1,128)S(1)}, f32[1,1,256]{2,1,0:T(1,128)}, u32[]{:S(2)}) copy-start(f32[1,1,256]{2,1,0:T(1,128)} %get-tuple-element.343) | copy-start | bytes 3076
  96.6 2.1 %copy-start.61 = (f32[1,1,256]{2,1,0:T(1,128)S(1)}, f32[1,1,256]{2,1,0:T(1,128)}, u32[]{:S(2)}) copy-start(f32[1,1,256]{2,1,0:T(1,128)} %get-tuple-element.344) | copy-start | bytes 3076
  96.6 2.1 %copy-start.72 = (f32[1,1,256]{2,1,0:T(1,128)S(1)}, f32[1,1,256]{2,1,0:T(1,128)}, u32[]{:S(2)}) copy-start(f32[1,1,256]{2,1,0:T(1,128)} %get-tuple-element.361) | copy-start | bytes 3076
  96.6 2.1 %copy-start.73 = (f32[1,1,256]{2,1,0:T(1,128)S(1)}, f32[1,1,256]{2,1,0:T(1,128)}, u32[]{:S(2)}) copy-start(f32[1,1,256]{2,1,0:T(1,128)} %get-tuple-element.366) | copy-start | bytes 3076
  96.6 2.4 %copy-start.9 = (f32[5,1,128,255]{2,3,1,0:T(8,128)S(1)}, f32[5,1,128,255]{2,3,1,0:T(8,128)}, u32[]{:S(2)}) copy-start(f32[5,1,128,255]{2,3,1,0:T(8,128)} %get-tuple-element.257) | copy-start | bytes 1958404
  97.5 1.5 %copy-start.111 = (pred[256]{0:T(512)(128)(4,1)S(1)}, pred[256]{0:T(512)(128)(4,1)}, u32[]{:S(2)}) copy-start(pred[256]{0:T(512)(128)(4,1)} %copy-done.110) | copy-start | bytes 772
  97.5 1.5 %copy-start.117 = (pred[256]{0:T(512)(128)(4,1)S(1)}, pred[256]{0:T(512)(128)(4,1)}, u32[]{:S(2)}) copy-start(pred[256]{0:T(512)(128)(4,1)} %get-tuple-element.423) | copy-start | bytes 772
  126.0 2.0 %copy-start.50 = (f32[1,1,256]{2,1,0:T(1,128)S(1)}, f32[1,1,256]{2,1,0:T(1,128)}, u32[]{:S(2)}) copy-start(f32[1,1,256]{2,1,0:T(1,128)} %get-tuple-element.331) | copy-start | bytes 3076
  126.0 2.0 %copy-start.51 = (f32[1,1,256]{2,1,0:T(1,128)S(1)}, f32[1,1,256]{2,1,0:T(1,128)}, u32[]{:S(2)}) copy-start(f32[1,1,256]{2,1,0:T(1,128)} %get-tuple-element.332) | copy-start | bytes 3076
  126.0 2.0 %copy-start.52 = (f32[1,1,256]{2,1,0:T(1,128)S(1)}, f32[1,1,256]{2,1,0:T(1,128)}, u32[]{:S(2)}) copy-start(f32[1,1,256]{2,1,0:T(1,128)} %get-tuple-element.333) | copy-start | bytes 3076
  126.0 2.0 %copy-start.53 = (f32[1,1,256]{2,1,0:T(1,128)S(1)}, f32[1,1,256]{2,1,0:T(1,128)}, u32[]{:S(2)}) copy-start(f32[1,1,256]{2,1,0:T(1,128)} %get-tuple-element.334) | copy-start | bytes 3076
  126.2 2.7 %copy-start.43 = (f32[1,1,256]{2,1,0:T(1,128)S(1)}, f32[1,1,256]{2,1,0:T(1,128)}, u32[]{:S(2)}) copy-start(f32[1,1,256]{2,1,0:T(1,128)} %get-tuple-element.326) | copy-start | bytes 3076
  126.2 2.7 %copy-start.44 = (f32[1,1,256]{2,1,0:T(1,128)S(1)}, f32[1,1,256]{2,1,0:T(1,128)}, u32[]{:S(2)}) copy-start(f32[1,1,256]{2,1,0:T(1,128)} %get-tuple-element.327) | copy-start | bytes 3076
  126.2 2.7 %copy-start.45 = (f32[1,1,256]{2,1,0:T(1,128)S(1)}, f32[1,1,256]{2,1,0:T(1,128)}, u32[]{:S(2)}) copy-start(f32[1,1,256]{2,1,0:T(1,128)} %get-tuple-element.328) | copy-start | bytes 3076
  126.2 2.7 %copy-start.46 = (f32[1,1,256]{2,1,0:T(1,128)S(1)}, f32[1,1,256]{2,1,0:T(1,128)}, u32[]{:S(2)}) copy-start(f32[1,1,256]{2,1,0:T(1,128)} %get-tuple-element.329) | copy-start | bytes 3076
  126.9 3.0 %copy-start.38 = (f32[1,1,256]{2,1,0:T(1,128)S(1)}, f32[1,1,256]{2,1,0:T(1,128)}, u32[]{:S(2)}) copy-start(f32[1,1,256]{2,1,0:T(1,128)} %get-tuple-element.321) | copy-start | bytes 3076
  126.9 3.0 %copy-start.39 = (f32[1,1,256]{2,1,0:T(1,128)S(1)}, f32[1,1,256]{2,1,0:T(1,128)}, u32[]{:S(2)}) copy-start(f32[1,1,256]{2,1,0:T(1,128)} %get-tuple-element.322) | copy-start | bytes 3076
  126.9 3.0 %copy-start.40 = (f32[1,1,256]{2,1,0:T(1,128)S(1)}, f32[1,1,256]{2,1,0:T(1,128)}, u32[]{:S(2)}) copy-start(f32[1,1,256]{2,1,0:T(1,128)} %get-tuple-element.323) | copy-start | bytes 3076
  126.9 3.0 %copy-start.41 = (f32[1,1,256]{2,1,0:T(1,128)S(1)}, f32[1,1,256]{2,1,0:T(1,128)}, u32[]{:S(2)}) copy-start(f32[1,1,256]{2,1,0:T(1,128)} %get-tuple-element.324) | copy-start | bytes 3076
  126.9 3.8 %copy-start.35 = (f32[1,1,256]{2,1,0:T(1,128)S(1)}, f32[1,1,256]{2,1,0:T(1,128)}, u32[]{:S(2)}) copy-start(f32[1,1,256]{2,1,0:T(1,128)} %get-tuple-element.318) | copy-start | bytes 3076
  126.9 3.8 %copy-start.36 = (f32[1,1,256]{2,1,0:T(1,128)S(1)}, f32[1,1,256]{2,1,0:T(1,128)}, u32[]{:S(2)}) copy-start(f32[1,1,256]{2,1,0:T(1,128)} %get-tuple-element.319) | copy-start | bytes 3076
  126.9 3.8 %copy-start.47 = (f32[1,1,256]{2,1,0:T(1,128)S(1)}, f32[1,1,256]{2,1,0:T(1,128)}, u32[]{:S(2)}) copy-start(f32[1,1,256]{2,1,0:T(1,128)} %get-tuple-element.336) | copy-start | bytes 3076
  126.9 3.8 %copy-start.48 = (f32[1,1,256]{2,1,0:T(1,128)S(1)}, f32[1,1,256]{2,1,0:T(1,128)}, u32[]{:S(2)}) copy-start(f32[1,1,256]{2,1,0:T(1,128)} %get-tuple-element.341) | copy-start | bytes 3076
  (75 other events, 69.6 us)

commit v2 on v1

--- a/solution.py
+++ b/solution.py
@@ -1,7 +1,10 @@
 import jax
 import jax.numpy as jnp
 from jax import lax
+from jax.experimental import pallas as pl
+from jax.experimental.pallas import tpu as pltpu
 from jax.sharding import PartitionSpec as P
+import functools
 
 
 def with_halo(block, sides, width, periodic):
@@ -48,11 +51,10 @@
     return lower, upper, rhs
 
 
-def row(values, index, axis):
-    return lax.slice_in_dim(values, index, index + 1, axis=axis)
-
-
-def solve_lines(lower, upper, target, axis, axis_name, periodic):
+def local_kernel(l_ref, u_ref, t_ref, ot_ref, oa_ref, ob_ref, *, axis):
+    lower = l_ref[0, 0]
+    upper = u_ref[0, 0]
+    target = t_ref[0, 0]
     length = lower.shape[axis]
     idx = lax.broadcasted_iota(jnp.int32, lower.shape, axis)
     edge = (idx == 0) | (idx == length - 1)
@@ -61,10 +63,42 @@
     zero = jnp.zeros_like(lower)
     il = jnp.where(edge | second, zero, lower)
     iu = jnp.where(edge | penult, zero, upper)
-    it = jnp.where(edge, zero, target)
-    ia = jnp.where(second, lower, zero)
-    ib = jnp.where(penult, upper, zero)
-    _, _, (it, ia, ib) = cyclic_reduce(il, iu, [it, ia, ib], axis, False, length - 2)
+    rhs = [jnp.where(edge, zero, target), jnp.where(second, lower, zero), jnp.where(penult, upper, zero)]
+    stride = 1
+    while stride < length - 2:
+        back = length - stride
+        ll, ul = pltpu.roll(il, stride, axis), pltpu.roll(iu, stride, axis)
+        lr, ur = pltpu.roll(il, back, axis), pltpu.roll(iu, back, axis)
+        inv = 1.0 / (1.0 - il * ul - iu * lr)
+        rhs = [(r - il * pltpu.roll(r, stride, axis) - iu * pltpu.roll(r, back, axis)) * inv for r in rhs]
+        il, iu = -il * ll * inv, -iu * ur * inv
+        stride = stride * 2
+    ot_ref[0, 0] = rhs[0]
+    oa_ref[0, 0] = rhs[1]
+    ob_ref[0, 0] = rhs[2]
+
+
+def local_reduce(lower, upper, target, axis):
+    nv, nz, na, nr = lower.shape
+    spec = pl.BlockSpec((1, 1, na, nr), lambda v, z: (v, z, 0, 0))
+    out = jax.ShapeDtypeStruct(lower.shape, lower.dtype)
+    return pl.pallas_call(
+        functools.partial(local_kernel, axis=axis - 2),
+        grid=(nv, nz),
+        in_specs=[spec, spec, spec],
+        out_specs=[spec, spec, spec],
+        out_shape=[out, out, out],
+    )(lower, upper, target)
+
+
+def row(values, index, axis):
+    return lax.slice_in_dim(values, index, index + 1, axis=axis)
+
+
+def solve_lines(lower, upper, target, axis, axis_name, periodic):
+    length = lower.shape[axis]
+    idx = lax.broadcasted_iota(jnp.int32, lower.shape, axis)
+    it, ia, ib = local_reduce(lower, upper, target, axis)
     l0, u0, t0 = row(lower, 0, axis), row(upper, 0, axis), row(target, 0, axis)
     le, ue, te = (row(v, length - 1, axis) for v in (lower, upper, target))
     a1, b1, t1 = row(ia, 1, axis), row(ib, 1, axis), row(it, 1, axis)

time: 133 us -> 80.7 us (0.61)
  local copies, waits for them, and re-layouts: 72.3 us -> 11 us
  other arithmetic: 32.1 us -> 11.2 us
  Pallas kernels: 0 us -> 20.8 us
  waiting for transfers between devices: 0.01 us -> 11.1 us
  between operations: 2.46 us -> 0.73 us
    pallas_call x0 -> x2, Pallas kernels: none -> 20.8 us  [local_reduce(): pl.pallas_call(functools.partial(local_kernel, axis=axis - 2), grid=(nv,...]
    mul x27 -> x2, other arithmetic: 17.3 us -> 0.12 us  [cyclic_reduce(): (r - lower * shifted(r, stride, axis, periodic) - upper * shifted(r, -str...]
    slice x18 -> x4, local copies, waits for them, and re-layouts: 17.1 us -> 0.02 us  [shifted(): kept = lax.slice_in_dim(values, -offset, length, axis=axis)]
    slice x65 -> x5, local copies, waits for them, and re-layouts: 13 us -> 0.03 us  [shifted(): kept = lax.slice_in_dim(values, 0, length - offset, axis=axis)]
    unnamed x250 -> x42, local copies, waits for them, and re-layouts: 16 us -> 5.2 us
    slice x10 -> x9, local copies, waits for them, and re-layouts: 11.2 us -> 1.24 us  [row(): return lax.slice_in_dim(values, index, index + 1, axis=axis)]
    ppermute x1, waiting for transfers between devices: 0.01 us -> 7 us  [with_halo(): lax.ppermute(lax.slice_in_dim(block, block.shape[dim] - width, None, axis...]
    ppermute x1, waiting for transfers between devices: 0.01 us -> 4.05 us  [with_halo(): lax.ppermute(lax.slice_in_dim(block, 0, width, axis=dim), axis, backward)]
  transfers between devices with their start and end apart: 2 -> 2, of which waited for: 0 -> 2; matrix products, arithmetic and copies ran while one was open for 16% -> 7% of each run, Pallas kernels for 0% -> 0%
where the time goes in v2:
time: 80.7 us; the launch traced here: 79.8 us
  Pallas kernels  20.8 us (26%)
  blocking collectives  18.8 us (23%)
  other arithmetic  11.2 us (14%)
  waiting for transfers between devices  11.1 us (14%)
  local copies, waits for them, and re-layouts  11 us (14%)
  starting transfers between devices  6.34 us (8%)
    pallas_call x2, Pallas kernels, local_reduce(): pl.pallas_call(functools.partial(local_kernel, axis=axis - 2), grid=(nv,...  20.8 us
    all_gather x2, blocking collectives, solve_lines(): red = lax.all_gather(red, axis_name, axis=axis + 1, tiled=True)  18.8 us
    ppermute x1, waiting for transfers between devices, with_halo(): lax.ppermute(lax.slice_in_dim(block, block.shape[dim] - width, None, axis...  7 us
    unnamed x42, local copies, waits for them, and re-layouts  5.2 us
    ppermute x1, starting transfers between devices, with_halo(): lax.ppermute(lax.slice_in_dim(block, block.shape[dim] - width, None, axis...  5.05 us
    ppermute x1, waiting for transfers between devices, with_halo(): lax.ppermute(lax.slice_in_dim(block, 0, width, axis=dim), axis, backward)  4.05 us
    slice x6, local copies, waits for them, and re-layouts, mix(): summed = summed + matrix[out_var, in_var][None, None, :] * values[in_var]  3.68 us
    mul x1, other arithmetic, solve_lines(): -le * a2 * inv_e  1.76 us
  transfers between devices with their start and end apart: 2, of which 2 were waited for; matrix products, arithmetic and copies ran while one was open for 7% of the time, Pallas kernels for 0%

profile of v2, /device:TPU:0, one launch (start us, length us, event | category | flops | bytes accessed | tf_op | source)
XLA Modules:
  0.0 79.8 jit_solution(16960783579992646872)
XLA Ops:
  0.0 5.0 %collective-permute-start = (f32[5,1,128,256]{3,2,0,1:T(8,128)}, f32[5,1,128,256]{3,2,0,1:T(8,128)S(1)}, u32[]{:S(2)}, u32[]{:S(2)}) collective-permute-start(f32[5,1,128,256]{3,2,0,1:T(8,128)} %bitcast.234), channel_id=1, source_target_pairs={{0,1},{2,3},{4,5},{6,7},{8,9},{10,11},{12,13},{14,15},{16,17},{18,... | collective-permute-start | bytes 1966088 | tf_op jit(solution)/shard_map/ppermute | solution.py:17
  5.1 1.3 %collective-permute-start.1 = (f32[5,1,128,256]{3,2,0,1:T(8,128)}, f32[5,1,128,256]{3,2,0,1:T(8,128)S(1)}, u32[]{:S(2)}, u32[]{:S(2)}) collective-permute-start(f32[5,1,128,256]{3,2,0,1:T(8,128)} %bitcast.235), channel_id=1, source_target_pairs={{1,0},{3,2},{5,4},{7,6},{9,8},{11,10},{13,12},{15,14},{17,16},{19,... | collective-permute-start | bytes 1966088 | tf_op jit(solution)/shard_map/ppermute | solution.py:20
  6.4 1.0 %fusion.114 = (f32[1,1,256]{2,1,0:T(1,128)S(1)}, f32[1,1,256]{2,1,0:T(1,128)S(1)}, f32[1,1,256]{2,1,0:T(1,128)S(1)}, f32[1,1,256]{2,1,0:T(1,128)S(1)}, f32[1,1,2...) fusion(f32[5,5,256]{2,1,0:T(8,128)} %param.19), kind=kLoop, calls=%fused_computation.207 | loop fusion | bytes 38912 | tf_op jit(solution)/shard_map/slice | solution.py:130
  7.4 0.9 %fusion.115 = (f32[1,1,256]{2,1,0:T(1,128)S(1)}, f32[1,1,256]{2,1,0:T(1,128)S(1)}, f32[1,1,256]{2,1,0:T(1,128)S(1)}, f32[1,1,256]{2,1,0:T(1,128)S(1)}, f32[1,1,256]{2,1,0:T(1,128)S(1)}, /*index=5*/f32[1,1,256]{2,1,0:T(1,128)S(1)}) fusion(f32[5,5,256]{2,1,0:T(8,128)} %param.19), kind=kLoop, calls=%fused_computation.208 | loop fusion | bytes 12288 | tf_op jit(solution)/shard_map/slice | solution.py:130
  8.3 0.7 broadcast_subtract_fusion
  9.0 0.9 %fusion.96 = (f32[1,1,256]{2,1,0:T(1,128)S(1)}, f32[1,1,256]{2,1,0:T(1,128)S(1)}, f32[1,1,256]{2,1,0:T(1,128)S(1)}, f32[1,1,256]{2,1,0:T(1,128)S(1)}, f32[1,1,256]{2,1,0:T(1,128)S(1)}, /*index=5*/f32[1,1,256]{2,1,0:T(1,128)S(1)}) fusion(f32[5,5,256]{2,1,0:T(8,128)} %param.21), kind=kLoop, calls=%fused_computation.189 | loop fusion | bytes 12288 | tf_op jit(solution)/shard_map/slice | solution.py:130
  9.9 1.0 %fusion.95 = (f32[1,1,256]{2,1,0:T(1,128)S(1)}, f32[1,1,256]{2,1,0:T(1,128)S(1)}, f32[1,1,256]{2,1,0:T(1,128)S(1)}, f32[1,1,256]{2,1,0:T(1,128)S(1)}, f32[1,1,25...) fusion(f32[5,5,256]{2,1,0:T(8,128)} %param.21), kind=kLoop, calls=%fused_computation.188 | loop fusion | bytes 38912 | tf_op jit(solution)/shard_map/slice | solution.py:130
  10.9 1.4 %fusion.3 = (f32[5,1,128,256]{3,2,0,1:T(8,128)S(1)}, f32[5,1,128,256]{3,2,1,0:T(8,128)}, f32[5,1,128,256]{3,2,1,0:T(8,128)}, f32[5,1,128,256]{3,2,0,1:T(8,128)S(1)}) fusion(f32[5,256]{1,0:T(8,128)S(1)} %get-tuple-element.193, f32[128,256]{1,0:T(8,128)S(1)} %bitcast.226, f32[5,256]{1,0:T(8,128)S(1)} %copy-done.13, f32[5,256]{1,0:T(8,128)S(1)} %get-tuple-element.194), kind=kLoop, calls=%fused_computation.7 | loop fusion | flops 1310720 | bytes 2767872 | tf_op jit(solution)/shard_map/div | solution.py:158
  12.3 7.0 %collective-permute-done = f32[5,1,128,256]{3,2,0,1:T(8,128)S(1)} collective-permute-done((f32[5,1,128,256]{3,2,0,1:T(8,128)}, f32[5,1,128,256]{3,2,0,1:T(8,128)S(1)}, u32[]{:S(2)}, u32[]{:S(2)}) %collective-permute-start) | collective-permute-done | bytes 655392 | tf_op jit(solution)/shard_map/ppermute | solution.py:17
  19.3 4.1 %collective-permute-done.1 = f32[5,1,128,256]{3,2,0,1:T(8,128)S(1)} collective-permute-done((f32[5,1,128,256]{3,2,0,1:T(8,128)}, f32[5,1,128,256]{3,2,0,1:T(8,128)S(1)}, u32[]{:S(2)}, u32[]{:S(2)}) %collective-permute-start.1) | collective-permute-done | bytes 655392 | tf_op jit(solution)/shard_map/ppermute | solution.py:20
  23.4 0.2 bitcast_add_fusion
  23.9 1.0 %fusion.11.t_ref = f32[5,1,128,256]{3,2,1,0:T(8,128)} fusion(f32[5,1,128,256]{3,2,0,1:T(8,128)S(1)} %add_dynamic-update-slice_fusion.8, f32[128,256]{1,0:T(8,128)S(1)} %bitcast.227, f32[5,256]{1,0:T(8,128)S(1)} %copy-done.13), kind=kLoop, calls=%fused_computation.15 | loop fusion | flops 655360 | bytes 1446912 | tf_op jit(solution)/shard_map/div | solution.py:159
  24.8 0.1 fusion.128
  24.9 6.6 %shard_map.109 = (f32[5,1,128,256]{3,2,1,0:T(8,128)}, f32[5,1,128,256]{3,2,1,0:T(8,128)}, f32[5,1,128,256]{3,2,1,0:T(8,128)}) custom-call(f32[5,1,128,256]{3,2,1,0:T(8,128)} %get-tuple-element.52.l_ref, f32[5,1,128,256]{3,2,1,0:T(8,128)} %get-tuple-element.47.u_ref, f32[5,1,128,256]{3,2,1,0:T(8,128)} %fusion.11.t_ref), custom_call_target="tpu_custom_call" | custom-call | tf_op jit(solution)/shard_map/pallas_call | solution.py:85
  31.5 0.9 %slice_multiply_fusion.9 = (f32[5,1,1,256]{3,2,0,1:T(1,128)S(1)}, f32[5,1,1,256]{3,2,0,1:T(1,128)S(1)}, f32[5,1,1,256]{3,2,0,1:T(1,128)S(1)}, f32[5,1,1,256]{3,2,0,1:T(1,128)S(1)}) fusion(f32[5,1,128,256]{3,2,0,1:T(8,128)S(1)} %get-tuple-element.53, f32[5,1,128,256]{3,2,0,1:T(8,128)} %bitcast.233, f32[5,1,128,256]{3,2,0,1:T(8,128)S(1)} %get-tuple-element.46, ...), kind=kLoop, calls=%fused_computation.167 | loop fusion | flops 12800 | bytes 51200 | tf_op jit(solution)/shard_map/mul | solution.py:110
  32.3 0.8 %fusion.76 = f32[5,1,1,256]{3,2,1,0:T(1,128)S(1)} fusion(f32[5,1,128,256]{3,2,0,1:T(8,128)} %bitcast.229, f32[5,1,128,256]{3,2,1,0:T(8,128)} %fusion.11.t_ref, f32[5,1,1,256]{3,2,0,1:T(1,128)S(1)} %get-tuple-element.34, f32[5,1,128,256]{3,2,0,1:T(8,128)S(1)} %get-tuple-element.53), kind=kLoop, calls=%fused_computation.154 | loop fusion | flops 3840 | bytes 25600 | tf_op jit(solution)/shard_map/mul | solution.py:112
  33.2 0.8 %fusion.79 = (f32[5,1,1,256]{3,2,0,1:T(1,128)S(1)}, f32[5,1,1,256]{3,2,1,0:T(1,128)S(1)}, f32[5,1,1,256]{3,2,0,1:T(1,128)S(1)}) fusion(f32[5,1,1,256]{3,2,0,1:T(1,128)S(1)} %get-tuple-element.26, f32[5,1,128,256]{3,2,0,1:T(8,128)} %bitcast.232, f32[5,1,128,256]{3,2,0,1:T(8,128)S(1)} %get-tuple-element.46, f32[5,1,128,256]{3,2,0,1:T(8,128)} %bitcast.230, ...), kind=kLoop, calls=%fused_computation.160 | loop fusion | flops 8960 | bytes 51200 | tf_op jit(solution)/shard_map/mul | solution.py:111
  34.1 5.4 %all_gather.6 = f32[3,5,1,8,256]{4,2,1,0,3:T(1,128)S(1)} all-gather(f32[3,5,1,2,256]{4,2,1,0,3:T(1,128)S(1)} %copy.277), channel_id=1, replica_groups=mesh['az'=4,'rad'=4,'ax'=2] {'az'}, dimensions={3}, use_global_device_ids=true | all-gather | bytes 153600 | tf_op jit(solution)/shard_map/all_gather | solution.py:115
  39.7 0.1 fusion.35
  40.1 0.1 fusion.57
  40.2 0.6 copy-done.9
  40.9 0.2 copy-done.7
  41.1 0.2 copy-done.8
  41.3 0.2 select_select_fusion.1
  41.8 0.8 %copy-done.12 = f32[1,128,256]{2,1,0:T(8,128)S(1)} copy-done((f32[1,128,256]{2,1,0:T(8,128)S(1)}, f32[1,128,256]{2,1,0:T(8,128)}, u32[]{:S(2)}) %copy-start.12) | copy-done | bytes 131096
  42.7 1.0 %fusion.8 = (f32[5,1,128,256]{3,2,1,0:T(8,128)S(1)}, f32[5,1,128,256]{3,2,1,0:T(8,128)}) fusion(f32[5,1,128,256]{3,2,1,0:T(8,128)S(1)} %add_dynamic-update-slice_fusion.4, f32[128,256]{1,0:T(8,128)S(1)} %bitcast.245, f32[5,256]{1,0:T(8,128)S(1)} %constant_dynamic-slice_fusion), kind=kLoop, calls=%fused_computation.12 | loop fusion | flops 983040 | bytes 2102272 | tf_op jit(solution)/shard_map/div | solution.py:165
  43.7 0.1 fusion.92
  43.8 0.7 copy-done.2
  44.5 14.2 %shard_map.110 = (f32[5,1,128,256]{3,2,1,0:T(8,128)}, f32[5,1,128,256]{3,2,1,0:T(8,128)}, f32[5,1,128,256]{3,2,1,0:T(8,128)}) custom-call(f32[5,1,128,256]{3,2,1,0:T(8,128)} %get-tuple-element.51.l_ref.u_ref, f32[5,1,128,256]{3,2,1,0:T(8,128)} %get-tuple-element.51.l_ref.u_ref, f32[5,1,128,256]{3,2,1,0:T(8,128)} %copy-done.2), custom_call_target="tpu_custom_call" | custom-call | tf_op jit(solution)/shard_map/pallas_call | solution.py:85
  58.8 1.8 %slice_multiply_fusion.1 = (f32[5,1,128,1]{3,2,1,0:T(8,128)S(1)}, f32[5,1,128,1]{3,2,1,0:T(8,128)S(1)}, f32[5,1,128,1]{3,2,1,0:T(8,128)S(1)}, f32[5,1,128,1]{3,2...) fusion(f32[5,1,128,256]{3,2,1,0:T(8,128)} %get-tuple-element.14, ...), kind=kLoop, calls=%fused_computation.22 | loop fusion | flops 6400 | bytes 30720 | tf_op jit(solution)/shard_map/mul | solution.py:110
  60.5 0.1 copy.283
  60.7 0.2 copy.284
  60.8 0.2 copy.289
  61.0 0.7 copy-done.3
  61.6 0.2 fusion.91
  61.9 0.1 copy.294
  62.0 0.2 copy.295
  62.1 0.2 copy.287
  62.3 0.2 copy.288
  62.4 0.2 copy.291
  62.6 0.2 copy.298
  62.7 0.2 copy.299
  63.0 13.3 %all_gather.7 = f32[3,5,1,128,8]{3,2,1,0,4:T(1,128)S(1)} all-gather(f32[3,5,1,128,2]{3,2,1,0,4:T(1,128)S(1)} %copy.301), channel_id=1, replica_groups=mesh['az'=4,'rad'=4,'ax'=2] {'rad'}, dimensions={4}, use_global_device_ids=true | all-gather | bytes 76800 | tf_op jit(solution)/shard_map/all_gather | solution.py:115
  76.8 0.8 %copy-done.5 = f32[5,1,128,256]{3,2,1,0:T(8,128)S(1)} copy-done((f32[5,1,128,256]{3,2,1,0:T(8,128)S(1)}, f32[5,1,128,256]{3,2,1,0:T(8,128)}, u32[]{:S(2)}) %copy-start.5) | copy-done | bytes 655384
  77.6 0.2 copy-done.4
  77.8 0.2 select_select_fusion
  78.3 0.8 %copy-done.14 = f32[5,1,128,256]{3,2,1,0:T(8,128)} copy-done((f32[5,1,128,256]{3,2,1,0:T(8,128)}, f32[5,1,128,256]{3,2,1,0:T(8,128)S(1)}, u32[]{:S(2)}) %copy-start.14) | copy-done | bytes 655384
  79.1 0.7 add_dynamic-update-slice_fusion
  (101 shorter events, 1.6 us)
Async XLA Ops:
  0.0 9.9 %copy-start = (f32[5,1024]{1,0:T(8,128)S(1)}, f32[5,1024]{1,0:T(8,128)}, u32[]{:S(2)}) copy-start(f32[5,1024]{1,0:T(8,128)} %param.17) | copy-start | bytes 61444
  0.0 8.2 %copy-start.15 = (f32[5,5,256]{2,1,0:T(8,128)S(1)}, f32[5,5,256]{2,1,0:T(8,128)}, u32[]{:S(2)}) copy-start(f32[5,5,256]{2,1,0:T(8,128)} %param.20) | copy-start | bytes 76804
  0.0 10.9 %copy-start.6 = (f32[1,128,256]{2,1,0:T(8,128)S(1)}, f32[1,128,256]{2,1,0:T(8,128)}, u32[]{:S(2)}) copy-start(f32[1,128,256]{2,1,0:T(8,128)} %param.13) | copy-start | bytes 393220
  0.0 19.3 %collective-permute-start = (f32[5,1,128,256]{3,2,0,1:T(8,128)}, f32[5,1,128,256]{3,2,0,1:T(8,128)S(1)}, u32[]{:S(2)}, u32[]{:S(2)}) collective-permute-start(f32[5,1,128,256]{3,2,0,1:T(8,128)} %bitcast.234), channel_id=1, source_target_pairs={{0,1},{2,3},{4,5},{6,7},{8,9},{10,11},{12,13},{14,15},{16,17},{18,... | collective-permute-start | bytes 1966088 | tf_op jit(solution)/shard_map/ppermute | solution.py:17
  5.1 18.3 %collective-permute-start.1 = (f32[5,1,128,256]{3,2,0,1:T(8,128)}, f32[5,1,128,256]{3,2,0,1:T(8,128)S(1)}, u32[]{:S(2)}, u32[]{:S(2)}) collective-permute-start(f32[5,1,128,256]{3,2,0,1:T(8,128)} %bitcast.235), channel_id=1, source_target_pairs={{1,0},{3,2},{5,4},{7,6},{9,8},{11,10},{13,12},{15,14},{17,16},{19,... | collective-permute-start | bytes 1966088 | tf_op jit(solution)/shard_map/ppermute | solution.py:20
  9.9 1.0 %copy-start.13 = (f32[5,256]{1,0:T(8,128)S(1)}, f32[5,256]{1,0:T(8,128)}, u32[]{:S(2)}) copy-start(f32[5,256]{1,0:T(8,128)} %param.15) | copy-start | bytes 15364
  10.9 12.5 %copy-start.10 = (f32[5,1,128,256]{3,2,1,0:T(8,128)S(1)}, f32[5,1,128,256]{3,2,1,0:T(8,128)}, u32[]{:S(2)}) copy-start(f32[5,1,128,256]{3,2,1,0:T(8,128)} %param.12) | copy-start | bytes 1966084
  10.9 12.5 %copy-start.11 = (f32[5,1,128,256]{3,2,1,0:T(8,128)S(1)}, f32[5,1,128,256]{3,2,1,0:T(8,128)}, u32[]{:S(2)}) copy-start(f32[5,1,128,256]{3,2,1,0:T(8,128)} %param.11) | copy-start | bytes 1966084
  10.9 12.5 %copy-start.16 = (f32[5,256]{1,0:T(8,128)S(1)}, f32[5,256]{1,0:T(8,128)}, u32[]{:S(2)}) copy-start(f32[5,256]{1,0:T(8,128)} %param.18) | copy-start | bytes 15364
  39.8 1.1 %copy-start.9 = (f32[5,1,128,256]{3,2,1,0:T(8,128)S(1)}, f32[5,1,128,256]{3,2,1,0:T(8,128)}, u32[]{:S(2)}) copy-start(f32[5,1,128,256]{3,2,1,0:T(8,128)} %get-tuple-element.11) | copy-start | bytes 1966084
  39.9 1.2 %copy-start.7 = (f32[5,1,128,256]{3,2,1,0:T(8,128)S(1)}, f32[5,1,128,256]{3,2,1,0:T(8,128)}, u32[]{:S(2)}) copy-start(f32[5,1,128,256]{3,2,1,0:T(8,128)} %get-tuple-element.13) | copy-start | bytes 1966084
  39.9 1.4 %copy-start.8 = (f32[5,1,128,256]{3,2,1,0:T(8,128)S(1)}, f32[5,1,128,256]{3,2,1,0:T(8,128)}, u32[]{:S(2)}) copy-start(f32[5,1,128,256]{3,2,1,0:T(8,128)} %get-tuple-element.12) | copy-start | bytes 1966084
  41.7 0.9 %copy-start.12 = (f32[1,128,256]{2,1,0:T(8,128)S(1)}, f32[1,128,256]{2,1,0:T(8,128)}, u32[]{:S(2)}) copy-start(f32[1,128,256]{2,1,0:T(8,128)} %param.14) | copy-start | bytes 393220
  43.7 0.9 %copy-start.2 = (f32[5,1,128,256]{3,2,1,0:T(8,128)}, f32[5,1,128,256]{3,2,1,0:T(8,128)S(1)}, u32[]{:S(2)}) copy-start(f32[5,1,128,256]{3,2,1,0:T(8,128)S(1)} %get-tuple-element.50.t_ref) | copy-start | bytes 1966084
  44.5 14.2 %copy-start.1 = (f32[5,1,128,256]{3,2,1,0:T(8,128)S(1)}, f32[5,1,128,256]{3,2,1,0:T(8,128)}, u32[]{:S(2)}) copy-start(f32[5,1,128,256]{3,2,1,0:T(8,128)} %get-tuple-element.51.l_ref.u_ref) | copy-start | bytes 1966084
  60.5 1.1 %copy-start.3 = (f32[5,1,128,256]{3,2,1,0:T(8,128)S(1)}, f32[5,1,128,256]{3,2,1,0:T(8,128)}, u32[]{:S(2)}) copy-start(f32[5,1,128,256]{3,2,1,0:T(8,128)} %get-tuple-element.16) | copy-start | bytes 1966084
  76.5 1.1 %copy-start.5 = (f32[5,1,128,256]{3,2,1,0:T(8,128)S(1)}, f32[5,1,128,256]{3,2,1,0:T(8,128)}, u32[]{:S(2)}) copy-start(f32[5,1,128,256]{3,2,1,0:T(8,128)} %get-tuple-element.15) | copy-start | bytes 1966084
  76.5 1.2 %copy-start.4 = (f32[5,1,128,256]{3,2,1,0:T(8,128)S(1)}, f32[5,1,128,256]{3,2,1,0:T(8,128)}, u32[]{:S(2)}) copy-start(f32[5,1,128,256]{3,2,1,0:T(8,128)} %get-tuple-element.14) | copy-start | bytes 1966084
  78.3 0.8 %copy-start.14 = (f32[5,1,128,256]{3,2,1,0:T(8,128)}, f32[5,1,128,256]{3,2,1,0:T(8,128)S(1)}, u32[]{:S(2)}) copy-start(f32[5,1,128,256]{3,2,1,0:T(8,128)S(1)} %add_dynamic-update-slice_fusion.1) | copy-start | bytes 1966084

commit v3 on v2

--- a/solution.py
+++ b/solution.py
@@ -91,6 +91,29 @@
     )(lower, upper, target)
 
 
+def gathered(block, axis_name, dim):
+    count = lax.axis_size(axis_name)
+    received = [block]
+    for offset in range(1, count):
+        pairs = [((i + offset) % count, i) for i in range(count)]
+        received.append(lax.ppermute(block, axis_name, pairs))
+    doubled = jnp.concatenate(received + received, axis=dim)
+    start = ((count - lax.axis_index(axis_name)) % count) * block.shape[dim]
+    return lax.dynamic_slice_in_dim(doubled, start, count * block.shape[dim], dim)
+
+
+def plane_halo(block, axis_name, dim):
+    count = lax.axis_size(axis_name)
+    if count != 2:
+        return with_halo(block, ((axis_name, dim),), 1, False)
+    swapped = lax.ppermute(block, axis_name, [(0, 1), (1, 0)])
+    zero = jnp.zeros_like(swapped)
+    first = lax.axis_index(axis_name) == 0
+    low = jnp.where(first, zero, swapped)
+    high = jnp.where(first, swapped, zero)
+    return jnp.concatenate([low, block, high], axis=dim)
+
+
 def row(values, index, axis):
     return lax.slice_in_dim(values, index, index + 1, axis=axis)
 
@@ -112,7 +135,7 @@
             jnp.concatenate([(t0 - u0 * t1) * inv_f, (te - le * t2) * inv_e], axis=axis),
         ]
     )
-    red = lax.all_gather(red, axis_name, axis=axis + 1, tiled=True)
+    red = gathered(red, axis_name, axis + 1)
     count = red.shape[axis + 1]
     rl, ru, (rt,) = cyclic_reduce(red[0], red[1], [red[2]], axis, periodic, count)
     ends = rt / (1.0 + rl + ru)
@@ -146,7 +169,7 @@
     mix_out,
 ):
     rad_cells = flow_state.shape[3]
-    padded = with_halo(flow_state, (("ax", 1),), 1, False)
+    padded = plane_halo(flow_state, "ax", 1)
     explicit = source + axial_diff[:, None, None, :] * (
         padded[:, :-2] - 2.0 * flow_state + padded[:, 2:]
     )

time: 80.7 us -> 71.1 us (0.88)
  blocking collectives: 18.8 us -> 0 us
  waiting for transfers between devices: 11.1 us -> 16.7 us
  starting transfers between devices: 6.34 us -> 9.71 us
    all_gather x2 -> x0, blocking collectives: 18.8 us -> none  [solve_lines(): red = lax.all_gather(red, axis_name, axis=axis + 1, tiled=True)]
    ppermute x2 -> x7, waiting for transfers between devices: 11.1 us -> 16.7 us  [the longest x1 9.05 us: plane_halo(): swapped = lax.ppermute(block, axis_name, [(0, 1), (1, 0)])]
    ppermute x2 -> x7, starting transfers between devices: 6.34 us -> 9.71 us  [the longest x6 6.67 us: gathered(): received.append(lax.ppermute(block, axis_name, pairs))]
    unnamed x42 -> x39, local copies, waits for them, and re-layouts: 5.2 us -> 5.17 us
  transfers between devices with their start and end apart: 2 -> 7, of which waited for: 2 -> 6; matrix products, arithmetic and copies ran while one was open for 7% -> 8% of each run, Pallas kernels for 0% -> 0%
where the time goes in v3:
time: 71.1 us; the launch traced here: 70.3 us
  Pallas kernels  20.8 us (29%)
  waiting for transfers between devices  16.7 us (23%)
  local copies, waits for them, and re-layouts  11.3 us (16%)
  other arithmetic  11.1 us (16%)
  starting transfers between devices  9.71 us (14%)
    pallas_call x2, Pallas kernels, local_reduce(): pl.pallas_call(functools.partial(local_kernel, axis=axis - 2), grid=(nv,...  20.8 us
    ppermute x1, waiting for transfers between devices, plane_halo(): swapped = lax.ppermute(block, axis_name, [(0, 1), (1, 0)])  9.05 us
    ppermute x6, waiting for transfers between devices, gathered(): received.append(lax.ppermute(block, axis_name, pairs))  7.65 us
    ppermute x6, starting transfers between devices, gathered(): received.append(lax.ppermute(block, axis_name, pairs))  6.67 us
    unnamed x39, local copies, waits for them, and re-layouts  5.17 us
    slice x6, local copies, waits for them, and re-layouts, mix(): summed = summed + matrix[out_var, in_var][None, None, :] * values[in_var]  3.68 us
    ppermute x1, starting transfers between devices, plane_halo(): swapped = lax.ppermute(block, axis_name, [(0, 1), (1, 0)])  3.04 us
    mul x1, other arithmetic, solve_lines(): -le * a2 * inv_e  1.76 us
  transfers between devices with their start and end apart: 7, of which 6 were waited for; matrix products, arithmetic and copies ran while one was open for 8% of the time, Pallas kernels for 0%

profile of v3, /device:TPU:0, one launch (start us, length us, event | category | flops | bytes accessed | tf_op | source)
XLA Modules:
  0.0 70.3 jit_solution(17819686958907237484)
XLA Ops:
  0.0 3.0 %collective-permute-start = (f32[5,1,128,256]{3,2,0,1:T(8,128)}, f32[5,1,128,256]{3,2,0,1:T(8,128)S(1)}, u32[]{:S(2)}, u32[]{:S(2)}) collective-permute-start(f32[5,1,128,256]{3,2,0,1:T(8,128)} %bitcast.221), channel_id=1, source_target_pairs={{0,1},{1,0},{2,3},{3,2},{4,5},{5,4},{6,7},{7,6},{8,9},{9,8},{10,11... | collective-permute-start | bytes 1966088 | tf_op jit(solution)/shard_map/ppermute | solution.py:109
  3.0 1.0 %fusion.112 = (f32[1,1,256]{2,1,0:T(1,128)S(1)}, f32[1,1,256]{2,1,0:T(1,128)S(1)}, f32[1,1,256]{2,1,0:T(1,128)S(1)}, f32[1,1,256]{2,1,0:T(1,128)S(1)}, f32[1,1,2...) fusion(f32[5,5,256]{2,1,0:T(8,128)} %param.19), kind=kLoop, calls=%fused_computation.208 | loop fusion | bytes 38912 | tf_op jit(solution)/shard_map/slice | solution.py:153
  4.0 0.9 %fusion.113 = (f32[1,1,256]{2,1,0:T(1,128)S(1)}, f32[1,1,256]{2,1,0:T(1,128)S(1)}, f32[1,1,256]{2,1,0:T(1,128)S(1)}, f32[1,1,256]{2,1,0:T(1,128)S(1)}, f32[1,1,256]{2,1,0:T(1,128)S(1)}, /*index=5*/f32[1,1,256]{2,1,0:T(1,128)S(1)}) fusion(f32[5,5,256]{2,1,0:T(8,128)} %param.19), kind=kLoop, calls=%fused_computation.209 | loop fusion | bytes 12288 | tf_op jit(solution)/shard_map/slice | solution.py:153
  4.9 0.7 %broadcast_subtract_fusion = (f32[5,256]{1,0:T(8,128)S(1)}, f32[5,256]{1,0:T(8,128)S(1)}) fusion(f32[5,256]{1,0:T(8,128)} %param.16), kind=kLoop, calls=%fused_computation.179 | loop fusion | flops 2560 | bytes 15360 | tf_op jit(solution)/shard_map/sub | solution.py:181
  5.6 0.9 %fusion.94 = (f32[1,1,256]{2,1,0:T(1,128)S(1)}, f32[1,1,256]{2,1,0:T(1,128)S(1)}, f32[1,1,256]{2,1,0:T(1,128)S(1)}, f32[1,1,256]{2,1,0:T(1,128)S(1)}, f32[1,1,256]{2,1,0:T(1,128)S(1)}, /*index=5*/f32[1,1,256]{2,1,0:T(1,128)S(1)}) fusion(f32[5,5,256]{2,1,0:T(8,128)} %param.21), kind=kLoop, calls=%fused_computation.190 | loop fusion | bytes 12288 | tf_op jit(solution)/shard_map/slice | solution.py:153
  6.5 1.0 %fusion.93 = (f32[1,1,256]{2,1,0:T(1,128)S(1)}, f32[1,1,256]{2,1,0:T(1,128)S(1)}, f32[1,1,256]{2,1,0:T(1,128)S(1)}, f32[1,1,256]{2,1,0:T(1,128)S(1)}, f32[1,1,25...) fusion(f32[5,5,256]{2,1,0:T(8,128)} %param.21), kind=kLoop, calls=%fused_computation.189 | loop fusion | bytes 38912 | tf_op jit(solution)/shard_map/slice | solution.py:153
  7.6 1.4 %fusion.3 = (f32[5,1,128,256]{3,2,0,1:T(8,128)S(1)}, f32[5,1,128,256]{3,2,1,0:T(8,128)}, f32[5,1,128,256]{3,2,1,0:T(8,128)}, f32[5,1,128,256]{3,2,0,1:T(8,128)S(1)}) fusion(f32[5,256]{1,0:T(8,128)S(1)} %get-tuple-element.193, f32[128,256]{1,0:T(8,128)S(1)} %bitcast.213, f32[5,256]{1,0:T(8,128)S(1)} %copy-done.13, f32[5,256]{1,0:T(8,128)S(1)} %get-tuple-element.194), kind=kLoop, calls=%fused_computation.7 | loop fusion | flops 1310720 | bytes 2767872 | tf_op jit(solution)/shard_map/div | solution.py:181
  8.9 9.1 %collective-permute-done = f32[5,1,128,256]{3,2,0,1:T(8,128)S(1)} collective-permute-done((f32[5,1,128,256]{3,2,0,1:T(8,128)}, f32[5,1,128,256]{3,2,0,1:T(8,128)S(1)}, u32[]{:S(2)}, u32[]{:S(2)}) %collective-permute-start) | collective-permute-done | bytes 655392 | tf_op jit(solution)/shard_map/ppermute | solution.py:109
  18.0 0.2 bitcast_add_fusion
  18.5 0.9 %fusion.11.t_ref = f32[5,1,128,256]{3,2,1,0:T(8,128)} fusion(f32[5,1,128,256]{3,2,0,1:T(8,128)S(1)} %add_dynamic-update-slice_fusion.8, f32[128,256]{1,0:T(8,128)S(1)} %bitcast.214, f32[5,256]{1,0:T(8,128)S(1)} %copy-done.13), kind=kLoop, calls=%fused_computation.15 | loop fusion | flops 655360 | bytes 1446912 | tf_op jit(solution)/shard_map/div | solution.py:182
  19.5 6.6 %shard_map.109 = (f32[5,1,128,256]{3,2,1,0:T(8,128)}, f32[5,1,128,256]{3,2,1,0:T(8,128)}, f32[5,1,128,256]{3,2,1,0:T(8,128)}) custom-call(f32[5,1,128,256]{3,2,1,0:T(8,128)} %get-tuple-element.55.l_ref, f32[5,1,128,256]{3,2,1,0:T(8,128)} %get-tuple-element.50.u_ref, f32[5,1,128,256]{3,2,1,0:T(8,128)} %fusion.11.t_ref), custom_call_target="tpu_custom_call" | custom-call | tf_op jit(solution)/shard_map/pallas_call | solution.py:85
  26.1 0.9 %slice_multiply_fusion.9 = (f32[5,1,1,256]{3,2,0,1:T(1,128)S(1)}, f32[5,1,1,256]{3,2,0,1:T(1,128)S(1)}, f32[5,1,1,256]{3,2,0,1:T(1,128)S(1)}, f32[5,1,1,256]{3,2,0,1:T(1,128)S(1)}) fusion(f32[5,1,128,256]{3,2,0,1:T(8,128)S(1)} %get-tuple-element.56, f32[5,1,128,256]{3,2,0,1:T(8,128)} %bitcast.220, f32[5,1,128,256]{3,2,0,1:T(8,128)S(1)} %get-tuple-element.49, ...), kind=kLoop, calls=%fused_computation.170 | loop fusion | flops 12800 | bytes 51200 | tf_op jit(solution)/shard_map/mul | solution.py:133
  27.0 0.8 %fusion.76 = f32[5,1,1,256]{3,2,1,0:T(1,128)S(1)} fusion(f32[5,1,128,256]{3,2,0,1:T(8,128)} %bitcast.216, f32[5,1,128,256]{3,2,1,0:T(8,128)} %fusion.11.t_ref, f32[5,1,1,256]{3,2,0,1:T(1,128)S(1)} %get-tuple-element.34, f32[5,1,128,256]{3,2,0,1:T(8,128)S(1)} %get-tuple-element.56), kind=kLoop, calls=%fused_computation.157 | loop fusion | flops 3840 | bytes 25600 | tf_op jit(solution)/shard_map/mul | solution.py:135
  27.8 0.8 %fusion.79 = (f32[5,1,1,256]{3,2,0,1:T(1,128)S(1)}, f32[5,1,1,256]{3,2,1,0:T(1,128)S(1)}, f32[5,1,1,256]{3,2,0,1:T(1,128)S(1)}) fusion(f32[5,1,1,256]{3,2,0,1:T(1,128)S(1)} %get-tuple-element.26, f32[5,1,128,256]{3,2,0,1:T(8,128)} %bitcast.219, f32[5,1,128,256]{3,2,0,1:T(8,128)S(1)} %get-tuple-element.49, f32[5,1,128,256]{3,2,0,1:T(8,128)} %bitcast.217, ...), kind=kLoop, calls=%fused_computation.163 | loop fusion | flops 8960 | bytes 51200 | tf_op jit(solution)/shard_map/mul | solution.py:134
  28.7 0.3 collective-permute-start.1
  29.0 1.5 %collective-permute-start.2 = (f32[3,5,1,2,256]{4,3,1,2,0:T(2,128)S(1)}, f32[3,5,1,2,256]{4,3,1,2,0:T(2,128)S(1)}, u32[]{:S(2)}, u32[]{:S(2)}) collective-permute-start(f32[3,5,1,2,256]{4,3,1,2,0:T(2,128)S(1)} %pad_maximum_fusion.2), channel_id=1, source_target_pairs={{16,0},{24,8},{0,16},{8,24},{17,1},{25,9},{1,17},{9,25},{18,2},{26... | collective-permute-start | bytes 92168 | tf_op jit(solution)/shard_map/ppermute | solution.py:99
  30.5 0.2 collective-permute-start.3
  30.7 2.2 %collective-permute-done.2 = f32[3,5,1,2,256]{4,3,1,2,0:T(2,128)S(1)} collective-permute-done((f32[3,5,1,2,256]{4,3,1,2,0:T(2,128)S(1)}, f32[3,5,1,2,256]{4,3,1,2,0:T(2,128)S(1)}, u32[]{:S(2)}, u32[]{:S(2)}) %collective-permute-start.2) | collective-permute-done | bytes 30752 | tf_op jit(solution)/shard_map/ppermute | solution.py:99
  32.9 0.9 %collective-permute-done.3 = f32[3,5,1,2,256]{4,3,1,2,0:T(2,128)S(1)} collective-permute-done((f32[3,5,1,2,256]{4,3,1,2,0:T(2,128)S(1)}, f32[3,5,1,2,256]{4,3,1,2,0:T(2,128)S(1)}, u32[]{:S(2)}, u32[]{:S(2)}) %collective-permute-start.3) | collective-permute-done | bytes 30752 | tf_op jit(solution)/shard_map/ppermute | solution.py:99
  33.8 0.2 concatenate.431
  34.7 0.6 copy-done.9
  35.4 0.2 copy-done.7
  35.6 0.2 copy-done.8
  35.8 0.2 select_select_fusion.1
  36.3 0.8 %copy-done.12 = f32[1,128,256]{2,1,0:T(8,128)S(1)} copy-done((f32[1,128,256]{2,1,0:T(8,128)S(1)}, f32[1,128,256]{2,1,0:T(8,128)}, u32[]{:S(2)}) %copy-start.12) | copy-done | bytes 131096
  37.2 1.0 %fusion.8 = (f32[5,1,128,256]{3,2,1,0:T(8,128)S(1)}, f32[5,1,128,256]{3,2,1,0:T(8,128)}) fusion(f32[5,1,128,256]{3,2,1,0:T(8,128)S(1)} %add_dynamic-update-slice_fusion.4, f32[128,256]{1,0:T(8,128)S(1)} %bitcast.225, f32[5,256]{1,0:T(8,128)S(1)} %constant_dynamic-slice_fusion.3), kind=kLoop, calls=%fused_computation.12 | loop fusion | flops 983040 | bytes 2102272 | tf_op jit(solution)/shard_map/div | solution.py:188
  38.3 0.7 copy-done.2
  39.0 14.2 %shard_map.110 = (f32[5,1,128,256]{3,2,1,0:T(8,128)}, f32[5,1,128,256]{3,2,1,0:T(8,128)}, f32[5,1,128,256]{3,2,1,0:T(8,128)}) custom-call(f32[5,1,128,256]{3,2,1,0:T(8,128)} %get-tuple-element.54.l_ref.u_ref, f32[5,1,128,256]{3,2,1,0:T(8,128)} %get-tuple-element.54.l_ref.u_ref, f32[5,1,128,256]{3,2,1,0:T(8,128)} %copy-done.2), custom_call_target="tpu_custom_call" | custom-call | tf_op jit(solution)/shard_map/pallas_call | solution.py:85
  53.2 1.8 %slice_multiply_fusion.1 = (f32[5,1,128,1]{3,2,1,0:T(8,128)S(1)}, f32[5,1,128,1]{3,2,1,0:T(8,128)S(1)}, f32[5,1,128,1]{3,2,1,0:T(8,128)S(1)}, f32[5,1,128,1]{3,2...) fusion(f32[5,1,128,256]{3,2,1,0:T(8,128)} %get-tuple-element.14, ...), kind=kLoop, calls=%fused_computation.22 | loop fusion | flops 6400 | bytes 30720 | tf_op jit(solution)/shard_map/mul | solution.py:133
  55.1 0.2 copy.127
  55.3 0.2 copy.132
  55.4 0.7 copy-done.3
  56.1 0.2 fusion.91
  56.5 0.2 copy.138
  56.6 0.2 copy.130
  56.8 0.2 copy.131
  56.9 0.2 copy.134
  57.1 0.2 copy.141
  57.5 3.7 %collective-permute-start.4 = (f32[3,5,1,128,2]{3,4,2,1,0:T(2,128)S(1)}, f32[3,5,1,128,2]{3,4,2,1,0:T(2,128)S(1)}, u32[]{:S(2)}, u32[]{:S(2)}) collective-permute-start(f32[3,5,1,128,2]{3,4,2,1,0:T(2,128)S(1)} %pad_maximum_fusion.3), channel_id=1, source_target_pairs={{2,0},{4,2},{6,4},{0,6},{3,1},{5,3},{7,5},{1,7},{10,8},{12,10},{14... | collective-permute-start | bytes 46088 | tf_op jit(solution)/shard_map/ppermute | solution.py:99
  61.2 1.0 %collective-permute-start.6 = (f32[3,5,1,128,2]{3,4,2,1,0:T(2,128)S(1)}, f32[3,5,1,128,2]{3,4,2,1,0:T(2,128)S(1)}, u32[]{:S(2)}, u32[]{:S(2)}) collective-permute-start(f32[3,5,1,128,2]{3,4,2,1,0:T(2,128)S(1)} %pad_maximum_fusion.3), channel_id=1, source_target_pairs={{6,0},{0,2},{2,4},{4,6},{7,1},{1,3},{3,5},{5,7},{14,8},{8,10},{10,... | collective-permute-start | bytes 46088 | tf_op jit(solution)/shard_map/ppermute | solution.py:99
  62.2 0.4 collective-permute-done.4
  62.6 3.2 %collective-permute-done.5 = f32[3,5,1,128,2]{3,4,2,1,0:T(2,128)S(1)} collective-permute-done((f32[3,5,1,128,2]{3,4,2,1,0:T(2,128)S(1)}, f32[3,5,1,128,2]{3,4,2,1,0:T(2,128)S(1)}, u32[]{:S(2)}, u32[]{:S(2)}) %collective-permute-start.5) | collective-permute-done | bytes 15392 | tf_op jit(solution)/shard_map/ppermute | solution.py:99
  65.8 0.9 %collective-permute-done.6 = f32[3,5,1,128,2]{3,4,2,1,0:T(2,128)S(1)} collective-permute-done((f32[3,5,1,128,2]{3,4,2,1,0:T(2,128)S(1)}, f32[3,5,1,128,2]{3,4,2,1,0:T(2,128)S(1)}, u32[]{:S(2)}, u32[]{:S(2)}) %collective-permute-start.6) | collective-permute-done | bytes 15392 | tf_op jit(solution)/shard_map/ppermute | solution.py:99
  67.2 0.8 %copy-done.5 = f32[5,1,128,256]{3,2,1,0:T(8,128)S(1)} copy-done((f32[5,1,128,256]{3,2,1,0:T(8,128)S(1)}, f32[5,1,128,256]{3,2,1,0:T(8,128)}, u32[]{:S(2)}) %copy-start.5) | copy-done | bytes 655384
  68.0 0.2 copy-done.4
  68.2 0.2 select_select_fusion
  68.7 0.8 %copy-done.14 = f32[5,1,128,256]{3,2,1,0:T(8,128)} copy-done((f32[5,1,128,256]{3,2,1,0:T(8,128)}, f32[5,1,128,256]{3,2,1,0:T(8,128)S(1)}, u32[]{:S(2)}) %copy-start.14) | copy-done | bytes 655384
  69.5 0.7 %add_dynamic-update-slice_fusion = f32[5,1,128,256]{3,2,1,0:T(8,128)} fusion(f32[5,1,128,256]{3,2,1,0:T(8,128)} %copy-done.14, f32[5,1,128,256]{3,2,1,0:T(8,128)S(1)} %select_select_fusion, f32[256]{0:T(256)S(1)} %bitcast.229, f32[256]{0:T(256)S(1)} %bitcast.228, f32[256]{0:T(256)S(1)} %bitcast.235, f32[256]{0:T(256)S(1)} %bitcast.236, f32[256]{0:T(256)S(1)} %bitcast.234), kind=kLoop, calls=%fused_computation.42 | loop fusion | flops 327680 | bytes 791552 | tf_op jit(solution)/shard_map/stack | solution.py:155
  (106 shorter events, 2.5 us)
Async XLA Ops:
  0.0 6.5 %copy-start = (f32[5,1024]{1,0:T(8,128)S(1)}, f32[5,1024]{1,0:T(8,128)}, u32[]{:S(2)}) copy-start(f32[5,1024]{1,0:T(8,128)} %param.17) | copy-start | bytes 61444
  0.0 4.9 %copy-start.15 = (f32[5,5,256]{2,1,0:T(8,128)S(1)}, f32[5,5,256]{2,1,0:T(8,128)}, u32[]{:S(2)}) copy-start(f32[5,5,256]{2,1,0:T(8,128)} %param.20) | copy-start | bytes 76804
  0.0 7.5 %copy-start.6 = (f32[1,128,256]{2,1,0:T(8,128)S(1)}, f32[1,128,256]{2,1,0:T(8,128)}, u32[]{:S(2)}) copy-start(f32[1,128,256]{2,1,0:T(8,128)} %param.13) | copy-start | bytes 393220
  0.0 18.0 %collective-permute-start = (f32[5,1,128,256]{3,2,0,1:T(8,128)}, f32[5,1,128,256]{3,2,0,1:T(8,128)S(1)}, u32[]{:S(2)}, u32[]{:S(2)}) collective-permute-start(f32[5,1,128,256]{3,2,0,1:T(8,128)} %bitcast.221), channel_id=1, source_target_pairs={{0,1},{1,0},{2,3},{3,2},{4,5},{5,4},{6,7},{7,6},{8,9},{9,8},{10,11... | collective-permute-start | bytes 1966088 | tf_op jit(solution)/shard_map/ppermute | solution.py:109
  6.5 1.0 %copy-start.13 = (f32[5,256]{1,0:T(8,128)S(1)}, f32[5,256]{1,0:T(8,128)}, u32[]{:S(2)}) copy-start(f32[5,256]{1,0:T(8,128)} %param.15) | copy-start | bytes 15364
  7.5 10.5 %copy-start.10 = (f32[5,1,128,256]{3,2,1,0:T(8,128)S(1)}, f32[5,1,128,256]{3,2,1,0:T(8,128)}, u32[]{:S(2)}) copy-start(f32[5,1,128,256]{3,2,1,0:T(8,128)} %param.12) | copy-start | bytes 1966084
  7.5 10.4 %copy-start.11 = (f32[5,1,128,256]{3,2,1,0:T(8,128)S(1)}, f32[5,1,128,256]{3,2,1,0:T(8,128)}, u32[]{:S(2)}) copy-start(f32[5,1,128,256]{3,2,1,0:T(8,128)} %param.11) | copy-start | bytes 1966084
  7.6 10.4 %copy-start.16 = (f32[5,256]{1,0:T(8,128)S(1)}, f32[5,256]{1,0:T(8,128)}, u32[]{:S(2)}) copy-start(f32[5,256]{1,0:T(8,128)} %param.18) | copy-start | bytes 15364
  28.7 2.0 %collective-permute-start.1 = (f32[3,5,1,2,256]{4,3,1,2,0:T(2,128)S(1)}, f32[3,5,1,2,256]{4,3,1,2,0:T(2,128)S(1)}, u32[]{:S(2)}, u32[]{:S(2)}) collective-permute-start(f32[3,5,1,2,256]{4,3,1,2,0:T(2,128)S(1)} %pad_maximum_fusion.2), channel_id=1, source_target_pairs={{8,0},{16,8},{24,16},{0,24},{9,1},{17,9},{25,17},{1,25},{10,2},{18... | collective-permute-start | bytes 92168 | tf_op jit(solution)/shard_map/ppermute | solution.py:99
  29.0 3.9 %collective-permute-start.2 = (f32[3,5,1,2,256]{4,3,1,2,0:T(2,128)S(1)}, f32[3,5,1,2,256]{4,3,1,2,0:T(2,128)S(1)}, u32[]{:S(2)}, u32[]{:S(2)}) collective-permute-start(f32[3,5,1,2,256]{4,3,1,2,0:T(2,128)S(1)} %pad_maximum_fusion.2), channel_id=1, source_target_pairs={{16,0},{24,8},{0,16},{8,24},{17,1},{25,9},{1,17},{9,25},{18,2},{26... | collective-permute-start | bytes 92168 | tf_op jit(solution)/shard_map/ppermute | solution.py:99
  30.5 3.3 %collective-permute-start.3 = (f32[3,5,1,2,256]{4,3,1,2,0:T(2,128)S(1)}, f32[3,5,1,2,256]{4,3,1,2,0:T(2,128)S(1)}, u32[]{:S(2)}, u32[]{:S(2)}) collective-permute-start(f32[3,5,1,2,256]{4,3,1,2,0:T(2,128)S(1)} %pad_maximum_fusion.2), channel_id=1, source_target_pairs={{24,0},{0,8},{8,16},{16,24},{25,1},{1,9},{9,17},{17,25},{26,2},{2,... | collective-permute-start | bytes 92168 | tf_op jit(solution)/shard_map/ppermute | solution.py:99
  34.3 1.1 %copy-start.9 = (f32[5,1,128,256]{3,2,1,0:T(8,128)S(1)}, f32[5,1,128,256]{3,2,1,0:T(8,128)}, u32[]{:S(2)}) copy-start(f32[5,1,128,256]{3,2,1,0:T(8,128)} %get-tuple-element.11) | copy-start | bytes 1966084
  34.4 1.2 %copy-start.7 = (f32[5,1,128,256]{3,2,1,0:T(8,128)S(1)}, f32[5,1,128,256]{3,2,1,0:T(8,128)}, u32[]{:S(2)}) copy-start(f32[5,1,128,256]{3,2,1,0:T(8,128)} %get-tuple-element.13) | copy-start | bytes 1966084
  34.4 1.4 %copy-start.8 = (f32[5,1,128,256]{3,2,1,0:T(8,128)S(1)}, f32[5,1,128,256]{3,2,1,0:T(8,128)}, u32[]{:S(2)}) copy-start(f32[5,1,128,256]{3,2,1,0:T(8,128)} %get-tuple-element.12) | copy-start | bytes 1966084
  36.3 0.9 %copy-start.12 = (f32[1,128,256]{2,1,0:T(8,128)S(1)}, f32[1,128,256]{2,1,0:T(8,128)}, u32[]{:S(2)}) copy-start(f32[1,128,256]{2,1,0:T(8,128)} %param.14) | copy-start | bytes 393220
  38.2 0.9 %copy-start.2 = (f32[5,1,128,256]{3,2,1,0:T(8,128)}, f32[5,1,128,256]{3,2,1,0:T(8,128)S(1)}, u32[]{:S(2)}) copy-start(f32[5,1,128,256]{3,2,1,0:T(8,128)S(1)} %get-tuple-element.53.t_ref) | copy-start | bytes 1966084
  39.0 14.2 %copy-start.1 = (f32[5,1,128,256]{3,2,1,0:T(8,128)S(1)}, f32[5,1,128,256]{3,2,1,0:T(8,128)}, u32[]{:S(2)}) copy-start(f32[5,1,128,256]{3,2,1,0:T(8,128)} %get-tuple-element.54.l_ref.u_ref) | copy-start | bytes 1966084
  55.0 1.1 %copy-start.3 = (f32[5,1,128,256]{3,2,1,0:T(8,128)S(1)}, f32[5,1,128,256]{3,2,1,0:T(8,128)}, u32[]{:S(2)}) copy-start(f32[5,1,128,256]{3,2,1,0:T(8,128)} %get-tuple-element.16) | copy-start | bytes 1966084
  57.5 5.1 %collective-permute-start.4 = (f32[3,5,1,128,2]{3,4,2,1,0:T(2,128)S(1)}, f32[3,5,1,128,2]{3,4,2,1,0:T(2,128)S(1)}, u32[]{:S(2)}, u32[]{:S(2)}) collective-permute-start(f32[3,5,1,128,2]{3,4,2,1,0:T(2,128)S(1)} %pad_maximum_fusion.3), channel_id=1, source_target_pairs={{2,0},{4,2},{6,4},{0,6},{3,1},{5,3},{7,5},{1,7},{10,8},{12,10},{14... | collective-permute-start | bytes 46088 | tf_op jit(solution)/shard_map/ppermute | solution.py:99
  61.2 4.6 %collective-permute-start.5 = (f32[3,5,1,128,2]{3,4,2,1,0:T(2,128)S(1)}, f32[3,5,1,128,2]{3,4,2,1,0:T(2,128)S(1)}, u32[]{:S(2)}, u32[]{:S(2)}) collective-permute-start(f32[3,5,1,128,2]{3,4,2,1,0:T(2,128)S(1)} %pad_maximum_fusion.3), channel_id=1, source_target_pairs={{4,0},{6,2},{0,4},{2,6},{5,1},{7,3},{1,5},{3,7},{12,8},{14,10},{8,... | collective-permute-start | bytes 46088 | tf_op jit(solution)/shard_map/ppermute | solution.py:99
  61.2 5.5 %collective-permute-start.6 = (f32[3,5,1,128,2]{3,4,2,1,0:T(2,128)S(1)}, f32[3,5,1,128,2]{3,4,2,1,0:T(2,128)S(1)}, u32[]{:S(2)}, u32[]{:S(2)}) collective-permute-start(f32[3,5,1,128,2]{3,4,2,1,0:T(2,128)S(1)} %pad_maximum_fusion.3), channel_id=1, source_target_pairs={{6,0},{0,2},{2,4},{4,6},{7,1},{1,3},{3,5},{5,7},{14,8},{8,10},{10,... | collective-permute-start | bytes 46088 | tf_op jit(solution)/shard_map/ppermute | solution.py:99
  66.9 1.1 %copy-start.5 = (f32[5,1,128,256]{3,2,1,0:T(8,128)S(1)}, f32[5,1,128,256]{3,2,1,0:T(8,128)}, u32[]{:S(2)}) copy-start(f32[5,1,128,256]{3,2,1,0:T(8,128)} %get-tuple-element.15) | copy-start | bytes 1966084
  67.0 1.2 %copy-start.4 = (f32[5,1,128,256]{3,2,1,0:T(8,128)S(1)}, f32[5,1,128,256]{3,2,1,0:T(8,128)}, u32[]{:S(2)}) copy-start(f32[5,1,128,256]{3,2,1,0:T(8,128)} %get-tuple-element.14) | copy-start | bytes 1966084
  68.7 0.8 %copy-start.14 = (f32[5,1,128,256]{3,2,1,0:T(8,128)}, f32[5,1,128,256]{3,2,1,0:T(8,128)S(1)}, u32[]{:S(2)}) copy-start(f32[5,1,128,256]{3,2,1,0:T(8,128)S(1)} %add_dynamic-update-slice_fusion.1) | copy-start | bytes 1966084

commit v4 on v3

--- a/solution.py
+++ b/solution.py
@@ -55,6 +55,9 @@
     lower = l_ref[0, 0]
     upper = u_ref[0, 0]
     target = t_ref[0, 0]
+    flip = axis == 1
+    if flip:
+        lower, upper, target, axis = lower.T, upper.T, target.T, 0
     length = lower.shape[axis]
     idx = lax.broadcasted_iota(jnp.int32, lower.shape, axis)
     edge = (idx == 0) | (idx == length - 1)
@@ -73,6 +76,8 @@
         rhs = [(r - il * pltpu.roll(r, stride, axis) - iu * pltpu.roll(r, back, axis)) * inv for r in rhs]
         il, iu = -il * ll * inv, -iu * ur * inv
         stride = stride * 2
+    if flip:
+        rhs = [r.T for r in rhs]
     ot_ref[0, 0] = rhs[0]
     oa_ref[0, 0] = rhs[1]
     ob_ref[0, 0] = rhs[2]

time: 71.1 us -> 64.4 us (0.906)
  Pallas kernels: 20.8 us -> 14.1 us
    pallas_call x2, Pallas kernels: 20.8 us -> 14.1 us  [local_reduce(): pl.pallas_call(functools.partial(local_kernel, axis=axis - 2), grid=(nv,...]
  transfers between devices with their start and end apart: 7 -> 7, of which waited for: 6 -> 6; matrix products, arithmetic and copies ran while one was open for 8% -> 9% of each run, Pallas kernels for 0% -> 0%
where the time goes in v4:
time: 64.4 us; the launch traced here: 63.5 us
  waiting for transfers between devices  16.7 us (26%)
  Pallas kernels  14.1 us (22%)
  local copies, waits for them, and re-layouts  11.3 us (18%)
  other arithmetic  11.1 us (17%)
  starting transfers between devices  9.71 us (15%)
  between operations  0.69 us (1%)
    pallas_call x2, Pallas kernels, local_reduce(): pl.pallas_call(functools.partial(local_kernel, axis=axis - 2), grid=(nv,...  14.1 us
    ppermute x1, waiting for transfers between devices, plane_halo(): swapped = lax.ppermute(block, axis_name, [(0, 1), (1, 0)])  9.05 us
    ppermute x6, waiting for transfers between devices, gathered(): received.append(lax.ppermute(block, axis_name, pairs))  7.65 us
    ppermute x6, starting transfers between devices, gathered(): received.append(lax.ppermute(block, axis_name, pairs))  6.67 us
    unnamed x39, local copies, waits for them, and re-layouts  5.17 us
    slice x6, local copies, waits for them, and re-layouts, mix(): summed = summed + matrix[out_var, in_var][None, None, :] * values[in_var]  3.68 us
    ppermute x1, starting transfers between devices, plane_halo(): swapped = lax.ppermute(block, axis_name, [(0, 1), (1, 0)])  3.04 us
    mul x1, other arithmetic, solve_lines(): -le * a2 * inv_e  1.76 us
  transfers between devices with their start and end apart: 7, of which 6 were waited for; matrix products, arithmetic and copies ran while one was open for 9% of the time, Pallas kernels for 0%

profile of v4, /device:TPU:0, one launch (start us, length us, event | category | flops | bytes accessed | tf_op | source)
XLA Modules:
  0.0 63.5 jit_solution(7859590453073327598)
XLA Ops:
  0.0 3.0 %collective-permute-start = (f32[5,1,128,256]{3,2,0,1:T(8,128)}, f32[5,1,128,256]{3,2,0,1:T(8,128)S(1)}, u32[]{:S(2)}, u32[]{:S(2)}) collective-permute-start(f32[5,1,128,256]{3,2,0,1:T(8,128)} %bitcast.221), channel_id=1, source_target_pairs={{0,1},{1,0},{2,3},{3,2},{4,5},{5,4},{6,7},{7,6},{8,9},{9,8},{10,11... | collective-permute-start | bytes 1966088 | tf_op jit(solution)/shard_map/ppermute | solution.py:114
  3.0 1.0 %fusion.112 = (f32[1,1,256]{2,1,0:T(1,128)S(1)}, f32[1,1,256]{2,1,0:T(1,128)S(1)}, f32[1,1,256]{2,1,0:T(1,128)S(1)}, f32[1,1,256]{2,1,0:T(1,128)S(1)}, f32[1,1,2...) fusion(f32[5,5,256]{2,1,0:T(8,128)} %param.19), kind=kLoop, calls=%fused_computation.208 | loop fusion | bytes 38912 | tf_op jit(solution)/shard_map/slice | solution.py:158
  4.0 0.9 %fusion.113 = (f32[1,1,256]{2,1,0:T(1,128)S(1)}, f32[1,1,256]{2,1,0:T(1,128)S(1)}, f32[1,1,256]{2,1,0:T(1,128)S(1)}, f32[1,1,256]{2,1,0:T(1,128)S(1)}, f32[1,1,256]{2,1,0:T(1,128)S(1)}, /*index=5*/f32[1,1,256]{2,1,0:T(1,128)S(1)}) fusion(f32[5,5,256]{2,1,0:T(8,128)} %param.19), kind=kLoop, calls=%fused_computation.209 | loop fusion | bytes 12288 | tf_op jit(solution)/shard_map/slice | solution.py:158
  4.9 0.7 %broadcast_subtract_fusion = (f32[5,256]{1,0:T(8,128)S(1)}, f32[5,256]{1,0:T(8,128)S(1)}) fusion(f32[5,256]{1,0:T(8,128)} %param.16), kind=kLoop, calls=%fused_computation.179 | loop fusion | flops 2560 | bytes 15360 | tf_op jit(solution)/shard_map/sub | solution.py:186
  5.6 0.9 %fusion.94 = (f32[1,1,256]{2,1,0:T(1,128)S(1)}, f32[1,1,256]{2,1,0:T(1,128)S(1)}, f32[1,1,256]{2,1,0:T(1,128)S(1)}, f32[1,1,256]{2,1,0:T(1,128)S(1)}, f32[1,1,256]{2,1,0:T(1,128)S(1)}, /*index=5*/f32[1,1,256]{2,1,0:T(1,128)S(1)}) fusion(f32[5,5,256]{2,1,0:T(8,128)} %param.21), kind=kLoop, calls=%fused_computation.190 | loop fusion | bytes 12288 | tf_op jit(solution)/shard_map/slice | solution.py:158
  6.5 1.0 %fusion.93 = (f32[1,1,256]{2,1,0:T(1,128)S(1)}, f32[1,1,256]{2,1,0:T(1,128)S(1)}, f32[1,1,256]{2,1,0:T(1,128)S(1)}, f32[1,1,256]{2,1,0:T(1,128)S(1)}, f32[1,1,25...) fusion(f32[5,5,256]{2,1,0:T(8,128)} %param.21), kind=kLoop, calls=%fused_computation.189 | loop fusion | bytes 38912 | tf_op jit(solution)/shard_map/slice | solution.py:158
  7.6 1.4 %fusion.3 = (f32[5,1,128,256]{3,2,0,1:T(8,128)S(1)}, f32[5,1,128,256]{3,2,1,0:T(8,128)}, f32[5,1,128,256]{3,2,1,0:T(8,128)}, f32[5,1,128,256]{3,2,0,1:T(8,128)S(1)}) fusion(f32[5,256]{1,0:T(8,128)S(1)} %get-tuple-element.193, f32[128,256]{1,0:T(8,128)S(1)} %bitcast.213, f32[5,256]{1,0:T(8,128)S(1)} %copy-done.13, f32[5,256]{1,0:T(8,128)S(1)} %get-tuple-element.194), kind=kLoop, calls=%fused_computation.7 | loop fusion | flops 1310720 | bytes 2767872 | tf_op jit(solution)/shard_map/div | solution.py:186
  8.9 9.1 %collective-permute-done = f32[5,1,128,256]{3,2,0,1:T(8,128)S(1)} collective-permute-done((f32[5,1,128,256]{3,2,0,1:T(8,128)}, f32[5,1,128,256]{3,2,0,1:T(8,128)S(1)}, u32[]{:S(2)}, u32[]{:S(2)}) %collective-permute-start) | collective-permute-done | bytes 655392 | tf_op jit(solution)/shard_map/ppermute | solution.py:114
  18.0 0.2 bitcast_add_fusion
  18.5 0.9 %fusion.11.t_ref = f32[5,1,128,256]{3,2,1,0:T(8,128)} fusion(f32[5,1,128,256]{3,2,0,1:T(8,128)S(1)} %add_dynamic-update-slice_fusion.8, f32[128,256]{1,0:T(8,128)S(1)} %bitcast.214, f32[5,256]{1,0:T(8,128)S(1)} %copy-done.13), kind=kLoop, calls=%fused_computation.15 | loop fusion | flops 655360 | bytes 1446912 | tf_op jit(solution)/shard_map/div | solution.py:187
  19.5 6.6 %shard_map.109 = (f32[5,1,128,256]{3,2,1,0:T(8,128)}, f32[5,1,128,256]{3,2,1,0:T(8,128)}, f32[5,1,128,256]{3,2,1,0:T(8,128)}) custom-call(f32[5,1,128,256]{3,2,1,0:T(8,128)} %get-tuple-element.55.l_ref, f32[5,1,128,256]{3,2,1,0:T(8,128)} %get-tuple-element.50.u_ref, f32[5,1,128,256]{3,2,1,0:T(8,128)} %fusion.11.t_ref), custom_call_target="tpu_custom_call" | custom-call | tf_op jit(solution)/shard_map/pallas_call | solution.py:90
  26.1 0.9 %slice_multiply_fusion.9 = (f32[5,1,1,256]{3,2,0,1:T(1,128)S(1)}, f32[5,1,1,256]{3,2,0,1:T(1,128)S(1)}, f32[5,1,1,256]{3,2,0,1:T(1,128)S(1)}, f32[5,1,1,256]{3,2,0,1:T(1,128)S(1)}) fusion(f32[5,1,128,256]{3,2,0,1:T(8,128)S(1)} %get-tuple-element.56, f32[5,1,128,256]{3,2,0,1:T(8,128)} %bitcast.220, f32[5,1,128,256]{3,2,0,1:T(8,128)S(1)} %get-tuple-element.49, ...), kind=kLoop, calls=%fused_computation.170 | loop fusion | flops 12800 | bytes 51200 | tf_op jit(solution)/shard_map/mul | solution.py:138
  27.0 0.8 %fusion.76 = f32[5,1,1,256]{3,2,1,0:T(1,128)S(1)} fusion(f32[5,1,128,256]{3,2,0,1:T(8,128)} %bitcast.216, f32[5,1,128,256]{3,2,1,0:T(8,128)} %fusion.11.t_ref, f32[5,1,1,256]{3,2,0,1:T(1,128)S(1)} %get-tuple-element.34, f32[5,1,128,256]{3,2,0,1:T(8,128)S(1)} %get-tuple-element.56), kind=kLoop, calls=%fused_computation.157 | loop fusion | flops 3840 | bytes 25600 | tf_op jit(solution)/shard_map/mul | solution.py:140
  27.8 0.8 %fusion.79 = (f32[5,1,1,256]{3,2,0,1:T(1,128)S(1)}, f32[5,1,1,256]{3,2,1,0:T(1,128)S(1)}, f32[5,1,1,256]{3,2,0,1:T(1,128)S(1)}) fusion(f32[5,1,1,256]{3,2,0,1:T(1,128)S(1)} %get-tuple-element.26, f32[5,1,128,256]{3,2,0,1:T(8,128)} %bitcast.219, f32[5,1,128,256]{3,2,0,1:T(8,128)S(1)} %get-tuple-element.49, f32[5,1,128,256]{3,2,0,1:T(8,128)} %bitcast.217, ...), kind=kLoop, calls=%fused_computation.163 | loop fusion | flops 8960 | bytes 51200 | tf_op jit(solution)/shard_map/mul | solution.py:139
  28.7 0.3 collective-permute-start.1
  29.0 1.5 %collective-permute-start.2 = (f32[3,5,1,2,256]{4,3,1,2,0:T(2,128)S(1)}, f32[3,5,1,2,256]{4,3,1,2,0:T(2,128)S(1)}, u32[]{:S(2)}, u32[]{:S(2)}) collective-permute-start(f32[3,5,1,2,256]{4,3,1,2,0:T(2,128)S(1)} %pad_maximum_fusion.2), channel_id=1, source_target_pairs={{16,0},{24,8},{0,16},{8,24},{17,1},{25,9},{1,17},{9,25},{18,2},{26... | collective-permute-start | bytes 92168 | tf_op jit(solution)/shard_map/ppermute | solution.py:104
  30.5 0.2 collective-permute-start.3
  30.7 2.2 %collective-permute-done.2 = f32[3,5,1,2,256]{4,3,1,2,0:T(2,128)S(1)} collective-permute-done((f32[3,5,1,2,256]{4,3,1,2,0:T(2,128)S(1)}, f32[3,5,1,2,256]{4,3,1,2,0:T(2,128)S(1)}, u32[]{:S(2)}, u32[]{:S(2)}) %collective-permute-start.2) | collective-permute-done | bytes 30752 | tf_op jit(solution)/shard_map/ppermute | solution.py:104
  32.9 0.9 %collective-permute-done.3 = f32[3,5,1,2,256]{4,3,1,2,0:T(2,128)S(1)} collective-permute-done((f32[3,5,1,2,256]{4,3,1,2,0:T(2,128)S(1)}, f32[3,5,1,2,256]{4,3,1,2,0:T(2,128)S(1)}, u32[]{:S(2)}, u32[]{:S(2)}) %collective-permute-start.3) | collective-permute-done | bytes 30752 | tf_op jit(solution)/shard_map/ppermute | solution.py:104
  33.8 0.2 concatenate.431
  34.7 0.6 copy-done.9
  35.4 0.2 copy-done.7
  35.6 0.2 copy-done.8
  35.8 0.2 select_select_fusion.1
  36.3 0.8 %copy-done.12 = f32[1,128,256]{2,1,0:T(8,128)S(1)} copy-done((f32[1,128,256]{2,1,0:T(8,128)S(1)}, f32[1,128,256]{2,1,0:T(8,128)}, u32[]{:S(2)}) %copy-start.12) | copy-done | bytes 131096
  37.2 1.0 %fusion.8 = (f32[5,1,128,256]{3,2,1,0:T(8,128)S(1)}, f32[5,1,128,256]{3,2,1,0:T(8,128)}) fusion(f32[5,1,128,256]{3,2,1,0:T(8,128)S(1)} %add_dynamic-update-slice_fusion.4, f32[128,256]{1,0:T(8,128)S(1)} %bitcast.225, f32[5,256]{1,0:T(8,128)S(1)} %constant_dynamic-slice_fusion.3), kind=kLoop, calls=%fused_computation.12 | loop fusion | flops 983040 | bytes 2102272 | tf_op jit(solution)/shard_map/div | solution.py:193
  38.3 0.7 %copy-done.2 = f32[5,1,128,256]{3,2,1,0:T(8,128)} copy-done((f32[5,1,128,256]{3,2,1,0:T(8,128)}, f32[5,1,128,256]{3,2,1,0:T(8,128)S(1)}, u32[]{:S(2)}) %copy-start.2) | copy-done | bytes 655384
  39.0 7.5 %shard_map.110 = (f32[5,1,128,256]{3,2,1,0:T(8,128)}, f32[5,1,128,256]{3,2,1,0:T(8,128)}, f32[5,1,128,256]{3,2,1,0:T(8,128)}) custom-call(f32[5,1,128,256]{3,2,1,0:T(8,128)} %get-tuple-element.54.l_ref.u_ref, f32[5,1,128,256]{3,2,1,0:T(8,128)} %get-tuple-element.54.l_ref.u_ref, f32[5,1,128,256]{3,2,1,0:T(8,128)} %copy-done.2), custom_call_target="tpu_custom_call" | custom-call | tf_op jit(solution)/shard_map/pallas_call | solution.py:90
  46.5 1.8 %slice_multiply_fusion.1 = (f32[5,1,128,1]{3,2,1,0:T(8,128)S(1)}, f32[5,1,128,1]{3,2,1,0:T(8,128)S(1)}, f32[5,1,128,1]{3,2,1,0:T(8,128)S(1)}, f32[5,1,128,1]{3,2...) fusion(f32[5,1,128,256]{3,2,1,0:T(8,128)} %get-tuple-element.14, ...), kind=kLoop, calls=%fused_computation.22 | loop fusion | flops 6400 | bytes 30720 | tf_op jit(solution)/shard_map/mul | solution.py:138
  48.4 0.2 copy.127
  48.6 0.2 copy.132
  48.7 0.7 %copy-done.3 = f32[5,1,128,256]{3,2,1,0:T(8,128)S(1)} copy-done((f32[5,1,128,256]{3,2,1,0:T(8,128)S(1)}, f32[5,1,128,256]{3,2,1,0:T(8,128)}, u32[]{:S(2)}) %copy-start.3) | copy-done | bytes 655384
  49.4 0.2 fusion.91
  49.7 0.2 copy.138
  50.0 0.2 copy.131
  50.2 0.2 copy.134
  50.3 0.2 copy.141
  50.5 0.2 copy.142
  50.8 3.7 %collective-permute-start.4 = (f32[3,5,1,128,2]{3,4,2,1,0:T(2,128)S(1)}, f32[3,5,1,128,2]{3,4,2,1,0:T(2,128)S(1)}, u32[]{:S(2)}, u32[]{:S(2)}) collective-permute-start(f32[3,5,1,128,2]{3,4,2,1,0:T(2,128)S(1)} %pad_maximum_fusion.3), channel_id=1, source_target_pairs={{2,0},{4,2},{6,4},{0,6},{3,1},{5,3},{7,5},{1,7},{10,8},{12,10},{14... | collective-permute-start | bytes 46088 | tf_op jit(solution)/shard_map/ppermute | solution.py:104
  54.4 1.0 %collective-permute-start.6 = (f32[3,5,1,128,2]{3,4,2,1,0:T(2,128)S(1)}, f32[3,5,1,128,2]{3,4,2,1,0:T(2,128)S(1)}, u32[]{:S(2)}, u32[]{:S(2)}) collective-permute-start(f32[3,5,1,128,2]{3,4,2,1,0:T(2,128)S(1)} %pad_maximum_fusion.3), channel_id=1, source_target_pairs={{6,0},{0,2},{2,4},{4,6},{7,1},{1,3},{3,5},{5,7},{14,8},{8,10},{10,... | collective-permute-start | bytes 46088 | tf_op jit(solution)/shard_map/ppermute | solution.py:104
  55.4 0.4 collective-permute-done.4
  55.9 3.2 %collective-permute-done.5 = f32[3,5,1,128,2]{3,4,2,1,0:T(2,128)S(1)} collective-permute-done((f32[3,5,1,128,2]{3,4,2,1,0:T(2,128)S(1)}, f32[3,5,1,128,2]{3,4,2,1,0:T(2,128)S(1)}, u32[]{:S(2)}, u32[]{:S(2)}) %collective-permute-start.5) | collective-permute-done | bytes 15392 | tf_op jit(solution)/shard_map/ppermute | solution.py:104
  59.0 0.9 %collective-permute-done.6 = f32[3,5,1,128,2]{3,4,2,1,0:T(2,128)S(1)} collective-permute-done((f32[3,5,1,128,2]{3,4,2,1,0:T(2,128)S(1)}, f32[3,5,1,128,2]{3,4,2,1,0:T(2,128)S(1)}, u32[]{:S(2)}, u32[]{:S(2)}) %collective-permute-start.6) | collective-permute-done | bytes 15392 | tf_op jit(solution)/shard_map/ppermute | solution.py:104
  60.5 0.8 %copy-done.5 = f32[5,1,128,256]{3,2,1,0:T(8,128)S(1)} copy-done((f32[5,1,128,256]{3,2,1,0:T(8,128)S(1)}, f32[5,1,128,256]{3,2,1,0:T(8,128)}, u32[]{:S(2)}) %copy-start.5) | copy-done | bytes 655384
  61.3 0.2 copy-done.4
  61.5 0.2 select_select_fusion
  62.0 0.8 %copy-done.14 = f32[5,1,128,256]{3,2,1,0:T(8,128)} copy-done((f32[5,1,128,256]{3,2,1,0:T(8,128)}, f32[5,1,128,256]{3,2,1,0:T(8,128)S(1)}, u32[]{:S(2)}) %copy-start.14) | copy-done | bytes 655384
  62.8 0.7 %add_dynamic-update-slice_fusion = f32[5,1,128,256]{3,2,1,0:T(8,128)} fusion(f32[5,1,128,256]{3,2,1,0:T(8,128)} %copy-done.14, f32[5,1,128,256]{3,2,1,0:T(8,128)S(1)} %select_select_fusion, f32[256]{0:T(256)S(1)} %bitcast.229, f32[256]{0:T(256)S(1)} %bitcast.228, f32[256]{0:T(256)S(1)} %bitcast.235, f32[256]{0:T(256)S(1)} %bitcast.236, f32[256]{0:T(256)S(1)} %bitcast.234), kind=kLoop, calls=%fused_computation.42 | loop fusion | flops 327680 | bytes 791552 | tf_op jit(solution)/shard_map/stack | solution.py:160
  (106 shorter events, 2.5 us)
Async XLA Ops:
  0.0 6.5 %copy-start = (f32[5,1024]{1,0:T(8,128)S(1)}, f32[5,1024]{1,0:T(8,128)}, u32[]{:S(2)}) copy-start(f32[5,1024]{1,0:T(8,128)} %param.17) | copy-start | bytes 61444
  0.0 4.9 %copy-start.15 = (f32[5,5,256]{2,1,0:T(8,128)S(1)}, f32[5,5,256]{2,1,0:T(8,128)}, u32[]{:S(2)}) copy-start(f32[5,5,256]{2,1,0:T(8,128)} %param.20) | copy-start | bytes 76804
  0.0 7.5 %copy-start.6 = (f32[1,128,256]{2,1,0:T(8,128)S(1)}, f32[1,128,256]{2,1,0:T(8,128)}, u32[]{:S(2)}) copy-start(f32[1,128,256]{2,1,0:T(8,128)} %param.13) | copy-start | bytes 393220
  0.0 18.0 %collective-permute-start = (f32[5,1,128,256]{3,2,0,1:T(8,128)}, f32[5,1,128,256]{3,2,0,1:T(8,128)S(1)}, u32[]{:S(2)}, u32[]{:S(2)}) collective-permute-start(f32[5,1,128,256]{3,2,0,1:T(8,128)} %bitcast.221), channel_id=1, source_target_pairs={{0,1},{1,0},{2,3},{3,2},{4,5},{5,4},{6,7},{7,6},{8,9},{9,8},{10,11... | collective-permute-start | bytes 1966088 | tf_op jit(solution)/shard_map/ppermute | solution.py:114
  6.5 1.0 %copy-start.13 = (f32[5,256]{1,0:T(8,128)S(1)}, f32[5,256]{1,0:T(8,128)}, u32[]{:S(2)}) copy-start(f32[5,256]{1,0:T(8,128)} %param.15) | copy-start | bytes 15364
  7.5 10.5 %copy-start.10 = (f32[5,1,128,256]{3,2,1,0:T(8,128)S(1)}, f32[5,1,128,256]{3,2,1,0:T(8,128)}, u32[]{:S(2)}) copy-start(f32[5,1,128,256]{3,2,1,0:T(8,128)} %param.12) | copy-start | bytes 1966084
  7.5 10.4 %copy-start.11 = (f32[5,1,128,256]{3,2,1,0:T(8,128)S(1)}, f32[5,1,128,256]{3,2,1,0:T(8,128)}, u32[]{:S(2)}) copy-start(f32[5,1,128,256]{3,2,1,0:T(8,128)} %param.11) | copy-start | bytes 1966084
  7.6 10.4 %copy-start.16 = (f32[5,256]{1,0:T(8,128)S(1)}, f32[5,256]{1,0:T(8,128)}, u32[]{:S(2)}) copy-start(f32[5,256]{1,0:T(8,128)} %param.18) | copy-start | bytes 15364
  28.7 2.0 %collective-permute-start.1 = (f32[3,5,1,2,256]{4,3,1,2,0:T(2,128)S(1)}, f32[3,5,1,2,256]{4,3,1,2,0:T(2,128)S(1)}, u32[]{:S(2)}, u32[]{:S(2)}) collective-permute-start(f32[3,5,1,2,256]{4,3,1,2,0:T(2,128)S(1)} %pad_maximum_fusion.2), channel_id=1, source_target_pairs={{8,0},{16,8},{24,16},{0,24},{9,1},{17,9},{25,17},{1,25},{10,2},{18... | collective-permute-start | bytes 92168 | tf_op jit(solution)/shard_map/ppermute | solution.py:104
  29.0 3.9 %collective-permute-start.2 = (f32[3,5,1,2,256]{4,3,1,2,0:T(2,128)S(1)}, f32[3,5,1,2,256]{4,3,1,2,0:T(2,128)S(1)}, u32[]{:S(2)}, u32[]{:S(2)}) collective-permute-start(f32[3,5,1,2,256]{4,3,1,2,0:T(2,128)S(1)} %pad_maximum_fusion.2), channel_id=1, source_target_pairs={{16,0},{24,8},{0,16},{8,24},{17,1},{25,9},{1,17},{9,25},{18,2},{26... | collective-permute-start | bytes 92168 | tf_op jit(solution)/shard_map/ppermute | solution.py:104
  30.5 3.3 %collective-permute-start.3 = (f32[3,5,1,2,256]{4,3,1,2,0:T(2,128)S(1)}, f32[3,5,1,2,256]{4,3,1,2,0:T(2,128)S(1)}, u32[]{:S(2)}, u32[]{:S(2)}) collective-permute-start(f32[3,5,1,2,256]{4,3,1,2,0:T(2,128)S(1)} %pad_maximum_fusion.2), channel_id=1, source_target_pairs={{24,0},{0,8},{8,16},{16,24},{25,1},{1,9},{9,17},{17,25},{26,2},{2,... | collective-permute-start | bytes 92168 | tf_op jit(solution)/shard_map/ppermute | solution.py:104
  34.3 1.1 %copy-start.9 = (f32[5,1,128,256]{3,2,1,0:T(8,128)S(1)}, f32[5,1,128,256]{3,2,1,0:T(8,128)}, u32[]{:S(2)}) copy-start(f32[5,1,128,256]{3,2,1,0:T(8,128)} %get-tuple-element.11) | copy-start | bytes 1966084
  34.4 1.2 %copy-start.7 = (f32[5,1,128,256]{3,2,1,0:T(8,128)S(1)}, f32[5,1,128,256]{3,2,1,0:T(8,128)}, u32[]{:S(2)}) copy-start(f32[5,1,128,256]{3,2,1,0:T(8,128)} %get-tuple-element.13) | copy-start | bytes 1966084
  34.4 1.4 %copy-start.8 = (f32[5,1,128,256]{3,2,1,0:T(8,128)S(1)}, f32[5,1,128,256]{3,2,1,0:T(8,128)}, u32[]{:S(2)}) copy-start(f32[5,1,128,256]{3,2,1,0:T(8,128)} %get-tuple-element.12) | copy-start | bytes 1966084
  36.3 0.9 %copy-start.12 = (f32[1,128,256]{2,1,0:T(8,128)S(1)}, f32[1,128,256]{2,1,0:T(8,128)}, u32[]{:S(2)}) copy-start(f32[1,128,256]{2,1,0:T(8,128)} %param.14) | copy-start | bytes 393220
  38.2 0.9 %copy-start.2 = (f32[5,1,128,256]{3,2,1,0:T(8,128)}, f32[5,1,128,256]{3,2,1,0:T(8,128)S(1)}, u32[]{:S(2)}) copy-start(f32[5,1,128,256]{3,2,1,0:T(8,128)S(1)} %get-tuple-element.53.t_ref) | copy-start | bytes 1966084
  39.0 7.5 %copy-start.1 = (f32[5,1,128,256]{3,2,1,0:T(8,128)S(1)}, f32[5,1,128,256]{3,2,1,0:T(8,128)}, u32[]{:S(2)}) copy-start(f32[5,1,128,256]{3,2,1,0:T(8,128)} %get-tuple-element.54.l_ref.u_ref) | copy-start | bytes 1966084
  48.3 1.1 %copy-start.3 = (f32[5,1,128,256]{3,2,1,0:T(8,128)S(1)}, f32[5,1,128,256]{3,2,1,0:T(8,128)}, u32[]{:S(2)}) copy-start(f32[5,1,128,256]{3,2,1,0:T(8,128)} %get-tuple-element.16) | copy-start | bytes 1966084
  50.8 5.1 %collective-permute-start.4 = (f32[3,5,1,128,2]{3,4,2,1,0:T(2,128)S(1)}, f32[3,5,1,128,2]{3,4,2,1,0:T(2,128)S(1)}, u32[]{:S(2)}, u32[]{:S(2)}) collective-permute-start(f32[3,5,1,128,2]{3,4,2,1,0:T(2,128)S(1)} %pad_maximum_fusion.3), channel_id=1, source_target_pairs={{2,0},{4,2},{6,4},{0,6},{3,1},{5,3},{7,5},{1,7},{10,8},{12,10},{14... | collective-permute-start | bytes 46088 | tf_op jit(solution)/shard_map/ppermute | solution.py:104
  54.4 4.6 %collective-permute-start.5 = (f32[3,5,1,128,2]{3,4,2,1,0:T(2,128)S(1)}, f32[3,5,1,128,2]{3,4,2,1,0:T(2,128)S(1)}, u32[]{:S(2)}, u32[]{:S(2)}) collective-permute-start(f32[3,5,1,128,2]{3,4,2,1,0:T(2,128)S(1)} %pad_maximum_fusion.3), channel_id=1, source_target_pairs={{4,0},{6,2},{0,4},{2,6},{5,1},{7,3},{1,5},{3,7},{12,8},{14,10},{8,... | collective-permute-start | bytes 46088 | tf_op jit(solution)/shard_map/ppermute | solution.py:104
  54.4 5.5 %collective-permute-start.6 = (f32[3,5,1,128,2]{3,4,2,1,0:T(2,128)S(1)}, f32[3,5,1,128,2]{3,4,2,1,0:T(2,128)S(1)}, u32[]{:S(2)}, u32[]{:S(2)}) collective-permute-start(f32[3,5,1,128,2]{3,4,2,1,0:T(2,128)S(1)} %pad_maximum_fusion.3), channel_id=1, source_target_pairs={{6,0},{0,2},{2,4},{4,6},{7,1},{1,3},{3,5},{5,7},{14,8},{8,10},{10,... | collective-permute-start | bytes 46088 | tf_op jit(solution)/shard_map/ppermute | solution.py:104
  60.2 1.1 %copy-start.5 = (f32[5,1,128,256]{3,2,1,0:T(8,128)S(1)}, f32[5,1,128,256]{3,2,1,0:T(8,128)}, u32[]{:S(2)}) copy-start(f32[5,1,128,256]{3,2,1,0:T(8,128)} %get-tuple-element.15) | copy-start | bytes 1966084
  60.2 1.2 %copy-start.4 = (f32[5,1,128,256]{3,2,1,0:T(8,128)S(1)}, f32[5,1,128,256]{3,2,1,0:T(8,128)}, u32[]{:S(2)}) copy-start(f32[5,1,128,256]{3,2,1,0:T(8,128)} %get-tuple-element.14) | copy-start | bytes 1966084
  62.0 0.8 %copy-start.14 = (f32[5,1,128,256]{3,2,1,0:T(8,128)}, f32[5,1,128,256]{3,2,1,0:T(8,128)S(1)}, u32[]{:S(2)}) copy-start(f32[5,1,128,256]{3,2,1,0:T(8,128)S(1)} %add_dynamic-update-slice_fusion.1) | copy-start | bytes 1966084

commit v5 on v1

--- a/solution.py
+++ b/solution.py
@@ -1,7 +1,10 @@
 import jax
 import jax.numpy as jnp
 from jax import lax
+from jax.experimental import pallas as pl
+from jax.experimental.pallas import tpu as pltpu
 from jax.sharding import PartitionSpec as P
+import functools
 
 
 def with_halo(block, sides, width, periodic):
@@ -48,44 +51,151 @@
     return lower, upper, rhs
 
 
-def row(values, index, axis):
-    return lax.slice_in_dim(values, index, index + 1, axis=axis)
-
-
-def solve_lines(lower, upper, target, axis, axis_name, periodic):
-    length = lower.shape[axis]
-    idx = lax.broadcasted_iota(jnp.int32, lower.shape, axis)
+def reduce_block(lower, upper, target, red_ref, index):
+    length = lower.shape[0]
+    idx = lax.broadcasted_iota(jnp.int32, lower.shape, 0)
     edge = (idx == 0) | (idx == length - 1)
     second = idx == 1
     penult = idx == length - 2
     zero = jnp.zeros_like(lower)
     il = jnp.where(edge | second, zero, lower)
     iu = jnp.where(edge | penult, zero, upper)
-    it = jnp.where(edge, zero, target)
-    ia = jnp.where(second, lower, zero)
-    ib = jnp.where(penult, upper, zero)
-    _, _, (it, ia, ib) = cyclic_reduce(il, iu, [it, ia, ib], axis, False, length - 2)
-    l0, u0, t0 = row(lower, 0, axis), row(upper, 0, axis), row(target, 0, axis)
-    le, ue, te = (row(v, length - 1, axis) for v in (lower, upper, target))
-    a1, b1, t1 = row(ia, 1, axis), row(ib, 1, axis), row(it, 1, axis)
-    a2, b2, t2 = (row(v, length - 2, axis) for v in (ia, ib, it))
+    rhs = [jnp.where(edge, zero, target), jnp.where(second, lower, zero), jnp.where(penult, upper, zero)]
+    stride = 1
+    while stride < length - 2:
+        back = length - stride
+        ll, ul = pltpu.roll(il, stride, 0), pltpu.roll(iu, stride, 0)
+        lr, ur = pltpu.roll(il, back, 0), pltpu.roll(iu, back, 0)
+        inv = 1.0 / (1.0 - il * ul - iu * lr)
+        rhs = [(r - il * pltpu.roll(r, stride, 0) - iu * pltpu.roll(r, back, 0)) * inv for r in rhs]
+        il, iu = -il * ll * inv, -iu * ur * inv
+        stride = stride * 2
+    it, ia, ib = rhs
+    l0, u0, t0 = lower[0:1], upper[0:1], target[0:1]
+    le, ue, te = lower[length - 1 :], upper[length - 1 :], target[length - 1 :]
+    a1, b1, t1 = ia[1:2], ib[1:2], it[1:2]
+    a2, b2, t2 = ia[length - 2 : length - 1], ib[length - 2 : length - 1], it[length - 2 : length - 1]
     inv_f = 1.0 / (1.0 - u0 * a1)
     inv_e = 1.0 / (1.0 - le * b2)
-    red = jnp.stack(
-        [
-            jnp.concatenate([l0 * inv_f, -le * a2 * inv_e], axis=axis),
-            jnp.concatenate([-u0 * b1 * inv_f, ue * inv_e], axis=axis),
-            jnp.concatenate([(t0 - u0 * t1) * inv_f, (te - le * t2) * inv_e], axis=axis),
-        ]
+    rows = (
+        l0 * inv_f,
+        -le * a2 * inv_e,
+        -u0 * b1 * inv_f,
+        ue * inv_e,
+        (t0 - u0 * t1) * inv_f,
+        (te - le * t2) * inv_e,
     )
-    red = lax.all_gather(red, axis_name, axis=axis + 1, tiled=True)
-    count = red.shape[axis + 1]
-    rl, ru, (rt,) = cyclic_reduce(red[0], red[1], [red[2]], axis, periodic, count)
+    for k, value in enumerate(rows):
+        red_ref[index, 0, k : k + 1, :] = value
+    return it, ia, ib
+
+
+def az_kernel(fs_ref, nb_ref, src_ref, cell_ref, visc_ref, beta_ref, diff_ref, mix_ref, ot_ref, oa_ref, ob_ref, red_ref):
+    count = fs_ref.shape[0]
+    explicit = []
+    for w in range(count):
+        explicit.append(src_ref[w, 0] + diff_ref[w : w + 1, :] * (nb_ref[w, 0] - 2.0 * fs_ref[w, 0]))
+    cell = cell_ref[0]
+    for v in range(count):
+        summed = explicit[v]
+        for w in range(count):
+            summed = summed + mix_ref[v, w : w + 1, :] * explicit[w]
+        coupling = visc_ref[v : v + 1, :] * cell
+        centre = 1.0 + 2.0 * coupling
+        tilt = beta_ref[v : v + 1, :]
+        lower = -coupling * (1.0 + tilt) / centre
+        upper = -coupling * (1.0 - tilt) / centre
+        it, ia, ib = reduce_block(lower, upper, summed / centre, red_ref, v)
+        ot_ref[v, 0] = it
+        oa_ref[v, 0] = ia
+        ob_ref[v, 0] = ib
+
+
+def rad_kernel(it_ref, ia_ref, ib_ref, ends_ref, mix_ref, cell_ref, visc_ref, ot_ref, oa_ref, ob_ref, red_ref):
+    count = it_ref.shape[0]
+    length = it_ref.shape[2]
+    idx = lax.broadcasted_iota(jnp.int32, it_ref.shape[2:], 0)
+    solved = []
+    for w in range(count):
+        first = ends_ref[w, 0, 0:1, :]
+        last = ends_ref[w, 0, 1:2, :]
+        inner = it_ref[w, 0] - ia_ref[w, 0] * first - ib_ref[w, 0] * last
+        solved.append(jnp.where(idx == 0, first, jnp.where(idx == length - 1, last, inner)))
+    cell = cell_ref[0]
+    for v in range(count):
+        summed = solved[v]
+        for w in range(count):
+            summed = summed + mix_ref[v, w : w + 1, :] * solved[w]
+        coupling = visc_ref[v : v + 1, :] * cell
+        centre = 1.0 + 2.0 * coupling
+        side = (-coupling / centre).T
+        it, ia, ib = reduce_block(side, side, (summed / centre).T, red_ref, v)
+        ot_ref[v, 0] = it.T
+        oa_ref[v, 0] = ia.T
+        ob_ref[v, 0] = ib.T
+
+
+def az_sweep(flow_state, nb, source, cell_az, visc_az, beta_az, axial_diff, mix_in):
+    nv, nz, na, nr = flow_state.shape
+    chunk = 128 if nr % 128 == 0 else nr
+    big = pl.BlockSpec((nv, 1, na, chunk), lambda z, c: (0, z, 0, c))
+    cell = pl.BlockSpec((1, na, chunk), lambda z, c: (z, 0, c))
+    par = pl.BlockSpec((nv, chunk), lambda z, c: (0, c))
+    mixs = pl.BlockSpec((nv, nv, chunk), lambda z, c: (0, 0, c))
+    red = pl.BlockSpec((nv, 1, 6, chunk), lambda z, c: (0, z, 0, c))
+    out = jax.ShapeDtypeStruct(flow_state.shape, flow_state.dtype)
+    return pl.pallas_call(
+        az_kernel,
+        grid=(nz, nr // chunk),
+        in_specs=[big, big, big, cell, par, par, par, mixs],
+        out_specs=[big, big, big, red],
+        out_shape=[out, out, out, jax.ShapeDtypeStruct((nv, nz, 6, nr), flow_state.dtype)],
+    )(flow_state, nb, source, cell_az, visc_az, beta_az, axial_diff, mix_in)
+
+
+def rad_sweep(it, ia, ib, ends, mix_mid, cell_rad, visc_local):
+    nv, nz, na, nr = it.shape
+    big = pl.BlockSpec((nv, 1, na, nr), lambda z: (0, z, 0, 0))
+    endspec = pl.BlockSpec((nv, 1, 2, nr), lambda z: (0, z, 0, 0))
+    mixs = pl.BlockSpec((nv, nv, nr), lambda z: (0, 0, 0))
+    cell = pl.BlockSpec((1, na, nr), lambda z: (z, 0, 0))
+    par = pl.BlockSpec((nv, nr), lambda z: (0, 0))
+    red = pl.BlockSpec((nv, 1, 6, na), lambda z: (0, z, 0, 0))
+    out = jax.ShapeDtypeStruct(it.shape, it.dtype)
+    return pl.pallas_call(
+        rad_kernel,
+        grid=(nz,),
+        in_specs=[big, big, big, endspec, mixs, cell, par],
+        out_specs=[big, big, big, red],
+        out_shape=[out, out, out, jax.ShapeDtypeStruct((nv, nz, 6, na), it.dtype)],
+    )(it, ia, ib, ends, mix_mid, cell_rad, visc_local)
+
+
+def gathered(block, axis_name, dim):
+    count = lax.axis_size(axis_name)
+    received = [block]
+    for offset in range(1, count):
+        pairs = [((i + offset) % count, i) for i in range(count)]
+        received.append(lax.ppermute(block, axis_name, pairs))
+    doubled = jnp.concatenate(received + received, axis=dim)
+    start = ((count - lax.axis_index(axis_name)) % count) * block.shape[dim]
+    return lax.dynamic_slice_in_dim(doubled, start, count * block.shape[dim], dim)
+
+
+def reduced_solve(red, axis_name, periodic):
+    stacked = jnp.stack([red[:, :, 0:2], red[:, :, 2:4], red[:, :, 4:6]])
+    full = gathered(stacked, axis_name, 3)
+    rl, ru, (rt,) = cyclic_reduce(full[0], full[1], [full[2]], 2, periodic, full.shape[3])
     ends = rt / (1.0 + rl + ru)
-    mine = lax.dynamic_slice_in_dim(ends, 2 * lax.axis_index(axis_name), 2, axis)
-    first, last = row(mine, 0, axis), row(mine, 1, axis)
-    inner = it - ia * first - ib * last
-    return jnp.where(idx == 0, first, jnp.where(idx == length - 1, last, inner))
+    return lax.dynamic_slice_in_dim(ends, 2 * lax.axis_index(axis_name), 2, 2)
+
+
+def neighbour_planes(block, axis_name):
+    count = lax.axis_size(axis_name)
+    if count == 2:
+        return lax.ppermute(block, axis_name, [(0, 1), (1, 0)])
+    padded = with_halo(block, ((axis_name, 1),), 1, False)
+    return padded[:, :-2] + padded[:, 2:]
 
 
 def mix(matrix, values):
@@ -112,23 +222,17 @@
     mix_out,
 ):
     rad_cells = flow_state.shape[3]
-    padded = with_halo(flow_state, (("ax", 1),), 1, False)
-    explicit = source + axial_diff[:, None, None, :] * (
-        padded[:, :-2] - 2.0 * flow_state + padded[:, 2:]
-    )
-    section_one = mix(mix_in, explicit)
-    coupling = visc_az[:, None, None, :] * cell_az[None]
-    centre = 1.0 + 2.0 * coupling
-    tilt = beta_az[:, None, None, :]
-    lower = -coupling * (1.0 + tilt) / centre
-    upper = -coupling * (1.0 - tilt) / centre
-    section_two = solve_lines(lower, upper, section_one / centre, 2, "az", True)
-    section_three = mix(mix_mid, section_two)
+    nb = neighbour_planes(flow_state, "ax")
+    it, ia, ib, red = az_sweep(flow_state, nb, source, cell_az, visc_az, beta_az, axial_diff, mix_in)
+    ends = reduced_solve(red, "az", True)
     visc_local = lax.dynamic_slice_in_dim(visc_rad, lax.axis_index("rad") * rad_cells, rad_cells, 1)
-    coupling = visc_local[:, None, None, :] * cell_rad[None]
-    centre = 1.0 + 2.0 * coupling
-    side = -coupling / centre
-    section_four = solve_lines(side, side, section_three / centre, 3, "rad", False)
+    it, ia, ib, red = rad_sweep(it, ia, ib, ends, mix_mid, cell_rad, visc_local)
+    ends = reduced_solve(red, "rad", False)
+    first = ends[:, :, 0, :, None]
+    last = ends[:, :, 1, :, None]
+    idx = lax.broadcasted_iota(jnp.int32, it.shape, 3)
+    inner = it - ia * first - ib * last
+    section_four = jnp.where(idx == 0, first, jnp.where(idx == rad_cells - 1, last, inner))
     return mix(mix_out, section_four)
 
 

time: 133 us -> 57.2 us (0.43)
  local copies, waits for them, and re-layouts: 72.3 us -> 8.03 us
  other arithmetic: 32.1 us -> 3.36 us
  waiting for transfers between devices: 0.01 us -> 20.2 us
  blocking collectives: 18.8 us -> 0 us
  Pallas kernels: 0 us -> 15.1 us
  starting transfers between devices: 7.13 us -> 9.65 us
  between operations: 2.46 us -> 0.35 us
    ppermute x2 -> x7, waiting for transfers between devices: 0.01 us -> 20.2 us  [the longest x1 13.1 us: neighbour_planes(): return lax.ppermute(block, axis_name, [(0, 1), (1, 0)])]
    all_gather x2 -> x0, blocking collectives: 18.8 us -> none  [solve_lines(): red = lax.all_gather(red, axis_name, axis=axis + 1, tiled=True)]
    mul x27 -> x2, other arithmetic: 17.3 us -> 0.12 us  [cyclic_reduce(): (r - lower * shifted(r, stride, axis, periodic) - upper * shifted(r, -str...]
    slice x18 -> x4, local copies, waits for them, and re-layouts: 17.1 us -> 0.02 us  [shifted(): kept = lax.slice_in_dim(values, -offset, length, axis=axis)]
    pallas_call x0 -> x2, Pallas kernels: none -> 15.1 us  [the longest x1 8.04 us: rad_sweep(): pl.pallas_call(rad_kernel, grid=(nz,), in_specs=[big, big, big, endspec,...]
    unnamed x250 -> x12, local copies, waits for them, and re-layouts: 16 us -> 2.63 us
    slice x65 -> x5, local copies, waits for them, and re-layouts: 13 us -> 0.03 us  [shifted(): kept = lax.slice_in_dim(values, 0, length - offset, axis=axis)]
    slice x12 -> x1, local copies, waits for them, and re-layouts: 11.3 us -> 0.01 us  [per_device(): first = ends[:, :, 0, :, None]]
  transfers between devices with their start and end apart: 2 -> 7, of which waited for: 0 -> 6; matrix products, arithmetic and copies ran while one was open for 16% -> 4% of each run, Pallas kernels for 0% -> 0%
where the time goes in v5:
time: 57.2 us; the launch traced here: 56.7 us
  waiting for transfers between devices  20.2 us (35%)
  Pallas kernels  15.1 us (26%)
  starting transfers between devices  9.65 us (17%)
  local copies, waits for them, and re-layouts  8.03 us (14%)
  other arithmetic  3.36 us (6%)
    ppermute x1, waiting for transfers between devices, neighbour_planes(): return lax.ppermute(block, axis_name, [(0, 1), (1, 0)])  13.1 us
    pallas_call x1, Pallas kernels, rad_sweep(): pl.pallas_call(rad_kernel, grid=(nz,), in_specs=[big, big, big, endspec,...  8.04 us
    pallas_call x1, Pallas kernels, az_sweep(): pl.pallas_call(az_kernel, grid=(nz, nr // chunk), in_specs=[big, big, big...  7.08 us
    ppermute x6, waiting for transfers between devices, gathered(): received.append(lax.ppermute(block, axis_name, pairs))  7.07 us
    ppermute x6, starting transfers between devices, gathered(): received.append(lax.ppermute(block, axis_name, pairs))  6.68 us
    ppermute x1, starting transfers between devices, neighbour_planes(): return lax.ppermute(block, axis_name, [(0, 1), (1, 0)])  2.97 us
    unnamed x12, local copies, waits for them, and re-layouts  2.63 us
    another operation x3, local copies, waits for them, and re-layouts, reduced_solve(): stacked = jnp.stack([red[:, :, 0:2], red[:, :, 2:4], red[:, :, 4:6]])  2.45 us
  transfers between devices with their start and end apart: 7, of which 6 were waited for; matrix products, arithmetic and copies ran while one was open for 4% of the time, Pallas kernels for 0%

profile of v5, /device:TPU:0, one launch (start us, length us, event | category | flops | bytes accessed | tf_op | source)
XLA Modules:
  0.0 56.7 jit_solution(8652162084683557239)
XLA Ops:
  0.0 0.0 copy-start
  0.0 3.0 %collective-permute-start = (f32[5,1,128,256]{3,2,1,0:T(8,128)}, f32[5,1,128,256]{3,2,1,0:T(8,128)S(1)}, u32[]{:S(2)}, u32[]{:S(2)}) collective-permute-start(f32[5,1,128,256]{3,2,1,0:T(8,128)} %fs_ref.1), channel_id=1, source_target_pairs={{0,1},{1,0},{2,3},{3,2},{4,5},{5,4},{6,7},{7,6},{8,9},{9,8},{10,11... | collective-permute-start | bytes 1966088 | tf_op jit(solution)/shard_map/ppermute | solution.py:196
  3.0 0.9 %fusion.54 = (f32[1,1,256]{2,1,0:T(1,128)S(1)}, f32[1,1,256]{2,1,0:T(1,128)S(1)}, f32[1,1,256]{2,1,0:T(1,128)S(1)}, f32[1,1,256]{2,1,0:T(1,128)S(1)}, f32[1,1,256]{2,1,0:T(1,128)S(1)}, /*index=5*/f32[1,1,256]{2,1,0:T(1,128)S(1)}) fusion(f32[5,5,256]{2,1,0:T(8,128)} %param.21), kind=kLoop, calls=%fused_computation.117 | loop fusion | bytes 12288 | tf_op jit(solution)/shard_map/slice | solution.py:206
  3.8 1.0 %fusion.53 = (f32[1,1,256]{2,1,0:T(1,128)S(1)}, f32[1,1,256]{2,1,0:T(1,128)S(1)}, f32[1,1,256]{2,1,0:T(1,128)S(1)}, f32[1,1,256]{2,1,0:T(1,128)S(1)}, f32[1,1,25...) fusion(f32[5,5,256]{2,1,0:T(8,128)} %param.21), kind=kLoop, calls=%fused_computation.116 | loop fusion | bytes 38912 | tf_op jit(solution)/shard_map/slice | solution.py:206
  4.8 13.1 %collective-permute-done.nb_ref = f32[5,1,128,256]{3,2,1,0:T(8,128)S(1)} collective-permute-done((f32[5,1,128,256]{3,2,1,0:T(8,128)}, f32[5,1,128,256]{3,2,1,0:T(8,128)S(1)}, u32[]{:S(2)}, u32[]{:S(2)}) %collective-permute-start) | collective-permute-done | bytes 655392 | tf_op jit(solution)/shard_map/ppermute | solution.py:196
  17.9 0.0 copy-start.1
  17.9 0.8 %copy-done.1 = f32[5,1,128,256]{3,2,1,0:T(8,128)} copy-done((f32[5,1,128,256]{3,2,1,0:T(8,128)}, f32[5,1,128,256]{3,2,1,0:T(8,128)S(1)}, u32[]{:S(2)}) %copy-start.1) | copy-done | bytes 655384
  18.7 7.1 %shard_map.109 = (f32[5,1,128,256]{3,2,1,0:T(8,128)}, f32[5,1,128,256]{3,2,1,0:T(8,128)}, f32[5,1,128,256]{3,2,1,0:T(8,128)}, f32[5,1,6,256]{3,2,1,0:T(8,128)}) custom-call(f32[5,1,128,256]{3,2,1,0:T(8,128)} %fs_ref.1, f32[5,1,128,256]{3,2,1,0:T(8,128)} %copy-done.1, f32[5,1,128,256]{3,2,1,0:T(8,128)} %src_ref.1, f32[1,128,256]{2,1,0:T(8,128)} %cell_ref.2, ...), custom_call_target="tpu_custom_call" | custom-call | tf_op jit(solution)/shard_map/pallas_call | solution.py:147
  25.8 0.9 %slice_bitcast_fusion.2 = (f32[1,5,1,2,256]{4,3,1,2,0:T(2,128)S(1)}, f32[1,5,1,2,256]{4,3,1,2,0:T(2,128)S(1)}, f32[1,5,1,2,256]{4,3,1,2,0:T(2,128)S(1)}) fusion(f32[5,1,6,256]{3,2,0,1:T(8,128)} %bitcast.57), kind=kLoop, calls=%fused_computation.88 | loop fusion | bytes 61440 | tf_op jit(solution)/shard_map/stack | solution.py:186
  26.8 0.3 collective-permute-start.1
  27.1 1.5 %collective-permute-start.2 = (f32[3,5,1,2,256]{4,3,1,2,0:T(2,128)S(1)}, f32[3,5,1,2,256]{4,3,1,2,0:T(2,128)S(1)}, u32[]{:S(2)}, u32[]{:S(2)}) collective-permute-start(f32[3,5,1,2,256]{4,3,1,2,0:T(2,128)S(1)} %pad_maximum_fusion.2), channel_id=1, source_target_pairs={{16,0},{24,8},{0,16},{8,24},{17,1},{25,9},{1,17},{9,25},{18,2},{26... | collective-permute-start | bytes 92168 | tf_op jit(solution)/shard_map/ppermute | solution.py:179
  28.6 0.2 collective-permute-start.3
  28.8 0.0 copy-done
  28.8 0.6 %constant_dynamic-slice_fusion.5.visc_ref = f32[5,256]{1,0:T(8,128)} fusion(f32[5,1024]{1,0:T(8,128)S(1)} %copy-done, s32[]{:T(128)S(6)} %select_n.36), kind=kLoop, calls=%fused_computation.94 | loop fusion | bytes 10244 | tf_op jit(solution)/shard_map/dynamic_slice | solution.py:228
  29.4 0.0 collective-permute-done.1
  29.4 1.6 %collective-permute-done.2 = f32[3,5,1,2,256]{4,3,1,2,0:T(2,128)S(1)} collective-permute-done((f32[3,5,1,2,256]{4,3,1,2,0:T(2,128)S(1)}, f32[3,5,1,2,256]{4,3,1,2,0:T(2,128)S(1)}, u32[]{:S(2)}, u32[]{:S(2)}) %collective-permute-start.2) | collective-permute-done | bytes 30752 | tf_op jit(solution)/shard_map/ppermute | solution.py:179
  31.0 0.9 %collective-permute-done.3 = f32[3,5,1,2,256]{4,3,1,2,0:T(2,128)S(1)} collective-permute-done((f32[3,5,1,2,256]{4,3,1,2,0:T(2,128)S(1)}, f32[3,5,1,2,256]{4,3,1,2,0:T(2,128)S(1)}, u32[]{:S(2)}, u32[]{:S(2)}) %collective-permute-start.3) | collective-permute-done | bytes 30752 | tf_op jit(solution)/shard_map/ppermute | solution.py:179
  31.9 0.2 concatenate.394
  32.2 0.1 fusion.10
  32.4 0.1 fusion.17
  32.6 0.7 %fusion.32.ends_ref = f32[5,1,2,256]{3,2,1,0:T(2,128)} fusion(s32[]{:T(128)S(6)} %select_n.35, f32[5,1,4,256]{3,2,1,0:T(4,128)S(1)} %get-tuple-element.73, f32[5,1,4,256]{3,2,1,0:T(4,128)S(1)} %get-tuple-element.72, f32[5,1,8,256]{3,2,1,0:T(8,128)S(1)} %get-tuple-element.25, f32[5,1,4,256]{3,2,1,0:T(4,128)S(1)} %get-tuple-element.67, ...), kind=kLoop, calls=%fused_computation.80 | loop fusion | flops 48640 | bytes 184324 | tf_op jit(solution)/shard_map/div | solution.py:189
  33.4 8.0 %shard_map.110 = (f32[5,1,128,256]{3,2,1,0:T(8,128)}, f32[5,1,128,256]{3,2,1,0:T(8,128)}, f32[5,1,128,256]{3,2,1,0:T(8,128)}, f32[5,1,6,128]{3,2,1,0:T(8,128)}) custom-call(f32[5,1,128,256]{3,2,1,0:T(8,128)} %get-tuple-element.13.it_ref, f32[5,1,128,256]{3,2,1,0:T(8,128)} %get-tuple-element.14.ia_ref, f32[5,1,128,256]{3,2,1,0:T(8,128)} %get-tuple-element.15.ib_ref, ...), custom_call_target="tpu_custom_call" | custom-call | tf_op jit(solution)/shard_map/pallas_call | solution.py:165
  41.4 0.7 %slice_bitcast_fusion.5 = f32[1,5,1,2,128]{4,3,1,2,0:T(2,128)S(1)} fusion(f32[5,1,6,128]{3,2,1,0:T(8,128)} %get-tuple-element.17), kind=kLoop, calls=%fused_computation.111 | loop fusion | bytes 10240 | tf_op jit(solution)/shard_map/stack | solution.py:186
  42.1 0.8 %slice_bitcast_fusion.4 = (f32[1,5,1,2,128]{4,3,1,2,0:T(2,128)S(1)}, f32[1,5,1,2,128]{4,3,1,2,0:T(2,128)S(1)}) fusion(f32[5,1,6,128]{3,2,0,1:T(8,128)} %bitcast.60), kind=kLoop, calls=%fused_computation.110 | loop fusion | bytes 20480 | tf_op jit(solution)/shard_map/stack | solution.py:186
  42.9 3.7 %collective-permute-start.4 = (f32[3,5,1,2,128]{4,3,1,2,0:T(2,128)S(1)}, f32[3,5,1,2,128]{4,3,1,2,0:T(2,128)S(1)}, u32[]{:S(2)}, u32[]{:S(2)}) collective-permute-start(f32[3,5,1,2,128]{4,3,1,2,0:T(2,128)S(1)} %pad_maximum_fusion.3), channel_id=1, source_target_pairs={{2,0},{4,2},{6,4},{0,6},{3,1},{5,3},{7,5},{1,7},{10,8},{12,10},{14... | collective-permute-start | bytes 46088 | tf_op jit(solution)/shard_map/ppermute | solution.py:179
  46.6 0.0 collective-permute-start.5
  46.6 1.0 %collective-permute-start.6 = (f32[3,5,1,2,128]{4,3,1,2,0:T(2,128)S(1)}, f32[3,5,1,2,128]{4,3,1,2,0:T(2,128)S(1)}, u32[]{:S(2)}, u32[]{:S(2)}) collective-permute-start(f32[3,5,1,2,128]{4,3,1,2,0:T(2,128)S(1)} %pad_maximum_fusion.3), channel_id=1, source_target_pairs={{6,0},{0,2},{2,4},{4,6},{7,1},{1,3},{3,5},{5,7},{14,8},{8,10},{10,... | collective-permute-start | bytes 46088 | tf_op jit(solution)/shard_map/ppermute | solution.py:179
  47.6 0.4 collective-permute-done.4
  48.0 3.2 %collective-permute-done.5 = f32[3,5,1,2,128]{4,3,1,2,0:T(2,128)S(1)} collective-permute-done((f32[3,5,1,2,128]{4,3,1,2,0:T(2,128)S(1)}, f32[3,5,1,2,128]{4,3,1,2,0:T(2,128)S(1)}, u32[]{:S(2)}, u32[]{:S(2)}) %collective-permute-start.5) | collective-permute-done | bytes 15392 | tf_op jit(solution)/shard_map/ppermute | solution.py:179
  51.2 0.9 %collective-permute-done.6 = f32[3,5,1,2,128]{4,3,1,2,0:T(2,128)S(1)} collective-permute-done((f32[3,5,1,2,128]{4,3,1,2,0:T(2,128)S(1)}, f32[3,5,1,2,128]{4,3,1,2,0:T(2,128)S(1)}, u32[]{:S(2)}, u32[]{:S(2)}) %collective-permute-start.6) | collective-permute-done | bytes 15392 | tf_op jit(solution)/shard_map/ppermute | solution.py:179
  52.1 0.1 concatenate.410
  52.3 0.0 copy-start.2
  52.3 0.0 copy-start.3
  52.5 0.1 fusion.41
  52.6 0.7 %copy-done.2 = f32[5,1,128,256]{3,2,1,0:T(8,128)S(1)} copy-done((f32[5,1,128,256]{3,2,1,0:T(8,128)S(1)}, f32[5,1,128,256]{3,2,1,0:T(8,128)}, u32[]{:S(2)}) %copy-start.2) | copy-done | bytes 655384
  53.4 0.2 copy-done.3
  53.6 1.3 %select_select_fusion = f32[5,1,128,256]{3,2,1,0:T(8,128)S(1)} fusion(f32[5,1,128,256]{3,2,1,0:T(8,128)} %get-tuple-element.20, f32[5,1,128,256]{3,2,1,0:T(8,128)S(1)} %copy-done.2, f32[5,1,128,256]{3,2,1,0:T(8,128)S(1)} %copy-done.3, f32[5,128]{1,0:T(8,128)S(1)} %bitcast.58, f32[5,128]{1,0:T(8,128)S(1)} %bitcast.59, pred[256]{0:T(512)(128)(4,1)S(1)} %get-tuple-element.125, ...), kind=kLoop, calls=%fused_computation | loop fusion | flops 983040 | bytes 2627072 | tf_op jit(solution)/shard_map/jit(_where)/select_n | solution.py:235
  54.9 0.1 fusion.4
  55.0 0.1 add_dynamic-update-slice_fusion.3
  55.0 0.1 add_dynamic-update-slice_fusion.2
  55.1 0.1 add_dynamic-update-slice_fusion.1
  55.1 0.0 copy-start.4
  55.2 0.8 %copy-done.4 = f32[5,1,128,256]{3,2,1,0:T(8,128)} copy-done((f32[5,1,128,256]{3,2,1,0:T(8,128)}, f32[5,1,128,256]{3,2,1,0:T(8,128)S(1)}, u32[]{:S(2)}) %copy-start.4) | copy-done | bytes 655384
  56.0 0.7 %add_dynamic-update-slice_fusion = f32[5,1,128,256]{3,2,1,0:T(8,128)} fusion(f32[5,1,128,256]{3,2,1,0:T(8,128)} %copy-done.4, f32[5,1,128,256]{3,2,1,0:T(8,128)S(1)} %select_select_fusion, f32[256]{0:T(256)S(1)} %bitcast.62, f32[256]{0:T(256)S(1)} %bitcast.61, f32[256]{0:T(256)S(1)} %bitcast.64, f32[256]{0:T(256)S(1)} %bitcast.65, f32[256]{0:T(256)S(1)} %bitcast.63), kind=kLoop, calls=%fused_computation.7 | loop fusion | flops 327680 | bytes 791552 | tf_op jit(solution)/shard_map/stack | solution.py:208
  (38 shorter events, 0.5 us)
Async XLA Ops:
  0.0 28.8 %copy-start = (f32[5,1024]{1,0:T(8,128)S(1)}, f32[5,1024]{1,0:T(8,128)}, u32[]{:S(2)}) copy-start(f32[5,1024]{1,0:T(8,128)} %param.17) | copy-start | bytes 61444
  0.0 17.9 %collective-permute-start = (f32[5,1,128,256]{3,2,1,0:T(8,128)}, f32[5,1,128,256]{3,2,1,0:T(8,128)S(1)}, u32[]{:S(2)}, u32[]{:S(2)}) collective-permute-start(f32[5,1,128,256]{3,2,1,0:T(8,128)} %fs_ref.1), channel_id=1, source_target_pairs={{0,1},{1,0},{2,3},{3,2},{4,5},{5,4},{6,7},{7,6},{8,9},{9,8},{10,11... | collective-permute-start | bytes 1966088 | tf_op jit(solution)/shard_map/ppermute | solution.py:196
  17.9 0.8 %copy-start.1 = (f32[5,1,128,256]{3,2,1,0:T(8,128)}, f32[5,1,128,256]{3,2,1,0:T(8,128)S(1)}, u32[]{:S(2)}) copy-start(f32[5,1,128,256]{3,2,1,0:T(8,128)S(1)} %collective-permute-done.nb_ref) | copy-start | bytes 1966084
  26.8 2.6 %collective-permute-start.1 = (f32[3,5,1,2,256]{4,3,1,2,0:T(2,128)S(1)}, f32[3,5,1,2,256]{4,3,1,2,0:T(2,128)S(1)}, u32[]{:S(2)}, u32[]{:S(2)}) collective-permute-start(f32[3,5,1,2,256]{4,3,1,2,0:T(2,128)S(1)} %pad_maximum_fusion.2), channel_id=1, source_target_pairs={{8,0},{16,8},{24,16},{0,24},{9,1},{17,9},{25,17},{1,25},{10,2},{18... | collective-permute-start | bytes 92168 | tf_op jit(solution)/shard_map/ppermute | solution.py:179
  27.1 3.9 %collective-permute-start.2 = (f32[3,5,1,2,256]{4,3,1,2,0:T(2,128)S(1)}, f32[3,5,1,2,256]{4,3,1,2,0:T(2,128)S(1)}, u32[]{:S(2)}, u32[]{:S(2)}) collective-permute-start(f32[3,5,1,2,256]{4,3,1,2,0:T(2,128)S(1)} %pad_maximum_fusion.2), channel_id=1, source_target_pairs={{16,0},{24,8},{0,16},{8,24},{17,1},{25,9},{1,17},{9,25},{18,2},{26... | collective-permute-start | bytes 92168 | tf_op jit(solution)/shard_map/ppermute | solution.py:179
  28.6 3.3 %collective-permute-start.3 = (f32[3,5,1,2,256]{4,3,1,2,0:T(2,128)S(1)}, f32[3,5,1,2,256]{4,3,1,2,0:T(2,128)S(1)}, u32[]{:S(2)}, u32[]{:S(2)}) collective-permute-start(f32[3,5,1,2,256]{4,3,1,2,0:T(2,128)S(1)} %pad_maximum_fusion.2), channel_id=1, source_target_pairs={{24,0},{0,8},{8,16},{16,24},{25,1},{1,9},{9,17},{17,25},{26,2},{2,... | collective-permute-start | bytes 92168 | tf_op jit(solution)/shard_map/ppermute | solution.py:179
  42.9 5.1 %collective-permute-start.4 = (f32[3,5,1,2,128]{4,3,1,2,0:T(2,128)S(1)}, f32[3,5,1,2,128]{4,3,1,2,0:T(2,128)S(1)}, u32[]{:S(2)}, u32[]{:S(2)}) collective-permute-start(f32[3,5,1,2,128]{4,3,1,2,0:T(2,128)S(1)} %pad_maximum_fusion.3), channel_id=1, source_target_pairs={{2,0},{4,2},{6,4},{0,6},{3,1},{5,3},{7,5},{1,7},{10,8},{12,10},{14... | collective-permute-start | bytes 46088 | tf_op jit(solution)/shard_map/ppermute | solution.py:179
  46.6 4.6 %collective-permute-start.5 = (f32[3,5,1,2,128]{4,3,1,2,0:T(2,128)S(1)}, f32[3,5,1,2,128]{4,3,1,2,0:T(2,128)S(1)}, u32[]{:S(2)}, u32[]{:S(2)}) collective-permute-start(f32[3,5,1,2,128]{4,3,1,2,0:T(2,128)S(1)} %pad_maximum_fusion.3), channel_id=1, source_target_pairs={{4,0},{6,2},{0,4},{2,6},{5,1},{7,3},{1,5},{3,7},{12,8},{14,10},{8,... | collective-permute-start | bytes 46088 | tf_op jit(solution)/shard_map/ppermute | solution.py:179
  46.6 5.5 %collective-permute-start.6 = (f32[3,5,1,2,128]{4,3,1,2,0:T(2,128)S(1)}, f32[3,5,1,2,128]{4,3,1,2,0:T(2,128)S(1)}, u32[]{:S(2)}, u32[]{:S(2)}) collective-permute-start(f32[3,5,1,2,128]{4,3,1,2,0:T(2,128)S(1)} %pad_maximum_fusion.3), channel_id=1, source_target_pairs={{6,0},{0,2},{2,4},{4,6},{7,1},{1,3},{3,5},{5,7},{14,8},{8,10},{10,... | collective-permute-start | bytes 46088 | tf_op jit(solution)/shard_map/ppermute | solution.py:179
  52.3 1.1 %copy-start.2 = (f32[5,1,128,256]{3,2,1,0:T(8,128)S(1)}, f32[5,1,128,256]{3,2,1,0:T(8,128)}, u32[]{:S(2)}) copy-start(f32[5,1,128,256]{3,2,1,0:T(8,128)} %get-tuple-element.18) | copy-start | bytes 1966084
  52.3 1.3 %copy-start.3 = (f32[5,1,128,256]{3,2,1,0:T(8,128)S(1)}, f32[5,1,128,256]{3,2,1,0:T(8,128)}, u32[]{:S(2)}) copy-start(f32[5,1,128,256]{3,2,1,0:T(8,128)} %get-tuple-element.19) | copy-start | bytes 1966084
  55.1 0.8 %copy-start.4 = (f32[5,1,128,256]{3,2,1,0:T(8,128)}, f32[5,1,128,256]{3,2,1,0:T(8,128)S(1)}, u32[]{:S(2)}) copy-start(f32[5,1,128,256]{3,2,1,0:T(8,128)S(1)} %add_dynamic-update-slice_fusion.1) | copy-start | bytes 1966084

commit v6 on v5

--- a/solution.py
+++ b/solution.py
@@ -51,7 +51,7 @@
     return lower, upper, rhs
 
 
-def reduce_block(lower, upper, target, red_ref, index):
+def reduce_block(lower, upper, target):
     length = lower.shape[0]
     idx = lax.broadcasted_iota(jnp.int32, lower.shape, 0)
     edge = (idx == 0) | (idx == length - 1)
@@ -78,16 +78,50 @@
     inv_f = 1.0 / (1.0 - u0 * a1)
     inv_e = 1.0 / (1.0 - le * b2)
     rows = (
-        l0 * inv_f,
-        -le * a2 * inv_e,
-        -u0 * b1 * inv_f,
-        ue * inv_e,
-        (t0 - u0 * t1) * inv_f,
-        (te - le * t2) * inv_e,
+        (l0 * inv_f, -le * a2 * inv_e),
+        (-u0 * b1 * inv_f, ue * inv_e),
+        ((t0 - u0 * t1) * inv_f, (te - le * t2) * inv_e),
     )
-    for k, value in enumerate(rows):
-        red_ref[index, 0, k : k + 1, :] = value
-    return it, ia, ib
+    return it, ia, ib, rows
+
+
+def store_rows(red_ref, v, rows):
+    for q, pair in enumerate(rows):
+        for i, value in enumerate(pair):
+            red_ref[v, 0, q, i : i + 1, :] = value
+
+
+def reduced_ends(red_ref, v):
+    lower, upper, target = red_ref[v, 0, 0], red_ref[v, 0, 1], red_ref[v, 0, 2]
+    length = lower.shape[0]
+    stride = 1
+    while stride < length:
+        back = length - stride
+        ll, ul = pltpu.roll(lower, stride, 0), pltpu.roll(upper, stride, 0)
+        lr, ur = pltpu.roll(lower, back, 0), pltpu.roll(upper, back, 0)
+        inv = 1.0 / (1.0 - lower * ul - upper * lr)
+        target = (target - lower * pltpu.roll(target, stride, 0) - upper * pltpu.roll(target, back, 0)) * inv
+        lower, upper = -lower * ll * inv, -upper * ur * inv
+        stride = stride * 2
+    ends = target / (1.0 + lower + upper)
+    return ends[0:1], ends[1:2]
+
+
+def back_substitute(it, ia, ib, first, last):
+    length = it.shape[0]
+    idx = lax.broadcasted_iota(jnp.int32, it.shape, 0)
+    inner = it - ia * first - ib * last
+    return jnp.where(idx == 0, first, jnp.where(idx == length - 1, last, inner))
+
+
+def mixed(mix_ref, values):
+    out = []
+    for v in range(len(values)):
+        summed = values[v]
+        for w in range(len(values)):
+            summed = summed + mix_ref[v, w : w + 1, :] * values[w]
+        out.append(summed)
+    return out
 
 
 def az_kernel(fs_ref, nb_ref, src_ref, cell_ref, visc_ref, beta_ref, diff_ref, mix_ref, ot_ref, oa_ref, ob_ref, red_ref):
@@ -95,44 +129,52 @@
     explicit = []
     for w in range(count):
         explicit.append(src_ref[w, 0] + diff_ref[w : w + 1, :] * (nb_ref[w, 0] - 2.0 * fs_ref[w, 0]))
+    section_one = mixed(mix_ref, explicit)
     cell = cell_ref[0]
     for v in range(count):
-        summed = explicit[v]
-        for w in range(count):
-            summed = summed + mix_ref[v, w : w + 1, :] * explicit[w]
         coupling = visc_ref[v : v + 1, :] * cell
         centre = 1.0 + 2.0 * coupling
         tilt = beta_ref[v : v + 1, :]
         lower = -coupling * (1.0 + tilt) / centre
         upper = -coupling * (1.0 - tilt) / centre
-        it, ia, ib = reduce_block(lower, upper, summed / centre, red_ref, v)
+        it, ia, ib, rows = reduce_block(lower, upper, section_one[v] / centre)
+        store_rows(red_ref, v, rows)
         ot_ref[v, 0] = it
         oa_ref[v, 0] = ia
         ob_ref[v, 0] = ib
 
 
-def rad_kernel(it_ref, ia_ref, ib_ref, ends_ref, mix_ref, cell_ref, visc_ref, ot_ref, oa_ref, ob_ref, red_ref):
+def rad_kernel(it_ref, ia_ref, ib_ref, red_in_ref, mix_ref, cell_ref, visc_ref, ot_ref, oa_ref, ob_ref, red_ref, *, axis_name, devices):
     count = it_ref.shape[0]
-    length = it_ref.shape[2]
-    idx = lax.broadcasted_iota(jnp.int32, it_ref.shape[2:], 0)
     solved = []
     for w in range(count):
-        first = ends_ref[w, 0, 0:1, :]
-        last = ends_ref[w, 0, 1:2, :]
-        inner = it_ref[w, 0] - ia_ref[w, 0] * first - ib_ref[w, 0] * last
-        solved.append(jnp.where(idx == 0, first, jnp.where(idx == length - 1, last, inner)))
+        first, last = reduced_ends(red_in_ref, w)
+        solved.append(back_substitute(it_ref[w, 0], ia_ref[w, 0], ib_ref[w, 0], first, last))
+    section_three = mixed(mix_ref, solved)
     cell = cell_ref[0]
+    place = lax.axis_index(axis_name)
     for v in range(count):
-        summed = solved[v]
-        for w in range(count):
-            summed = summed + mix_ref[v, w : w + 1, :] * solved[w]
         coupling = visc_ref[v : v + 1, :] * cell
         centre = 1.0 + 2.0 * coupling
         side = (-coupling / centre).T
-        it, ia, ib = reduce_block(side, side, (summed / centre).T, red_ref, v)
-        ot_ref[v, 0] = it.T
-        oa_ref[v, 0] = ia.T
-        ob_ref[v, 0] = ib.T
+        it, ia, ib, rows = reduce_block(side, side, (section_three[v] / centre).T)
+        (lf, le), (uf, ue), trow = rows
+        lf = jnp.where(place == 0, jnp.zeros_like(lf), lf)
+        ue = jnp.where(place == devices - 1, jnp.zeros_like(ue), ue)
+        store_rows(red_ref, v, ((lf, le), (uf, ue), trow))
+        ot_ref[v, 0] = it
+        oa_ref[v, 0] = ia
+        ob_ref[v, 0] = ib
+
+
+def out_kernel(it_ref, ia_ref, ib_ref, red_in_ref, mix_ref, out_ref):
+    count = it_ref.shape[0]
+    solved = []
+    for w in range(count):
+        first, last = reduced_ends(red_in_ref, w)
+        solved.append(back_substitute(it_ref[w, 0], ia_ref[w, 0], ib_ref[w, 0], first, last).T)
+    for v, value in enumerate(mixed(mix_ref, solved)):
+        out_ref[v, 0] = value
 
 
 def az_sweep(flow_state, nb, source, cell_az, visc_az, beta_az, axial_diff, mix_in):
@@ -142,33 +184,50 @@
     cell = pl.BlockSpec((1, na, chunk), lambda z, c: (z, 0, c))
     par = pl.BlockSpec((nv, chunk), lambda z, c: (0, c))
     mixs = pl.BlockSpec((nv, nv, chunk), lambda z, c: (0, 0, c))
-    red = pl.BlockSpec((nv, 1, 6, chunk), lambda z, c: (0, z, 0, c))
+    red = pl.BlockSpec((nv, 1, 3, 2, chunk), lambda z, c: (0, z, 0, 0, c))
     out = jax.ShapeDtypeStruct(flow_state.shape, flow_state.dtype)
     return pl.pallas_call(
         az_kernel,
         grid=(nz, nr // chunk),
         in_specs=[big, big, big, cell, par, par, par, mixs],
         out_specs=[big, big, big, red],
-        out_shape=[out, out, out, jax.ShapeDtypeStruct((nv, nz, 6, nr), flow_state.dtype)],
+        out_shape=[out, out, out, jax.ShapeDtypeStruct((nv, nz, 3, 2, nr), flow_state.dtype)],
     )(flow_state, nb, source, cell_az, visc_az, beta_az, axial_diff, mix_in)
 
 
-def rad_sweep(it, ia, ib, ends, mix_mid, cell_rad, visc_local):
+def rad_sweep(it, ia, ib, red_in, mix_mid, cell_rad, visc_local):
     nv, nz, na, nr = it.shape
     big = pl.BlockSpec((nv, 1, na, nr), lambda z: (0, z, 0, 0))
-    endspec = pl.BlockSpec((nv, 1, 2, nr), lambda z: (0, z, 0, 0))
+    big_t = pl.BlockSpec((nv, 1, nr, na), lambda z: (0, z, 0, 0))
+    red_in_spec = pl.BlockSpec((nv, 1) + red_in.shape[2:], lambda z: (0, z, 0, 0, 0))
     mixs = pl.BlockSpec((nv, nv, nr), lambda z: (0, 0, 0))
     cell = pl.BlockSpec((1, na, nr), lambda z: (z, 0, 0))
     par = pl.BlockSpec((nv, nr), lambda z: (0, 0))
-    red = pl.BlockSpec((nv, 1, 6, na), lambda z: (0, z, 0, 0))
-    out = jax.ShapeDtypeStruct(it.shape, it.dtype)
+    red = pl.BlockSpec((nv, 1, 3, 2, na), lambda z: (0, z, 0, 0, 0))
+    out = jax.ShapeDtypeStruct((nv, nz, nr, na), it.dtype)
+    kernel = functools.partial(rad_kernel, axis_name="rad", devices=lax.axis_size("rad"))
     return pl.pallas_call(
-        rad_kernel,
+        kernel,
         grid=(nz,),
-        in_specs=[big, big, big, endspec, mixs, cell, par],
-        out_specs=[big, big, big, red],
-        out_shape=[out, out, out, jax.ShapeDtypeStruct((nv, nz, 6, na), it.dtype)],
-    )(it, ia, ib, ends, mix_mid, cell_rad, visc_local)
+        in_specs=[big, big, big, red_in_spec, mixs, cell, par],
+        out_specs=[big_t, big_t, big_t, red],
+        out_shape=[out, out, out, jax.ShapeDtypeStruct((nv, nz, 3, 2, na), it.dtype)],
+    )(it, ia, ib, red_in, mix_mid, cell_rad, visc_local)
+
+
+def out_sweep(it, ia, ib, red_in, mix_out):
+    nv, nz, nr, na = it.shape
+    big_t = pl.BlockSpec((nv, 1, nr, na), lambda z: (0, z, 0, 0))
+    big = pl.BlockSpec((nv, 1, na, nr), lambda z: (0, z, 0, 0))
+    red_in_spec = pl.BlockSpec((nv, 1) + red_in.shape[2:], lambda z: (0, z, 0, 0, 0))
+    mixs = pl.BlockSpec((nv, nv, nr), lambda z: (0, 0, 0))
+    return pl.pallas_call(
+        out_kernel,
+        grid=(nz,),
+        in_specs=[big_t, big_t, big_t, red_in_spec, mixs],
+        out_specs=big,
+        out_shape=jax.ShapeDtypeStruct((nv, nz, na, nr), it.dtype),
+    )(it, ia, ib, red_in, mix_out)
 
 
 def gathered(block, axis_name, dim):
@@ -177,17 +236,7 @@
     for offset in range(1, count):
         pairs = [((i + offset) % count, i) for i in range(count)]
         received.append(lax.ppermute(block, axis_name, pairs))
-    doubled = jnp.concatenate(received + received, axis=dim)
-    start = ((count - lax.axis_index(axis_name)) % count) * block.shape[dim]
-    return lax.dynamic_slice_in_dim(doubled, start, count * block.shape[dim], dim)
-
-
-def reduced_solve(red, axis_name, periodic):
-    stacked = jnp.stack([red[:, :, 0:2], red[:, :, 2:4], red[:, :, 4:6]])
-    full = gathered(stacked, axis_name, 3)
-    rl, ru, (rt,) = cyclic_reduce(full[0], full[1], [full[2]], 2, periodic, full.shape[3])
-    ends = rt / (1.0 + rl + ru)
-    return lax.dynamic_slice_in_dim(ends, 2 * lax.axis_index(axis_name), 2, 2)
+    return jnp.concatenate(received, axis=dim)
 
 
 def neighbour_planes(block, axis_name):
@@ -224,16 +273,11 @@
     rad_cells = flow_state.shape[3]
     nb = neighbour_planes(flow_state, "ax")
     it, ia, ib, red = az_sweep(flow_state, nb, source, cell_az, visc_az, beta_az, axial_diff, mix_in)
-    ends = reduced_solve(red, "az", True)
+    red = gathered(red, "az", 3)
     visc_local = lax.dynamic_slice_in_dim(visc_rad, lax.axis_index("rad") * rad_cells, rad_cells, 1)
-    it, ia, ib, red = rad_sweep(it, ia, ib, ends, mix_mid, cell_rad, visc_local)
-    ends = reduced_solve(red, "rad", False)
-    first = ends[:, :, 0, :, None]
-    last = ends[:, :, 1, :, None]
-    idx = lax.broadcasted_iota(jnp.int32, it.shape, 3)
-    inner = it - ia * first - ib * last
-    section_four = jnp.where(idx == 0, first, jnp.where(idx == rad_cells - 1, last, inner))
-    return mix(mix_out, section_four)
+    it, ia, ib, red = rad_sweep(it, ia, ib, red, mix_mid, cell_rad, visc_local)
+    red = gathered(red, "rad", 3)
+    return out_sweep(it, ia, ib, red, mix_out)
 
 
 def solution(mesh):

time: 57.2 us -> 53.3 us (0.932)
  local copies, waits for them, and re-layouts: 8.03 us -> 1.44 us
  Pallas kernels: 15.1 us -> 18.2 us
  starting transfers between devices: 9.65 us -> 11.7 us
  waiting for transfers between devices: 20.2 us -> 18.7 us
    ppermute x6, waiting for transfers between devices: 7.07 us -> 3.78 us  [gathered(): received.append(lax.ppermute(block, axis_name, pairs))]
    pallas_call x1 -> x2, Pallas kernels: 8.04 us -> 11.2 us  [the longest x1 8.41 us: rad_sweep(): pl.pallas_call(kernel, grid=(nz,), in_specs=[big, big, big, red_in_spec,...]
    concatenate x0 -> x2, other arithmetic: none -> 2.83 us  [gathered(): return jnp.concatenate(received, axis=dim)]
    another operation x3 -> x0, local copies, waits for them, and re-layouts: 2.45 us -> none  [reduced_solve(): stacked = jnp.stack([red[:, :, 0:2], red[:, :, 2:4], red[:, :, 4:6]])]
    ppermute x6, starting transfers between devices: 6.68 us -> 8.75 us  [gathered(): received.append(lax.ppermute(block, axis_name, pairs))]
    slice x25 -> x0, local copies, waits for them, and re-layouts: 2 us -> none  [the longest x2 1.81 us: mix(): summed = summed + matrix[out_var, in_var][None, None, :] * values[in_var]]
    ppermute x1, waiting for transfers between devices: 13.1 us -> 14.9 us  [neighbour_planes(): return lax.ppermute(block, axis_name, [(0, 1), (1, 0)])]
    unnamed x12 -> x4, local copies, waits for them, and re-layouts: 2.63 us -> 0.84 us
  transfers between devices with their start and end apart: 7 -> 7, of which waited for: 6 -> 6; matrix products, arithmetic and copies ran while one was open for 4% -> 1% of each run, Pallas kernels for 0% -> 0%
where the time goes in v6:
time: 53.3 us; the launch traced here: 53 us
  waiting for transfers between devices  18.7 us (35%)
  Pallas kernels  18.2 us (34%)
  starting transfers between devices  11.7 us (22%)
  other arithmetic  2.83 us (5%)
  local copies, waits for them, and re-layouts  1.44 us (3%)
    ppermute x1, waiting for transfers between devices, neighbour_planes(): return lax.ppermute(block, axis_name, [(0, 1), (1, 0)])  14.9 us
    ppermute x6, starting transfers between devices, gathered(): received.append(lax.ppermute(block, axis_name, pairs))  8.75 us
    pallas_call x1, Pallas kernels, rad_sweep(): pl.pallas_call(kernel, grid=(nz,), in_specs=[big, big, big, red_in_spec,...  8.41 us
    pallas_call x1, Pallas kernels, az_sweep(): pl.pallas_call(az_kernel, grid=(nz, nr // chunk), in_specs=[big, big, big...  7.08 us
    ppermute x6, waiting for transfers between devices, gathered(): received.append(lax.ppermute(block, axis_name, pairs))  3.78 us
    ppermute x1, starting transfers between devices, neighbour_planes(): return lax.ppermute(block, axis_name, [(0, 1), (1, 0)])  2.97 us
    concatenate x2, other arithmetic, gathered(): return jnp.concatenate(received, axis=dim)  2.83 us
    pallas_call x1, Pallas kernels, out_sweep(): pl.pallas_call(out_kernel, grid=(nz,), in_specs=[big_t, big_t, big_t, red...  2.75 us
  transfers between devices with their start and end apart: 7, of which 6 were waited for; matrix products, arithmetic and copies ran while one was open for 1% of the time, Pallas kernels for 0%

profile of v6, /device:TPU:0, one launch (start us, length us, event | category | flops | bytes accessed | tf_op | source)
XLA Modules:
  0.0 53.0 jit_solution(11560872033358972455)
XLA Ops:
  0.0 0.0 copy-start
  0.0 3.0 %collective-permute-start = (f32[5,1,128,256]{3,2,1,0:T(8,128)}, f32[5,1,128,256]{3,2,1,0:T(8,128)S(1)}, u32[]{:S(2)}, u32[]{:S(2)}) collective-permute-start(f32[5,1,128,256]{3,2,1,0:T(8,128)} %fs_ref.1), channel_id=1, source_target_pairs={{0,1},{1,0},{2,3},{3,2},{4,5},{5,4},{6,7},{7,6},{8,9},{9,8},{10,11... | collective-permute-start | bytes 1966088 | tf_op jit(solution)/shard_map/ppermute | solution.py:245
  3.0 14.9 %collective-permute-done.nb_ref = f32[5,1,128,256]{3,2,1,0:T(8,128)S(1)} collective-permute-done((f32[5,1,128,256]{3,2,1,0:T(8,128)}, f32[5,1,128,256]{3,2,1,0:T(8,128)S(1)}, u32[]{:S(2)}, u32[]{:S(2)}) %collective-permute-start) | collective-permute-done | bytes 655392 | tf_op jit(solution)/shard_map/ppermute | solution.py:245
  17.9 0.0 copy-start.1
  17.9 0.8 %copy-done.1 = f32[5,1,128,256]{3,2,1,0:T(8,128)} copy-done((f32[5,1,128,256]{3,2,1,0:T(8,128)}, f32[5,1,128,256]{3,2,1,0:T(8,128)S(1)}, u32[]{:S(2)}) %copy-start.1) | copy-done | bytes 655384
  18.7 7.1 %shard_map.109 = (f32[5,1,128,256]{3,2,1,0:T(8,128)}, f32[5,1,128,256]{3,2,1,0:T(8,128)}, f32[5,1,128,256]{3,2,1,0:T(8,128)}, f32[5,1,3,2,256]{4,3,2,1,0:T(2,128)}) custom-call(f32[5,1,128,256]{3,2,1,0:T(8,128)} %fs_ref.1, f32[5,1,128,256]{3,2,1,0:T(8,128)} %copy-done.1, f32[5,1,128,256]{3,2,1,0:T(8,128)} %src_ref.1, f32[1,128,256]{2,1,0:T(8,128)} %cell_ref.2, ...), custom_call_target="tpu_custom_call" | custom-call | tf_op jit(solution)/shard_map/pallas_call | solution.py:189
  25.8 0.1 collective-permute-start.3
  25.9 1.8 %collective-permute-start.2 = (f32[5,1,3,2,256]{4,3,2,1,0:T(2,128)}, f32[5,1,3,2,256]{4,3,2,1,0:T(2,128)S(1)}, u32[]{:S(2)}, u32[]{:S(2)}) collective-permute-start(f32[5,1,3,2,256]{4,3,2,1,0:T(2,128)} %get-tuple-element.16), channel_id=1, source_target_pairs={{16,0},{24,8},{0,16},{8,24},{17,1},{25,9},{1,17},{9,25},{18,2},{26... | collective-permute-start | bytes 92168 | tf_op jit(solution)/shard_map/ppermute | solution.py:238
  27.7 1.4 %collective-permute-start.1 = (f32[5,1,3,2,256]{4,3,2,1,0:T(2,128)}, f32[5,1,3,2,256]{4,3,2,1,0:T(2,128)S(1)}, u32[]{:S(2)}, u32[]{:S(2)}) collective-permute-start(f32[5,1,3,2,256]{4,3,2,1,0:T(2,128)} %get-tuple-element.16), channel_id=1, source_target_pairs={{8,0},{16,8},{24,16},{0,24},{9,1},{17,9},{25,17},{1,25},{10,2},{18... | collective-permute-start | bytes 92168 | tf_op jit(solution)/shard_map/ppermute | solution.py:238
  29.1 0.0 copy-done
  29.1 0.6 %constant_dynamic-slice_fusion.visc_ref = f32[5,256]{1,0:T(8,128)} fusion(f32[5,1024]{1,0:T(8,128)S(1)} %copy-done, s32[]{:T(128)S(6)} %select_n.3), kind=kLoop, calls=%fused_computation.2 | loop fusion | bytes 10244 | tf_op jit(solution)/shard_map/dynamic_slice | solution.py:277
  29.7 0.0 collective-permute-done.3
  29.7 0.4 collective-permute-done.2
  30.1 0.8 %collective-permute-done.1 = f32[5,1,3,2,256]{4,3,2,1,0:T(2,128)S(1)} collective-permute-done((f32[5,1,3,2,256]{4,3,2,1,0:T(2,128)}, f32[5,1,3,2,256]{4,3,2,1,0:T(2,128)S(1)}, u32[]{:S(2)}, u32[]{:S(2)}) %collective-permute-start.1) | collective-permute-done | bytes 30752 | tf_op jit(solution)/shard_map/ppermute | solution.py:238
  30.9 1.5 %pad_maximum_fusion.red_in_ref = f32[5,1,3,8,256]{4,3,2,1,0:T(8,128)} fusion(f32[5,1,3,2,256]{4,3,2,1,0:T(2,128)S(1)} %collective-permute-done.3, f32[5,1,3,2,256]{4,3,2,1,0:T(2,128)S(1)} %collective-permute-done.2, f32[5,1,3,2,256]{4,3,2,1,0:T(2,128)S(1)} %collective-permute-done.1, f32[5,1,3,2,256]{4,3,2,1,0:T(2,128)} %get-tuple-element.16), kind=kLoop, calls=%fused_computation | loop fusion | flops 92160 | bytes 245760 | tf_op jit(solution)/shard_map/concatenate | solution.py:239
  32.3 8.4 %shard_map.110 = (f32[5,1,256,128]{3,2,1,0:T(8,128)}, f32[5,1,256,128]{3,2,1,0:T(8,128)}, f32[5,1,256,128]{3,2,1,0:T(8,128)}, f32[5,1,3,2,128]{4,3,2,1,0:T(2,128)}) custom-call(f32[5,1,128,256]{3,2,1,0:T(8,128)} %get-tuple-element.13.it_ref, f32[5,1,128,256]{3,2,1,0:T(8,128)} %get-tuple-element.14.ia_ref, f32[5,1,128,256]{3,2,1,0:T(8,128)} %get-tuple-element.15.ib_ref, ...), custom_call_target="tpu_custom_call" | custom-call | tf_op jit(solution)/shard_map/pallas_call | solution.py:209
  40.7 1.6 %collective-permute-start.6 = (f32[5,1,3,2,128]{4,3,2,1,0:T(2,128)}, f32[5,1,3,2,128]{4,3,2,1,0:T(2,128)S(1)}, u32[]{:S(2)}, u32[]{:S(2)}) collective-permute-start(f32[5,1,3,2,128]{4,3,2,1,0:T(2,128)} %get-tuple-element.20), channel_id=1, source_target_pairs={{6,0},{0,2},{2,4},{4,6},{7,1},{1,3},{3,5},{5,7},{14,8},{8,10},{10,... | collective-permute-start | bytes 46088 | tf_op jit(solution)/shard_map/ppermute | solution.py:238
  42.3 2.6 %collective-permute-start.5 = (f32[5,1,3,2,128]{4,3,2,1,0:T(2,128)}, f32[5,1,3,2,128]{4,3,2,1,0:T(2,128)S(1)}, u32[]{:S(2)}, u32[]{:S(2)}) collective-permute-start(f32[5,1,3,2,128]{4,3,2,1,0:T(2,128)} %get-tuple-element.20), channel_id=1, source_target_pairs={{4,0},{6,2},{0,4},{2,6},{5,1},{7,3},{1,5},{3,7},{12,8},{14,10},{8,... | collective-permute-start | bytes 46088 | tf_op jit(solution)/shard_map/ppermute | solution.py:238
  44.9 1.3 %collective-permute-start.4 = (f32[5,1,3,2,128]{4,3,2,1,0:T(2,128)}, f32[5,1,3,2,128]{4,3,2,1,0:T(2,128)S(1)}, u32[]{:S(2)}, u32[]{:S(2)}) collective-permute-start(f32[5,1,3,2,128]{4,3,2,1,0:T(2,128)} %get-tuple-element.20), channel_id=1, source_target_pairs={{2,0},{4,2},{6,4},{0,6},{3,1},{5,3},{7,5},{1,7},{10,8},{12,10},{14... | collective-permute-start | bytes 46088 | tf_op jit(solution)/shard_map/ppermute | solution.py:238
  46.3 0.2 collective-permute-done.6
  46.5 0.7 %collective-permute-done.5 = f32[5,1,3,2,128]{4,3,2,1,0:T(2,128)S(1)} collective-permute-done((f32[5,1,3,2,128]{4,3,2,1,0:T(2,128)}, f32[5,1,3,2,128]{4,3,2,1,0:T(2,128)S(1)}, u32[]{:S(2)}, u32[]{:S(2)}) %collective-permute-start.5) | collective-permute-done | bytes 15392 | tf_op jit(solution)/shard_map/ppermute | solution.py:238
  47.2 1.7 %collective-permute-done.4 = f32[5,1,3,2,128]{4,3,2,1,0:T(2,128)S(1)} collective-permute-done((f32[5,1,3,2,128]{4,3,2,1,0:T(2,128)}, f32[5,1,3,2,128]{4,3,2,1,0:T(2,128)S(1)}, u32[]{:S(2)}, u32[]{:S(2)}) %collective-permute-start.4) | collective-permute-done | bytes 15392 | tf_op jit(solution)/shard_map/ppermute | solution.py:238
  48.8 1.4 %pad_maximum_fusion.1.red_in_ref = f32[5,1,3,8,128]{4,3,2,1,0:T(8,128)} fusion(f32[5,1,3,2,128]{4,3,2,1,0:T(2,128)S(1)} %collective-permute-done.6, f32[5,1,3,2,128]{4,3,2,1,0:T(2,128)S(1)} %collective-permute-done.5, f32[5,1,3,2,128]{4,3,2,1,0:T(2,128)S(1)} %collective-permute-done.4, f32[5,1,3,2,128]{4,3,2,1,0:T(2,128)} %get-tuple-element.20), kind=kLoop, calls=%fused_computation.1 | loop fusion | flops 46080 | bytes 122880 | tf_op jit(solution)/shard_map/concatenate | solution.py:239
  50.2 2.8 %shard_map.111 = f32[5,1,128,256]{3,2,1,0:T(8,128)} custom-call(f32[5,1,256,128]{3,2,1,0:T(8,128)} %get-tuple-element.17.it_ref, f32[5,1,256,128]{3,2,1,0:T(8,128)} %get-tuple-element.18.ia_ref, f32[5,1,256,128]{3,2,1,0:T(8,128)} %get-tuple-element.19.ib_ref, f32[5,1,3,8,128]{4,3,2,1,0:T(8,128)} %pad_maximum_fusion.1.red_in_ref, f32[5,5,256]{2,1,0:T(8,128)} %mix_ref.5), custom_call_target="tpu_custom_call" | custom-call | tf_op jit(solution)/shard_map/pallas_call | solution.py:224
Async XLA Ops:
  0.0 29.1 %copy-start = (f32[5,1024]{1,0:T(8,128)S(1)}, f32[5,1024]{1,0:T(8,128)}, u32[]{:S(2)}) copy-start(f32[5,1024]{1,0:T(8,128)} %param.17) | copy-start | bytes 61444
  0.0 17.9 %collective-permute-start = (f32[5,1,128,256]{3,2,1,0:T(8,128)}, f32[5,1,128,256]{3,2,1,0:T(8,128)S(1)}, u32[]{:S(2)}, u32[]{:S(2)}) collective-permute-start(f32[5,1,128,256]{3,2,1,0:T(8,128)} %fs_ref.1), channel_id=1, source_target_pairs={{0,1},{1,0},{2,3},{3,2},{4,5},{5,4},{6,7},{7,6},{8,9},{9,8},{10,11... | collective-permute-start | bytes 1966088 | tf_op jit(solution)/shard_map/ppermute | solution.py:245
  17.9 0.8 %copy-start.1 = (f32[5,1,128,256]{3,2,1,0:T(8,128)}, f32[5,1,128,256]{3,2,1,0:T(8,128)S(1)}, u32[]{:S(2)}) copy-start(f32[5,1,128,256]{3,2,1,0:T(8,128)S(1)} %collective-permute-done.nb_ref) | copy-start | bytes 1966084
  25.8 3.8 %collective-permute-start.3 = (f32[5,1,3,2,256]{4,3,2,1,0:T(2,128)}, f32[5,1,3,2,256]{4,3,2,1,0:T(2,128)S(1)}, u32[]{:S(2)}, u32[]{:S(2)}) collective-permute-start(f32[5,1,3,2,256]{4,3,2,1,0:T(2,128)} %get-tuple-element.16), channel_id=1, source_target_pairs={{24,0},{0,8},{8,16},{16,24},{25,1},{1,9},{9,17},{17,25},{26,2},{2,... | collective-permute-start | bytes 92168 | tf_op jit(solution)/shard_map/ppermute | solution.py:238
  25.9 4.2 %collective-permute-start.2 = (f32[5,1,3,2,256]{4,3,2,1,0:T(2,128)}, f32[5,1,3,2,256]{4,3,2,1,0:T(2,128)S(1)}, u32[]{:S(2)}, u32[]{:S(2)}) collective-permute-start(f32[5,1,3,2,256]{4,3,2,1,0:T(2,128)} %get-tuple-element.16), channel_id=1, source_target_pairs={{16,0},{24,8},{0,16},{8,24},{17,1},{25,9},{1,17},{9,25},{18,2},{26... | collective-permute-start | bytes 92168 | tf_op jit(solution)/shard_map/ppermute | solution.py:238
  27.7 3.2 %collective-permute-start.1 = (f32[5,1,3,2,256]{4,3,2,1,0:T(2,128)}, f32[5,1,3,2,256]{4,3,2,1,0:T(2,128)S(1)}, u32[]{:S(2)}, u32[]{:S(2)}) collective-permute-start(f32[5,1,3,2,256]{4,3,2,1,0:T(2,128)} %get-tuple-element.16), channel_id=1, source_target_pairs={{8,0},{16,8},{24,16},{0,24},{9,1},{17,9},{25,17},{1,25},{10,2},{18... | collective-permute-start | bytes 92168 | tf_op jit(solution)/shard_map/ppermute | solution.py:238
  40.7 5.7 %collective-permute-start.6 = (f32[5,1,3,2,128]{4,3,2,1,0:T(2,128)}, f32[5,1,3,2,128]{4,3,2,1,0:T(2,128)S(1)}, u32[]{:S(2)}, u32[]{:S(2)}) collective-permute-start(f32[5,1,3,2,128]{4,3,2,1,0:T(2,128)} %get-tuple-element.20), channel_id=1, source_target_pairs={{6,0},{0,2},{2,4},{4,6},{7,1},{1,3},{3,5},{5,7},{14,8},{8,10},{10,... | collective-permute-start | bytes 46088 | tf_op jit(solution)/shard_map/ppermute | solution.py:238
  42.3 4.9 %collective-permute-start.5 = (f32[5,1,3,2,128]{4,3,2,1,0:T(2,128)}, f32[5,1,3,2,128]{4,3,2,1,0:T(2,128)S(1)}, u32[]{:S(2)}, u32[]{:S(2)}) collective-permute-start(f32[5,1,3,2,128]{4,3,2,1,0:T(2,128)} %get-tuple-element.20), channel_id=1, source_target_pairs={{4,0},{6,2},{0,4},{2,6},{5,1},{7,3},{1,5},{3,7},{12,8},{14,10},{8,... | collective-permute-start | bytes 46088 | tf_op jit(solution)/shard_map/ppermute | solution.py:238
  44.9 3.9 %collective-permute-start.4 = (f32[5,1,3,2,128]{4,3,2,1,0:T(2,128)}, f32[5,1,3,2,128]{4,3,2,1,0:T(2,128)S(1)}, u32[]{:S(2)}, u32[]{:S(2)}) collective-permute-start(f32[5,1,3,2,128]{4,3,2,1,0:T(2,128)} %get-tuple-element.20), channel_id=1, source_target_pairs={{2,0},{4,2},{6,4},{0,6},{3,1},{5,3},{7,5},{1,7},{10,8},{12,10},{14... | collective-permute-start | bytes 46088 | tf_op jit(solution)/shard_map/ppermute | solution.py:238

commit v7 on v6

--- a/solution.py
+++ b/solution.py
@@ -91,8 +91,10 @@
             red_ref[v, 0, q, i : i + 1, :] = value
 
 
-def reduced_ends(red_ref, v):
-    lower, upper, target = red_ref[v, 0, 0], red_ref[v, 0, 1], red_ref[v, 0, 2]
+def reduced_ends(red_refs, rows_ref, v):
+    for k, ref in enumerate(red_refs):
+        rows_ref[:, 2 * k : 2 * k + 2, :] = ref[v, 0]
+    lower, upper, target = rows_ref[0], rows_ref[1], rows_ref[2]
     length = lower.shape[0]
     stride = 1
     while stride < length:
@@ -144,17 +146,22 @@
         ob_ref[v, 0] = ib
 
 
-def rad_kernel(it_ref, ia_ref, ib_ref, red_in_ref, mix_ref, cell_ref, visc_ref, ot_ref, oa_ref, ob_ref, red_ref, *, axis_name, devices):
+def rad_kernel(*refs, axis_name, devices, pieces):
+    it_ref, ia_ref, ib_ref = refs[:3]
+    red_in = refs[3 : 3 + pieces]
+    mix_ref, cell_ref, visc_ref, ot_ref, oa_ref, ob_ref, red_ref, rows_ref = refs[3 + pieces :]
     count = it_ref.shape[0]
+    cells = it_ref.shape[3]
+    place = lax.axis_index(axis_name)
+    visc = visc_ref[:, pl.ds(pl.multiple_of(place * cells, cells), cells)]
     solved = []
     for w in range(count):
-        first, last = reduced_ends(red_in_ref, w)
+        first, last = reduced_ends(red_in, rows_ref, w)
         solved.append(back_substitute(it_ref[w, 0], ia_ref[w, 0], ib_ref[w, 0], first, last))
     section_three = mixed(mix_ref, solved)
     cell = cell_ref[0]
-    place = lax.axis_index(axis_name)
     for v in range(count):
-        coupling = visc_ref[v : v + 1, :] * cell
+        coupling = visc[v : v + 1, :] * cell
         centre = 1.0 + 2.0 * coupling
         side = (-coupling / centre).T
         it, ia, ib, rows = reduce_block(side, side, (section_three[v] / centre).T)
@@ -167,11 +174,14 @@
         ob_ref[v, 0] = ib
 
 
-def out_kernel(it_ref, ia_ref, ib_ref, red_in_ref, mix_ref, out_ref):
+def out_kernel(*refs, pieces):
+    it_ref, ia_ref, ib_ref = refs[:3]
+    red_in = refs[3 : 3 + pieces]
+    mix_ref, out_ref, rows_ref = refs[3 + pieces :]
     count = it_ref.shape[0]
     solved = []
     for w in range(count):
-        first, last = reduced_ends(red_in_ref, w)
+        first, last = reduced_ends(red_in, rows_ref, w)
         solved.append(back_substitute(it_ref[w, 0], ia_ref[w, 0], ib_ref[w, 0], first, last).T)
     for v, value in enumerate(mixed(mix_ref, solved)):
         out_ref[v, 0] = value
@@ -195,48 +205,52 @@
     )(flow_state, nb, source, cell_az, visc_az, beta_az, axial_diff, mix_in)
 
 
-def rad_sweep(it, ia, ib, red_in, mix_mid, cell_rad, visc_local):
+def rad_sweep(it, ia, ib, red_in, mix_mid, cell_rad, visc_rad):
     nv, nz, na, nr = it.shape
     big = pl.BlockSpec((nv, 1, na, nr), lambda z: (0, z, 0, 0))
     big_t = pl.BlockSpec((nv, 1, nr, na), lambda z: (0, z, 0, 0))
-    red_in_spec = pl.BlockSpec((nv, 1) + red_in.shape[2:], lambda z: (0, z, 0, 0, 0))
+    red_in_spec = pl.BlockSpec((nv, 1) + red_in[0].shape[2:], lambda z: (0, z, 0, 0, 0))
     mixs = pl.BlockSpec((nv, nv, nr), lambda z: (0, 0, 0))
     cell = pl.BlockSpec((1, na, nr), lambda z: (z, 0, 0))
-    par = pl.BlockSpec((nv, nr), lambda z: (0, 0))
+    par = pl.BlockSpec(visc_rad.shape, lambda z: (0, 0))
     red = pl.BlockSpec((nv, 1, 3, 2, na), lambda z: (0, z, 0, 0, 0))
     out = jax.ShapeDtypeStruct((nv, nz, nr, na), it.dtype)
-    kernel = functools.partial(rad_kernel, axis_name="rad", devices=lax.axis_size("rad"))
+    pieces = len(red_in)
+    kernel = functools.partial(rad_kernel, axis_name="rad", devices=lax.axis_size("rad"), pieces=pieces)
     return pl.pallas_call(
         kernel,
         grid=(nz,),
-        in_specs=[big, big, big, red_in_spec, mixs, cell, par],
+        in_specs=[big, big, big] + [red_in_spec] * pieces + [mixs, cell, par],
         out_specs=[big_t, big_t, big_t, red],
         out_shape=[out, out, out, jax.ShapeDtypeStruct((nv, nz, 3, 2, na), it.dtype)],
-    )(it, ia, ib, red_in, mix_mid, cell_rad, visc_local)
+        scratch_shapes=[pltpu.VMEM((3, 2 * pieces, nr), it.dtype)],
+    )(it, ia, ib, *red_in, mix_mid, cell_rad, visc_rad)
 
 
 def out_sweep(it, ia, ib, red_in, mix_out):
     nv, nz, nr, na = it.shape
     big_t = pl.BlockSpec((nv, 1, nr, na), lambda z: (0, z, 0, 0))
     big = pl.BlockSpec((nv, 1, na, nr), lambda z: (0, z, 0, 0))
-    red_in_spec = pl.BlockSpec((nv, 1) + red_in.shape[2:], lambda z: (0, z, 0, 0, 0))
+    red_in_spec = pl.BlockSpec((nv, 1) + red_in[0].shape[2:], lambda z: (0, z, 0, 0, 0))
     mixs = pl.BlockSpec((nv, nv, nr), lambda z: (0, 0, 0))
+    pieces = len(red_in)
     return pl.pallas_call(
-        out_kernel,
+        functools.partial(out_kernel, pieces=pieces),
         grid=(nz,),
-        in_specs=[big_t, big_t, big_t, red_in_spec, mixs],
+        in_specs=[big_t, big_t, big_t] + [red_in_spec] * pieces + [mixs],
         out_specs=big,
         out_shape=jax.ShapeDtypeStruct((nv, nz, na, nr), it.dtype),
-    )(it, ia, ib, red_in, mix_out)
-
-
-def gathered(block, axis_name, dim):
+        scratch_shapes=[pltpu.VMEM((3, 2 * pieces, na), it.dtype)],
+    )(it, ia, ib, *red_in, mix_out)
+
+
+def gathered(block, axis_name):
     count = lax.axis_size(axis_name)
     received = [block]
     for offset in range(1, count):
         pairs = [((i + offset) % count, i) for i in range(count)]
         received.append(lax.ppermute(block, axis_name, pairs))
-    return jnp.concatenate(received, axis=dim)
+    return received
 
 
 def neighbour_planes(block, axis_name):
@@ -273,10 +287,9 @@
     rad_cells = flow_state.shape[3]
     nb = neighbour_planes(flow_state, "ax")
     it, ia, ib, red = az_sweep(flow_state, nb, source, cell_az, visc_az, beta_az, axial_diff, mix_in)
-    red = gathered(red, "az", 3)
-    visc_local = lax.dynamic_slice_in_dim(visc_rad, lax.axis_index("rad") * rad_cells, rad_cells, 1)
-    it, ia, ib, red = rad_sweep(it, ia, ib, red, mix_mid, cell_rad, visc_local)
-    red = gathered(red, "rad", 3)
+    red = gathered(red, "az")
+    it, ia, ib, red = rad_sweep(it, ia, ib, red, mix_mid, cell_rad, visc_rad)
+    red = gathered(red, "rad")
     return out_sweep(it, ia, ib, red, mix_out)
 
 

time: 53.3 us -> 51.7 us (0.970)
  other arithmetic: 2.83 us -> 0 us
  local copies, waits for them, and re-layouts: 1.44 us -> 2.05 us
  waiting for transfers between devices: 18.7 us -> 19.3 us
    concatenate x2 -> x0, other arithmetic: 2.83 us -> none  [gathered(): return jnp.concatenate(received, axis=dim)]
    unnamed x4 -> x14, local copies, waits for them, and re-layouts: 0.84 us -> 2.05 us
    dynamic_slice x1 -> x0, local copies, waits for them, and re-layouts: 0.6 us -> none  [per_device(): lax.dynamic_slice_in_dim(visc_rad, lax.axis_index('rad') * rad_cells, rad...]
    ppermute x6, waiting for transfers between devices: 3.78 us -> 4.36 us  [gathered(): received.append(lax.ppermute(block, axis_name, pairs))]
  transfers between devices with their start and end apart: 7 -> 7, of which waited for: 6 -> 7; matrix products, arithmetic and copies ran while one was open for 1% -> 0% of each run, Pallas kernels for 0% -> 0%
where the time goes in v7:
time: 51.7 us; the launch traced here: 51.5 us
  waiting for transfers between devices  19.3 us (37%)
  Pallas kernels  18.4 us (36%)
  starting transfers between devices  11.7 us (23%)
  local copies, waits for them, and re-layouts  2.05 us (4%)
    ppermute x1, waiting for transfers between devices, neighbour_planes(): return lax.ppermute(block, axis_name, [(0, 1), (1, 0)])  14.9 us
    ppermute x6, starting transfers between devices, gathered(): received.append(lax.ppermute(block, axis_name, pairs))  8.75 us
    pallas_call x1, Pallas kernels, rad_sweep(): pl.pallas_call(kernel, grid=(nz,), in_specs=[big, big, big] + [red_in_spe...  8.52 us
    pallas_call x1, Pallas kernels, az_sweep(): pl.pallas_call(az_kernel, grid=(nz, nr // chunk), in_specs=[big, big, big...  7.15 us
    ppermute x6, waiting for transfers between devices, gathered(): received.append(lax.ppermute(block, axis_name, pairs))  4.36 us
    ppermute x1, starting transfers between devices, neighbour_planes(): return lax.ppermute(block, axis_name, [(0, 1), (1, 0)])  2.97 us
    pallas_call x1, Pallas kernels, out_sweep(): pl.pallas_call(functools.partial(out_kernel, pieces=pieces), grid=(nz,),...  2.79 us
    unnamed x14, local copies, waits for them, and re-layouts  2.05 us
  transfers between devices with their start and end apart: 7, of which 7 were waited for; matrix products, arithmetic and copies ran while one was open for 0% of the time, Pallas kernels for 0%

profile of v7, /device:TPU:0, one launch (start us, length us, event | category | flops | bytes accessed | tf_op | source)
XLA Modules:
  0.0 51.5 jit_solution(14680415396501341254)
XLA Ops:
  0.0 3.0 %collective-permute-start = (f32[5,1,128,256]{3,2,1,0:T(8,128)}, f32[5,1,128,256]{3,2,1,0:T(8,128)S(1)}, u32[]{:S(2)}, u32[]{:S(2)}) collective-permute-start(f32[5,1,128,256]{3,2,1,0:T(8,128)} %fs_ref.1), channel_id=1, source_target_pairs={{0,1},{1,0},{2,3},{3,2},{4,5},{5,4},{6,7},{7,6},{8,9},{9,8},{10,11... | collective-permute-start | bytes 1966088 | tf_op jit(solution)/shard_map/ppermute | solution.py:259
  3.0 14.9 %collective-permute-done.nb_ref = f32[5,1,128,256]{3,2,1,0:T(8,128)S(1)} collective-permute-done((f32[5,1,128,256]{3,2,1,0:T(8,128)}, f32[5,1,128,256]{3,2,1,0:T(8,128)S(1)}, u32[]{:S(2)}, u32[]{:S(2)}) %collective-permute-start) | collective-permute-done | bytes 655392 | tf_op jit(solution)/shard_map/ppermute | solution.py:259
  17.9 0.0 copy-start
  17.9 0.8 %copy-done = f32[5,1,128,256]{3,2,1,0:T(8,128)} copy-done((f32[5,1,128,256]{3,2,1,0:T(8,128)}, f32[5,1,128,256]{3,2,1,0:T(8,128)S(1)}, u32[]{:S(2)}) %copy-start) | copy-done | bytes 655384
  18.7 7.1 %shard_map.109 = (f32[5,1,128,256]{3,2,1,0:T(8,128)}, f32[5,1,128,256]{3,2,1,0:T(8,128)}, f32[5,1,128,256]{3,2,1,0:T(8,128)}, f32[5,1,3,2,256]{4,3,2,1,0:T(2,128)}) custom-call(f32[5,1,128,256]{3,2,1,0:T(8,128)} %fs_ref.1, f32[5,1,128,256]{3,2,1,0:T(8,128)} %copy-done, f32[5,1,128,256]{3,2,1,0:T(8,128)} %src_ref.1, f32[1,128,256]{2,1,0:T(8,128)} %cell_ref.1, ...), custom_call_target="tpu_custom_call" | custom-call | tf_op jit(solution)/shard_map/pallas_call | solution.py:199
  25.9 0.1 collective-permute-start.3
  26.0 1.8 %collective-permute-start.2 = (f32[5,1,3,2,256]{4,3,2,1,0:T(2,128)}, f32[5,1,3,2,256]{4,3,2,1,0:T(2,128)S(1)}, u32[]{:S(2)}, u32[]{:S(2)}) collective-permute-start(f32[5,1,3,2,256]{4,3,2,1,0:T(2,128)} %get-tuple-element.16.refs_3_), channel_id=1, source_target_pairs={{16,0},{24,8},{0,16},{8,24},{17,1},{25,9},{1,17},{9,25},{18,2},{26... | collective-permute-start | bytes 92168 | tf_op jit(solution)/shard_map/ppermute | solution.py:252
  27.7 1.4 %collective-permute-start.1 = (f32[5,1,3,2,256]{4,3,2,1,0:T(2,128)}, f32[5,1,3,2,256]{4,3,2,1,0:T(2,128)S(1)}, u32[]{:S(2)}, u32[]{:S(2)}) collective-permute-start(f32[5,1,3,2,256]{4,3,2,1,0:T(2,128)} %get-tuple-element.16.refs_3_), channel_id=1, source_target_pairs={{8,0},{16,8},{24,16},{0,24},{9,1},{17,9},{25,17},{1,25},{10,2},{18... | collective-permute-start | bytes 92168 | tf_op jit(solution)/shard_map/ppermute | solution.py:252
  29.1 0.3 collective-permute-done.3.refs_6_
  29.5 0.0 copy-start.1
  29.5 0.7 %collective-permute-done.2.refs_5_ = f32[5,1,3,2,256]{4,3,2,1,0:T(2,128)S(1)} collective-permute-done((f32[5,1,3,2,256]{4,3,2,1,0:T(2,128)}, f32[5,1,3,2,256]{4,3,2,1,0:T(2,128)S(1)}, u32[]{:S(2)}, u32[]{:S(2)}) %collective-permute-start.2) | collective-permute-done | bytes 30752 | tf_op jit(solution)/shard_map/ppermute | solution.py:252
  30.1 0.0 copy-start.2
  30.1 0.8 %collective-permute-done.1.refs_4_ = f32[5,1,3,2,256]{4,3,2,1,0:T(2,128)S(1)} collective-permute-done((f32[5,1,3,2,256]{4,3,2,1,0:T(2,128)}, f32[5,1,3,2,256]{4,3,2,1,0:T(2,128)S(1)}, u32[]{:S(2)}, u32[]{:S(2)}) %collective-permute-start.1) | collective-permute-done | bytes 30752 | tf_op jit(solution)/shard_map/ppermute | solution.py:252
  30.9 0.0 copy-start.3
  30.9 0.0 copy-done.1
  30.9 0.0 copy-done.2
  30.9 0.6 %copy-done.3 = f32[5,1,3,2,256]{4,3,2,1,0:T(2,128)} copy-done((f32[5,1,3,2,256]{4,3,2,1,0:T(2,128)}, f32[5,1,3,2,256]{4,3,2,1,0:T(2,128)S(1)}, u32[]{:S(2)}) %copy-start.3) | copy-done | bytes 30744
  31.5 8.5 %shard_map.110 = (f32[5,1,256,128]{3,2,1,0:T(8,128)}, f32[5,1,256,128]{3,2,1,0:T(8,128)}, f32[5,1,256,128]{3,2,1,0:T(8,128)}, f32[5,1,3,2,128]{4,3,2,1,0:T(2,128)}) custom-call(f32[5,1,128,256]{3,2,1,0:T(8,128)} %get-tuple-element.13.refs_0_, f32[5,1,128,256]{3,2,1,0:T(8,128)} %get-tuple-element.14.refs_1_, f32[5,1,128,256]{3,2,1,0:T(8,128)} %get-tuple-element.15.refs_2_, ...), custom_call_target="tpu_custom_call" | custom-call | tf_op jit(solution)/shard_map/pallas_call | solution.py:220
  40.0 1.6 %collective-permute-start.6 = (f32[5,1,3,2,128]{4,3,2,1,0:T(2,128)}, f32[5,1,3,2,128]{4,3,2,1,0:T(2,128)S(1)}, u32[]{:S(2)}, u32[]{:S(2)}) collective-permute-start(f32[5,1,3,2,128]{4,3,2,1,0:T(2,128)} %get-tuple-element.20.refs_3_), channel_id=1, source_target_pairs={{6,0},{0,2},{2,4},{4,6},{7,1},{1,3},{3,5},{5,7},{14,8},{8,10},{10,... | collective-permute-start | bytes 46088 | tf_op jit(solution)/shard_map/ppermute | solution.py:252
  41.6 2.6 %collective-permute-start.5 = (f32[5,1,3,2,128]{4,3,2,1,0:T(2,128)}, f32[5,1,3,2,128]{4,3,2,1,0:T(2,128)S(1)}, u32[]{:S(2)}, u32[]{:S(2)}) collective-permute-start(f32[5,1,3,2,128]{4,3,2,1,0:T(2,128)} %get-tuple-element.20.refs_3_), channel_id=1, source_target_pairs={{4,0},{6,2},{0,4},{2,6},{5,1},{7,3},{1,5},{3,7},{12,8},{14,10},{8,... | collective-permute-start | bytes 46088 | tf_op jit(solution)/shard_map/ppermute | solution.py:252
  44.2 1.4 %collective-permute-start.4 = (f32[5,1,3,2,128]{4,3,2,1,0:T(2,128)}, f32[5,1,3,2,128]{4,3,2,1,0:T(2,128)S(1)}, u32[]{:S(2)}, u32[]{:S(2)}) collective-permute-start(f32[5,1,3,2,128]{4,3,2,1,0:T(2,128)} %get-tuple-element.20.refs_3_), channel_id=1, source_target_pairs={{2,0},{4,2},{6,4},{0,6},{3,1},{5,3},{7,5},{1,7},{10,8},{12,10},{14... | collective-permute-start | bytes 46088 | tf_op jit(solution)/shard_map/ppermute | solution.py:252
  45.6 0.2 collective-permute-done.6.refs_6_
  45.8 0.0 copy-start.4
  45.8 0.7 %collective-permute-done.5.refs_5_ = f32[5,1,3,2,128]{4,3,2,1,0:T(2,128)S(1)} collective-permute-done((f32[5,1,3,2,128]{4,3,2,1,0:T(2,128)}, f32[5,1,3,2,128]{4,3,2,1,0:T(2,128)S(1)}, u32[]{:S(2)}, u32[]{:S(2)}) %collective-permute-start.5) | collective-permute-done | bytes 15392 | tf_op jit(solution)/shard_map/ppermute | solution.py:252
  46.5 0.0 copy-start.5
  46.5 1.7 %collective-permute-done.4.refs_4_ = f32[5,1,3,2,128]{4,3,2,1,0:T(2,128)S(1)} collective-permute-done((f32[5,1,3,2,128]{4,3,2,1,0:T(2,128)}, f32[5,1,3,2,128]{4,3,2,1,0:T(2,128)S(1)}, u32[]{:S(2)}, u32[]{:S(2)}) %collective-permute-start.4) | collective-permute-done | bytes 15392 | tf_op jit(solution)/shard_map/ppermute | solution.py:252
  48.2 0.0 copy-start.6
  48.2 0.0 copy-done.4
  48.2 0.0 copy-done.5
  48.2 0.6 %copy-done.6 = f32[5,1,3,2,128]{4,3,2,1,0:T(2,128)} copy-done((f32[5,1,3,2,128]{4,3,2,1,0:T(2,128)}, f32[5,1,3,2,128]{4,3,2,1,0:T(2,128)S(1)}, u32[]{:S(2)}) %copy-start.6) | copy-done | bytes 15384
  48.8 2.8 %shard_map.111 = f32[5,1,128,256]{3,2,1,0:T(8,128)} custom-call(f32[5,1,256,128]{3,2,1,0:T(8,128)} %get-tuple-element.17.refs_0_, f32[5,1,256,128]{3,2,1,0:T(8,128)} %get-tuple-element.18.refs_1_, f32[5,1,256,128]{3,2,1,0:T(8,128)} %get-tuple-element.19.refs_2_, f32[5,1,3,2,128]{4,3,2,1,0:T(2,128)} %get-tuple-element.20.refs_3_, ...), custom_call_target="tpu_custom_call" | custom-call | tf_op jit(solution)/shard_map/pallas_call | solution.py:237
Async XLA Ops:
  0.0 17.9 %collective-permute-start = (f32[5,1,128,256]{3,2,1,0:T(8,128)}, f32[5,1,128,256]{3,2,1,0:T(8,128)S(1)}, u32[]{:S(2)}, u32[]{:S(2)}) collective-permute-start(f32[5,1,128,256]{3,2,1,0:T(8,128)} %fs_ref.1), channel_id=1, source_target_pairs={{0,1},{1,0},{2,3},{3,2},{4,5},{5,4},{6,7},{7,6},{8,9},{9,8},{10,11... | collective-permute-start | bytes 1966088 | tf_op jit(solution)/shard_map/ppermute | solution.py:259
  17.9 0.8 %copy-start = (f32[5,1,128,256]{3,2,1,0:T(8,128)}, f32[5,1,128,256]{3,2,1,0:T(8,128)S(1)}, u32[]{:S(2)}) copy-start(f32[5,1,128,256]{3,2,1,0:T(8,128)S(1)} %collective-permute-done.nb_ref) | copy-start | bytes 1966084
  25.9 3.6 %collective-permute-start.3 = (f32[5,1,3,2,256]{4,3,2,1,0:T(2,128)}, f32[5,1,3,2,256]{4,3,2,1,0:T(2,128)S(1)}, u32[]{:S(2)}, u32[]{:S(2)}) collective-permute-start(f32[5,1,3,2,256]{4,3,2,1,0:T(2,128)} %get-tuple-element.16.refs_3_), channel_id=1, source_target_pairs={{24,0},{0,8},{8,16},{16,24},{25,1},{1,9},{9,17},{17,25},{26,2},{2,... | collective-permute-start | bytes 92168 | tf_op jit(solution)/shard_map/ppermute | solution.py:252
  26.0 4.2 %collective-permute-start.2 = (f32[5,1,3,2,256]{4,3,2,1,0:T(2,128)}, f32[5,1,3,2,256]{4,3,2,1,0:T(2,128)S(1)}, u32[]{:S(2)}, u32[]{:S(2)}) collective-permute-start(f32[5,1,3,2,256]{4,3,2,1,0:T(2,128)} %get-tuple-element.16.refs_3_), channel_id=1, source_target_pairs={{16,0},{24,8},{0,16},{8,24},{17,1},{25,9},{1,17},{9,25},{18,2},{26... | collective-permute-start | bytes 92168 | tf_op jit(solution)/shard_map/ppermute | solution.py:252
  27.7 3.2 %collective-permute-start.1 = (f32[5,1,3,2,256]{4,3,2,1,0:T(2,128)}, f32[5,1,3,2,256]{4,3,2,1,0:T(2,128)S(1)}, u32[]{:S(2)}, u32[]{:S(2)}) collective-permute-start(f32[5,1,3,2,256]{4,3,2,1,0:T(2,128)} %get-tuple-element.16.refs_3_), channel_id=1, source_target_pairs={{8,0},{16,8},{24,16},{0,24},{9,1},{17,9},{25,17},{1,25},{10,2},{18... | collective-permute-start | bytes 92168 | tf_op jit(solution)/shard_map/ppermute | solution.py:252
  29.5 1.4 %copy-start.1 = (f32[5,1,3,2,256]{4,3,2,1,0:T(2,128)}, f32[5,1,3,2,256]{4,3,2,1,0:T(2,128)S(1)}, u32[]{:S(2)}) copy-start(f32[5,1,3,2,256]{4,3,2,1,0:T(2,128)S(1)} %collective-permute-done.3.refs_6_) | copy-start | bytes 92164
  30.1 0.8 %copy-start.2 = (f32[5,1,3,2,256]{4,3,2,1,0:T(2,128)}, f32[5,1,3,2,256]{4,3,2,1,0:T(2,128)S(1)}, u32[]{:S(2)}) copy-start(f32[5,1,3,2,256]{4,3,2,1,0:T(2,128)S(1)} %collective-permute-done.2.refs_5_) | copy-start | bytes 92164
  30.9 0.6 %copy-start.3 = (f32[5,1,3,2,256]{4,3,2,1,0:T(2,128)}, f32[5,1,3,2,256]{4,3,2,1,0:T(2,128)S(1)}, u32[]{:S(2)}) copy-start(f32[5,1,3,2,256]{4,3,2,1,0:T(2,128)S(1)} %collective-permute-done.1.refs_4_) | copy-start | bytes 92164
  40.0 5.7 %collective-permute-start.6 = (f32[5,1,3,2,128]{4,3,2,1,0:T(2,128)}, f32[5,1,3,2,128]{4,3,2,1,0:T(2,128)S(1)}, u32[]{:S(2)}, u32[]{:S(2)}) collective-permute-start(f32[5,1,3,2,128]{4,3,2,1,0:T(2,128)} %get-tuple-element.20.refs_3_), channel_id=1, source_target_pairs={{6,0},{0,2},{2,4},{4,6},{7,1},{1,3},{3,5},{5,7},{14,8},{8,10},{10,... | collective-permute-start | bytes 46088 | tf_op jit(solution)/shard_map/ppermute | solution.py:252
  41.6 4.9 %collective-permute-start.5 = (f32[5,1,3,2,128]{4,3,2,1,0:T(2,128)}, f32[5,1,3,2,128]{4,3,2,1,0:T(2,128)S(1)}, u32[]{:S(2)}, u32[]{:S(2)}) collective-permute-start(f32[5,1,3,2,128]{4,3,2,1,0:T(2,128)} %get-tuple-element.20.refs_3_), channel_id=1, source_target_pairs={{4,0},{6,2},{0,4},{2,6},{5,1},{7,3},{1,5},{3,7},{12,8},{14,10},{8,... | collective-permute-start | bytes 46088 | tf_op jit(solution)/shard_map/ppermute | solution.py:252
  44.2 3.9 %collective-permute-start.4 = (f32[5,1,3,2,128]{4,3,2,1,0:T(2,128)}, f32[5,1,3,2,128]{4,3,2,1,0:T(2,128)S(1)}, u32[]{:S(2)}, u32[]{:S(2)}) collective-permute-start(f32[5,1,3,2,128]{4,3,2,1,0:T(2,128)} %get-tuple-element.20.refs_3_), channel_id=1, source_target_pairs={{2,0},{4,2},{6,4},{0,6},{3,1},{5,3},{7,5},{1,7},{10,8},{12,10},{14... | collective-permute-start | bytes 46088 | tf_op jit(solution)/shard_map/ppermute | solution.py:252
  45.8 2.4 %copy-start.4 = (f32[5,1,3,2,128]{4,3,2,1,0:T(2,128)}, f32[5,1,3,2,128]{4,3,2,1,0:T(2,128)S(1)}, u32[]{:S(2)}) copy-start(f32[5,1,3,2,128]{4,3,2,1,0:T(2,128)S(1)} %collective-permute-done.6.refs_6_) | copy-start | bytes 46084
  46.5 1.7 %copy-start.5 = (f32[5,1,3,2,128]{4,3,2,1,0:T(2,128)}, f32[5,1,3,2,128]{4,3,2,1,0:T(2,128)S(1)}, u32[]{:S(2)}) copy-start(f32[5,1,3,2,128]{4,3,2,1,0:T(2,128)S(1)} %collective-permute-done.5.refs_5_) | copy-start | bytes 46084
  48.2 0.6 %copy-start.6 = (f32[5,1,3,2,128]{4,3,2,1,0:T(2,128)}, f32[5,1,3,2,128]{4,3,2,1,0:T(2,128)S(1)}, u32[]{:S(2)}) copy-start(f32[5,1,3,2,128]{4,3,2,1,0:T(2,128)S(1)} %collective-permute-done.4.refs_4_) | copy-start | bytes 46084

commit v8 on v7

--- a/solution.py
+++ b/solution.py
@@ -126,11 +126,13 @@
     return out
 
 
-def az_kernel(fs_ref, nb_ref, src_ref, cell_ref, visc_ref, beta_ref, diff_ref, mix_ref, ot_ref, oa_ref, ob_ref, red_ref):
+def az_kernel(fs_ref, nb_lo_ref, nb_hi_ref, src_ref, cell_ref, visc_ref, beta_ref, diff_ref, mix_ref, ot_ref, oa_ref, ob_ref, red_ref):
     count = fs_ref.shape[0]
+    split = nb_lo_ref.shape[0]
     explicit = []
     for w in range(count):
-        explicit.append(src_ref[w, 0] + diff_ref[w : w + 1, :] * (nb_ref[w, 0] - 2.0 * fs_ref[w, 0]))
+        nb = nb_lo_ref[w, 0] if w < split else nb_hi_ref[w - split, 0]
+        explicit.append(src_ref[w, 0] + diff_ref[w : w + 1, :] * (nb - 2.0 * fs_ref[w, 0]))
     section_one = mixed(mix_ref, explicit)
     cell = cell_ref[0]
     for v in range(count):
@@ -191,6 +193,8 @@
     nv, nz, na, nr = flow_state.shape
     chunk = 128 if nr % 128 == 0 else nr
     big = pl.BlockSpec((nv, 1, na, chunk), lambda z, c: (0, z, 0, c))
+    lo = pl.BlockSpec((nb[0].shape[0], 1, na, chunk), lambda z, c: (0, z, 0, c))
+    hi = pl.BlockSpec((nb[1].shape[0], 1, na, chunk), lambda z, c: (0, z, 0, c))
     cell = pl.BlockSpec((1, na, chunk), lambda z, c: (z, 0, c))
     par = pl.BlockSpec((nv, chunk), lambda z, c: (0, c))
     mixs = pl.BlockSpec((nv, nv, chunk), lambda z, c: (0, 0, c))
@@ -199,10 +203,10 @@
     return pl.pallas_call(
         az_kernel,
         grid=(nz, nr // chunk),
-        in_specs=[big, big, big, cell, par, par, par, mixs],
+        in_specs=[big, lo, hi, big, cell, par, par, par, mixs],
         out_specs=[big, big, big, red],
         out_shape=[out, out, out, jax.ShapeDtypeStruct((nv, nz, 3, 2, nr), flow_state.dtype)],
-    )(flow_state, nb, source, cell_az, visc_az, beta_az, axial_diff, mix_in)
+    )(flow_state, nb[0], nb[1], source, cell_az, visc_az, beta_az, axial_diff, mix_in)
 
 
 def rad_sweep(it, ia, ib, red_in, mix_mid, cell_rad, visc_rad):
@@ -255,10 +259,15 @@
 
 def neighbour_planes(block, axis_name):
     count = lax.axis_size(axis_name)
+    split = (block.shape[0] + 1) // 2
+    pieces = (block[:split], block[split:])
     if count == 2:
-        return lax.ppermute(block, axis_name, [(0, 1), (1, 0)])
-    padded = with_halo(block, ((axis_name, 1),), 1, False)
-    return padded[:, :-2] + padded[:, 2:]
+        return [lax.ppermute(piece, axis_name, [(0, 1), (1, 0)]) for piece in pieces]
+    out = []
+    for piece in pieces:
+        padded = with_halo(piece, ((axis_name, 1),), 1, False)
+        out.append(padded[:, :-2] + padded[:, 2:])
+    return out
 
 
 def mix(matrix, values):

time: 51.7 us -> 53.2 us (1.029)
  local copies, waits for them, and re-layouts: 2.05 us -> 4.65 us
  waiting for transfers between devices: 19.3 us -> 18 us
    slice x0 -> x2, local copies, waits for them, and re-layouts: none -> 1.99 us  [neighbour_planes(): pieces = (block[:split], block[split:])]
    ppermute x1 -> x2, waiting for transfers between devices: 14.9 us -> 13.7 us  [neighbour_planes(): lax.ppermute(piece, axis_name, [(0, 1), (1, 0)])]
    unnamed x14 -> x16, local copies, waits for them, and re-layouts: 2.05 us -> 2.67 us
    ppermute x1 -> x2, starting transfers between devices: 2.97 us -> 3.11 us  [neighbour_planes(): lax.ppermute(piece, axis_name, [(0, 1), (1, 0)])]
  transfers between devices with their start and end apart: 7 -> 8, of which waited for: 7 -> 7; matrix products, arithmetic and copies ran while one was open for 0% -> 2% of each run, Pallas kernels for 0% -> 0%
where the time goes in v8:
time: 53.2 us; the launch traced here: 53 us
  Pallas kernels  18.4 us (35%)
  waiting for transfers between devices  18 us (34%)
  starting transfers between devices  11.9 us (22%)
  local copies, waits for them, and re-layouts  4.65 us (9%)
    ppermute x2, waiting for transfers between devices, neighbour_planes(): lax.ppermute(piece, axis_name, [(0, 1), (1, 0)])  13.7 us
    ppermute x6, starting transfers between devices, gathered(): received.append(lax.ppermute(block, axis_name, pairs))  8.75 us
    pallas_call x1, Pallas kernels, rad_sweep(): pl.pallas_call(kernel, grid=(nz,), in_specs=[big, big, big] + [red_in_spe...  8.51 us
    pallas_call x1, Pallas kernels, az_sweep(): pl.pallas_call(az_kernel, grid=(nz, nr // chunk), in_specs=[big, lo, hi,...  7.09 us
    ppermute x6, waiting for transfers between devices, gathered(): received.append(lax.ppermute(block, axis_name, pairs))  4.36 us
    ppermute x2, starting transfers between devices, neighbour_planes(): lax.ppermute(piece, axis_name, [(0, 1), (1, 0)])  3.11 us
    pallas_call x1, Pallas kernels, out_sweep(): pl.pallas_call(functools.partial(out_kernel, pieces=pieces), grid=(nz,),...  2.79 us
    unnamed x16, local copies, waits for them, and re-layouts  2.67 us
  transfers between devices with their start and end apart: 8, of which 7 were waited for; matrix products, arithmetic and copies ran while one was open for 2% of the time, Pallas kernels for 0%

profile of v8, /device:TPU:0, one launch (start us, length us, event | category | flops | bytes accessed | tf_op | source)
XLA Modules:
  0.0 53.0 jit_solution(7936061957566434903)
XLA Ops:
  0.0 1.0 %slice.6 = f32[3,1,128,256]{3,2,1,0:T(8,128)S(1)} slice(f32[5,1,128,256]{3,2,1,0:T(8,128)} %fs_ref.1), slice={[0:3], [0:1], [0:128], [0:256]} | slice | bytes 786432 | tf_op jit(solution)/shard_map/slice | solution.py:263
  1.0 3.0 %collective-permute-start = (f32[3,1,128,256]{3,2,1,0:T(8,128)S(1)}, f32[3,1,128,256]{3,2,1,0:T(8,128)S(1)}, u32[]{:S(2)}, u32[]{:S(2)}) collective-permute-start(f32[3,1,128,256]{3,2,1,0:T(8,128)S(1)} %slice.6), channel_id=1, source_target_pairs={{0,1},{1,0},{2,3},{3,2},{4,5},{5,4},{6,7},{7,6},{8,9},{9,8},{10,11... | collective-permute-start | bytes 1179656 | tf_op jit(solution)/shard_map/ppermute | solution.py:265
  4.1 1.0 %slice.7 = f32[2,1,128,256]{3,2,1,0:T(8,128)S(1)} slice(f32[5,1,128,256]{3,2,1,0:T(8,128)} %fs_ref.1), slice={[3:5], [0:1], [0:128], [0:256]} | slice | bytes 524288 | tf_op jit(solution)/shard_map/slice | solution.py:263
  5.0 0.1 collective-permute-start.1
  5.1 13.7 %collective-permute-done.1.nb_hi_ref = f32[2,1,128,256]{3,2,1,0:T(8,128)S(1)} collective-permute-done((f32[2,1,128,256]{3,2,1,0:T(8,128)S(1)}, f32[2,1,128,256]{3,2,1,0:T(8,128)S(1)}, u32[]{:S(2)}, u32[]{:S(2)}) %collective-permute-start.1) | collective-permute-done | bytes 262176 | tf_op jit(solution)/shard_map/ppermute | solution.py:265
  18.8 0.0 copy-start.1
  18.8 0.0 collective-permute-done.nb_lo_ref
  18.8 0.7 %copy-done.1 = f32[2,1,128,256]{3,2,1,0:T(8,128)} copy-done((f32[2,1,128,256]{3,2,1,0:T(8,128)}, f32[2,1,128,256]{3,2,1,0:T(8,128)S(1)}, u32[]{:S(2)}) %copy-start.1) | copy-done | bytes 262168
  19.5 0.0 copy-start
  19.5 0.8 %copy-done = f32[3,1,128,256]{3,2,1,0:T(8,128)} copy-done((f32[3,1,128,256]{3,2,1,0:T(8,128)}, f32[3,1,128,256]{3,2,1,0:T(8,128)S(1)}, u32[]{:S(2)}) %copy-start) | copy-done | bytes 393240
  20.2 7.1 %shard_map.109 = (f32[5,1,128,256]{3,2,1,0:T(8,128)}, f32[5,1,128,256]{3,2,1,0:T(8,128)}, f32[5,1,128,256]{3,2,1,0:T(8,128)}, f32[5,1,3,2,256]{4,3,2,1,0:T(2,128)}) custom-call(f32[5,1,128,256]{3,2,1,0:T(8,128)} %fs_ref.1, f32[3,1,128,256]{3,2,1,0:T(8,128)} %copy-done, f32[2,1,128,256]{3,2,1,0:T(8,128)} %copy-done.1, f32[5,1,128,256]{3,2,1,0:T(8,128)} %src_ref.1, ...), custom_call_target="tpu_custom_call" | custom-call | tf_op jit(solution)/shard_map/pallas_call | solution.py:203
  27.3 0.1 collective-permute-start.4
  27.4 1.8 %collective-permute-start.3 = (f32[5,1,3,2,256]{4,3,2,1,0:T(2,128)}, f32[5,1,3,2,256]{4,3,2,1,0:T(2,128)S(1)}, u32[]{:S(2)}, u32[]{:S(2)}) collective-permute-start(f32[5,1,3,2,256]{4,3,2,1,0:T(2,128)} %get-tuple-element.16.refs_3_), channel_id=1, source_target_pairs={{16,0},{24,8},{0,16},{8,24},{17,1},{25,9},{1,17},{9,25},{18,2},{26... | collective-permute-start | bytes 92168 | tf_op jit(solution)/shard_map/ppermute | solution.py:256
  29.2 1.4 %collective-permute-start.2 = (f32[5,1,3,2,256]{4,3,2,1,0:T(2,128)}, f32[5,1,3,2,256]{4,3,2,1,0:T(2,128)S(1)}, u32[]{:S(2)}, u32[]{:S(2)}) collective-permute-start(f32[5,1,3,2,256]{4,3,2,1,0:T(2,128)} %get-tuple-element.16.refs_3_), channel_id=1, source_target_pairs={{8,0},{16,8},{24,16},{0,24},{9,1},{17,9},{25,17},{1,25},{10,2},{18... | collective-permute-start | bytes 92168 | tf_op jit(solution)/shard_map/ppermute | solution.py:256
  30.6 0.3 collective-permute-done.4.refs_6_
  30.9 0.0 copy-start.2
  30.9 0.7 %collective-permute-done.3.refs_5_ = f32[5,1,3,2,256]{4,3,2,1,0:T(2,128)S(1)} collective-permute-done((f32[5,1,3,2,256]{4,3,2,1,0:T(2,128)}, f32[5,1,3,2,256]{4,3,2,1,0:T(2,128)S(1)}, u32[]{:S(2)}, u32[]{:S(2)}) %collective-permute-start.3) | collective-permute-done | bytes 30752 | tf_op jit(solution)/shard_map/ppermute | solution.py:256
  31.6 0.0 copy-start.3
  31.6 0.8 %collective-permute-done.2.refs_4_ = f32[5,1,3,2,256]{4,3,2,1,0:T(2,128)S(1)} collective-permute-done((f32[5,1,3,2,256]{4,3,2,1,0:T(2,128)}, f32[5,1,3,2,256]{4,3,2,1,0:T(2,128)S(1)}, u32[]{:S(2)}, u32[]{:S(2)}) %collective-permute-start.2) | collective-permute-done | bytes 30752 | tf_op jit(solution)/shard_map/ppermute | solution.py:256
  32.4 0.0 copy-start.4
  32.4 0.0 copy-done.2
  32.4 0.0 copy-done.3
  32.4 0.6 %copy-done.4 = f32[5,1,3,2,256]{4,3,2,1,0:T(2,128)} copy-done((f32[5,1,3,2,256]{4,3,2,1,0:T(2,128)}, f32[5,1,3,2,256]{4,3,2,1,0:T(2,128)S(1)}, u32[]{:S(2)}) %copy-start.4) | copy-done | bytes 30744
  33.0 8.5 %shard_map.110 = (f32[5,1,256,128]{3,2,1,0:T(8,128)}, f32[5,1,256,128]{3,2,1,0:T(8,128)}, f32[5,1,256,128]{3,2,1,0:T(8,128)}, f32[5,1,3,2,128]{4,3,2,1,0:T(2,128)}) custom-call(f32[5,1,128,256]{3,2,1,0:T(8,128)} %get-tuple-element.13.refs_0_, f32[5,1,128,256]{3,2,1,0:T(8,128)} %get-tuple-element.14.refs_1_, f32[5,1,128,256]{3,2,1,0:T(8,128)} %get-tuple-element.15.refs_2_, ...), custom_call_target="tpu_custom_call" | custom-call | tf_op jit(solution)/shard_map/pallas_call | solution.py:224
  41.5 1.6 %collective-permute-start.7 = (f32[5,1,3,2,128]{4,3,2,1,0:T(2,128)}, f32[5,1,3,2,128]{4,3,2,1,0:T(2,128)S(1)}, u32[]{:S(2)}, u32[]{:S(2)}) collective-permute-start(f32[5,1,3,2,128]{4,3,2,1,0:T(2,128)} %get-tuple-element.20.refs_3_), channel_id=1, source_target_pairs={{6,0},{0,2},{2,4},{4,6},{7,1},{1,3},{3,5},{5,7},{14,8},{8,10},{10,... | collective-permute-start | bytes 46088 | tf_op jit(solution)/shard_map/ppermute | solution.py:256
  43.0 2.6 %collective-permute-start.6 = (f32[5,1,3,2,128]{4,3,2,1,0:T(2,128)}, f32[5,1,3,2,128]{4,3,2,1,0:T(2,128)S(1)}, u32[]{:S(2)}, u32[]{:S(2)}) collective-permute-start(f32[5,1,3,2,128]{4,3,2,1,0:T(2,128)} %get-tuple-element.20.refs_3_), channel_id=1, source_target_pairs={{4,0},{6,2},{0,4},{2,6},{5,1},{7,3},{1,5},{3,7},{12,8},{14,10},{8,... | collective-permute-start | bytes 46088 | tf_op jit(solution)/shard_map/ppermute | solution.py:256
  45.7 1.4 %collective-permute-start.5 = (f32[5,1,3,2,128]{4,3,2,1,0:T(2,128)}, f32[5,1,3,2,128]{4,3,2,1,0:T(2,128)S(1)}, u32[]{:S(2)}, u32[]{:S(2)}) collective-permute-start(f32[5,1,3,2,128]{4,3,2,1,0:T(2,128)} %get-tuple-element.20.refs_3_), channel_id=1, source_target_pairs={{2,0},{4,2},{6,4},{0,6},{3,1},{5,3},{7,5},{1,7},{10,8},{12,10},{14... | collective-permute-start | bytes 46088 | tf_op jit(solution)/shard_map/ppermute | solution.py:256
  47.0 0.2 collective-permute-done.7.refs_6_
  47.2 0.0 copy-start.5
  47.2 0.7 %collective-permute-done.6.refs_5_ = f32[5,1,3,2,128]{4,3,2,1,0:T(2,128)S(1)} collective-permute-done((f32[5,1,3,2,128]{4,3,2,1,0:T(2,128)}, f32[5,1,3,2,128]{4,3,2,1,0:T(2,128)S(1)}, u32[]{:S(2)}, u32[]{:S(2)}) %collective-permute-start.6) | collective-permute-done | bytes 15392 | tf_op jit(solution)/shard_map/ppermute | solution.py:256
  47.9 0.0 copy-start.6
  47.9 1.7 %collective-permute-done.5.refs_4_ = f32[5,1,3,2,128]{4,3,2,1,0:T(2,128)S(1)} collective-permute-done((f32[5,1,3,2,128]{4,3,2,1,0:T(2,128)}, f32[5,1,3,2,128]{4,3,2,1,0:T(2,128)S(1)}, u32[]{:S(2)}, u32[]{:S(2)}) %collective-permute-start.5) | collective-permute-done | bytes 15392 | tf_op jit(solution)/shard_map/ppermute | solution.py:256
  49.6 0.0 copy-start.7
  49.6 0.0 copy-done.5
  49.6 0.0 copy-done.6
  49.6 0.6 %copy-done.7 = f32[5,1,3,2,128]{4,3,2,1,0:T(2,128)} copy-done((f32[5,1,3,2,128]{4,3,2,1,0:T(2,128)}, f32[5,1,3,2,128]{4,3,2,1,0:T(2,128)S(1)}, u32[]{:S(2)}) %copy-start.7) | copy-done | bytes 15384
  50.2 2.8 %shard_map.111 = f32[5,1,128,256]{3,2,1,0:T(8,128)} custom-call(f32[5,1,256,128]{3,2,1,0:T(8,128)} %get-tuple-element.17.refs_0_, f32[5,1,256,128]{3,2,1,0:T(8,128)} %get-tuple-element.18.refs_1_, f32[5,1,256,128]{3,2,1,0:T(8,128)} %get-tuple-element.19.refs_2_, f32[5,1,3,2,128]{4,3,2,1,0:T(2,128)} %get-tuple-element.20.refs_3_, ...), custom_call_target="tpu_custom_call" | custom-call | tf_op jit(solution)/shard_map/pallas_call | solution.py:241
Async XLA Ops:
  1.0 17.8 %collective-permute-start = (f32[3,1,128,256]{3,2,1,0:T(8,128)S(1)}, f32[3,1,128,256]{3,2,1,0:T(8,128)S(1)}, u32[]{:S(2)}, u32[]{:S(2)}) collective-permute-start(f32[3,1,128,256]{3,2,1,0:T(8,128)S(1)} %slice.6), channel_id=1, source_target_pairs={{0,1},{1,0},{2,3},{3,2},{4,5},{5,4},{6,7},{7,6},{8,9},{9,8},{10,11... | collective-permute-start | bytes 1179656 | tf_op jit(solution)/shard_map/ppermute | solution.py:265
  5.0 13.8 %collective-permute-start.1 = (f32[2,1,128,256]{3,2,1,0:T(8,128)S(1)}, f32[2,1,128,256]{3,2,1,0:T(8,128)S(1)}, u32[]{:S(2)}, u32[]{:S(2)}) collective-permute-start(f32[2,1,128,256]{3,2,1,0:T(8,128)S(1)} %slice.7), channel_id=1, source_target_pairs={{0,1},{1,0},{2,3},{3,2},{4,5},{5,4},{6,7},{7,6},{8,9},{9,8},{10,11... | collective-permute-start | bytes 786440 | tf_op jit(solution)/shard_map/ppermute | solution.py:265
  18.8 0.7 %copy-start.1 = (f32[2,1,128,256]{3,2,1,0:T(8,128)}, f32[2,1,128,256]{3,2,1,0:T(8,128)S(1)}, u32[]{:S(2)}) copy-start(f32[2,1,128,256]{3,2,1,0:T(8,128)S(1)} %collective-permute-done.1.nb_hi_ref) | copy-start | bytes 786436
  19.5 0.8 %copy-start = (f32[3,1,128,256]{3,2,1,0:T(8,128)}, f32[3,1,128,256]{3,2,1,0:T(8,128)S(1)}, u32[]{:S(2)}) copy-start(f32[3,1,128,256]{3,2,1,0:T(8,128)S(1)} %collective-permute-done.nb_lo_ref) | copy-start | bytes 1179652
  27.3 3.6 %collective-permute-start.4 = (f32[5,1,3,2,256]{4,3,2,1,0:T(2,128)}, f32[5,1,3,2,256]{4,3,2,1,0:T(2,128)S(1)}, u32[]{:S(2)}, u32[]{:S(2)}) collective-permute-start(f32[5,1,3,2,256]{4,3,2,1,0:T(2,128)} %get-tuple-element.16.refs_3_), channel_id=1, source_target_pairs={{24,0},{0,8},{8,16},{16,24},{25,1},{1,9},{9,17},{17,25},{26,2},{2,... | collective-permute-start | bytes 92168 | tf_op jit(solution)/shard_map/ppermute | solution.py:256
  27.4 4.2 %collective-permute-start.3 = (f32[5,1,3,2,256]{4,3,2,1,0:T(2,128)}, f32[5,1,3,2,256]{4,3,2,1,0:T(2,128)S(1)}, u32[]{:S(2)}, u32[]{:S(2)}) collective-permute-start(f32[5,1,3,2,256]{4,3,2,1,0:T(2,128)} %get-tuple-element.16.refs_3_), channel_id=1, source_target_pairs={{16,0},{24,8},{0,16},{8,24},{17,1},{25,9},{1,17},{9,25},{18,2},{26... | collective-permute-start | bytes 92168 | tf_op jit(solution)/shard_map/ppermute | solution.py:256
  29.2 3.2 %collective-permute-start.2 = (f32[5,1,3,2,256]{4,3,2,1,0:T(2,128)}, f32[5,1,3,2,256]{4,3,2,1,0:T(2,128)S(1)}, u32[]{:S(2)}, u32[]{:S(2)}) collective-permute-start(f32[5,1,3,2,256]{4,3,2,1,0:T(2,128)} %get-tuple-element.16.refs_3_), channel_id=1, source_target_pairs={{8,0},{16,8},{24,16},{0,24},{9,1},{17,9},{25,17},{1,25},{10,2},{18... | collective-permute-start | bytes 92168 | tf_op jit(solution)/shard_map/ppermute | solution.py:256
  30.9 1.4 %copy-start.2 = (f32[5,1,3,2,256]{4,3,2,1,0:T(2,128)}, f32[5,1,3,2,256]{4,3,2,1,0:T(2,128)S(1)}, u32[]{:S(2)}) copy-start(f32[5,1,3,2,256]{4,3,2,1,0:T(2,128)S(1)} %collective-permute-done.4.refs_6_) | copy-start | bytes 92164
  31.6 0.8 %copy-start.3 = (f32[5,1,3,2,256]{4,3,2,1,0:T(2,128)}, f32[5,1,3,2,256]{4,3,2,1,0:T(2,128)S(1)}, u32[]{:S(2)}) copy-start(f32[5,1,3,2,256]{4,3,2,1,0:T(2,128)S(1)} %collective-permute-done.3.refs_5_) | copy-start | bytes 92164
  32.4 0.6 %copy-start.4 = (f32[5,1,3,2,256]{4,3,2,1,0:T(2,128)}, f32[5,1,3,2,256]{4,3,2,1,0:T(2,128)S(1)}, u32[]{:S(2)}) copy-start(f32[5,1,3,2,256]{4,3,2,1,0:T(2,128)S(1)} %collective-permute-done.2.refs_4_) | copy-start | bytes 92164
  41.5 5.7 %collective-permute-start.7 = (f32[5,1,3,2,128]{4,3,2,1,0:T(2,128)}, f32[5,1,3,2,128]{4,3,2,1,0:T(2,128)S(1)}, u32[]{:S(2)}, u32[]{:S(2)}) collective-permute-start(f32[5,1,3,2,128]{4,3,2,1,0:T(2,128)} %get-tuple-element.20.refs_3_), channel_id=1, source_target_pairs={{6,0},{0,2},{2,4},{4,6},{7,1},{1,3},{3,5},{5,7},{14,8},{8,10},{10,... | collective-permute-start | bytes 46088 | tf_op jit(solution)/shard_map/ppermute | solution.py:256
  43.0 4.9 %collective-permute-start.6 = (f32[5,1,3,2,128]{4,3,2,1,0:T(2,128)}, f32[5,1,3,2,128]{4,3,2,1,0:T(2,128)S(1)}, u32[]{:S(2)}, u32[]{:S(2)}) collective-permute-start(f32[5,1,3,2,128]{4,3,2,1,0:T(2,128)} %get-tuple-element.20.refs_3_), channel_id=1, source_target_pairs={{4,0},{6,2},{0,4},{2,6},{5,1},{7,3},{1,5},{3,7},{12,8},{14,10},{8,... | collective-permute-start | bytes 46088 | tf_op jit(solution)/shard_map/ppermute | solution.py:256
  45.7 3.9 %collective-permute-start.5 = (f32[5,1,3,2,128]{4,3,2,1,0:T(2,128)}, f32[5,1,3,2,128]{4,3,2,1,0:T(2,128)S(1)}, u32[]{:S(2)}, u32[]{:S(2)}) collective-permute-start(f32[5,1,3,2,128]{4,3,2,1,0:T(2,128)} %get-tuple-element.20.refs_3_), channel_id=1, source_target_pairs={{2,0},{4,2},{6,4},{0,6},{3,1},{5,3},{7,5},{1,7},{10,8},{12,10},{14... | collective-permute-start | bytes 46088 | tf_op jit(solution)/shard_map/ppermute | solution.py:256
  47.2 2.4 %copy-start.5 = (f32[5,1,3,2,128]{4,3,2,1,0:T(2,128)}, f32[5,1,3,2,128]{4,3,2,1,0:T(2,128)S(1)}, u32[]{:S(2)}) copy-start(f32[5,1,3,2,128]{4,3,2,1,0:T(2,128)S(1)} %collective-permute-done.7.refs_6_) | copy-start | bytes 46084
  47.9 1.7 %copy-start.6 = (f32[5,1,3,2,128]{4,3,2,1,0:T(2,128)}, f32[5,1,3,2,128]{4,3,2,1,0:T(2,128)S(1)}, u32[]{:S(2)}) copy-start(f32[5,1,3,2,128]{4,3,2,1,0:T(2,128)S(1)} %collective-permute-done.6.refs_5_) | copy-start | bytes 46084
  49.6 0.6 %copy-start.7 = (f32[5,1,3,2,128]{4,3,2,1,0:T(2,128)}, f32[5,1,3,2,128]{4,3,2,1,0:T(2,128)S(1)}, u32[]{:S(2)}) copy-start(f32[5,1,3,2,128]{4,3,2,1,0:T(2,128)S(1)} %collective-permute-done.5.refs_4_) | copy-start | bytes 46084

commit v9 on v7

--- a/solution.py
+++ b/solution.py
@@ -51,7 +51,7 @@
     return lower, upper, rhs
 
 
-def reduce_block(lower, upper, target):
+def interior(lower, upper):
     length = lower.shape[0]
     idx = lax.broadcasted_iota(jnp.int32, lower.shape, 0)
     edge = (idx == 0) | (idx == length - 1)
@@ -60,7 +60,11 @@
     zero = jnp.zeros_like(lower)
     il = jnp.where(edge | second, zero, lower)
     iu = jnp.where(edge | penult, zero, upper)
-    rhs = [jnp.where(edge, zero, target), jnp.where(second, lower, zero), jnp.where(penult, upper, zero)]
+    return il, iu, jnp.where(edge, zero, 1.0), jnp.where(second, lower, zero), jnp.where(penult, upper, zero)
+
+
+def pcr_levels(il, iu, rhs):
+    length = il.shape[0]
     stride = 1
     while stride < length - 2:
         back = length - stride
@@ -70,17 +74,30 @@
         rhs = [(r - il * pltpu.roll(r, stride, 0) - iu * pltpu.roll(r, back, 0)) * inv for r in rhs]
         il, iu = -il * ll * inv, -iu * ur * inv
         stride = stride * 2
-    it, ia, ib = rhs
-    l0, u0, t0 = lower[0:1], upper[0:1], target[0:1]
-    le, ue, te = lower[length - 1 :], upper[length - 1 :], target[length - 1 :]
-    a1, b1, t1 = ia[1:2], ib[1:2], it[1:2]
-    a2, b2, t2 = ia[length - 2 : length - 1], ib[length - 2 : length - 1], it[length - 2 : length - 1]
+    return rhs
+
+
+def interface_rows(lower, upper, t0, te, t1, t2, a1, b1, a2, b2):
+    length = lower.shape[0]
+    l0, u0 = lower[0:1], upper[0:1]
+    le, ue = lower[length - 1 :], upper[length - 1 :]
     inv_f = 1.0 / (1.0 - u0 * a1)
     inv_e = 1.0 / (1.0 - le * b2)
-    rows = (
+    return (
         (l0 * inv_f, -le * a2 * inv_e),
         (-u0 * b1 * inv_f, ue * inv_e),
         ((t0 - u0 * t1) * inv_f, (te - le * t2) * inv_e),
+    )
+
+
+def reduce_block(lower, upper, target):
+    length = lower.shape[0]
+    il, iu, keep, a_init, b_init = interior(lower, upper)
+    it, ia, ib = pcr_levels(il, iu, [target * keep, a_init, b_init])
+    n2 = length - 2
+    rows = interface_rows(
+        lower, upper, target[0:1], target[length - 1 :], it[1:2], it[n2 : n2 + 1],
+        ia[1:2], ib[1:2], ia[n2 : n2 + 1], ib[n2 : n2 + 1],
     )
     return it, ia, ib, rows
 
@@ -126,24 +143,56 @@
     return out
 
 
-def az_kernel(fs_ref, nb_ref, src_ref, cell_ref, visc_ref, beta_ref, diff_ref, mix_ref, ot_ref, oa_ref, ob_ref, red_ref):
+def az_coefficients(cell, visc_ref, beta_ref, v):
+    coupling = visc_ref[v : v + 1, :] * cell
+    centre = 1.0 + 2.0 * coupling
+    tilt = beta_ref[v : v + 1, :]
+    lower = -coupling * (1.0 + tilt) / centre
+    upper = -coupling * (1.0 - tilt) / centre
+    return lower, upper, centre
+
+
+def az_local_kernel(fs_ref, src_ref, cell_ref, visc_ref, beta_ref, diff_ref, mix_ref, ot_ref, oa_ref, ob_ref, edge_ref):
     count = fs_ref.shape[0]
-    explicit = []
-    for w in range(count):
-        explicit.append(src_ref[w, 0] + diff_ref[w : w + 1, :] * (nb_ref[w, 0] - 2.0 * fs_ref[w, 0]))
+    explicit = [src_ref[w, 0] + diff_ref[w : w + 1, :] * (-2.0 * fs_ref[w, 0]) for w in range(count)]
     section_one = mixed(mix_ref, explicit)
     cell = cell_ref[0]
     for v in range(count):
-        coupling = visc_ref[v : v + 1, :] * cell
-        centre = 1.0 + 2.0 * coupling
-        tilt = beta_ref[v : v + 1, :]
-        lower = -coupling * (1.0 + tilt) / centre
-        upper = -coupling * (1.0 - tilt) / centre
-        it, ia, ib, rows = reduce_block(lower, upper, section_one[v] / centre)
-        store_rows(red_ref, v, rows)
+        lower, upper, centre = az_coefficients(cell, visc_ref, beta_ref, v)
+        target = section_one[v] / centre
+        length = lower.shape[0]
+        il, iu, keep, a_init, b_init = interior(lower, upper)
+        it, ia, ib = pcr_levels(il, iu, [target * keep, a_init, b_init])
         ot_ref[v, 0] = it
         oa_ref[v, 0] = ia
         ob_ref[v, 0] = ib
+        n2 = length - 2
+        for k, value in enumerate(
+            (target[0:1], target[length - 1 :], ia[1:2], ib[1:2], ia[n2 : n2 + 1], ib[n2 : n2 + 1])
+        ):
+            edge_ref[v, 0, k : k + 1, :] = value
+
+
+def az_plane_kernel(nb_ref, cell_ref, visc_ref, beta_ref, diff_ref, mix_ref, it_in_ref, edge_ref, ot_ref, red_ref):
+    count = nb_ref.shape[0]
+    explicit = [diff_ref[w : w + 1, :] * nb_ref[w, 0] for w in range(count)]
+    section_one = mixed(mix_ref, explicit)
+    cell = cell_ref[0]
+    for v in range(count):
+        lower, upper, centre = az_coefficients(cell, visc_ref, beta_ref, v)
+        target = section_one[v] / centre
+        length = lower.shape[0]
+        il, iu, keep, _, _ = interior(lower, upper)
+        (it,) = pcr_levels(il, iu, [target * keep])
+        it = it_in_ref[v, 0] + it
+        ot_ref[v, 0] = it
+        edge = edge_ref[v, 0]
+        n2 = length - 2
+        rows = interface_rows(
+            lower, upper, edge[0:1] + target[0:1], edge[1:2] + target[length - 1 :], it[1:2], it[n2 : n2 + 1],
+            edge[2:3], edge[3:4], edge[4:5], edge[5:6],
+        )
+        store_rows(red_ref, v, rows)
 
 
 def rad_kernel(*refs, axis_name, devices, pieces):
@@ -190,19 +239,30 @@
 def az_sweep(flow_state, nb, source, cell_az, visc_az, beta_az, axial_diff, mix_in):
     nv, nz, na, nr = flow_state.shape
     chunk = 128 if nr % 128 == 0 else nr
+    grid = (nz, nr // chunk)
     big = pl.BlockSpec((nv, 1, na, chunk), lambda z, c: (0, z, 0, c))
     cell = pl.BlockSpec((1, na, chunk), lambda z, c: (z, 0, c))
     par = pl.BlockSpec((nv, chunk), lambda z, c: (0, c))
     mixs = pl.BlockSpec((nv, nv, chunk), lambda z, c: (0, 0, c))
+    edge = pl.BlockSpec((nv, 1, 6, chunk), lambda z, c: (0, z, 0, c))
     red = pl.BlockSpec((nv, 1, 3, 2, chunk), lambda z, c: (0, z, 0, 0, c))
     out = jax.ShapeDtypeStruct(flow_state.shape, flow_state.dtype)
-    return pl.pallas_call(
-        az_kernel,
-        grid=(nz, nr // chunk),
-        in_specs=[big, big, big, cell, par, par, par, mixs],
-        out_specs=[big, big, big, red],
-        out_shape=[out, out, out, jax.ShapeDtypeStruct((nv, nz, 3, 2, nr), flow_state.dtype)],
-    )(flow_state, nb, source, cell_az, visc_az, beta_az, axial_diff, mix_in)
+    it, ia, ib, edges = pl.pallas_call(
+        az_local_kernel,
+        grid=grid,
+        in_specs=[big, big, cell, par, par, par, mixs],
+        out_specs=[big, big, big, edge],
+        out_shape=[out, out, out, jax.ShapeDtypeStruct((nv, nz, 6, nr), flow_state.dtype)],
+    )(flow_state, source, cell_az, visc_az, beta_az, axial_diff, mix_in)
+    it, red = pl.pallas_call(
+        az_plane_kernel,
+        grid=grid,
+        in_specs=[big, cell, par, par, par, mixs, big, edge],
+        out_specs=[big, red],
+        out_shape=[out, jax.ShapeDtypeStruct((nv, nz, 3, 2, nr), flow_state.dtype)],
+        input_output_aliases={6: 0},
+    )(nb, cell_az, visc_az, beta_az, axial_diff, mix_in, it, edges)
+    return it, ia, ib, red
 
 
 def rad_sweep(it, ia, ib, red_in, mix_mid, cell_rad, visc_rad):

time: 51.7 us -> 50.2 us (0.971)
  waiting for transfers between devices: 19.3 us -> 12.4 us
  Pallas kernels: 18.4 us -> 23.8 us
    ppermute x1, waiting for transfers between devices: 14.9 us -> 8.01 us  [neighbour_planes(): return lax.ppermute(block, axis_name, [(0, 1), (1, 0)])]
    pallas_call x1 -> x2, Pallas kernels: 7.15 us -> 12.5 us  [the longest x1 6.93 us: az_sweep(): pl.pallas_call(az_local_kernel, grid=grid, in_specs=[big, big, cell, par,...]
  transfers between devices with their start and end apart: 7 -> 7, of which waited for: 7 -> 7; matrix products, arithmetic and copies ran while one was open for 0% -> 0% of each run, Pallas kernels for 0% -> 14%
where the time goes in v9:
time: 50.2 us; the launch traced here: 50 us
  Pallas kernels  23.8 us (47%)
  waiting for transfers between devices  12.4 us (25%)
  starting transfers between devices  11.7 us (23%)
  local copies, waits for them, and re-layouts  2.04 us (4%)
    ppermute x6, starting transfers between devices, gathered(): received.append(lax.ppermute(block, axis_name, pairs))  8.75 us
    pallas_call x1, Pallas kernels, rad_sweep(): pl.pallas_call(kernel, grid=(nz,), in_specs=[big, big, big] + [red_in_spe...  8.54 us
    ppermute x1, waiting for transfers between devices, neighbour_planes(): return lax.ppermute(block, axis_name, [(0, 1), (1, 0)])  8.01 us
    pallas_call x1, Pallas kernels, az_sweep(): pl.pallas_call(az_local_kernel, grid=grid, in_specs=[big, big, cell, par,...  6.93 us
    pallas_call x1, Pallas kernels, az_sweep(): pl.pallas_call(az_plane_kernel, grid=grid, in_specs=[big, cell, par, par,...  5.56 us
    ppermute x6, waiting for transfers between devices, gathered(): received.append(lax.ppermute(block, axis_name, pairs))  4.36 us
    ppermute x1, starting transfers between devices, neighbour_planes(): return lax.ppermute(block, axis_name, [(0, 1), (1, 0)])  2.97 us
    pallas_call x1, Pallas kernels, out_sweep(): pl.pallas_call(functools.partial(out_kernel, pieces=pieces), grid=(nz,),...  2.79 us
  transfers between devices with their start and end apart: 7, of which 7 were waited for; matrix products, arithmetic and copies ran while one was open for 0% of the time, Pallas kernels for 14%

profile of v9, /device:TPU:0, one launch (start us, length us, event | category | flops | bytes accessed | tf_op | source)
XLA Modules:
  0.0 50.0 jit_solution(12467957203810771438)
XLA Ops:
  0.0 3.0 %collective-permute-start = (f32[5,1,128,256]{3,2,1,0:T(8,128)}, f32[5,1,128,256]{3,2,1,0:T(8,128)S(1)}, u32[]{:S(2)}, u32[]{:S(2)}) collective-permute-start(f32[5,1,128,256]{3,2,1,0:T(8,128)} %fs_ref.1), channel_id=1, source_target_pairs={{0,1},{1,0},{2,3},{3,2},{4,5},{5,4},{6,7},{7,6},{8,9},{9,8},{10,11... | collective-permute-start | bytes 1966088 | tf_op jit(solution)/shard_map/ppermute | solution.py:319
  3.0 6.9 %shard_map.109 = (f32[5,1,128,256]{3,2,1,0:T(8,128)}, f32[5,1,128,256]{3,2,1,0:T(8,128)}, f32[5,1,128,256]{3,2,1,0:T(8,128)}, f32[5,1,6,256]{3,2,1,0:T(8,128)}) custom-call(f32[5,1,128,256]{3,2,1,0:T(8,128)} %fs_ref.1, f32[5,1,128,256]{3,2,1,0:T(8,128)} %src_ref.1, f32[1,128,256]{2,1,0:T(8,128)} %cell_ref.3, f32[5,256]{1,0:T(8,128)} %visc_ref.3, ...), custom_call_target="tpu_custom_call" | custom-call | tf_op jit(solution)/shard_map/pallas_call | solution.py:250
  9.9 8.0 %collective-permute-done.nb_ref = f32[5,1,128,256]{3,2,1,0:T(8,128)S(1)} collective-permute-done((f32[5,1,128,256]{3,2,1,0:T(8,128)}, f32[5,1,128,256]{3,2,1,0:T(8,128)S(1)}, u32[]{:S(2)}, u32[]{:S(2)}) %collective-permute-start) | collective-permute-done | bytes 655392 | tf_op jit(solution)/shard_map/ppermute | solution.py:319
  17.9 0.0 copy-start
  17.9 0.8 %copy-done = f32[5,1,128,256]{3,2,1,0:T(8,128)} copy-done((f32[5,1,128,256]{3,2,1,0:T(8,128)}, f32[5,1,128,256]{3,2,1,0:T(8,128)S(1)}, u32[]{:S(2)}) %copy-start) | copy-done | bytes 655384
  18.7 5.6 %shard_map.110 = (f32[5,1,128,256]{3,2,1,0:T(8,128)}, f32[5,1,3,2,256]{4,3,2,1,0:T(2,128)}) custom-call(f32[5,1,128,256]{3,2,1,0:T(8,128)} %copy-done, f32[1,128,256]{2,1,0:T(8,128)} %cell_ref.3, f32[5,256]{1,0:T(8,128)} %visc_ref.3, f32[5,256]{1,0:T(8,128)} %beta_ref.3, f32[5,256]{1,0:T(8,128)} %diff_ref.3, ...), custom_call_target="tpu_custom_call", output_to_operand_aliasing={{0}: (6, {})} | custom-call | tf_op jit(solution)/shard_map/pallas_call | solution.py:257
  24.3 0.1 collective-permute-start.3
  24.4 1.8 %collective-permute-start.2 = (f32[5,1,3,2,256]{4,3,2,1,0:T(2,128)}, f32[5,1,3,2,256]{4,3,2,1,0:T(2,128)S(1)}, u32[]{:S(2)}, u32[]{:S(2)}) collective-permute-start(f32[5,1,3,2,256]{4,3,2,1,0:T(2,128)} %get-tuple-element.20.refs_3_), channel_id=1, source_target_pairs={{16,0},{24,8},{0,16},{8,24},{17,1},{25,9},{1,17},{9,25},{18,2},{26... | collective-permute-start | bytes 92168 | tf_op jit(solution)/shard_map/ppermute | solution.py:312
  26.1 1.4 %collective-permute-start.1 = (f32[5,1,3,2,256]{4,3,2,1,0:T(2,128)}, f32[5,1,3,2,256]{4,3,2,1,0:T(2,128)S(1)}, u32[]{:S(2)}, u32[]{:S(2)}) collective-permute-start(f32[5,1,3,2,256]{4,3,2,1,0:T(2,128)} %get-tuple-element.20.refs_3_), channel_id=1, source_target_pairs={{8,0},{16,8},{24,16},{0,24},{9,1},{17,9},{25,17},{1,25},{10,2},{18... | collective-permute-start | bytes 92168 | tf_op jit(solution)/shard_map/ppermute | solution.py:312
  27.5 0.3 collective-permute-done.3.refs_6_
  27.9 0.0 copy-start.1
  27.9 0.7 %collective-permute-done.2.refs_5_ = f32[5,1,3,2,256]{4,3,2,1,0:T(2,128)S(1)} collective-permute-done((f32[5,1,3,2,256]{4,3,2,1,0:T(2,128)}, f32[5,1,3,2,256]{4,3,2,1,0:T(2,128)S(1)}, u32[]{:S(2)}, u32[]{:S(2)}) %collective-permute-start.2) | collective-permute-done | bytes 30752 | tf_op jit(solution)/shard_map/ppermute | solution.py:312
  28.5 0.0 copy-start.2
  28.5 0.8 %collective-permute-done.1.refs_4_ = f32[5,1,3,2,256]{4,3,2,1,0:T(2,128)S(1)} collective-permute-done((f32[5,1,3,2,256]{4,3,2,1,0:T(2,128)}, f32[5,1,3,2,256]{4,3,2,1,0:T(2,128)S(1)}, u32[]{:S(2)}, u32[]{:S(2)}) %collective-permute-start.1) | collective-permute-done | bytes 30752 | tf_op jit(solution)/shard_map/ppermute | solution.py:312
  29.3 0.0 copy-start.3
  29.3 0.0 copy-done.1
  29.3 0.0 copy-done.2
  29.3 0.6 %copy-done.3 = f32[5,1,3,2,256]{4,3,2,1,0:T(2,128)} copy-done((f32[5,1,3,2,256]{4,3,2,1,0:T(2,128)}, f32[5,1,3,2,256]{4,3,2,1,0:T(2,128)S(1)}, u32[]{:S(2)}) %copy-start.3) | copy-done | bytes 30744
  29.9 8.5 %shard_map.111 = (f32[5,1,256,128]{3,2,1,0:T(8,128)}, f32[5,1,256,128]{3,2,1,0:T(8,128)}, f32[5,1,256,128]{3,2,1,0:T(8,128)}, f32[5,1,3,2,128]{4,3,2,1,0:T(2,128)}) custom-call(f32[5,1,128,256]{3,2,1,0:T(8,128)} %get-tuple-element.17.refs_0_, f32[5,1,128,256]{3,2,1,0:T(8,128)} %get-tuple-element.18.refs_1_, f32[5,1,128,256]{3,2,1,0:T(8,128)} %get-tuple-element.19.refs_2_, ...), custom_call_target="tpu_custom_call" | custom-call | tf_op jit(solution)/shard_map/pallas_call | solution.py:280
  38.5 1.6 %collective-permute-start.6 = (f32[5,1,3,2,128]{4,3,2,1,0:T(2,128)}, f32[5,1,3,2,128]{4,3,2,1,0:T(2,128)S(1)}, u32[]{:S(2)}, u32[]{:S(2)}) collective-permute-start(f32[5,1,3,2,128]{4,3,2,1,0:T(2,128)} %get-tuple-element.24.refs_3_), channel_id=1, source_target_pairs={{6,0},{0,2},{2,4},{4,6},{7,1},{1,3},{3,5},{5,7},{14,8},{8,10},{10,... | collective-permute-start | bytes 46088 | tf_op jit(solution)/shard_map/ppermute | solution.py:312
  40.0 2.6 %collective-permute-start.5 = (f32[5,1,3,2,128]{4,3,2,1,0:T(2,128)}, f32[5,1,3,2,128]{4,3,2,1,0:T(2,128)S(1)}, u32[]{:S(2)}, u32[]{:S(2)}) collective-permute-start(f32[5,1,3,2,128]{4,3,2,1,0:T(2,128)} %get-tuple-element.24.refs_3_), channel_id=1, source_target_pairs={{4,0},{6,2},{0,4},{2,6},{5,1},{7,3},{1,5},{3,7},{12,8},{14,10},{8,... | collective-permute-start | bytes 46088 | tf_op jit(solution)/shard_map/ppermute | solution.py:312
  42.6 1.4 %collective-permute-start.4 = (f32[5,1,3,2,128]{4,3,2,1,0:T(2,128)}, f32[5,1,3,2,128]{4,3,2,1,0:T(2,128)S(1)}, u32[]{:S(2)}, u32[]{:S(2)}) collective-permute-start(f32[5,1,3,2,128]{4,3,2,1,0:T(2,128)} %get-tuple-element.24.refs_3_), channel_id=1, source_target_pairs={{2,0},{4,2},{6,4},{0,6},{3,1},{5,3},{7,5},{1,7},{10,8},{12,10},{14... | collective-permute-start | bytes 46088 | tf_op jit(solution)/shard_map/ppermute | solution.py:312
  44.0 0.2 collective-permute-done.6.refs_6_
  44.2 0.0 copy-start.4
  44.2 0.7 %collective-permute-done.5.refs_5_ = f32[5,1,3,2,128]{4,3,2,1,0:T(2,128)S(1)} collective-permute-done((f32[5,1,3,2,128]{4,3,2,1,0:T(2,128)}, f32[5,1,3,2,128]{4,3,2,1,0:T(2,128)S(1)}, u32[]{:S(2)}, u32[]{:S(2)}) %collective-permute-start.5) | collective-permute-done | bytes 15392 | tf_op jit(solution)/shard_map/ppermute | solution.py:312
  44.9 0.0 copy-start.5
  44.9 1.7 %collective-permute-done.4.refs_4_ = f32[5,1,3,2,128]{4,3,2,1,0:T(2,128)S(1)} collective-permute-done((f32[5,1,3,2,128]{4,3,2,1,0:T(2,128)}, f32[5,1,3,2,128]{4,3,2,1,0:T(2,128)S(1)}, u32[]{:S(2)}, u32[]{:S(2)}) %collective-permute-start.4) | collective-permute-done | bytes 15392 | tf_op jit(solution)/shard_map/ppermute | solution.py:312
  46.6 0.0 copy-start.6
  46.6 0.0 copy-done.4
  46.6 0.0 copy-done.5
  46.6 0.6 %copy-done.6 = f32[5,1,3,2,128]{4,3,2,1,0:T(2,128)} copy-done((f32[5,1,3,2,128]{4,3,2,1,0:T(2,128)}, f32[5,1,3,2,128]{4,3,2,1,0:T(2,128)S(1)}, u32[]{:S(2)}) %copy-start.6) | copy-done | bytes 15384
  47.2 2.8 %shard_map.112 = f32[5,1,128,256]{3,2,1,0:T(8,128)} custom-call(f32[5,1,256,128]{3,2,1,0:T(8,128)} %get-tuple-element.21.refs_0_, f32[5,1,256,128]{3,2,1,0:T(8,128)} %get-tuple-element.22.refs_1_, f32[5,1,256,128]{3,2,1,0:T(8,128)} %get-tuple-element.23.refs_2_, f32[5,1,3,2,128]{4,3,2,1,0:T(2,128)} %get-tuple-element.24.refs_3_, ...), custom_call_target="tpu_custom_call" | custom-call | tf_op jit(solution)/shard_map/pallas_call | solution.py:297
Async XLA Ops:
  0.0 17.9 %collective-permute-start = (f32[5,1,128,256]{3,2,1,0:T(8,128)}, f32[5,1,128,256]{3,2,1,0:T(8,128)S(1)}, u32[]{:S(2)}, u32[]{:S(2)}) collective-permute-start(f32[5,1,128,256]{3,2,1,0:T(8,128)} %fs_ref.1), channel_id=1, source_target_pairs={{0,1},{1,0},{2,3},{3,2},{4,5},{5,4},{6,7},{7,6},{8,9},{9,8},{10,11... | collective-permute-start | bytes 1966088 | tf_op jit(solution)/shard_map/ppermute | solution.py:319
  17.9 0.8 %copy-start = (f32[5,1,128,256]{3,2,1,0:T(8,128)}, f32[5,1,128,256]{3,2,1,0:T(8,128)S(1)}, u32[]{:S(2)}) copy-start(f32[5,1,128,256]{3,2,1,0:T(8,128)S(1)} %collective-permute-done.nb_ref) | copy-start | bytes 1966084
  24.3 3.6 %collective-permute-start.3 = (f32[5,1,3,2,256]{4,3,2,1,0:T(2,128)}, f32[5,1,3,2,256]{4,3,2,1,0:T(2,128)S(1)}, u32[]{:S(2)}, u32[]{:S(2)}) collective-permute-start(f32[5,1,3,2,256]{4,3,2,1,0:T(2,128)} %get-tuple-element.20.refs_3_), channel_id=1, source_target_pairs={{24,0},{0,8},{8,16},{16,24},{25,1},{1,9},{9,17},{17,25},{26,2},{2,... | collective-permute-start | bytes 92168 | tf_op jit(solution)/shard_map/ppermute | solution.py:312
  24.4 4.2 %collective-permute-start.2 = (f32[5,1,3,2,256]{4,3,2,1,0:T(2,128)}, f32[5,1,3,2,256]{4,3,2,1,0:T(2,128)S(1)}, u32[]{:S(2)}, u32[]{:S(2)}) collective-permute-start(f32[5,1,3,2,256]{4,3,2,1,0:T(2,128)} %get-tuple-element.20.refs_3_), channel_id=1, source_target_pairs={{16,0},{24,8},{0,16},{8,24},{17,1},{25,9},{1,17},{9,25},{18,2},{26... | collective-permute-start | bytes 92168 | tf_op jit(solution)/shard_map/ppermute | solution.py:312
  26.1 3.2 %collective-permute-start.1 = (f32[5,1,3,2,256]{4,3,2,1,0:T(2,128)}, f32[5,1,3,2,256]{4,3,2,1,0:T(2,128)S(1)}, u32[]{:S(2)}, u32[]{:S(2)}) collective-permute-start(f32[5,1,3,2,256]{4,3,2,1,0:T(2,128)} %get-tuple-element.20.refs_3_), channel_id=1, source_target_pairs={{8,0},{16,8},{24,16},{0,24},{9,1},{17,9},{25,17},{1,25},{10,2},{18... | collective-permute-start | bytes 92168 | tf_op jit(solution)/shard_map/ppermute | solution.py:312
  27.9 1.4 %copy-start.1 = (f32[5,1,3,2,256]{4,3,2,1,0:T(2,128)}, f32[5,1,3,2,256]{4,3,2,1,0:T(2,128)S(1)}, u32[]{:S(2)}) copy-start(f32[5,1,3,2,256]{4,3,2,1,0:T(2,128)S(1)} %collective-permute-done.3.refs_6_) | copy-start | bytes 92164
  28.5 0.8 %copy-start.2 = (f32[5,1,3,2,256]{4,3,2,1,0:T(2,128)}, f32[5,1,3,2,256]{4,3,2,1,0:T(2,128)S(1)}, u32[]{:S(2)}) copy-start(f32[5,1,3,2,256]{4,3,2,1,0:T(2,128)S(1)} %collective-permute-done.2.refs_5_) | copy-start | bytes 92164
  29.3 0.6 %copy-start.3 = (f32[5,1,3,2,256]{4,3,2,1,0:T(2,128)}, f32[5,1,3,2,256]{4,3,2,1,0:T(2,128)S(1)}, u32[]{:S(2)}) copy-start(f32[5,1,3,2,256]{4,3,2,1,0:T(2,128)S(1)} %collective-permute-done.1.refs_4_) | copy-start | bytes 92164
  38.5 5.7 %collective-permute-start.6 = (f32[5,1,3,2,128]{4,3,2,1,0:T(2,128)}, f32[5,1,3,2,128]{4,3,2,1,0:T(2,128)S(1)}, u32[]{:S(2)}, u32[]{:S(2)}) collective-permute-start(f32[5,1,3,2,128]{4,3,2,1,0:T(2,128)} %get-tuple-element.24.refs_3_), channel_id=1, source_target_pairs={{6,0},{0,2},{2,4},{4,6},{7,1},{1,3},{3,5},{5,7},{14,8},{8,10},{10,... | collective-permute-start | bytes 46088 | tf_op jit(solution)/shard_map/ppermute | solution.py:312
  40.0 4.9 %collective-permute-start.5 = (f32[5,1,3,2,128]{4,3,2,1,0:T(2,128)}, f32[5,1,3,2,128]{4,3,2,1,0:T(2,128)S(1)}, u32[]{:S(2)}, u32[]{:S(2)}) collective-permute-start(f32[5,1,3,2,128]{4,3,2,1,0:T(2,128)} %get-tuple-element.24.refs_3_), channel_id=1, source_target_pairs={{4,0},{6,2},{0,4},{2,6},{5,1},{7,3},{1,5},{3,7},{12,8},{14,10},{8,... | collective-permute-start | bytes 46088 | tf_op jit(solution)/shard_map/ppermute | solution.py:312
  42.6 3.9 %collective-permute-start.4 = (f32[5,1,3,2,128]{4,3,2,1,0:T(2,128)}, f32[5,1,3,2,128]{4,3,2,1,0:T(2,128)S(1)}, u32[]{:S(2)}, u32[]{:S(2)}) collective-permute-start(f32[5,1,3,2,128]{4,3,2,1,0:T(2,128)} %get-tuple-element.24.refs_3_), channel_id=1, source_target_pairs={{2,0},{4,2},{6,4},{0,6},{3,1},{5,3},{7,5},{1,7},{10,8},{12,10},{14... | collective-permute-start | bytes 46088 | tf_op jit(solution)/shard_map/ppermute | solution.py:312
  44.2 2.4 %copy-start.4 = (f32[5,1,3,2,128]{4,3,2,1,0:T(2,128)}, f32[5,1,3,2,128]{4,3,2,1,0:T(2,128)S(1)}, u32[]{:S(2)}) copy-start(f32[5,1,3,2,128]{4,3,2,1,0:T(2,128)S(1)} %collective-permute-done.6.refs_6_) | copy-start | bytes 46084
  44.9 1.7 %copy-start.5 = (f32[5,1,3,2,128]{4,3,2,1,0:T(2,128)}, f32[5,1,3,2,128]{4,3,2,1,0:T(2,128)S(1)}, u32[]{:S(2)}) copy-start(f32[5,1,3,2,128]{4,3,2,1,0:T(2,128)S(1)} %collective-permute-done.5.refs_5_) | copy-start | bytes 46084
  46.6 0.6 %copy-start.6 = (f32[5,1,3,2,128]{4,3,2,1,0:T(2,128)}, f32[5,1,3,2,128]{4,3,2,1,0:T(2,128)S(1)}, u32[]{:S(2)}) copy-start(f32[5,1,3,2,128]{4,3,2,1,0:T(2,128)S(1)} %collective-permute-done.4.refs_4_) | copy-start | bytes 46084

commit v10 on v9

--- a/solution.py
+++ b/solution.py
@@ -173,7 +173,7 @@
             edge_ref[v, 0, k : k + 1, :] = value
 
 
-def az_plane_kernel(nb_ref, cell_ref, visc_ref, beta_ref, diff_ref, mix_ref, it_in_ref, edge_ref, ot_ref, red_ref):
+def az_plane_kernel(nb_ref, cell_ref, visc_ref, beta_ref, diff_ref, mix_ref, it_in_ref, edge_ref, order_ref, ot_ref, red_ref):
     count = nb_ref.shape[0]
     explicit = [diff_ref[w : w + 1, :] * nb_ref[w, 0] for w in range(count)]
     section_one = mixed(mix_ref, explicit)
@@ -195,14 +195,43 @@
         store_rows(red_ref, v, rows)
 
 
+def rad_side(cell, visc, v):
+    coupling = visc[v : v + 1, :] * cell
+    centre = 1.0 + 2.0 * coupling
+    return -coupling / centre, centre
+
+
+def local_visc(visc_ref, axis_name, cells):
+    place = lax.axis_index(axis_name)
+    return visc_ref[:, pl.ds(pl.multiple_of(place * cells, cells), cells)]
+
+
+def rad_pre_kernel(cell_ref, visc_ref, oa_ref, ob_ref, edge_ref, *, axis_name):
+    count = oa_ref.shape[0]
+    cells = cell_ref.shape[2]
+    visc = local_visc(visc_ref, axis_name, cells)
+    cell = cell_ref[0]
+    for v in range(count):
+        side, _ = rad_side(cell, visc, v)
+        side = side.T
+        length = side.shape[0]
+        il, iu, _, a_init, b_init = interior(side, side)
+        ia, ib = pcr_levels(il, iu, [a_init, b_init])
+        oa_ref[v, 0] = ia
+        ob_ref[v, 0] = ib
+        n2 = length - 2
+        for k, value in enumerate((ia[1:2], ib[1:2], ia[n2 : n2 + 1], ib[n2 : n2 + 1])):
+            edge_ref[v, 0, k : k + 1, :] = value
+
+
 def rad_kernel(*refs, axis_name, devices, pieces):
     it_ref, ia_ref, ib_ref = refs[:3]
     red_in = refs[3 : 3 + pieces]
-    mix_ref, cell_ref, visc_ref, ot_ref, oa_ref, ob_ref, red_ref, rows_ref = refs[3 + pieces :]
+    mix_ref, cell_ref, visc_ref, edge_ref, ot_ref, red_ref, rows_ref = refs[3 + pieces :]
     count = it_ref.shape[0]
     cells = it_ref.shape[3]
     place = lax.axis_index(axis_name)
-    visc = visc_ref[:, pl.ds(pl.multiple_of(place * cells, cells), cells)]
+    visc = local_visc(visc_ref, axis_name, cells)
     solved = []
     for w in range(count):
         first, last = reduced_ends(red_in, rows_ref, w)
@@ -210,17 +239,22 @@
     section_three = mixed(mix_ref, solved)
     cell = cell_ref[0]
     for v in range(count):
-        coupling = visc[v : v + 1, :] * cell
-        centre = 1.0 + 2.0 * coupling
-        side = (-coupling / centre).T
-        it, ia, ib, rows = reduce_block(side, side, (section_three[v] / centre).T)
-        (lf, le), (uf, ue), trow = rows
+        side, centre = rad_side(cell, visc, v)
+        side = side.T
+        target = (section_three[v] / centre).T
+        length = side.shape[0]
+        il, iu, keep, _, _ = interior(side, side)
+        (it,) = pcr_levels(il, iu, [target * keep])
+        edge = edge_ref[v, 0]
+        n2 = length - 2
+        (lf, le), (uf, ue), trow = interface_rows(
+            side, side, target[0:1], target[length - 1 :], it[1:2], it[n2 : n2 + 1],
+            edge[0:1], edge[1:2], edge[2:3], edge[3:4],
+        )
         lf = jnp.where(place == 0, jnp.zeros_like(lf), lf)
         ue = jnp.where(place == devices - 1, jnp.zeros_like(ue), ue)
         store_rows(red_ref, v, ((lf, le), (uf, ue), trow))
         ot_ref[v, 0] = it
-        oa_ref[v, 0] = ia
-        ob_ref[v, 0] = ib
 
 
 def out_kernel(*refs, pieces):
@@ -236,7 +270,7 @@
         out_ref[v, 0] = value
 
 
-def az_sweep(flow_state, nb, source, cell_az, visc_az, beta_az, axial_diff, mix_in):
+def az_sweep(flow_state, nb, source, cell_az, visc_az, beta_az, axial_diff, mix_in, order):
     nv, nz, na, nr = flow_state.shape
     chunk = 128 if nr % 128 == 0 else nr
     grid = (nz, nr // chunk)
@@ -257,15 +291,31 @@
     it, red = pl.pallas_call(
         az_plane_kernel,
         grid=grid,
-        in_specs=[big, cell, par, par, par, mixs, big, edge],
+        in_specs=[big, cell, par, par, par, mixs, big, edge, pl.BlockSpec(memory_space=pl.ANY)],
         out_specs=[big, red],
         out_shape=[out, jax.ShapeDtypeStruct((nv, nz, 3, 2, nr), flow_state.dtype)],
         input_output_aliases={6: 0},
-    )(nb, cell_az, visc_az, beta_az, axial_diff, mix_in, it, edges)
+    )(nb, cell_az, visc_az, beta_az, axial_diff, mix_in, it, edges, order)
     return it, ia, ib, red
 
 
-def rad_sweep(it, ia, ib, red_in, mix_mid, cell_rad, visc_rad):
+def rad_pre(cell_rad, visc_rad, nv):
+    nz, na, nr = cell_rad.shape
+    big_t = pl.BlockSpec((nv, 1, nr, na), lambda z: (0, z, 0, 0))
+    cell = pl.BlockSpec((1, na, nr), lambda z: (z, 0, 0))
+    par = pl.BlockSpec(visc_rad.shape, lambda z: (0, 0))
+    edge = pl.BlockSpec((nv, 1, 4, na), lambda z: (0, z, 0, 0))
+    out = jax.ShapeDtypeStruct((nv, nz, nr, na), cell_rad.dtype)
+    return pl.pallas_call(
+        functools.partial(rad_pre_kernel, axis_name="rad"),
+        grid=(nz,),
+        in_specs=[cell, par],
+        out_specs=[big_t, big_t, edge],
+        out_shape=[out, out, jax.ShapeDtypeStruct((nv, nz, 4, na), cell_rad.dtype)],
+    )(cell_rad, visc_rad)
+
+
+def rad_sweep(it, ia, ib, red_in, mix_mid, cell_rad, visc_rad, edges):
     nv, nz, na, nr = it.shape
     big = pl.BlockSpec((nv, 1, na, nr), lambda z: (0, z, 0, 0))
     big_t = pl.BlockSpec((nv, 1, nr, na), lambda z: (0, z, 0, 0))
@@ -273,6 +323,7 @@
     mixs = pl.BlockSpec((nv, nv, nr), lambda z: (0, 0, 0))
     cell = pl.BlockSpec((1, na, nr), lambda z: (z, 0, 0))
     par = pl.BlockSpec(visc_rad.shape, lambda z: (0, 0))
+    edge = pl.BlockSpec((nv, 1, 4, na), lambda z: (0, z, 0, 0))
     red = pl.BlockSpec((nv, 1, 3, 2, na), lambda z: (0, z, 0, 0, 0))
     out = jax.ShapeDtypeStruct((nv, nz, nr, na), it.dtype)
     pieces = len(red_in)
@@ -280,11 +331,11 @@
     return pl.pallas_call(
         kernel,
         grid=(nz,),
-        in_specs=[big, big, big] + [red_in_spec] * pieces + [mixs, cell, par],
-        out_specs=[big_t, big_t, big_t, red],
-        out_shape=[out, out, out, jax.ShapeDtypeStruct((nv, nz, 3, 2, na), it.dtype)],
+        in_specs=[big, big, big] + [red_in_spec] * pieces + [mixs, cell, par, edge],
+        out_specs=[big_t, red],
+        out_shape=[out, jax.ShapeDtypeStruct((nv, nz, 3, 2, na), it.dtype)],
         scratch_shapes=[pltpu.VMEM((3, 2 * pieces, nr), it.dtype)],
-    )(it, ia, ib, *red_in, mix_mid, cell_rad, visc_rad)
+    )(it, ia, ib, *red_in, mix_mid, cell_rad, visc_rad, edges)
 
 
 def out_sweep(it, ia, ib, red_in, mix_out):
@@ -346,9 +397,11 @@
 ):
     rad_cells = flow_state.shape[3]
     nb = neighbour_planes(flow_state, "ax")
-    it, ia, ib, red = az_sweep(flow_state, nb, source, cell_az, visc_az, beta_az, axial_diff, mix_in)
+    rad_a, rad_b, rad_edges = rad_pre(cell_rad, visc_rad, flow_state.shape[0])
+    it, ia, ib, red = az_sweep(flow_state, nb, source, cell_az, visc_az, beta_az, axial_diff, mix_in, rad_edges)
     red = gathered(red, "az")
-    it, ia, ib, red = rad_sweep(it, ia, ib, red, mix_mid, cell_rad, visc_rad)
+    it, red = rad_sweep(it, ia, ib, red, mix_mid, cell_rad, visc_rad, rad_edges)
+    ia, ib = rad_a, rad_b
     red = gathered(red, "rad")
     return out_sweep(it, ia, ib, red, mix_out)
 

time: 50.2 us -> 48.2 us (0.960)
  waiting for transfers between devices: 12.4 us -> 6.24 us
  Pallas kernels: 23.8 us -> 28 us
    pallas_call x0 -> x1, Pallas kernels: none -> 6.14 us  [rad_pre(): pl.pallas_call(functools.partial(rad_pre_kernel, axis_name='rad'), grid=(...]
    ppermute x1, waiting for transfers between devices: 8.01 us -> 1.88 us  [neighbour_planes(): return lax.ppermute(block, axis_name, [(0, 1), (1, 0)])]
    pallas_call x1, Pallas kernels: 8.54 us -> 6.57 us  [rad_sweep(): pl.pallas_call(kernel, grid=(nz,), in_specs=[big, big, big] + [red_in_spe...]
  transfers between devices with their start and end apart: 7 -> 7, of which waited for: 7 -> 7; matrix products, arithmetic and copies ran while one was open for 0% -> 0% of each run, Pallas kernels for 14% -> 27%
where the time goes in v10:
time: 48.2 us; the launch traced here: 48 us
  Pallas kernels  28 us (58%)
  starting transfers between devices  11.7 us (24%)
  waiting for transfers between devices  6.24 us (13%)
  local copies, waits for them, and re-layouts  2.05 us (4%)
    ppermute x6, starting transfers between devices, gathered(): received.append(lax.ppermute(block, axis_name, pairs))  8.75 us
    pallas_call x1, Pallas kernels, az_sweep(): pl.pallas_call(az_local_kernel, grid=grid, in_specs=[big, big, cell, par,...  6.92 us
    pallas_call x1, Pallas kernels, rad_sweep(): pl.pallas_call(kernel, grid=(nz,), in_specs=[big, big, big] + [red_in_spe...  6.57 us
    pallas_call x1, Pallas kernels, rad_pre(): pl.pallas_call(functools.partial(rad_pre_kernel, axis_name='rad'), grid=(...  6.14 us
    pallas_call x1, Pallas kernels, az_sweep(): pl.pallas_call(az_plane_kernel, grid=grid, in_specs=[big, cell, par, par,...  5.55 us
    ppermute x6, waiting for transfers between devices, gathered(): received.append(lax.ppermute(block, axis_name, pairs))  4.36 us
    ppermute x1, starting transfers between devices, neighbour_planes(): return lax.ppermute(block, axis_name, [(0, 1), (1, 0)])  2.97 us
    pallas_call x1, Pallas kernels, out_sweep(): pl.pallas_call(functools.partial(out_kernel, pieces=pieces), grid=(nz,),...  2.79 us
  transfers between devices with their start and end apart: 7, of which 7 were waited for; matrix products, arithmetic and copies ran while one was open for 0% of the time, Pallas kernels for 27%

profile of v10, /device:TPU:0, one launch (start us, length us, event | category | flops | bytes accessed | tf_op | source)
XLA Modules:
  0.0 48.0 jit_solution(5597049061815095242)
XLA Ops:
  0.0 3.0 %collective-permute-start = (f32[5,1,128,256]{3,2,1,0:T(8,128)}, f32[5,1,128,256]{3,2,1,0:T(8,128)S(1)}, u32[]{:S(2)}, u32[]{:S(2)}) collective-permute-start(f32[5,1,128,256]{3,2,1,0:T(8,128)} %fs_ref.1), channel_id=1, source_target_pairs={{0,1},{1,0},{2,3},{3,2},{4,5},{5,4},{6,7},{7,6},{8,9},{9,8},{10,11... | collective-permute-start | bytes 1966088 | tf_op jit(solution)/shard_map/ppermute | solution.py:370
  3.0 6.1 %shard_map.110 = (f32[5,1,256,128]{3,2,1,0:T(8,128)}, f32[5,1,256,128]{3,2,1,0:T(8,128)}, f32[5,1,4,128]{3,2,1,0:T(4,128)}) custom-call(f32[1,128,256]{2,1,0:T(8,128)} %refs_8_.1, f32[5,1024]{1,0:T(8,128)} %refs_9_.1), custom_call_target="tpu_custom_call" | custom-call | tf_op jit(solution)/shard_map/pallas_call | solution.py:309
  9.1 6.9 %shard_map.109 = (f32[5,1,128,256]{3,2,1,0:T(8,128)}, f32[5,1,128,256]{3,2,1,0:T(8,128)}, f32[5,1,128,256]{3,2,1,0:T(8,128)}, f32[5,1,6,256]{3,2,1,0:T(8,128)}) custom-call(f32[5,1,128,256]{3,2,1,0:T(8,128)} %fs_ref.1, f32[5,1,128,256]{3,2,1,0:T(8,128)} %src_ref.1, f32[1,128,256]{2,1,0:T(8,128)} %cell_ref.5, f32[5,256]{1,0:T(8,128)} %visc_ref.5, ...), custom_call_target="tpu_custom_call" | custom-call | tf_op jit(solution)/shard_map/pallas_call | solution.py:284
  16.0 1.9 %collective-permute-done.nb_ref = f32[5,1,128,256]{3,2,1,0:T(8,128)S(1)} collective-permute-done((f32[5,1,128,256]{3,2,1,0:T(8,128)}, f32[5,1,128,256]{3,2,1,0:T(8,128)S(1)}, u32[]{:S(2)}, u32[]{:S(2)}) %collective-permute-start) | collective-permute-done | bytes 655392 | tf_op jit(solution)/shard_map/ppermute | solution.py:370
  17.9 0.0 copy-start
  17.9 0.8 %copy-done = f32[5,1,128,256]{3,2,1,0:T(8,128)} copy-done((f32[5,1,128,256]{3,2,1,0:T(8,128)}, f32[5,1,128,256]{3,2,1,0:T(8,128)S(1)}, u32[]{:S(2)}) %copy-start) | copy-done | bytes 655384
  18.7 5.6 %shard_map.111 = (f32[5,1,128,256]{3,2,1,0:T(8,128)}, f32[5,1,3,2,256]{4,3,2,1,0:T(2,128)}) custom-call(f32[5,1,128,256]{3,2,1,0:T(8,128)} %copy-done, f32[1,128,256]{2,1,0:T(8,128)} %cell_ref.5, f32[5,256]{1,0:T(8,128)} %visc_ref.5, f32[5,256]{1,0:T(8,128)} %beta_ref.3, f32[5,256]{1,0:T(8,128)} %diff_ref.3, ...), custom_call_target="tpu_custom_call", output_to_operand_aliasing={{0}: (6, {})} | custom-call | tf_op jit(solution)/shard_map/pallas_call | solution.py:291
  24.3 0.1 collective-permute-start.3
  24.4 1.8 %collective-permute-start.2 = (f32[5,1,3,2,256]{4,3,2,1,0:T(2,128)}, f32[5,1,3,2,256]{4,3,2,1,0:T(2,128)S(1)}, u32[]{:S(2)}, u32[]{:S(2)}) collective-permute-start(f32[5,1,3,2,256]{4,3,2,1,0:T(2,128)} %get-tuple-element.22.refs_3_), channel_id=1, source_target_pairs={{16,0},{24,8},{0,16},{8,24},{17,1},{25,9},{1,17},{9,25},{18,2},{26... | collective-permute-start | bytes 92168 | tf_op jit(solution)/shard_map/ppermute | solution.py:363
  26.1 1.4 %collective-permute-start.1 = (f32[5,1,3,2,256]{4,3,2,1,0:T(2,128)}, f32[5,1,3,2,256]{4,3,2,1,0:T(2,128)S(1)}, u32[]{:S(2)}, u32[]{:S(2)}) collective-permute-start(f32[5,1,3,2,256]{4,3,2,1,0:T(2,128)} %get-tuple-element.22.refs_3_), channel_id=1, source_target_pairs={{8,0},{16,8},{24,16},{0,24},{9,1},{17,9},{25,17},{1,25},{10,2},{18... | collective-permute-start | bytes 92168 | tf_op jit(solution)/shard_map/ppermute | solution.py:363
  27.5 0.3 collective-permute-done.3.refs_6_
  27.9 0.0 copy-start.1
  27.9 0.7 %collective-permute-done.2.refs_5_ = f32[5,1,3,2,256]{4,3,2,1,0:T(2,128)S(1)} collective-permute-done((f32[5,1,3,2,256]{4,3,2,1,0:T(2,128)}, f32[5,1,3,2,256]{4,3,2,1,0:T(2,128)S(1)}, u32[]{:S(2)}, u32[]{:S(2)}) %collective-permute-start.2) | collective-permute-done | bytes 30752 | tf_op jit(solution)/shard_map/ppermute | solution.py:363
  28.5 0.0 copy-start.2
  28.5 0.8 %collective-permute-done.1.refs_4_ = f32[5,1,3,2,256]{4,3,2,1,0:T(2,128)S(1)} collective-permute-done((f32[5,1,3,2,256]{4,3,2,1,0:T(2,128)}, f32[5,1,3,2,256]{4,3,2,1,0:T(2,128)S(1)}, u32[]{:S(2)}, u32[]{:S(2)}) %collective-permute-start.1) | collective-permute-done | bytes 30752 | tf_op jit(solution)/shard_map/ppermute | solution.py:363
  29.3 0.0 copy-start.3
  29.3 0.0 copy-done.1
  29.3 0.0 copy-done.2
  29.3 0.6 %copy-done.3 = f32[5,1,3,2,256]{4,3,2,1,0:T(2,128)} copy-done((f32[5,1,3,2,256]{4,3,2,1,0:T(2,128)}, f32[5,1,3,2,256]{4,3,2,1,0:T(2,128)S(1)}, u32[]{:S(2)}) %copy-start.3) | copy-done | bytes 30744
  29.9 6.6 %shard_map.112 = (f32[5,1,256,128]{3,2,1,0:T(8,128)}, f32[5,1,3,2,128]{4,3,2,1,0:T(2,128)}) custom-call(f32[5,1,128,256]{3,2,1,0:T(8,128)} %get-tuple-element.19.refs_0_, f32[5,1,128,256]{3,2,1,0:T(8,128)} %get-tuple-element.20.refs_1_, f32[5,1,128,256]{3,2,1,0:T(8,128)} %get-tuple-element.21.refs_2_, f32[5,1,3,2,256]{4,3,2,1,0:T(2,128)} %get-tuple-element.22.refs_3_, ...), custom_call_target="tpu_custom_call" | custom-call | tf_op jit(solution)/shard_map/pallas_call | solution.py:331
  36.5 1.6 %collective-permute-start.6 = (f32[5,1,3,2,128]{4,3,2,1,0:T(2,128)}, f32[5,1,3,2,128]{4,3,2,1,0:T(2,128)S(1)}, u32[]{:S(2)}, u32[]{:S(2)}) collective-permute-start(f32[5,1,3,2,128]{4,3,2,1,0:T(2,128)} %get-tuple-element.26.refs_3_), channel_id=1, source_target_pairs={{6,0},{0,2},{2,4},{4,6},{7,1},{1,3},{3,5},{5,7},{14,8},{8,10},{10,... | collective-permute-start | bytes 46088 | tf_op jit(solution)/shard_map/ppermute | solution.py:363
  38.1 2.6 %collective-permute-start.5 = (f32[5,1,3,2,128]{4,3,2,1,0:T(2,128)}, f32[5,1,3,2,128]{4,3,2,1,0:T(2,128)S(1)}, u32[]{:S(2)}, u32[]{:S(2)}) collective-permute-start(f32[5,1,3,2,128]{4,3,2,1,0:T(2,128)} %get-tuple-element.26.refs_3_), channel_id=1, source_target_pairs={{4,0},{6,2},{0,4},{2,6},{5,1},{7,3},{1,5},{3,7},{12,8},{14,10},{8,... | collective-permute-start | bytes 46088 | tf_op jit(solution)/shard_map/ppermute | solution.py:363
  40.7 1.4 %collective-permute-start.4 = (f32[5,1,3,2,128]{4,3,2,1,0:T(2,128)}, f32[5,1,3,2,128]{4,3,2,1,0:T(2,128)S(1)}, u32[]{:S(2)}, u32[]{:S(2)}) collective-permute-start(f32[5,1,3,2,128]{4,3,2,1,0:T(2,128)} %get-tuple-element.26.refs_3_), channel_id=1, source_target_pairs={{2,0},{4,2},{6,4},{0,6},{3,1},{5,3},{7,5},{1,7},{10,8},{12,10},{14... | collective-permute-start | bytes 46088 | tf_op jit(solution)/shard_map/ppermute | solution.py:363
  42.0 0.2 collective-permute-done.6.refs_6_
  42.2 0.0 copy-start.4
  42.2 0.7 %collective-permute-done.5.refs_5_ = f32[5,1,3,2,128]{4,3,2,1,0:T(2,128)S(1)} collective-permute-done((f32[5,1,3,2,128]{4,3,2,1,0:T(2,128)}, f32[5,1,3,2,128]{4,3,2,1,0:T(2,128)S(1)}, u32[]{:S(2)}, u32[]{:S(2)}) %collective-permute-start.5) | collective-permute-done | bytes 15392 | tf_op jit(solution)/shard_map/ppermute | solution.py:363
  42.9 0.0 copy-start.5
  42.9 1.7 %collective-permute-done.4.refs_4_ = f32[5,1,3,2,128]{4,3,2,1,0:T(2,128)S(1)} collective-permute-done((f32[5,1,3,2,128]{4,3,2,1,0:T(2,128)}, f32[5,1,3,2,128]{4,3,2,1,0:T(2,128)S(1)}, u32[]{:S(2)}, u32[]{:S(2)}) %collective-permute-start.4) | collective-permute-done | bytes 15392 | tf_op jit(solution)/shard_map/ppermute | solution.py:363
  44.6 0.0 copy-start.6
  44.6 0.0 copy-done.4
  44.6 0.0 copy-done.5
  44.6 0.6 %copy-done.6 = f32[5,1,3,2,128]{4,3,2,1,0:T(2,128)} copy-done((f32[5,1,3,2,128]{4,3,2,1,0:T(2,128)}, f32[5,1,3,2,128]{4,3,2,1,0:T(2,128)S(1)}, u32[]{:S(2)}) %copy-start.6) | copy-done | bytes 15384
  45.2 2.8 %shard_map.113 = f32[5,1,128,256]{3,2,1,0:T(8,128)} custom-call(f32[5,1,256,128]{3,2,1,0:T(8,128)} %get-tuple-element.23.refs_0_, f32[5,1,256,128]{3,2,1,0:T(8,128)} %get-tuple-element.24.refs_1_, f32[5,1,256,128]{3,2,1,0:T(8,128)} %get-tuple-element.25.refs_2_, f32[5,1,3,2,128]{4,3,2,1,0:T(2,128)} %get-tuple-element.26.refs_3_, ...), custom_call_target="tpu_custom_call" | custom-call | tf_op jit(solution)/shard_map/pallas_call | solution.py:348
Async XLA Ops:
  0.0 17.9 %collective-permute-start = (f32[5,1,128,256]{3,2,1,0:T(8,128)}, f32[5,1,128,256]{3,2,1,0:T(8,128)S(1)}, u32[]{:S(2)}, u32[]{:S(2)}) collective-permute-start(f32[5,1,128,256]{3,2,1,0:T(8,128)} %fs_ref.1), channel_id=1, source_target_pairs={{0,1},{1,0},{2,3},{3,2},{4,5},{5,4},{6,7},{7,6},{8,9},{9,8},{10,11... | collective-permute-start | bytes 1966088 | tf_op jit(solution)/shard_map/ppermute | solution.py:370
  17.9 0.8 %copy-start = (f32[5,1,128,256]{3,2,1,0:T(8,128)}, f32[5,1,128,256]{3,2,1,0:T(8,128)S(1)}, u32[]{:S(2)}) copy-start(f32[5,1,128,256]{3,2,1,0:T(8,128)S(1)} %collective-permute-done.nb_ref) | copy-start | bytes 1966084
  24.3 3.6 %collective-permute-start.3 = (f32[5,1,3,2,256]{4,3,2,1,0:T(2,128)}, f32[5,1,3,2,256]{4,3,2,1,0:T(2,128)S(1)}, u32[]{:S(2)}, u32[]{:S(2)}) collective-permute-start(f32[5,1,3,2,256]{4,3,2,1,0:T(2,128)} %get-tuple-element.22.refs_3_), channel_id=1, source_target_pairs={{24,0},{0,8},{8,16},{16,24},{25,1},{1,9},{9,17},{17,25},{26,2},{2,... | collective-permute-start | bytes 92168 | tf_op jit(solution)/shard_map/ppermute | solution.py:363
  24.4 4.2 %collective-permute-start.2 = (f32[5,1,3,2,256]{4,3,2,1,0:T(2,128)}, f32[5,1,3,2,256]{4,3,2,1,0:T(2,128)S(1)}, u32[]{:S(2)}, u32[]{:S(2)}) collective-permute-start(f32[5,1,3,2,256]{4,3,2,1,0:T(2,128)} %get-tuple-element.22.refs_3_), channel_id=1, source_target_pairs={{16,0},{24,8},{0,16},{8,24},{17,1},{25,9},{1,17},{9,25},{18,2},{26... | collective-permute-start | bytes 92168 | tf_op jit(solution)/shard_map/ppermute | solution.py:363
  26.1 3.2 %collective-permute-start.1 = (f32[5,1,3,2,256]{4,3,2,1,0:T(2,128)}, f32[5,1,3,2,256]{4,3,2,1,0:T(2,128)S(1)}, u32[]{:S(2)}, u32[]{:S(2)}) collective-permute-start(f32[5,1,3,2,256]{4,3,2,1,0:T(2,128)} %get-tuple-element.22.refs_3_), channel_id=1, source_target_pairs={{8,0},{16,8},{24,16},{0,24},{9,1},{17,9},{25,17},{1,25},{10,2},{18... | collective-permute-start | bytes 92168 | tf_op jit(solution)/shard_map/ppermute | solution.py:363
  27.9 1.4 %copy-start.1 = (f32[5,1,3,2,256]{4,3,2,1,0:T(2,128)}, f32[5,1,3,2,256]{4,3,2,1,0:T(2,128)S(1)}, u32[]{:S(2)}) copy-start(f32[5,1,3,2,256]{4,3,2,1,0:T(2,128)S(1)} %collective-permute-done.3.refs_6_) | copy-start | bytes 92164
  28.5 0.8 %copy-start.2 = (f32[5,1,3,2,256]{4,3,2,1,0:T(2,128)}, f32[5,1,3,2,256]{4,3,2,1,0:T(2,128)S(1)}, u32[]{:S(2)}) copy-start(f32[5,1,3,2,256]{4,3,2,1,0:T(2,128)S(1)} %collective-permute-done.2.refs_5_) | copy-start | bytes 92164
  29.3 0.6 %copy-start.3 = (f32[5,1,3,2,256]{4,3,2,1,0:T(2,128)}, f32[5,1,3,2,256]{4,3,2,1,0:T(2,128)S(1)}, u32[]{:S(2)}) copy-start(f32[5,1,3,2,256]{4,3,2,1,0:T(2,128)S(1)} %collective-permute-done.1.refs_4_) | copy-start | bytes 92164
  36.5 5.7 %collective-permute-start.6 = (f32[5,1,3,2,128]{4,3,2,1,0:T(2,128)}, f32[5,1,3,2,128]{4,3,2,1,0:T(2,128)S(1)}, u32[]{:S(2)}, u32[]{:S(2)}) collective-permute-start(f32[5,1,3,2,128]{4,3,2,1,0:T(2,128)} %get-tuple-element.26.refs_3_), channel_id=1, source_target_pairs={{6,0},{0,2},{2,4},{4,6},{7,1},{1,3},{3,5},{5,7},{14,8},{8,10},{10,... | collective-permute-start | bytes 46088 | tf_op jit(solution)/shard_map/ppermute | solution.py:363
  38.1 4.9 %collective-permute-start.5 = (f32[5,1,3,2,128]{4,3,2,1,0:T(2,128)}, f32[5,1,3,2,128]{4,3,2,1,0:T(2,128)S(1)}, u32[]{:S(2)}, u32[]{:S(2)}) collective-permute-start(f32[5,1,3,2,128]{4,3,2,1,0:T(2,128)} %get-tuple-element.26.refs_3_), channel_id=1, source_target_pairs={{4,0},{6,2},{0,4},{2,6},{5,1},{7,3},{1,5},{3,7},{12,8},{14,10},{8,... | collective-permute-start | bytes 46088 | tf_op jit(solution)/shard_map/ppermute | solution.py:363
  40.7 3.9 %collective-permute-start.4 = (f32[5,1,3,2,128]{4,3,2,1,0:T(2,128)}, f32[5,1,3,2,128]{4,3,2,1,0:T(2,128)S(1)}, u32[]{:S(2)}, u32[]{:S(2)}) collective-permute-start(f32[5,1,3,2,128]{4,3,2,1,0:T(2,128)} %get-tuple-element.26.refs_3_), channel_id=1, source_target_pairs={{2,0},{4,2},{6,4},{0,6},{3,1},{5,3},{7,5},{1,7},{10,8},{12,10},{14... | collective-permute-start | bytes 46088 | tf_op jit(solution)/shard_map/ppermute | solution.py:363
  42.2 2.4 %copy-start.4 = (f32[5,1,3,2,128]{4,3,2,1,0:T(2,128)}, f32[5,1,3,2,128]{4,3,2,1,0:T(2,128)S(1)}, u32[]{:S(2)}) copy-start(f32[5,1,3,2,128]{4,3,2,1,0:T(2,128)S(1)} %collective-permute-done.6.refs_6_) | copy-start | bytes 46084
  42.9 1.7 %copy-start.5 = (f32[5,1,3,2,128]{4,3,2,1,0:T(2,128)}, f32[5,1,3,2,128]{4,3,2,1,0:T(2,128)S(1)}, u32[]{:S(2)}) copy-start(f32[5,1,3,2,128]{4,3,2,1,0:T(2,128)S(1)} %collective-permute-done.5.refs_5_) | copy-start | bytes 46084
  44.6 0.6 %copy-start.6 = (f32[5,1,3,2,128]{4,3,2,1,0:T(2,128)}, f32[5,1,3,2,128]{4,3,2,1,0:T(2,128)S(1)}, u32[]{:S(2)}) copy-start(f32[5,1,3,2,128]{4,3,2,1,0:T(2,128)S(1)} %collective-permute-done.4.refs_4_) | copy-start | bytes 46084

commit v11 on v10

--- a/solution.py
+++ b/solution.py
@@ -72,7 +72,8 @@
         lr, ur = pltpu.roll(il, back, 0), pltpu.roll(iu, back, 0)
         inv = 1.0 / (1.0 - il * ul - iu * lr)
         rhs = [(r - il * pltpu.roll(r, stride, 0) - iu * pltpu.roll(r, back, 0)) * inv for r in rhs]
-        il, iu = -il * ll * inv, -iu * ur * inv
+        flip = -inv
+        il, iu = il * ll * flip, iu * ur * flip
         stride = stride * 2
     return rhs
 
@@ -145,11 +146,11 @@
 
 def az_coefficients(cell, visc_ref, beta_ref, v):
     coupling = visc_ref[v : v + 1, :] * cell
-    centre = 1.0 + 2.0 * coupling
+    scale = -1.0 / (1.0 + 2.0 * coupling)
     tilt = beta_ref[v : v + 1, :]
-    lower = -coupling * (1.0 + tilt) / centre
-    upper = -coupling * (1.0 - tilt) / centre
-    return lower, upper, centre
+    lower = coupling * (1.0 + tilt) * scale
+    upper = coupling * (1.0 - tilt) * scale
+    return lower, upper, scale
 
 
 def az_local_kernel(fs_ref, src_ref, cell_ref, visc_ref, beta_ref, diff_ref, mix_ref, ot_ref, oa_ref, ob_ref, edge_ref):
@@ -158,8 +159,8 @@
     section_one = mixed(mix_ref, explicit)
     cell = cell_ref[0]
     for v in range(count):
-        lower, upper, centre = az_coefficients(cell, visc_ref, beta_ref, v)
-        target = section_one[v] / centre
+        lower, upper, scale = az_coefficients(cell, visc_ref, beta_ref, v)
+        target = section_one[v] * -scale
         length = lower.shape[0]
         il, iu, keep, a_init, b_init = interior(lower, upper)
         it, ia, ib = pcr_levels(il, iu, [target * keep, a_init, b_init])
@@ -179,8 +180,8 @@
     section_one = mixed(mix_ref, explicit)
     cell = cell_ref[0]
     for v in range(count):
-        lower, upper, centre = az_coefficients(cell, visc_ref, beta_ref, v)
-        target = section_one[v] / centre
+        lower, upper, scale = az_coefficients(cell, visc_ref, beta_ref, v)
+        target = section_one[v] * -scale
         length = lower.shape[0]
         il, iu, keep, _, _ = interior(lower, upper)
         (it,) = pcr_levels(il, iu, [target * keep])
@@ -197,8 +198,8 @@
 
 def rad_side(cell, visc, v):
     coupling = visc[v : v + 1, :] * cell
-    centre = 1.0 + 2.0 * coupling
-    return -coupling / centre, centre
+    scale = 1.0 / (1.0 + 2.0 * coupling)
+    return -coupling * scale, scale
 
 
 def local_visc(visc_ref, axis_name, cells):
@@ -239,9 +240,9 @@
     section_three = mixed(mix_ref, solved)
     cell = cell_ref[0]
     for v in range(count):
-        side, centre = rad_side(cell, visc, v)
+        side, scale = rad_side(cell, visc, v)
         side = side.T
-        target = (section_three[v] / centre).T
+        target = (section_three[v] * scale).T
         length = side.shape[0]
         il, iu, keep, _, _ = interior(side, side)
         (it,) = pcr_levels(il, iu, [target * keep])

time: 48.2 us -> 48 us (level)
  no operation moved by 1% of the time
where the time goes in v11:
time: 48 us; the launch traced here: 47.8 us
  Pallas kernels  27.6 us (58%)
  starting transfers between devices  11.7 us (24%)
  waiting for transfers between devices  6.41 us (13%)
  local copies, waits for them, and re-layouts  2.05 us (4%)
    ppermute x6, starting transfers between devices, gathered(): received.append(lax.ppermute(block, axis_name, pairs))  8.75 us
    pallas_call x1, Pallas kernels, az_sweep(): pl.pallas_call(az_local_kernel, grid=grid, in_specs=[big, big, cell, par,...  6.86 us
    pallas_call x1, Pallas kernels, rad_sweep(): pl.pallas_call(kernel, grid=(nz,), in_specs=[big, big, big] + [red_in_spe...  6.43 us
    pallas_call x1, Pallas kernels, rad_pre(): pl.pallas_call(functools.partial(rad_pre_kernel, axis_name='rad'), grid=(...  6.04 us
    pallas_call x1, Pallas kernels, az_sweep(): pl.pallas_call(az_plane_kernel, grid=grid, in_specs=[big, cell, par, par,...  5.45 us
    ppermute x6, waiting for transfers between devices, gathered(): received.append(lax.ppermute(block, axis_name, pairs))  4.37 us
    ppermute x1, starting transfers between devices, neighbour_planes(): return lax.ppermute(block, axis_name, [(0, 1), (1, 0)])  2.97 us
    pallas_call x1, Pallas kernels, out_sweep(): pl.pallas_call(functools.partial(out_kernel, pieces=pieces), grid=(nz,),...  2.79 us
  transfers between devices with their start and end apart: 7, of which 7 were waited for; matrix products, arithmetic and copies ran while one was open for 0% of the time, Pallas kernels for 27%

profile of v11, /device:TPU:0, one launch (start us, length us, event | category | flops | bytes accessed | tf_op | source)
XLA Modules:
  0.0 47.8 jit_solution(2413520852993956342)
XLA Ops:
  0.0 3.0 %collective-permute-start = (f32[5,1,128,256]{3,2,1,0:T(8,128)}, f32[5,1,128,256]{3,2,1,0:T(8,128)S(1)}, u32[]{:S(2)}, u32[]{:S(2)}) collective-permute-start(f32[5,1,128,256]{3,2,1,0:T(8,128)} %fs_ref.1), channel_id=1, source_target_pairs={{0,1},{1,0},{2,3},{3,2},{4,5},{5,4},{6,7},{7,6},{8,9},{9,8},{10,11... | collective-permute-start | bytes 1966088 | tf_op jit(solution)/shard_map/ppermute | solution.py:371
  3.0 6.0 %shard_map.110 = (f32[5,1,256,128]{3,2,1,0:T(8,128)}, f32[5,1,256,128]{3,2,1,0:T(8,128)}, f32[5,1,4,128]{3,2,1,0:T(4,128)}) custom-call(f32[1,128,256]{2,1,0:T(8,128)} %refs_8_.1, f32[5,1024]{1,0:T(8,128)} %refs_9_.1), custom_call_target="tpu_custom_call" | custom-call | tf_op jit(solution)/shard_map/pallas_call | solution.py:310
  9.0 6.9 %shard_map.109 = (f32[5,1,128,256]{3,2,1,0:T(8,128)}, f32[5,1,128,256]{3,2,1,0:T(8,128)}, f32[5,1,128,256]{3,2,1,0:T(8,128)}, f32[5,1,6,256]{3,2,1,0:T(8,128)}) custom-call(f32[5,1,128,256]{3,2,1,0:T(8,128)} %fs_ref.1, f32[5,1,128,256]{3,2,1,0:T(8,128)} %src_ref.1, f32[1,128,256]{2,1,0:T(8,128)} %cell_ref.5, f32[5,256]{1,0:T(8,128)} %visc_ref.5, ...), custom_call_target="tpu_custom_call" | custom-call | tf_op jit(solution)/shard_map/pallas_call | solution.py:285
  15.9 2.0 %collective-permute-done.nb_ref = f32[5,1,128,256]{3,2,1,0:T(8,128)S(1)} collective-permute-done((f32[5,1,128,256]{3,2,1,0:T(8,128)}, f32[5,1,128,256]{3,2,1,0:T(8,128)S(1)}, u32[]{:S(2)}, u32[]{:S(2)}) %collective-permute-start) | collective-permute-done | bytes 655392 | tf_op jit(solution)/shard_map/ppermute | solution.py:371
  17.9 0.0 copy-start
  17.9 0.8 %copy-done = f32[5,1,128,256]{3,2,1,0:T(8,128)} copy-done((f32[5,1,128,256]{3,2,1,0:T(8,128)}, f32[5,1,128,256]{3,2,1,0:T(8,128)S(1)}, u32[]{:S(2)}) %copy-start) | copy-done | bytes 655384
  18.7 5.5 %shard_map.111 = (f32[5,1,128,256]{3,2,1,0:T(8,128)}, f32[5,1,3,2,256]{4,3,2,1,0:T(2,128)}) custom-call(f32[5,1,128,256]{3,2,1,0:T(8,128)} %copy-done, f32[1,128,256]{2,1,0:T(8,128)} %cell_ref.5, f32[5,256]{1,0:T(8,128)} %visc_ref.5, f32[5,256]{1,0:T(8,128)} %beta_ref.3, f32[5,256]{1,0:T(8,128)} %diff_ref.3, ...), custom_call_target="tpu_custom_call", output_to_operand_aliasing={{0}: (6, {})} | custom-call | tf_op jit(solution)/shard_map/pallas_call | solution.py:292
  24.2 0.1 collective-permute-start.3
  24.3 1.8 %collective-permute-start.2 = (f32[5,1,3,2,256]{4,3,2,1,0:T(2,128)}, f32[5,1,3,2,256]{4,3,2,1,0:T(2,128)S(1)}, u32[]{:S(2)}, u32[]{:S(2)}) collective-permute-start(f32[5,1,3,2,256]{4,3,2,1,0:T(2,128)} %get-tuple-element.22.refs_3_), channel_id=1, source_target_pairs={{16,0},{24,8},{0,16},{8,24},{17,1},{25,9},{1,17},{9,25},{18,2},{26... | collective-permute-start | bytes 92168 | tf_op jit(solution)/shard_map/ppermute | solution.py:364
  26.0 1.4 %collective-permute-start.1 = (f32[5,1,3,2,256]{4,3,2,1,0:T(2,128)}, f32[5,1,3,2,256]{4,3,2,1,0:T(2,128)S(1)}, u32[]{:S(2)}, u32[]{:S(2)}) collective-permute-start(f32[5,1,3,2,256]{4,3,2,1,0:T(2,128)} %get-tuple-element.22.refs_3_), channel_id=1, source_target_pairs={{8,0},{16,8},{24,16},{0,24},{9,1},{17,9},{25,17},{1,25},{10,2},{18... | collective-permute-start | bytes 92168 | tf_op jit(solution)/shard_map/ppermute | solution.py:364
  27.4 0.3 collective-permute-done.3.refs_6_
  27.8 0.0 copy-start.1
  27.8 0.7 %collective-permute-done.2.refs_5_ = f32[5,1,3,2,256]{4,3,2,1,0:T(2,128)S(1)} collective-permute-done((f32[5,1,3,2,256]{4,3,2,1,0:T(2,128)}, f32[5,1,3,2,256]{4,3,2,1,0:T(2,128)S(1)}, u32[]{:S(2)}, u32[]{:S(2)}) %collective-permute-start.2) | collective-permute-done | bytes 30752 | tf_op jit(solution)/shard_map/ppermute | solution.py:364
  28.4 0.0 copy-start.2
  28.4 0.8 %collective-permute-done.1.refs_4_ = f32[5,1,3,2,256]{4,3,2,1,0:T(2,128)S(1)} collective-permute-done((f32[5,1,3,2,256]{4,3,2,1,0:T(2,128)}, f32[5,1,3,2,256]{4,3,2,1,0:T(2,128)S(1)}, u32[]{:S(2)}, u32[]{:S(2)}) %collective-permute-start.1) | collective-permute-done | bytes 30752 | tf_op jit(solution)/shard_map/ppermute | solution.py:364
  29.2 0.0 copy-start.3
  29.2 0.0 copy-done.1
  29.2 0.0 copy-done.2
  29.2 0.6 %copy-done.3 = f32[5,1,3,2,256]{4,3,2,1,0:T(2,128)} copy-done((f32[5,1,3,2,256]{4,3,2,1,0:T(2,128)}, f32[5,1,3,2,256]{4,3,2,1,0:T(2,128)S(1)}, u32[]{:S(2)}) %copy-start.3) | copy-done | bytes 30744
  29.8 6.4 %shard_map.112 = (f32[5,1,256,128]{3,2,1,0:T(8,128)}, f32[5,1,3,2,128]{4,3,2,1,0:T(2,128)}) custom-call(f32[5,1,128,256]{3,2,1,0:T(8,128)} %get-tuple-element.19.refs_0_, f32[5,1,128,256]{3,2,1,0:T(8,128)} %get-tuple-element.20.refs_1_, f32[5,1,128,256]{3,2,1,0:T(8,128)} %get-tuple-element.21.refs_2_, f32[5,1,3,2,256]{4,3,2,1,0:T(2,128)} %get-tuple-element.22.refs_3_, ...), custom_call_target="tpu_custom_call" | custom-call | tf_op jit(solution)/shard_map/pallas_call | solution.py:332
  36.3 1.6 %collective-permute-start.6 = (f32[5,1,3,2,128]{4,3,2,1,0:T(2,128)}, f32[5,1,3,2,128]{4,3,2,1,0:T(2,128)S(1)}, u32[]{:S(2)}, u32[]{:S(2)}) collective-permute-start(f32[5,1,3,2,128]{4,3,2,1,0:T(2,128)} %get-tuple-element.26.refs_3_), channel_id=1, source_target_pairs={{6,0},{0,2},{2,4},{4,6},{7,1},{1,3},{3,5},{5,7},{14,8},{8,10},{10,... | collective-permute-start | bytes 46088 | tf_op jit(solution)/shard_map/ppermute | solution.py:364
  37.8 2.6 %collective-permute-start.5 = (f32[5,1,3,2,128]{4,3,2,1,0:T(2,128)}, f32[5,1,3,2,128]{4,3,2,1,0:T(2,128)S(1)}, u32[]{:S(2)}, u32[]{:S(2)}) collective-permute-start(f32[5,1,3,2,128]{4,3,2,1,0:T(2,128)} %get-tuple-element.26.refs_3_), channel_id=1, source_target_pairs={{4,0},{6,2},{0,4},{2,6},{5,1},{7,3},{1,5},{3,7},{12,8},{14,10},{8,... | collective-permute-start | bytes 46088 | tf_op jit(solution)/shard_map/ppermute | solution.py:364
  40.4 1.4 %collective-permute-start.4 = (f32[5,1,3,2,128]{4,3,2,1,0:T(2,128)}, f32[5,1,3,2,128]{4,3,2,1,0:T(2,128)S(1)}, u32[]{:S(2)}, u32[]{:S(2)}) collective-permute-start(f32[5,1,3,2,128]{4,3,2,1,0:T(2,128)} %get-tuple-element.26.refs_3_), channel_id=1, source_target_pairs={{2,0},{4,2},{6,4},{0,6},{3,1},{5,3},{7,5},{1,7},{10,8},{12,10},{14... | collective-permute-start | bytes 46088 | tf_op jit(solution)/shard_map/ppermute | solution.py:364
  41.8 0.2 collective-permute-done.6.refs_6_
  42.0 0.0 copy-start.4
  42.0 0.7 %collective-permute-done.5.refs_5_ = f32[5,1,3,2,128]{4,3,2,1,0:T(2,128)S(1)} collective-permute-done((f32[5,1,3,2,128]{4,3,2,1,0:T(2,128)}, f32[5,1,3,2,128]{4,3,2,1,0:T(2,128)S(1)}, u32[]{:S(2)}, u32[]{:S(2)}) %collective-permute-start.5) | collective-permute-done | bytes 15392 | tf_op jit(solution)/shard_map/ppermute | solution.py:364
  42.7 0.0 copy-start.5
  42.7 1.7 %collective-permute-done.4.refs_4_ = f32[5,1,3,2,128]{4,3,2,1,0:T(2,128)S(1)} collective-permute-done((f32[5,1,3,2,128]{4,3,2,1,0:T(2,128)}, f32[5,1,3,2,128]{4,3,2,1,0:T(2,128)S(1)}, u32[]{:S(2)}, u32[]{:S(2)}) %collective-permute-start.4) | collective-permute-done | bytes 15392 | tf_op jit(solution)/shard_map/ppermute | solution.py:364
  44.4 0.0 copy-start.6
  44.4 0.0 copy-done.4
  44.4 0.0 copy-done.5
  44.4 0.6 %copy-done.6 = f32[5,1,3,2,128]{4,3,2,1,0:T(2,128)} copy-done((f32[5,1,3,2,128]{4,3,2,1,0:T(2,128)}, f32[5,1,3,2,128]{4,3,2,1,0:T(2,128)S(1)}, u32[]{:S(2)}) %copy-start.6) | copy-done | bytes 15384
  45.0 2.8 %shard_map.113 = f32[5,1,128,256]{3,2,1,0:T(8,128)} custom-call(f32[5,1,256,128]{3,2,1,0:T(8,128)} %get-tuple-element.23.refs_0_, f32[5,1,256,128]{3,2,1,0:T(8,128)} %get-tuple-element.24.refs_1_, f32[5,1,256,128]{3,2,1,0:T(8,128)} %get-tuple-element.25.refs_2_, f32[5,1,3,2,128]{4,3,2,1,0:T(2,128)} %get-tuple-element.26.refs_3_, ...), custom_call_target="tpu_custom_call" | custom-call | tf_op jit(solution)/shard_map/pallas_call | solution.py:349
Async XLA Ops:
  0.0 17.9 %collective-permute-start = (f32[5,1,128,256]{3,2,1,0:T(8,128)}, f32[5,1,128,256]{3,2,1,0:T(8,128)S(1)}, u32[]{:S(2)}, u32[]{:S(2)}) collective-permute-start(f32[5,1,128,256]{3,2,1,0:T(8,128)} %fs_ref.1), channel_id=1, source_target_pairs={{0,1},{1,0},{2,3},{3,2},{4,5},{5,4},{6,7},{7,6},{8,9},{9,8},{10,11... | collective-permute-start | bytes 1966088 | tf_op jit(solution)/shard_map/ppermute | solution.py:371
  17.9 0.8 %copy-start = (f32[5,1,128,256]{3,2,1,0:T(8,128)}, f32[5,1,128,256]{3,2,1,0:T(8,128)S(1)}, u32[]{:S(2)}) copy-start(f32[5,1,128,256]{3,2,1,0:T(8,128)S(1)} %collective-permute-done.nb_ref) | copy-start | bytes 1966084
  24.2 3.6 %collective-permute-start.3 = (f32[5,1,3,2,256]{4,3,2,1,0:T(2,128)}, f32[5,1,3,2,256]{4,3,2,1,0:T(2,128)S(1)}, u32[]{:S(2)}, u32[]{:S(2)}) collective-permute-start(f32[5,1,3,2,256]{4,3,2,1,0:T(2,128)} %get-tuple-element.22.refs_3_), channel_id=1, source_target_pairs={{24,0},{0,8},{8,16},{16,24},{25,1},{1,9},{9,17},{17,25},{26,2},{2,... | collective-permute-start | bytes 92168 | tf_op jit(solution)/shard_map/ppermute | solution.py:364
  24.3 4.2 %collective-permute-start.2 = (f32[5,1,3,2,256]{4,3,2,1,0:T(2,128)}, f32[5,1,3,2,256]{4,3,2,1,0:T(2,128)S(1)}, u32[]{:S(2)}, u32[]{:S(2)}) collective-permute-start(f32[5,1,3,2,256]{4,3,2,1,0:T(2,128)} %get-tuple-element.22.refs_3_), channel_id=1, source_target_pairs={{16,0},{24,8},{0,16},{8,24},{17,1},{25,9},{1,17},{9,25},{18,2},{26... | collective-permute-start | bytes 92168 | tf_op jit(solution)/shard_map/ppermute | solution.py:364
  26.0 3.2 %collective-permute-start.1 = (f32[5,1,3,2,256]{4,3,2,1,0:T(2,128)}, f32[5,1,3,2,256]{4,3,2,1,0:T(2,128)S(1)}, u32[]{:S(2)}, u32[]{:S(2)}) collective-permute-start(f32[5,1,3,2,256]{4,3,2,1,0:T(2,128)} %get-tuple-element.22.refs_3_), channel_id=1, source_target_pairs={{8,0},{16,8},{24,16},{0,24},{9,1},{17,9},{25,17},{1,25},{10,2},{18... | collective-permute-start | bytes 92168 | tf_op jit(solution)/shard_map/ppermute | solution.py:364
  27.8 1.4 %copy-start.1 = (f32[5,1,3,2,256]{4,3,2,1,0:T(2,128)}, f32[5,1,3,2,256]{4,3,2,1,0:T(2,128)S(1)}, u32[]{:S(2)}) copy-start(f32[5,1,3,2,256]{4,3,2,1,0:T(2,128)S(1)} %collective-permute-done.3.refs_6_) | copy-start | bytes 92164
  28.4 0.8 %copy-start.2 = (f32[5,1,3,2,256]{4,3,2,1,0:T(2,128)}, f32[5,1,3,2,256]{4,3,2,1,0:T(2,128)S(1)}, u32[]{:S(2)}) copy-start(f32[5,1,3,2,256]{4,3,2,1,0:T(2,128)S(1)} %collective-permute-done.2.refs_5_) | copy-start | bytes 92164
  29.2 0.6 %copy-start.3 = (f32[5,1,3,2,256]{4,3,2,1,0:T(2,128)}, f32[5,1,3,2,256]{4,3,2,1,0:T(2,128)S(1)}, u32[]{:S(2)}) copy-start(f32[5,1,3,2,256]{4,3,2,1,0:T(2,128)S(1)} %collective-permute-done.1.refs_4_) | copy-start | bytes 92164
  36.3 5.7 %collective-permute-start.6 = (f32[5,1,3,2,128]{4,3,2,1,0:T(2,128)}, f32[5,1,3,2,128]{4,3,2,1,0:T(2,128)S(1)}, u32[]{:S(2)}, u32[]{:S(2)}) collective-permute-start(f32[5,1,3,2,128]{4,3,2,1,0:T(2,128)} %get-tuple-element.26.refs_3_), channel_id=1, source_target_pairs={{6,0},{0,2},{2,4},{4,6},{7,1},{1,3},{3,5},{5,7},{14,8},{8,10},{10,... | collective-permute-start | bytes 46088 | tf_op jit(solution)/shard_map/ppermute | solution.py:364
  37.8 4.9 %collective-permute-start.5 = (f32[5,1,3,2,128]{4,3,2,1,0:T(2,128)}, f32[5,1,3,2,128]{4,3,2,1,0:T(2,128)S(1)}, u32[]{:S(2)}, u32[]{:S(2)}) collective-permute-start(f32[5,1,3,2,128]{4,3,2,1,0:T(2,128)} %get-tuple-element.26.refs_3_), channel_id=1, source_target_pairs={{4,0},{6,2},{0,4},{2,6},{5,1},{7,3},{1,5},{3,7},{12,8},{14,10},{8,... | collective-permute-start | bytes 46088 | tf_op jit(solution)/shard_map/ppermute | solution.py:364
  40.4 3.9 %collective-permute-start.4 = (f32[5,1,3,2,128]{4,3,2,1,0:T(2,128)}, f32[5,1,3,2,128]{4,3,2,1,0:T(2,128)S(1)}, u32[]{:S(2)}, u32[]{:S(2)}) collective-permute-start(f32[5,1,3,2,128]{4,3,2,1,0:T(2,128)} %get-tuple-element.26.refs_3_), channel_id=1, source_target_pairs={{2,0},{4,2},{6,4},{0,6},{3,1},{5,3},{7,5},{1,7},{10,8},{12,10},{14... | collective-permute-start | bytes 46088 | tf_op jit(solution)/shard_map/ppermute | solution.py:364
  42.0 2.4 %copy-start.4 = (f32[5,1,3,2,128]{4,3,2,1,0:T(2,128)}, f32[5,1,3,2,128]{4,3,2,1,0:T(2,128)S(1)}, u32[]{:S(2)}) copy-start(f32[5,1,3,2,128]{4,3,2,1,0:T(2,128)S(1)} %collective-permute-done.6.refs_6_) | copy-start | bytes 46084
  42.7 1.7 %copy-start.5 = (f32[5,1,3,2,128]{4,3,2,1,0:T(2,128)}, f32[5,1,3,2,128]{4,3,2,1,0:T(2,128)S(1)}, u32[]{:S(2)}) copy-start(f32[5,1,3,2,128]{4,3,2,1,0:T(2,128)S(1)} %collective-permute-done.5.refs_5_) | copy-start | bytes 46084
  44.4 0.6 %copy-start.6 = (f32[5,1,3,2,128]{4,3,2,1,0:T(2,128)}, f32[5,1,3,2,128]{4,3,2,1,0:T(2,128)S(1)}, u32[]{:S(2)}) copy-start(f32[5,1,3,2,128]{4,3,2,1,0:T(2,128)S(1)} %collective-permute-done.4.refs_4_) | copy-start | bytes 46084

commit v12 on v11

--- a/solution.py
+++ b/solution.py
@@ -51,22 +51,21 @@
     return lower, upper, rhs
 
 
-def interior(lower, upper):
-    length = lower.shape[0]
-    idx = lax.broadcasted_iota(jnp.int32, lower.shape, 0)
-    edge = (idx == 0) | (idx == length - 1)
+def interior(lower, upper, block):
+    idx = lax.broadcasted_iota(jnp.int32, lower.shape, 0) % block
+    edge = (idx == 0) | (idx == block - 1)
     second = idx == 1
-    penult = idx == length - 2
+    penult = idx == block - 2
     zero = jnp.zeros_like(lower)
     il = jnp.where(edge | second, zero, lower)
     iu = jnp.where(edge | penult, zero, upper)
     return il, iu, jnp.where(edge, zero, 1.0), jnp.where(second, lower, zero), jnp.where(penult, upper, zero)
 
 
-def pcr_levels(il, iu, rhs):
+def pcr_levels(il, iu, rhs, block):
     length = il.shape[0]
     stride = 1
-    while stride < length - 2:
+    while stride < block - 2:
         back = length - stride
         ll, ul = pltpu.roll(il, stride, 0), pltpu.roll(iu, stride, 0)
         lr, ur = pltpu.roll(il, back, 0), pltpu.roll(iu, back, 0)
@@ -78,10 +77,7 @@
     return rhs
 
 
-def interface_rows(lower, upper, t0, te, t1, t2, a1, b1, a2, b2):
-    length = lower.shape[0]
-    l0, u0 = lower[0:1], upper[0:1]
-    le, ue = lower[length - 1 :], upper[length - 1 :]
+def interface_rows(l0, u0, le, ue, t0, te, t1, t2, a1, b1, a2, b2):
     inv_f = 1.0 / (1.0 - u0 * a1)
     inv_e = 1.0 / (1.0 - le * b2)
     return (
@@ -91,27 +87,36 @@
     )
 
 
-def reduce_block(lower, upper, target):
-    length = lower.shape[0]
-    il, iu, keep, a_init, b_init = interior(lower, upper)
-    it, ia, ib = pcr_levels(il, iu, [target * keep, a_init, b_init])
-    n2 = length - 2
-    rows = interface_rows(
-        lower, upper, target[0:1], target[length - 1 :], it[1:2], it[n2 : n2 + 1],
-        ia[1:2], ib[1:2], ia[n2 : n2 + 1], ib[n2 : n2 + 1],
+def picked(values, block, offset):
+    return [values[k + offset : k + offset + 1] for k in range(0, values.shape[0], block)]
+
+
+def edge_rows(target, ia, ib, block):
+    return [
+        picked(target, block, 0), picked(target, block, block - 1),
+        picked(ia, block, 1), picked(ib, block, 1), picked(ia, block, block - 2), picked(ib, block, block - 2),
+    ]
+
+
+def block_rows(lower, upper, t0, te, it, edges, block):
+    parts = zip(
+        picked(lower, block, 0), picked(upper, block, 0), picked(lower, block, block - 1), picked(upper, block, block - 1),
+        t0, te, picked(it, block, 1), picked(it, block, block - 2), *edges,
     )
-    return it, ia, ib, rows
+    return [interface_rows(*p) for p in parts]
 
 
 def store_rows(red_ref, v, rows):
-    for q, pair in enumerate(rows):
-        for i, value in enumerate(pair):
-            red_ref[v, 0, q, i : i + 1, :] = value
+    for k, sub in enumerate(rows):
+        for q, pair in enumerate(sub):
+            for i, value in enumerate(pair):
+                red_ref[v, 0, q, 2 * k + i : 2 * k + i + 1, :] = value
 
 
 def reduced_ends(red_refs, rows_ref, v):
+    own = red_refs[0].shape[3]
     for k, ref in enumerate(red_refs):
-        rows_ref[:, 2 * k : 2 * k + 2, :] = ref[v, 0]
+        rows_ref[:, own * k : own * (k + 1), :] = ref[v, 0]
     lower, upper, target = rows_ref[0], rows_ref[1], rows_ref[2]
     length = lower.shape[0]
     stride = 1
@@ -124,14 +129,20 @@
         lower, upper = -lower * ll * inv, -upper * ur * inv
         stride = stride * 2
     ends = target / (1.0 + lower + upper)
-    return ends[0:1], ends[1:2]
-
-
-def back_substitute(it, ia, ib, first, last):
-    length = it.shape[0]
+    return ends[:own]
+
+
+def back_substitute(it, ia, ib, ends, block):
     idx = lax.broadcasted_iota(jnp.int32, it.shape, 0)
+    first = jnp.zeros_like(it)
+    last = jnp.zeros_like(it)
+    for k in range(it.shape[0] // block):
+        inside = idx // block == k
+        first = jnp.where(inside, ends[2 * k : 2 * k + 1], first)
+        last = jnp.where(inside, ends[2 * k + 1 : 2 * k + 2], last)
     inner = it - ia * first - ib * last
-    return jnp.where(idx == 0, first, jnp.where(idx == length - 1, last, inner))
+    local = idx % block
+    return jnp.where(local == 0, first, jnp.where(local == block - 1, last, inner))
 
 
 def mixed(mix_ref, values):
@@ -153,7 +164,7 @@
     return lower, upper, scale
 
 
-def az_local_kernel(fs_ref, src_ref, cell_ref, visc_ref, beta_ref, diff_ref, mix_ref, ot_ref, oa_ref, ob_ref, edge_ref):
+def az_local_kernel(fs_ref, src_ref, cell_ref, visc_ref, beta_ref, diff_ref, mix_ref, ot_ref, oa_ref, ob_ref, edge_ref, *, block):
     count = fs_ref.shape[0]
     explicit = [src_ref[w, 0] + diff_ref[w : w + 1, :] * (-2.0 * fs_ref[w, 0]) for w in range(count)]
     section_one = mixed(mix_ref, explicit)
@@ -161,20 +172,17 @@
     for v in range(count):
         lower, upper, scale = az_coefficients(cell, visc_ref, beta_ref, v)
         target = section_one[v] * -scale
-        length = lower.shape[0]
-        il, iu, keep, a_init, b_init = interior(lower, upper)
-        it, ia, ib = pcr_levels(il, iu, [target * keep, a_init, b_init])
+        il, iu, keep, a_init, b_init = interior(lower, upper, block)
+        it, ia, ib = pcr_levels(il, iu, [target * keep, a_init, b_init], block)
         ot_ref[v, 0] = it
         oa_ref[v, 0] = ia
         ob_ref[v, 0] = ib
-        n2 = length - 2
-        for k, value in enumerate(
-            (target[0:1], target[length - 1 :], ia[1:2], ib[1:2], ia[n2 : n2 + 1], ib[n2 : n2 + 1])
-        ):
+        rows = [value for group in edge_rows(target, ia, ib, block) for value in group]
+        for k, value in enumerate(rows):
             edge_ref[v, 0, k : k + 1, :] = value
 
 
-def az_plane_kernel(nb_ref, cell_ref, visc_ref, beta_ref, diff_ref, mix_ref, it_in_ref, edge_ref, order_ref, ot_ref, red_ref):
+def az_plane_kernel(nb_ref, cell_ref, visc_ref, beta_ref, diff_ref, mix_ref, it_in_ref, edge_ref, order_ref, ot_ref, red_ref, *, block):
     count = nb_ref.shape[0]
     explicit = [diff_ref[w : w + 1, :] * nb_ref[w, 0] for w in range(count)]
     section_one = mixed(mix_ref, explicit)
@@ -182,18 +190,16 @@
     for v in range(count):
         lower, upper, scale = az_coefficients(cell, visc_ref, beta_ref, v)
         target = section_one[v] * -scale
-        length = lower.shape[0]
-        il, iu, keep, _, _ = interior(lower, upper)
-        (it,) = pcr_levels(il, iu, [target * keep])
+        il, iu, keep, _, _ = interior(lower, upper, block)
+        (it,) = pcr_levels(il, iu, [target * keep], block)
         it = it_in_ref[v, 0] + it
         ot_ref[v, 0] = it
         edge = edge_ref[v, 0]
-        n2 = length - 2
-        rows = interface_rows(
-            lower, upper, edge[0:1] + target[0:1], edge[1:2] + target[length - 1 :], it[1:2], it[n2 : n2 + 1],
-            edge[2:3], edge[3:4], edge[4:5], edge[5:6],
-        )
-        store_rows(red_ref, v, rows)
+        count_sub = lower.shape[0] // block
+        groups = [[edge[g * count_sub + k : g * count_sub + k + 1] for k in range(count_sub)] for g in range(6)]
+        t0 = [a + b for a, b in zip(groups[0], picked(target, block, 0))]
+        te = [a + b for a, b in zip(groups[1], picked(target, block, block - 1))]
+        store_rows(red_ref, v, block_rows(lower, upper, t0, te, it, groups[2:], block))
 
 
 def rad_side(cell, visc, v):
@@ -207,7 +213,7 @@
     return visc_ref[:, pl.ds(pl.multiple_of(place * cells, cells), cells)]
 
 
-def rad_pre_kernel(cell_ref, visc_ref, oa_ref, ob_ref, edge_ref, *, axis_name):
+def rad_pre_kernel(cell_ref, visc_ref, oa_ref, ob_ref, edge_ref, *, axis_name, block):
     count = oa_ref.shape[0]
     cells = cell_ref.shape[2]
     visc = local_visc(visc_ref, axis_name, cells)
@@ -215,17 +221,16 @@
     for v in range(count):
         side, _ = rad_side(cell, visc, v)
         side = side.T
-        length = side.shape[0]
-        il, iu, _, a_init, b_init = interior(side, side)
-        ia, ib = pcr_levels(il, iu, [a_init, b_init])
+        il, iu, _, a_init, b_init = interior(side, side, block)
+        ia, ib = pcr_levels(il, iu, [a_init, b_init], block)
         oa_ref[v, 0] = ia
         ob_ref[v, 0] = ib
-        n2 = length - 2
-        for k, value in enumerate((ia[1:2], ib[1:2], ia[n2 : n2 + 1], ib[n2 : n2 + 1])):
+        rows = [value for group in edge_rows(ia, ia, ib, block)[2:] for value in group]
+        for k, value in enumerate(rows):
             edge_ref[v, 0, k : k + 1, :] = value
 
 
-def rad_kernel(*refs, axis_name, devices, pieces):
+def rad_kernel(*refs, axis_name, devices, pieces, block, az_block):
     it_ref, ia_ref, ib_ref = refs[:3]
     red_in = refs[3 : 3 + pieces]
     mix_ref, cell_ref, visc_ref, edge_ref, ot_ref, red_ref, rows_ref = refs[3 + pieces :]
@@ -235,40 +240,43 @@
     visc = local_visc(visc_ref, axis_name, cells)
     solved = []
     for w in range(count):
-        first, last = reduced_ends(red_in, rows_ref, w)
-        solved.append(back_substitute(it_ref[w, 0], ia_ref[w, 0], ib_ref[w, 0], first, last))
+        ends = reduced_ends(red_in, rows_ref, w)
+        solved.append(back_substitute(it_ref[w, 0], ia_ref[w, 0], ib_ref[w, 0], ends, az_block))
     section_three = mixed(mix_ref, solved)
     cell = cell_ref[0]
     for v in range(count):
         side, scale = rad_side(cell, visc, v)
         side = side.T
         target = (section_three[v] * scale).T
-        length = side.shape[0]
-        il, iu, keep, _, _ = interior(side, side)
-        (it,) = pcr_levels(il, iu, [target * keep])
+        il, iu, keep, _, _ = interior(side, side, block)
+        (it,) = pcr_levels(il, iu, [target * keep], block)
         edge = edge_ref[v, 0]
-        n2 = length - 2
-        (lf, le), (uf, ue), trow = interface_rows(
-            side, side, target[0:1], target[length - 1 :], it[1:2], it[n2 : n2 + 1],
-            edge[0:1], edge[1:2], edge[2:3], edge[3:4],
-        )
-        lf = jnp.where(place == 0, jnp.zeros_like(lf), lf)
-        ue = jnp.where(place == devices - 1, jnp.zeros_like(ue), ue)
-        store_rows(red_ref, v, ((lf, le), (uf, ue), trow))
+        count_sub = side.shape[0] // block
+        groups = [[edge[g * count_sub + k : g * count_sub + k + 1] for k in range(count_sub)] for g in range(4)]
+        rows = block_rows(side, side, picked(target, block, 0), picked(target, block, block - 1), it, groups, block)
+        (lf, le), upper_rows, trow = rows[0]
+        rows[0] = ((jnp.where(place == 0, jnp.zeros_like(lf), lf), le), upper_rows, trow)
+        lower_rows, (uf, ue), trow = rows[-1]
+        rows[-1] = (lower_rows, (uf, jnp.where(place == devices - 1, jnp.zeros_like(ue), ue)), trow)
+        store_rows(red_ref, v, rows)
         ot_ref[v, 0] = it
 
 
-def out_kernel(*refs, pieces):
+def out_kernel(*refs, pieces, block):
     it_ref, ia_ref, ib_ref = refs[:3]
     red_in = refs[3 : 3 + pieces]
     mix_ref, out_ref, rows_ref = refs[3 + pieces :]
     count = it_ref.shape[0]
     solved = []
     for w in range(count):
-        first, last = reduced_ends(red_in, rows_ref, w)
-        solved.append(back_substitute(it_ref[w, 0], ia_ref[w, 0], ib_ref[w, 0], first, last).T)
+        ends = reduced_ends(red_in, rows_ref, w)
+        solved.append(back_substitute(it_ref[w, 0], ia_ref[w, 0], ib_ref[w, 0], ends, block).T)
     for v, value in enumerate(mixed(mix_ref, solved)):
         out_ref[v, 0] = value
+
+
+def sub_block(length, size):
+    return size if length % size == 0 and length > size else length
 
 
 def az_sweep(flow_state, nb, source, cell_az, visc_az, beta_az, axial_diff, mix_in, order):
@@ -279,22 +287,24 @@
     cell = pl.BlockSpec((1, na, chunk), lambda z, c: (z, 0, c))
     par = pl.BlockSpec((nv, chunk), lambda z, c: (0, c))
     mixs = pl.BlockSpec((nv, nv, chunk), lambda z, c: (0, 0, c))
-    edge = pl.BlockSpec((nv, 1, 6, chunk), lambda z, c: (0, z, 0, c))
-    red = pl.BlockSpec((nv, 1, 3, 2, chunk), lambda z, c: (0, z, 0, 0, c))
+    block = sub_block(na, 32)
+    subs = na // block
+    edge = pl.BlockSpec((nv, 1, 6 * subs, chunk), lambda z, c: (0, z, 0, c))
+    red = pl.BlockSpec((nv, 1, 3, 2 * subs, chunk), lambda z, c: (0, z, 0, 0, c))
     out = jax.ShapeDtypeStruct(flow_state.shape, flow_state.dtype)
     it, ia, ib, edges = pl.pallas_call(
-        az_local_kernel,
+        functools.partial(az_local_kernel, block=block),
         grid=grid,
         in_specs=[big, big, cell, par, par, par, mixs],
         out_specs=[big, big, big, edge],
-        out_shape=[out, out, out, jax.ShapeDtypeStruct((nv, nz, 6, nr), flow_state.dtype)],
+        out_shape=[out, out, out, jax.ShapeDtypeStruct((nv, nz, 6 * subs, nr), flow_state.dtype)],
     )(flow_state, source, cell_az, visc_az, beta_az, axial_diff, mix_in)
     it, red = pl.pallas_call(
-        az_plane_kernel,
+        functools.partial(az_plane_kernel, block=block),
         grid=grid,
         in_specs=[big, cell, par, par, par, mixs, big, edge, pl.BlockSpec(memory_space=pl.ANY)],
         out_specs=[big, red],
-        out_shape=[out, jax.ShapeDtypeStruct((nv, nz, 3, 2, nr), flow_state.dtype)],
+        out_shape=[out, jax.ShapeDtypeStruct((nv, nz, 3, 2 * subs, nr), flow_state.dtype)],
         input_output_aliases={6: 0},
     )(nb, cell_az, visc_az, beta_az, axial_diff, mix_in, it, edges, order)
     return it, ia, ib, red
@@ -305,14 +315,16 @@
     big_t = pl.BlockSpec((nv, 1, nr, na), lambda z: (0, z, 0, 0))
     cell = pl.BlockSpec((1, na, nr), lambda z: (z, 0, 0))
     par = pl.BlockSpec(visc_rad.shape, lambda z: (0, 0))
-    edge = pl.BlockSpec((nv, 1, 4, na), lambda z: (0, z, 0, 0))
+    block = sub_block(nr, 64)
+    subs = nr // block
+    edge = pl.BlockSpec((nv, 1, 4 * subs, na), lambda z: (0, z, 0, 0))
     out = jax.ShapeDtypeStruct((nv, nz, nr, na), cell_rad.dtype)
     return pl.pallas_call(
-        functools.partial(rad_pre_kernel, axis_name="rad"),
+        functools.partial(rad_pre_kernel, axis_name="rad", block=block),
         grid=(nz,),
         in_specs=[cell, par],
         out_specs=[big_t, big_t, edge],
-        out_shape=[out, out, jax.ShapeDtypeStruct((nv, nz, 4, na), cell_rad.dtype)],
+        out_shape=[out, out, jax.ShapeDtypeStruct((nv, nz, 4 * subs, na), cell_rad.dtype)],
     )(cell_rad, visc_rad)
 
 
@@ -324,18 +336,22 @@
     mixs = pl.BlockSpec((nv, nv, nr), lambda z: (0, 0, 0))
     cell = pl.BlockSpec((1, na, nr), lambda z: (z, 0, 0))
     par = pl.BlockSpec(visc_rad.shape, lambda z: (0, 0))
-    edge = pl.BlockSpec((nv, 1, 4, na), lambda z: (0, z, 0, 0))
-    red = pl.BlockSpec((nv, 1, 3, 2, na), lambda z: (0, z, 0, 0, 0))
+    block = sub_block(nr, 64)
+    subs = nr // block
+    edge = pl.BlockSpec((nv, 1, 4 * subs, na), lambda z: (0, z, 0, 0))
+    red = pl.BlockSpec((nv, 1, 3, 2 * subs, na), lambda z: (0, z, 0, 0, 0))
     out = jax.ShapeDtypeStruct((nv, nz, nr, na), it.dtype)
     pieces = len(red_in)
-    kernel = functools.partial(rad_kernel, axis_name="rad", devices=lax.axis_size("rad"), pieces=pieces)
+    kernel = functools.partial(
+        rad_kernel, axis_name="rad", devices=lax.axis_size("rad"), pieces=pieces, block=block, az_block=sub_block(na, 32)
+    )
     return pl.pallas_call(
         kernel,
         grid=(nz,),
         in_specs=[big, big, big] + [red_in_spec] * pieces + [mixs, cell, par, edge],
         out_specs=[big_t, red],
-        out_shape=[out, jax.ShapeDtypeStruct((nv, nz, 3, 2, na), it.dtype)],
-        scratch_shapes=[pltpu.VMEM((3, 2 * pieces, nr), it.dtype)],
+        out_shape=[out, jax.ShapeDtypeStruct((nv, nz, 3, 2 * subs, na), it.dtype)],
+        scratch_shapes=[pltpu.VMEM((3, red_in[0].shape[3] * pieces, nr), it.dtype)],
     )(it, ia, ib, *red_in, mix_mid, cell_rad, visc_rad, edges)
 
 
@@ -347,12 +363,12 @@
     mixs = pl.BlockSpec((nv, nv, nr), lambda z: (0, 0, 0))
     pieces = len(red_in)
     return pl.pallas_call(
-        functools.partial(out_kernel, pieces=pieces),
+        functools.partial(out_kernel, pieces=pieces, block=sub_block(nr, 64)),
         grid=(nz,),
         in_specs=[big_t, big_t, big_t] + [red_in_spec] * pieces + [mixs],
         out_specs=big,
         out_shape=jax.ShapeDtypeStruct((nv, nz, na, nr), it.dtype),
-        scratch_shapes=[pltpu.VMEM((3, 2 * pieces, na), it.dtype)],
+        scratch_shapes=[pltpu.VMEM((3, red_in[0].shape[3] * pieces, na), it.dtype)],
     )(it, ia, ib, *red_in, mix_out)
 
 

time: 48 us -> 52 us (1.083)
  waiting for transfers between devices: 6.41 us -> 11.2 us
  Pallas kernels: 27.6 us -> 26.8 us
    ppermute x6, waiting for transfers between devices: 4.37 us -> 8.78 us  [gathered(): received.append(lax.ppermute(block, axis_name, pairs))]
    pallas_call x4, Pallas kernels: 21.1 us -> 20.6 us  [the longest x1 6.45 us: az_sweep(): pl.pallas_call(functools.partial(az_local_kernel, block=block), grid=grid...]
  transfers between devices with their start and end apart: 7 -> 7, of which waited for: 7 -> 7; matrix products, arithmetic and copies ran while one was open for 0% -> 0% of each run, Pallas kernels for 27% -> 24%
where the time goes in v12:
time: 52 us; the launch traced here: 51.8 us
  Pallas kernels  26.8 us (52%)
  starting transfers between devices  11.7 us (22%)
  waiting for transfers between devices  11.2 us (22%)
  local copies, waits for them, and re-layouts  2.11 us (4%)
    ppermute x6, waiting for transfers between devices, gathered(): received.append(lax.ppermute(block, axis_name, pairs))  8.78 us
    ppermute x6, starting transfers between devices, gathered(): received.append(lax.ppermute(block, axis_name, pairs))  8.72 us
    pallas_call x1, Pallas kernels, az_sweep(): pl.pallas_call(functools.partial(az_local_kernel, block=block), grid=grid...  6.45 us
    pallas_call x1, Pallas kernels, rad_sweep(): pl.pallas_call(kernel, grid=(nz,), in_specs=[big, big, big] + [red_in_spe...  6.21 us
    pallas_call x1, Pallas kernels, rad_pre(): pl.pallas_call(functools.partial(rad_pre_kernel, axis_name='rad', block=b...  6.1 us
    pallas_call x1, Pallas kernels, az_sweep(): pl.pallas_call(functools.partial(az_plane_kernel, block=block), grid=grid...  5.04 us
    pallas_call x1, Pallas kernels, out_sweep(): pl.pallas_call(functools.partial(out_kernel, pieces=pieces, block=sub_blo...  2.97 us
    ppermute x1, starting transfers between devices, neighbour_planes(): return lax.ppermute(block, axis_name, [(0, 1), (1, 0)])  2.97 us
  transfers between devices with their start and end apart: 7, of which 7 were waited for; matrix products, arithmetic and copies ran while one was open for 0% of the time, Pallas kernels for 24%

profile of v12, /device:TPU:0, one launch (start us, length us, event | category | flops | bytes accessed | tf_op | source)
XLA Modules:
  0.0 51.8 jit_solution(6327564553153831436)
XLA Ops:
  0.0 3.0 %collective-permute-start = (f32[5,1,128,256]{3,2,1,0:T(8,128)}, f32[5,1,128,256]{3,2,1,0:T(8,128)S(1)}, u32[]{:S(2)}, u32[]{:S(2)}) collective-permute-start(f32[5,1,128,256]{3,2,1,0:T(8,128)} %fs_ref.1), channel_id=1, source_target_pairs={{0,1},{1,0},{2,3},{3,2},{4,5},{5,4},{6,7},{7,6},{8,9},{9,8},{10,11... | collective-permute-start | bytes 1966088 | tf_op jit(solution)/shard_map/ppermute | solution.py:387
  3.0 6.1 %shard_map.110 = (f32[5,1,256,128]{3,2,1,0:T(8,128)}, f32[5,1,256,128]{3,2,1,0:T(8,128)}, f32[5,1,16,128]{3,2,1,0:T(8,128)}) custom-call(f32[1,128,256]{2,1,0:T(8,128)} %refs_8_.1, f32[5,1024]{1,0:T(8,128)} %refs_9_.1), custom_call_target="tpu_custom_call" | custom-call | tf_op jit(solution)/shard_map/pallas_call | solution.py:322
  9.1 6.5 %shard_map.109 = (f32[5,1,128,256]{3,2,1,0:T(8,128)}, f32[5,1,128,256]{3,2,1,0:T(8,128)}, f32[5,1,128,256]{3,2,1,0:T(8,128)}, f32[5,1,24,256]{3,2,1,0:T(8,128)}) custom-call(f32[5,1,128,256]{3,2,1,0:T(8,128)} %fs_ref.1, f32[5,1,128,256]{3,2,1,0:T(8,128)} %src_ref.1, f32[1,128,256]{2,1,0:T(8,128)} %cell_ref.5, f32[5,256]{1,0:T(8,128)} %visc_ref.5, ...), custom_call_target="tpu_custom_call" | custom-call | tf_op jit(solution)/shard_map/pallas_call | solution.py:295
  15.5 2.4 %collective-permute-done.nb_ref = f32[5,1,128,256]{3,2,1,0:T(8,128)S(1)} collective-permute-done((f32[5,1,128,256]{3,2,1,0:T(8,128)}, f32[5,1,128,256]{3,2,1,0:T(8,128)S(1)}, u32[]{:S(2)}, u32[]{:S(2)}) %collective-permute-start) | collective-permute-done | bytes 655392 | tf_op jit(solution)/shard_map/ppermute | solution.py:387
  17.9 0.0 copy-start
  17.9 0.8 %copy-done = f32[5,1,128,256]{3,2,1,0:T(8,128)} copy-done((f32[5,1,128,256]{3,2,1,0:T(8,128)}, f32[5,1,128,256]{3,2,1,0:T(8,128)S(1)}, u32[]{:S(2)}) %copy-start) | copy-done | bytes 655384
  18.7 5.0 %shard_map.111 = (f32[5,1,128,256]{3,2,1,0:T(8,128)}, f32[5,1,3,8,256]{4,3,2,1,0:T(8,128)}) custom-call(f32[5,1,128,256]{3,2,1,0:T(8,128)} %copy-done, f32[1,128,256]{2,1,0:T(8,128)} %cell_ref.5, f32[5,256]{1,0:T(8,128)} %visc_ref.5, f32[5,256]{1,0:T(8,128)} %beta_ref.3, f32[5,256]{1,0:T(8,128)} %diff_ref.3, ...), custom_call_target="tpu_custom_call", output_to_operand_aliasing={{0}: (6, {})} | custom-call | tf_op jit(solution)/shard_map/pallas_call | solution.py:302
  23.8 0.0 collective-permute-start.3
  23.8 1.8 %collective-permute-start.2 = (f32[5,1,3,8,256]{4,3,2,1,0:T(8,128)}, f32[5,1,3,8,256]{4,3,2,1,0:T(8,128)S(1)}, u32[]{:S(2)}, u32[]{:S(2)}) collective-permute-start(f32[5,1,3,8,256]{4,3,2,1,0:T(8,128)} %get-tuple-element.22.refs_3_), channel_id=1, source_target_pairs={{16,0},{24,8},{0,16},{8,24},{17,1},{25,9},{1,17},{9,25},{18,2},{26... | collective-permute-start | bytes 368648 | tf_op jit(solution)/shard_map/ppermute | solution.py:380
  25.6 1.4 %collective-permute-start.1 = (f32[5,1,3,8,256]{4,3,2,1,0:T(8,128)}, f32[5,1,3,8,256]{4,3,2,1,0:T(8,128)S(1)}, u32[]{:S(2)}, u32[]{:S(2)}) collective-permute-start(f32[5,1,3,8,256]{4,3,2,1,0:T(8,128)} %get-tuple-element.22.refs_3_), channel_id=1, source_target_pairs={{8,0},{16,8},{24,16},{0,24},{9,1},{17,9},{25,17},{1,25},{10,2},{18... | collective-permute-start | bytes 368648 | tf_op jit(solution)/shard_map/ppermute | solution.py:380
  27.0 2.0 %collective-permute-done.3.refs_6_ = f32[5,1,3,8,256]{4,3,2,1,0:T(8,128)S(1)} collective-permute-done((f32[5,1,3,8,256]{4,3,2,1,0:T(8,128)}, f32[5,1,3,8,256]{4,3,2,1,0:T(8,128)S(1)}, u32[]{:S(2)}, u32[]{:S(2)}) %collective-permute-start.3) | collective-permute-done | bytes 122912 | tf_op jit(solution)/shard_map/ppermute | solution.py:380
  29.1 0.0 copy-start.1
  29.1 1.2 %collective-permute-done.2.refs_5_ = f32[5,1,3,8,256]{4,3,2,1,0:T(8,128)S(1)} collective-permute-done((f32[5,1,3,8,256]{4,3,2,1,0:T(8,128)}, f32[5,1,3,8,256]{4,3,2,1,0:T(8,128)S(1)}, u32[]{:S(2)}, u32[]{:S(2)}) %collective-permute-start.2) | collective-permute-done | bytes 122912 | tf_op jit(solution)/shard_map/ppermute | solution.py:380
  30.3 0.0 copy-start.2
  30.3 1.4 %collective-permute-done.1.refs_4_ = f32[5,1,3,8,256]{4,3,2,1,0:T(8,128)S(1)} collective-permute-done((f32[5,1,3,8,256]{4,3,2,1,0:T(8,128)}, f32[5,1,3,8,256]{4,3,2,1,0:T(8,128)S(1)}, u32[]{:S(2)}, u32[]{:S(2)}) %collective-permute-start.1) | collective-permute-done | bytes 122912 | tf_op jit(solution)/shard_map/ppermute | solution.py:380
  31.6 0.0 copy-start.3
  31.6 0.0 copy-done.1
  31.6 0.0 copy-done.2
  31.6 0.6 %copy-done.3 = f32[5,1,3,8,256]{4,3,2,1,0:T(8,128)} copy-done((f32[5,1,3,8,256]{4,3,2,1,0:T(8,128)}, f32[5,1,3,8,256]{4,3,2,1,0:T(8,128)S(1)}, u32[]{:S(2)}) %copy-start.3) | copy-done | bytes 122904
  32.3 6.2 %shard_map.112 = (f32[5,1,256,128]{3,2,1,0:T(8,128)}, f32[5,1,3,8,128]{4,3,2,1,0:T(8,128)}) custom-call(f32[5,1,128,256]{3,2,1,0:T(8,128)} %get-tuple-element.19.refs_0_, f32[5,1,128,256]{3,2,1,0:T(8,128)} %get-tuple-element.20.refs_1_, f32[5,1,128,256]{3,2,1,0:T(8,128)} %get-tuple-element.21.refs_2_, f32[5,1,3,8,256]{4,3,2,1,0:T(8,128)} %get-tuple-element.22.refs_3_, ...), custom_call_target="tpu_custom_call" | custom-call | tf_op jit(solution)/shard_map/pallas_call | solution.py:348
  38.5 1.6 %collective-permute-start.6 = (f32[5,1,3,8,128]{4,3,2,1,0:T(8,128)}, f32[5,1,3,8,128]{4,3,2,1,0:T(8,128)S(1)}, u32[]{:S(2)}, u32[]{:S(2)}) collective-permute-start(f32[5,1,3,8,128]{4,3,2,1,0:T(8,128)} %get-tuple-element.26.refs_3_), channel_id=1, source_target_pairs={{6,0},{0,2},{2,4},{4,6},{7,1},{1,3},{3,5},{5,7},{14,8},{8,10},{10,... | collective-permute-start | bytes 184328 | tf_op jit(solution)/shard_map/ppermute | solution.py:380
  40.1 2.6 %collective-permute-start.5 = (f32[5,1,3,8,128]{4,3,2,1,0:T(8,128)}, f32[5,1,3,8,128]{4,3,2,1,0:T(8,128)S(1)}, u32[]{:S(2)}, u32[]{:S(2)}) collective-permute-start(f32[5,1,3,8,128]{4,3,2,1,0:T(8,128)} %get-tuple-element.26.refs_3_), channel_id=1, source_target_pairs={{4,0},{6,2},{0,4},{2,6},{5,1},{7,3},{1,5},{3,7},{12,8},{14,10},{8,... | collective-permute-start | bytes 184328 | tf_op jit(solution)/shard_map/ppermute | solution.py:380
  42.6 1.4 %collective-permute-start.4 = (f32[5,1,3,8,128]{4,3,2,1,0:T(8,128)}, f32[5,1,3,8,128]{4,3,2,1,0:T(8,128)S(1)}, u32[]{:S(2)}, u32[]{:S(2)}) collective-permute-start(f32[5,1,3,8,128]{4,3,2,1,0:T(8,128)} %get-tuple-element.26.refs_3_), channel_id=1, source_target_pairs={{2,0},{4,2},{6,4},{0,6},{3,1},{5,3},{7,5},{1,7},{10,8},{12,10},{14... | collective-permute-start | bytes 184328 | tf_op jit(solution)/shard_map/ppermute | solution.py:380
  44.0 1.3 %collective-permute-done.6.refs_6_ = f32[5,1,3,8,128]{4,3,2,1,0:T(8,128)S(1)} collective-permute-done((f32[5,1,3,8,128]{4,3,2,1,0:T(8,128)}, f32[5,1,3,8,128]{4,3,2,1,0:T(8,128)S(1)}, u32[]{:S(2)}, u32[]{:S(2)}) %collective-permute-start.6) | collective-permute-done | bytes 61472 | tf_op jit(solution)/shard_map/ppermute | solution.py:380
  45.3 0.0 copy-start.4
  45.3 2.6 %collective-permute-done.5.refs_5_ = f32[5,1,3,8,128]{4,3,2,1,0:T(8,128)S(1)} collective-permute-done((f32[5,1,3,8,128]{4,3,2,1,0:T(8,128)}, f32[5,1,3,8,128]{4,3,2,1,0:T(8,128)S(1)}, u32[]{:S(2)}, u32[]{:S(2)}) %collective-permute-start.5) | collective-permute-done | bytes 61472 | tf_op jit(solution)/shard_map/ppermute | solution.py:380
  47.9 0.0 copy-start.5
  47.9 0.3 collective-permute-done.4.refs_4_
  48.2 0.0 copy-start.6
  48.2 0.0 copy-done.4
  48.2 0.4 copy-done.5
  48.5 0.3 copy-done.6
  48.8 3.0 %shard_map.113 = f32[5,1,128,256]{3,2,1,0:T(8,128)} custom-call(f32[5,1,256,128]{3,2,1,0:T(8,128)} %get-tuple-element.23.refs_0_, f32[5,1,256,128]{3,2,1,0:T(8,128)} %get-tuple-element.24.refs_1_, f32[5,1,256,128]{3,2,1,0:T(8,128)} %get-tuple-element.25.refs_2_, f32[5,1,3,8,128]{4,3,2,1,0:T(8,128)} %get-tuple-element.26.refs_3_, ...), custom_call_target="tpu_custom_call" | custom-call | tf_op jit(solution)/shard_map/pallas_call | solution.py:365
Async XLA Ops:
  0.0 17.9 %collective-permute-start = (f32[5,1,128,256]{3,2,1,0:T(8,128)}, f32[5,1,128,256]{3,2,1,0:T(8,128)S(1)}, u32[]{:S(2)}, u32[]{:S(2)}) collective-permute-start(f32[5,1,128,256]{3,2,1,0:T(8,128)} %fs_ref.1), channel_id=1, source_target_pairs={{0,1},{1,0},{2,3},{3,2},{4,5},{5,4},{6,7},{7,6},{8,9},{9,8},{10,11... | collective-permute-start | bytes 1966088 | tf_op jit(solution)/shard_map/ppermute | solution.py:387
  17.9 0.8 %copy-start = (f32[5,1,128,256]{3,2,1,0:T(8,128)}, f32[5,1,128,256]{3,2,1,0:T(8,128)S(1)}, u32[]{:S(2)}) copy-start(f32[5,1,128,256]{3,2,1,0:T(8,128)S(1)} %collective-permute-done.nb_ref) | copy-start | bytes 1966084
  23.8 5.3 %collective-permute-start.3 = (f32[5,1,3,8,256]{4,3,2,1,0:T(8,128)}, f32[5,1,3,8,256]{4,3,2,1,0:T(8,128)S(1)}, u32[]{:S(2)}, u32[]{:S(2)}) collective-permute-start(f32[5,1,3,8,256]{4,3,2,1,0:T(8,128)} %get-tuple-element.22.refs_3_), channel_id=1, source_target_pairs={{24,0},{0,8},{8,16},{16,24},{25,1},{1,9},{9,17},{17,25},{26,2},{2,... | collective-permute-start | bytes 368648 | tf_op jit(solution)/shard_map/ppermute | solution.py:380
  23.8 6.4 %collective-permute-start.2 = (f32[5,1,3,8,256]{4,3,2,1,0:T(8,128)}, f32[5,1,3,8,256]{4,3,2,1,0:T(8,128)S(1)}, u32[]{:S(2)}, u32[]{:S(2)}) collective-permute-start(f32[5,1,3,8,256]{4,3,2,1,0:T(8,128)} %get-tuple-element.22.refs_3_), channel_id=1, source_target_pairs={{16,0},{24,8},{0,16},{8,24},{17,1},{25,9},{1,17},{9,25},{18,2},{26... | collective-permute-start | bytes 368648 | tf_op jit(solution)/shard_map/ppermute | solution.py:380
  25.6 6.0 %collective-permute-start.1 = (f32[5,1,3,8,256]{4,3,2,1,0:T(8,128)}, f32[5,1,3,8,256]{4,3,2,1,0:T(8,128)S(1)}, u32[]{:S(2)}, u32[]{:S(2)}) collective-permute-start(f32[5,1,3,8,256]{4,3,2,1,0:T(8,128)} %get-tuple-element.22.refs_3_), channel_id=1, source_target_pairs={{8,0},{16,8},{24,16},{0,24},{9,1},{17,9},{25,17},{1,25},{10,2},{18... | collective-permute-start | bytes 368648 | tf_op jit(solution)/shard_map/ppermute | solution.py:380
  29.1 2.6 %copy-start.1 = (f32[5,1,3,8,256]{4,3,2,1,0:T(8,128)}, f32[5,1,3,8,256]{4,3,2,1,0:T(8,128)S(1)}, u32[]{:S(2)}) copy-start(f32[5,1,3,8,256]{4,3,2,1,0:T(8,128)S(1)} %collective-permute-done.3.refs_6_) | copy-start | bytes 368644
  30.3 1.4 %copy-start.2 = (f32[5,1,3,8,256]{4,3,2,1,0:T(8,128)}, f32[5,1,3,8,256]{4,3,2,1,0:T(8,128)S(1)}, u32[]{:S(2)}) copy-start(f32[5,1,3,8,256]{4,3,2,1,0:T(8,128)S(1)} %collective-permute-done.2.refs_5_) | copy-start | bytes 368644
  31.6 0.6 %copy-start.3 = (f32[5,1,3,8,256]{4,3,2,1,0:T(8,128)}, f32[5,1,3,8,256]{4,3,2,1,0:T(8,128)S(1)}, u32[]{:S(2)}) copy-start(f32[5,1,3,8,256]{4,3,2,1,0:T(8,128)S(1)} %collective-permute-done.1.refs_4_) | copy-start | bytes 368644
  38.5 6.8 %collective-permute-start.6 = (f32[5,1,3,8,128]{4,3,2,1,0:T(8,128)}, f32[5,1,3,8,128]{4,3,2,1,0:T(8,128)S(1)}, u32[]{:S(2)}, u32[]{:S(2)}) collective-permute-start(f32[5,1,3,8,128]{4,3,2,1,0:T(8,128)} %get-tuple-element.26.refs_3_), channel_id=1, source_target_pairs={{6,0},{0,2},{2,4},{4,6},{7,1},{1,3},{3,5},{5,7},{14,8},{8,10},{10,... | collective-permute-start | bytes 184328 | tf_op jit(solution)/shard_map/ppermute | solution.py:380
  40.1 7.8 %collective-permute-start.5 = (f32[5,1,3,8,128]{4,3,2,1,0:T(8,128)}, f32[5,1,3,8,128]{4,3,2,1,0:T(8,128)S(1)}, u32[]{:S(2)}, u32[]{:S(2)}) collective-permute-start(f32[5,1,3,8,128]{4,3,2,1,0:T(8,128)} %get-tuple-element.26.refs_3_), channel_id=1, source_target_pairs={{4,0},{6,2},{0,4},{2,6},{5,1},{7,3},{1,5},{3,7},{12,8},{14,10},{8,... | collective-permute-start | bytes 184328 | tf_op jit(solution)/shard_map/ppermute | solution.py:380
  42.6 5.5 %collective-permute-start.4 = (f32[5,1,3,8,128]{4,3,2,1,0:T(8,128)}, f32[5,1,3,8,128]{4,3,2,1,0:T(8,128)S(1)}, u32[]{:S(2)}, u32[]{:S(2)}) collective-permute-start(f32[5,1,3,8,128]{4,3,2,1,0:T(8,128)} %get-tuple-element.26.refs_3_), channel_id=1, source_target_pairs={{2,0},{4,2},{6,4},{0,6},{3,1},{5,3},{7,5},{1,7},{10,8},{12,10},{14... | collective-permute-start | bytes 184328 | tf_op jit(solution)/shard_map/ppermute | solution.py:380
  45.3 2.9 %copy-start.4 = (f32[5,1,3,8,128]{4,3,2,1,0:T(8,128)}, f32[5,1,3,8,128]{4,3,2,1,0:T(8,128)S(1)}, u32[]{:S(2)}) copy-start(f32[5,1,3,8,128]{4,3,2,1,0:T(8,128)S(1)} %collective-permute-done.6.refs_6_) | copy-start | bytes 184324
  47.9 0.6 %copy-start.5 = (f32[5,1,3,8,128]{4,3,2,1,0:T(8,128)}, f32[5,1,3,8,128]{4,3,2,1,0:T(8,128)S(1)}, u32[]{:S(2)}) copy-start(f32[5,1,3,8,128]{4,3,2,1,0:T(8,128)S(1)} %collective-permute-done.5.refs_5_) | copy-start | bytes 184324
  48.2 0.6 %copy-start.6 = (f32[5,1,3,8,128]{4,3,2,1,0:T(8,128)}, f32[5,1,3,8,128]{4,3,2,1,0:T(8,128)S(1)}, u32[]{:S(2)}) copy-start(f32[5,1,3,8,128]{4,3,2,1,0:T(8,128)S(1)} %collective-permute-done.4.refs_4_) | copy-start | bytes 184324

commit v13 on v11

--- a/solution.py
+++ b/solution.py
@@ -228,7 +228,7 @@
 def rad_kernel(*refs, axis_name, devices, pieces):
     it_ref, ia_ref, ib_ref = refs[:3]
     red_in = refs[3 : 3 + pieces]
-    mix_ref, cell_ref, visc_ref, edge_ref, ot_ref, red_ref, rows_ref = refs[3 + pieces :]
+    mix_ref, cell_ref, visc_ref, edge_ref, ra_ref, rb_ref, tt_ref, red_ref, rows_ref = refs[3 + pieces :]
     count = it_ref.shape[0]
     cells = it_ref.shape[3]
     place = lax.axis_index(axis_name)
@@ -244,17 +244,31 @@
         side = side.T
         target = (section_three[v] * scale).T
         length = side.shape[0]
-        il, iu, keep, _, _ = interior(side, side)
-        (it,) = pcr_levels(il, iu, [target * keep])
+        _, _, keep, _, _ = interior(side, side)
+        inner = target * keep
+        tt_ref[v, 0] = inner
+        t1 = jnp.sum(ra_ref[v, 0] / side * inner, axis=0, keepdims=True)
+        t2 = jnp.sum(rb_ref[v, 0] / side * inner, axis=0, keepdims=True)
         edge = edge_ref[v, 0]
-        n2 = length - 2
         (lf, le), (uf, ue), trow = interface_rows(
-            side, side, target[0:1], target[length - 1 :], it[1:2], it[n2 : n2 + 1],
+            side, side, target[0:1], target[length - 1 :], t1, t2,
             edge[0:1], edge[1:2], edge[2:3], edge[3:4],
         )
         lf = jnp.where(place == 0, jnp.zeros_like(lf), lf)
         ue = jnp.where(place == devices - 1, jnp.zeros_like(ue), ue)
         store_rows(red_ref, v, ((lf, le), (uf, ue), trow))
+
+
+def rad_solve_kernel(tt_ref, cell_ref, visc_ref, ot_ref, *, axis_name):
+    count = tt_ref.shape[0]
+    cells = cell_ref.shape[2]
+    visc = local_visc(visc_ref, axis_name, cells)
+    cell = cell_ref[0]
+    for v in range(count):
+        side, _ = rad_side(cell, visc, v)
+        side = side.T
+        il, iu, _, _, _ = interior(side, side)
+        (it,) = pcr_levels(il, iu, [tt_ref[v, 0]])
         ot_ref[v, 0] = it
 
 
@@ -316,7 +330,7 @@
     )(cell_rad, visc_rad)
 
 
-def rad_sweep(it, ia, ib, red_in, mix_mid, cell_rad, visc_rad, edges):
+def rad_sweep(it, ia, ib, red_in, mix_mid, cell_rad, visc_rad, edges, rad_a, rad_b):
     nv, nz, na, nr = it.shape
     big = pl.BlockSpec((nv, 1, na, nr), lambda z: (0, z, 0, 0))
     big_t = pl.BlockSpec((nv, 1, nr, na), lambda z: (0, z, 0, 0))
@@ -329,14 +343,29 @@
     out = jax.ShapeDtypeStruct((nv, nz, nr, na), it.dtype)
     pieces = len(red_in)
     kernel = functools.partial(rad_kernel, axis_name="rad", devices=lax.axis_size("rad"), pieces=pieces)
-    return pl.pallas_call(
+    targets, red_out = pl.pallas_call(
         kernel,
         grid=(nz,),
-        in_specs=[big, big, big] + [red_in_spec] * pieces + [mixs, cell, par, edge],
+        in_specs=[big, big, big] + [red_in_spec] * pieces + [mixs, cell, par, edge, big_t, big_t],
         out_specs=[big_t, red],
         out_shape=[out, jax.ShapeDtypeStruct((nv, nz, 3, 2, na), it.dtype)],
         scratch_shapes=[pltpu.VMEM((3, 2 * pieces, nr), it.dtype)],
-    )(it, ia, ib, *red_in, mix_mid, cell_rad, visc_rad, edges)
+    )(it, ia, ib, *red_in, mix_mid, cell_rad, visc_rad, edges, rad_a, rad_b)
+    return targets, red_out
+
+
+def rad_solve(targets, cell_rad, visc_rad):
+    nv, nz, nr, na = targets.shape
+    big_t = pl.BlockSpec((nv, 1, nr, na), lambda z: (0, z, 0, 0))
+    cell = pl.BlockSpec((1, na, nr), lambda z: (z, 0, 0))
+    par = pl.BlockSpec(visc_rad.shape, lambda z: (0, 0))
+    return pl.pallas_call(
+        functools.partial(rad_solve_kernel, axis_name="rad"),
+        grid=(nz,),
+        in_specs=[big_t, cell, par],
+        out_specs=big_t,
+        out_shape=jax.ShapeDtypeStruct(targets.shape, targets.dtype),
+    )(targets, cell_rad, visc_rad)
 
 
 def out_sweep(it, ia, ib, red_in, mix_out):
@@ -401,9 +430,10 @@
     rad_a, rad_b, rad_edges = rad_pre(cell_rad, visc_rad, flow_state.shape[0])
     it, ia, ib, red = az_sweep(flow_state, nb, source, cell_az, visc_az, beta_az, axial_diff, mix_in, rad_edges)
     red = gathered(red, "az")
-    it, red = rad_sweep(it, ia, ib, red, mix_mid, cell_rad, visc_rad, rad_edges)
+    targets, red = rad_sweep(it, ia, ib, red, mix_mid, cell_rad, visc_rad, rad_edges, rad_a, rad_b)
+    red = gathered(red, "rad")
+    it = rad_solve(targets, cell_rad, visc_rad)
     ia, ib = rad_a, rad_b
-    red = gathered(red, "rad")
     return out_sweep(it, ia, ib, red, mix_out)
 
 

time: 48 us -> 49.4 us (1.029)
  Pallas kernels: 27.6 us -> 31 us
  waiting for transfers between devices: 6.41 us -> 3.77 us
  local copies, waits for them, and re-layouts: 2.05 us -> 2.62 us
    pallas_call x0 -> x1, Pallas kernels: none -> 6.13 us  [rad_solve(): pl.pallas_call(functools.partial(rad_solve_kernel, axis_name='rad'), grid...]
    pallas_call x1, Pallas kernels: 6.43 us -> 3.66 us  [rad_sweep(): pl.pallas_call(kernel, grid=(nz,), in_specs=[big, big, big] + [red_in_spe...]
    ppermute x6, waiting for transfers between devices: 4.37 us -> 1.79 us  [gathered(): received.append(lax.ppermute(block, axis_name, pairs))]
    unnamed x14, local copies, waits for them, and re-layouts: 2.05 us -> 2.62 us
  transfers between devices with their start and end apart: 7 -> 7, of which waited for: 7 -> 4; matrix products, arithmetic and copies ran while one was open for 0% -> 0% of each run, Pallas kernels for 27% -> 39%
where the time goes in v13:
time: 49.4 us; the launch traced here: 49.1 us
  Pallas kernels  31 us (63%)
  starting transfers between devices  11.7 us (24%)
  waiting for transfers between devices  3.77 us (8%)
  local copies, waits for them, and re-layouts  2.62 us (5%)
    ppermute x6, starting transfers between devices, gathered(): received.append(lax.ppermute(block, axis_name, pairs))  8.75 us
    pallas_call x1, Pallas kernels, az_sweep(): pl.pallas_call(az_local_kernel, grid=grid, in_specs=[big, big, cell, par,...  6.92 us
    pallas_call x1, Pallas kernels, rad_solve(): pl.pallas_call(functools.partial(rad_solve_kernel, axis_name='rad'), grid...  6.13 us
    pallas_call x1, Pallas kernels, rad_pre(): pl.pallas_call(functools.partial(rad_pre_kernel, axis_name='rad'), grid=(...  6.04 us
    pallas_call x1, Pallas kernels, az_sweep(): pl.pallas_call(az_plane_kernel, grid=grid, in_specs=[big, cell, par, par,...  5.45 us
    pallas_call x1, Pallas kernels, rad_sweep(): pl.pallas_call(kernel, grid=(nz,), in_specs=[big, big, big] + [red_in_spe...  3.66 us
    ppermute x1, starting transfers between devices, neighbour_planes(): return lax.ppermute(block, axis_name, [(0, 1), (1, 0)])  2.97 us
    pallas_call x1, Pallas kernels, out_sweep(): pl.pallas_call(functools.partial(out_kernel, pieces=pieces), grid=(nz,),...  2.79 us
  transfers between devices with their start and end apart: 7, of which 4 were waited for; matrix products, arithmetic and copies ran while one was open for 0% of the time, Pallas kernels for 39%

profile of v13, /device:TPU:0, one launch (start us, length us, event | category | flops | bytes accessed | tf_op | source)
XLA Modules:
  0.0 49.1 jit_solution(3100874559988321722)
XLA Ops:
  0.0 3.0 %collective-permute-start = (f32[5,1,128,256]{3,2,1,0:T(8,128)}, f32[5,1,128,256]{3,2,1,0:T(8,128)S(1)}, u32[]{:S(2)}, u32[]{:S(2)}) collective-permute-start(f32[5,1,128,256]{3,2,1,0:T(8,128)} %fs_ref.1), channel_id=1, source_target_pairs={{0,1},{1,0},{2,3},{3,2},{4,5},{5,4},{6,7},{7,6},{8,9},{9,8},{10,11... | collective-permute-start | bytes 1966088 | tf_op jit(solution)/shard_map/ppermute | solution.py:400
  3.0 6.0 %shard_map.110 = (f32[5,1,256,128]{3,2,1,0:T(8,128)}, f32[5,1,256,128]{3,2,1,0:T(8,128)}, f32[5,1,4,128]{3,2,1,0:T(4,128)}) custom-call(f32[1,128,256]{2,1,0:T(8,128)} %cell_ref.7, f32[5,1024]{1,0:T(8,128)} %visc_ref.7), custom_call_target="tpu_custom_call" | custom-call | tf_op jit(solution)/shard_map/pallas_call | solution.py:324
  9.0 6.9 %shard_map.109 = (f32[5,1,128,256]{3,2,1,0:T(8,128)}, f32[5,1,128,256]{3,2,1,0:T(8,128)}, f32[5,1,128,256]{3,2,1,0:T(8,128)}, f32[5,1,6,256]{3,2,1,0:T(8,128)}) custom-call(f32[5,1,128,256]{3,2,1,0:T(8,128)} %fs_ref.1, f32[5,1,128,256]{3,2,1,0:T(8,128)} %src_ref.1, f32[1,128,256]{2,1,0:T(8,128)} %cell_ref.6, f32[5,256]{1,0:T(8,128)} %visc_ref.6, ...), custom_call_target="tpu_custom_call" | custom-call | tf_op jit(solution)/shard_map/pallas_call | solution.py:299
  15.9 2.0 %collective-permute-done.nb_ref = f32[5,1,128,256]{3,2,1,0:T(8,128)S(1)} collective-permute-done((f32[5,1,128,256]{3,2,1,0:T(8,128)}, f32[5,1,128,256]{3,2,1,0:T(8,128)S(1)}, u32[]{:S(2)}, u32[]{:S(2)}) %collective-permute-start) | collective-permute-done | bytes 655392 | tf_op jit(solution)/shard_map/ppermute | solution.py:400
  17.9 0.0 copy-start
  17.9 0.8 %copy-done = f32[5,1,128,256]{3,2,1,0:T(8,128)} copy-done((f32[5,1,128,256]{3,2,1,0:T(8,128)}, f32[5,1,128,256]{3,2,1,0:T(8,128)S(1)}, u32[]{:S(2)}) %copy-start) | copy-done | bytes 655384
  18.7 5.5 %shard_map.111 = (f32[5,1,128,256]{3,2,1,0:T(8,128)}, f32[5,1,3,2,256]{4,3,2,1,0:T(2,128)}) custom-call(f32[5,1,128,256]{3,2,1,0:T(8,128)} %copy-done, f32[1,128,256]{2,1,0:T(8,128)} %cell_ref.6, f32[5,256]{1,0:T(8,128)} %visc_ref.6, f32[5,256]{1,0:T(8,128)} %beta_ref.3, f32[5,256]{1,0:T(8,128)} %diff_ref.3, ...), custom_call_target="tpu_custom_call", output_to_operand_aliasing={{0}: (6, {})} | custom-call | tf_op jit(solution)/shard_map/pallas_call | solution.py:306
  24.2 0.1 collective-permute-start.3
  24.3 1.8 %collective-permute-start.2 = (f32[5,1,3,2,256]{4,3,2,1,0:T(2,128)}, f32[5,1,3,2,256]{4,3,2,1,0:T(2,128)S(1)}, u32[]{:S(2)}, u32[]{:S(2)}) collective-permute-start(f32[5,1,3,2,256]{4,3,2,1,0:T(2,128)} %get-tuple-element.22.refs_3_), channel_id=1, source_target_pairs={{16,0},{24,8},{0,16},{8,24},{17,1},{25,9},{1,17},{9,25},{18,2},{26... | collective-permute-start | bytes 92168 | tf_op jit(solution)/shard_map/ppermute | solution.py:393
  26.0 1.4 %collective-permute-start.1 = (f32[5,1,3,2,256]{4,3,2,1,0:T(2,128)}, f32[5,1,3,2,256]{4,3,2,1,0:T(2,128)S(1)}, u32[]{:S(2)}, u32[]{:S(2)}) collective-permute-start(f32[5,1,3,2,256]{4,3,2,1,0:T(2,128)} %get-tuple-element.22.refs_3_), channel_id=1, source_target_pairs={{8,0},{16,8},{24,16},{0,24},{9,1},{17,9},{25,17},{1,25},{10,2},{18... | collective-permute-start | bytes 92168 | tf_op jit(solution)/shard_map/ppermute | solution.py:393
  27.4 0.3 collective-permute-done.3.refs_6_
  27.8 0.0 copy-start.1
  27.8 0.7 %collective-permute-done.2.refs_5_ = f32[5,1,3,2,256]{4,3,2,1,0:T(2,128)S(1)} collective-permute-done((f32[5,1,3,2,256]{4,3,2,1,0:T(2,128)}, f32[5,1,3,2,256]{4,3,2,1,0:T(2,128)S(1)}, u32[]{:S(2)}, u32[]{:S(2)}) %collective-permute-start.2) | collective-permute-done | bytes 30752 | tf_op jit(solution)/shard_map/ppermute | solution.py:393
  28.4 0.0 copy-start.2
  28.4 0.8 %collective-permute-done.1.refs_4_ = f32[5,1,3,2,256]{4,3,2,1,0:T(2,128)S(1)} collective-permute-done((f32[5,1,3,2,256]{4,3,2,1,0:T(2,128)}, f32[5,1,3,2,256]{4,3,2,1,0:T(2,128)S(1)}, u32[]{:S(2)}, u32[]{:S(2)}) %collective-permute-start.1) | collective-permute-done | bytes 30752 | tf_op jit(solution)/shard_map/ppermute | solution.py:393
  29.2 0.0 copy-start.3
  29.2 0.0 copy-done.1
  29.2 0.0 copy-done.2
  29.2 0.6 %copy-done.3 = f32[5,1,3,2,256]{4,3,2,1,0:T(2,128)} copy-done((f32[5,1,3,2,256]{4,3,2,1,0:T(2,128)}, f32[5,1,3,2,256]{4,3,2,1,0:T(2,128)S(1)}, u32[]{:S(2)}) %copy-start.3) | copy-done | bytes 30744
  29.8 3.7 %shard_map.112 = (f32[5,1,256,128]{3,2,1,0:T(8,128)}, f32[5,1,3,2,128]{4,3,2,1,0:T(2,128)}) custom-call(f32[5,1,128,256]{3,2,1,0:T(8,128)} %get-tuple-element.19.refs_0_, f32[5,1,128,256]{3,2,1,0:T(8,128)} %get-tuple-element.20.refs_1_, f32[5,1,128,256]{3,2,1,0:T(8,128)} %get-tuple-element.21.refs_2_, f32[5,1,3,2,256]{4,3,2,1,0:T(2,128)} %get-tuple-element.22.refs_3_, ...), custom_call_target="tpu_custom_call" | custom-call | tf_op jit(solution)/shard_map/pallas_call | solution.py:346
  33.5 1.6 %collective-permute-start.6 = (f32[5,1,3,2,128]{4,3,2,1,0:T(2,128)}, f32[5,1,3,2,128]{4,3,2,1,0:T(2,128)S(1)}, u32[]{:S(2)}, u32[]{:S(2)}) collective-permute-start(f32[5,1,3,2,128]{4,3,2,1,0:T(2,128)} %get-tuple-element.26.refs_3_), channel_id=1, source_target_pairs={{6,0},{0,2},{2,4},{4,6},{7,1},{1,3},{3,5},{5,7},{14,8},{8,10},{10,... | collective-permute-start | bytes 46088 | tf_op jit(solution)/shard_map/ppermute | solution.py:393
  35.0 2.6 %collective-permute-start.5 = (f32[5,1,3,2,128]{4,3,2,1,0:T(2,128)}, f32[5,1,3,2,128]{4,3,2,1,0:T(2,128)S(1)}, u32[]{:S(2)}, u32[]{:S(2)}) collective-permute-start(f32[5,1,3,2,128]{4,3,2,1,0:T(2,128)} %get-tuple-element.26.refs_3_), channel_id=1, source_target_pairs={{4,0},{6,2},{0,4},{2,6},{5,1},{7,3},{1,5},{3,7},{12,8},{14,10},{8,... | collective-permute-start | bytes 46088 | tf_op jit(solution)/shard_map/ppermute | solution.py:393
  37.7 1.3 %collective-permute-start.4 = (f32[5,1,3,2,128]{4,3,2,1,0:T(2,128)}, f32[5,1,3,2,128]{4,3,2,1,0:T(2,128)S(1)}, u32[]{:S(2)}, u32[]{:S(2)}) collective-permute-start(f32[5,1,3,2,128]{4,3,2,1,0:T(2,128)} %get-tuple-element.26.refs_3_), channel_id=1, source_target_pairs={{2,0},{4,2},{6,4},{0,6},{3,1},{5,3},{7,5},{1,7},{10,8},{12,10},{14... | collective-permute-start | bytes 46088 | tf_op jit(solution)/shard_map/ppermute | solution.py:393
  39.0 6.1 %shard_map.113.refs_0_ = f32[5,1,256,128]{3,2,1,0:T(8,128)} custom-call(f32[5,1,256,128]{3,2,1,0:T(8,128)} %get-tuple-element.25.tt_ref, f32[1,128,256]{2,1,0:T(8,128)} %cell_ref.7, f32[5,1024]{1,0:T(8,128)} %visc_ref.7), custom_call_target="tpu_custom_call" | custom-call | tf_op jit(solution)/shard_map/pallas_call | solution.py:362
  45.1 0.0 collective-permute-done.6.refs_6_
  45.1 0.0 copy-start.4
  45.1 0.0 collective-permute-done.5.refs_5_
  45.1 0.0 copy-start.5
  45.2 0.0 collective-permute-done.4.refs_4_
  45.2 0.6 %copy-done.4 = f32[5,1,3,2,128]{4,3,2,1,0:T(2,128)} copy-done((f32[5,1,3,2,128]{4,3,2,1,0:T(2,128)}, f32[5,1,3,2,128]{4,3,2,1,0:T(2,128)S(1)}, u32[]{:S(2)}) %copy-start.4) | copy-done | bytes 15384
  45.7 0.0 copy-done.5
  45.8 0.0 copy-start.6
  45.8 0.6 %copy-done.6 = f32[5,1,3,2,128]{4,3,2,1,0:T(2,128)} copy-done((f32[5,1,3,2,128]{4,3,2,1,0:T(2,128)}, f32[5,1,3,2,128]{4,3,2,1,0:T(2,128)S(1)}, u32[]{:S(2)}) %copy-start.6) | copy-done | bytes 15384
  46.3 2.8 %shard_map.114 = f32[5,1,128,256]{3,2,1,0:T(8,128)} custom-call(f32[5,1,256,128]{3,2,1,0:T(8,128)} %shard_map.113.refs_0_, f32[5,1,256,128]{3,2,1,0:T(8,128)} %get-tuple-element.23.refs_11_.refs_1_, f32[5,1,256,128]{3,2,1,0:T(8,128)} %get-tuple-element.24.refs_12_.refs_2_, f32[5,1,3,2,128]{4,3,2,1,0:T(2,128)} %get-tuple-element.26.refs_3_, ...), custom_call_target="tpu_custom_call" | custom-call | tf_op jit(solution)/shard_map/pallas_call | solution.py:378
Async XLA Ops:
  0.0 17.9 %collective-permute-start = (f32[5,1,128,256]{3,2,1,0:T(8,128)}, f32[5,1,128,256]{3,2,1,0:T(8,128)S(1)}, u32[]{:S(2)}, u32[]{:S(2)}) collective-permute-start(f32[5,1,128,256]{3,2,1,0:T(8,128)} %fs_ref.1), channel_id=1, source_target_pairs={{0,1},{1,0},{2,3},{3,2},{4,5},{5,4},{6,7},{7,6},{8,9},{9,8},{10,11... | collective-permute-start | bytes 1966088 | tf_op jit(solution)/shard_map/ppermute | solution.py:400
  17.9 0.8 %copy-start = (f32[5,1,128,256]{3,2,1,0:T(8,128)}, f32[5,1,128,256]{3,2,1,0:T(8,128)S(1)}, u32[]{:S(2)}) copy-start(f32[5,1,128,256]{3,2,1,0:T(8,128)S(1)} %collective-permute-done.nb_ref) | copy-start | bytes 1966084
  24.2 3.6 %collective-permute-start.3 = (f32[5,1,3,2,256]{4,3,2,1,0:T(2,128)}, f32[5,1,3,2,256]{4,3,2,1,0:T(2,128)S(1)}, u32[]{:S(2)}, u32[]{:S(2)}) collective-permute-start(f32[5,1,3,2,256]{4,3,2,1,0:T(2,128)} %get-tuple-element.22.refs_3_), channel_id=1, source_target_pairs={{24,0},{0,8},{8,16},{16,24},{25,1},{1,9},{9,17},{17,25},{26,2},{2,... | collective-permute-start | bytes 92168 | tf_op jit(solution)/shard_map/ppermute | solution.py:393
  24.3 4.2 %collective-permute-start.2 = (f32[5,1,3,2,256]{4,3,2,1,0:T(2,128)}, f32[5,1,3,2,256]{4,3,2,1,0:T(2,128)S(1)}, u32[]{:S(2)}, u32[]{:S(2)}) collective-permute-start(f32[5,1,3,2,256]{4,3,2,1,0:T(2,128)} %get-tuple-element.22.refs_3_), channel_id=1, source_target_pairs={{16,0},{24,8},{0,16},{8,24},{17,1},{25,9},{1,17},{9,25},{18,2},{26... | collective-permute-start | bytes 92168 | tf_op jit(solution)/shard_map/ppermute | solution.py:393
  26.0 3.2 %collective-permute-start.1 = (f32[5,1,3,2,256]{4,3,2,1,0:T(2,128)}, f32[5,1,3,2,256]{4,3,2,1,0:T(2,128)S(1)}, u32[]{:S(2)}, u32[]{:S(2)}) collective-permute-start(f32[5,1,3,2,256]{4,3,2,1,0:T(2,128)} %get-tuple-element.22.refs_3_), channel_id=1, source_target_pairs={{8,0},{16,8},{24,16},{0,24},{9,1},{17,9},{25,17},{1,25},{10,2},{18... | collective-permute-start | bytes 92168 | tf_op jit(solution)/shard_map/ppermute | solution.py:393
  27.8 1.4 %copy-start.1 = (f32[5,1,3,2,256]{4,3,2,1,0:T(2,128)}, f32[5,1,3,2,256]{4,3,2,1,0:T(2,128)S(1)}, u32[]{:S(2)}) copy-start(f32[5,1,3,2,256]{4,3,2,1,0:T(2,128)S(1)} %collective-permute-done.3.refs_6_) | copy-start | bytes 92164
  28.4 0.8 %copy-start.2 = (f32[5,1,3,2,256]{4,3,2,1,0:T(2,128)}, f32[5,1,3,2,256]{4,3,2,1,0:T(2,128)S(1)}, u32[]{:S(2)}) copy-start(f32[5,1,3,2,256]{4,3,2,1,0:T(2,128)S(1)} %collective-permute-done.2.refs_5_) | copy-start | bytes 92164
  29.2 0.6 %copy-start.3 = (f32[5,1,3,2,256]{4,3,2,1,0:T(2,128)}, f32[5,1,3,2,256]{4,3,2,1,0:T(2,128)S(1)}, u32[]{:S(2)}) copy-start(f32[5,1,3,2,256]{4,3,2,1,0:T(2,128)S(1)} %collective-permute-done.1.refs_4_) | copy-start | bytes 92164
  33.5 11.7 %collective-permute-start.6 = (f32[5,1,3,2,128]{4,3,2,1,0:T(2,128)}, f32[5,1,3,2,128]{4,3,2,1,0:T(2,128)S(1)}, u32[]{:S(2)}, u32[]{:S(2)}) collective-permute-start(f32[5,1,3,2,128]{4,3,2,1,0:T(2,128)} %get-tuple-element.26.refs_3_), channel_id=1, source_target_pairs={{6,0},{0,2},{2,4},{4,6},{7,1},{1,3},{3,5},{5,7},{14,8},{8,10},{10,... | collective-permute-start | bytes 46088 | tf_op jit(solution)/shard_map/ppermute | solution.py:393
  35.0 10.1 %collective-permute-start.5 = (f32[5,1,3,2,128]{4,3,2,1,0:T(2,128)}, f32[5,1,3,2,128]{4,3,2,1,0:T(2,128)S(1)}, u32[]{:S(2)}, u32[]{:S(2)}) collective-permute-start(f32[5,1,3,2,128]{4,3,2,1,0:T(2,128)} %get-tuple-element.26.refs_3_), channel_id=1, source_target_pairs={{4,0},{6,2},{0,4},{2,6},{5,1},{7,3},{1,5},{3,7},{12,8},{14,10},{8,... | collective-permute-start | bytes 46088 | tf_op jit(solution)/shard_map/ppermute | solution.py:393
  37.7 7.5 %collective-permute-start.4 = (f32[5,1,3,2,128]{4,3,2,1,0:T(2,128)}, f32[5,1,3,2,128]{4,3,2,1,0:T(2,128)S(1)}, u32[]{:S(2)}, u32[]{:S(2)}) collective-permute-start(f32[5,1,3,2,128]{4,3,2,1,0:T(2,128)} %get-tuple-element.26.refs_3_), channel_id=1, source_target_pairs={{2,0},{4,2},{6,4},{0,6},{3,1},{5,3},{7,5},{1,7},{10,8},{12,10},{14... | collective-permute-start | bytes 46088 | tf_op jit(solution)/shard_map/ppermute | solution.py:393
  45.1 0.6 %copy-start.4 = (f32[5,1,3,2,128]{4,3,2,1,0:T(2,128)}, f32[5,1,3,2,128]{4,3,2,1,0:T(2,128)S(1)}, u32[]{:S(2)}) copy-start(f32[5,1,3,2,128]{4,3,2,1,0:T(2,128)S(1)} %collective-permute-done.6.refs_6_) | copy-start | bytes 46084
  45.1 0.6 %copy-start.5 = (f32[5,1,3,2,128]{4,3,2,1,0:T(2,128)}, f32[5,1,3,2,128]{4,3,2,1,0:T(2,128)S(1)}, u32[]{:S(2)}) copy-start(f32[5,1,3,2,128]{4,3,2,1,0:T(2,128)S(1)} %collective-permute-done.5.refs_5_) | copy-start | bytes 46084
  45.8 0.6 %copy-start.6 = (f32[5,1,3,2,128]{4,3,2,1,0:T(2,128)}, f32[5,1,3,2,128]{4,3,2,1,0:T(2,128)S(1)}, u32[]{:S(2)}) copy-start(f32[5,1,3,2,128]{4,3,2,1,0:T(2,128)S(1)} %collective-permute-done.4.refs_4_) | copy-start | bytes 46084

commit v14 on v13

--- a/solution.py
+++ b/solution.py
@@ -207,7 +207,7 @@
     return visc_ref[:, pl.ds(pl.multiple_of(place * cells, cells), cells)]
 
 
-def rad_pre_kernel(cell_ref, visc_ref, oa_ref, ob_ref, edge_ref, *, axis_name):
+def rad_pre_kernel(cell_ref, visc_ref, oa_ref, ob_ref, os_ref, edge_ref, *, axis_name):
     count = oa_ref.shape[0]
     cells = cell_ref.shape[2]
     visc = local_visc(visc_ref, axis_name, cells)
@@ -215,6 +215,7 @@
     for v in range(count):
         side, _ = rad_side(cell, visc, v)
         side = side.T
+        os_ref[v, 0] = side
         length = side.shape[0]
         il, iu, _, a_init, b_init = interior(side, side)
         ia, ib = pcr_levels(il, iu, [a_init, b_init])
@@ -228,7 +229,7 @@
 def rad_kernel(*refs, axis_name, devices, pieces):
     it_ref, ia_ref, ib_ref = refs[:3]
     red_in = refs[3 : 3 + pieces]
-    mix_ref, cell_ref, visc_ref, edge_ref, ra_ref, rb_ref, tt_ref, red_ref, rows_ref = refs[3 + pieces :]
+    mix_ref, cell_ref, visc_ref, edge_ref, ra_ref, rb_ref, side_ref, tt_ref, red_ref, rows_ref = refs[3 + pieces :]
     count = it_ref.shape[0]
     cells = it_ref.shape[3]
     place = lax.axis_index(axis_name)
@@ -240,8 +241,8 @@
     section_three = mixed(mix_ref, solved)
     cell = cell_ref[0]
     for v in range(count):
-        side, scale = rad_side(cell, visc, v)
-        side = side.T
+        _, scale = rad_side(cell, visc, v)
+        side = side_ref[v, 0]
         target = (section_three[v] * scale).T
         length = side.shape[0]
         _, _, keep, _, _ = interior(side, side)
@@ -259,14 +260,10 @@
         store_rows(red_ref, v, ((lf, le), (uf, ue), trow))
 
 
-def rad_solve_kernel(tt_ref, cell_ref, visc_ref, ot_ref, *, axis_name):
+def rad_solve_kernel(tt_ref, side_ref, ot_ref):
     count = tt_ref.shape[0]
-    cells = cell_ref.shape[2]
-    visc = local_visc(visc_ref, axis_name, cells)
-    cell = cell_ref[0]
     for v in range(count):
-        side, _ = rad_side(cell, visc, v)
-        side = side.T
+        side = side_ref[v, 0]
         il, iu, _, _, _ = interior(side, side)
         (it,) = pcr_levels(il, iu, [tt_ref[v, 0]])
         ot_ref[v, 0] = it
@@ -325,12 +322,12 @@
         functools.partial(rad_pre_kernel, axis_name="rad"),
         grid=(nz,),
         in_specs=[cell, par],
-        out_specs=[big_t, big_t, edge],
-        out_shape=[out, out, jax.ShapeDtypeStruct((nv, nz, 4, na), cell_rad.dtype)],
+        out_specs=[big_t, big_t, big_t, edge],
+        out_shape=[out, out, out, jax.ShapeDtypeStruct((nv, nz, 4, na), cell_rad.dtype)],
     )(cell_rad, visc_rad)
 
 
-def rad_sweep(it, ia, ib, red_in, mix_mid, cell_rad, visc_rad, edges, rad_a, rad_b):
+def rad_sweep(it, ia, ib, red_in, mix_mid, cell_rad, visc_rad, edges, rad_a, rad_b, sides):
     nv, nz, na, nr = it.shape
     big = pl.BlockSpec((nv, 1, na, nr), lambda z: (0, z, 0, 0))
     big_t = pl.BlockSpec((nv, 1, nr, na), lambda z: (0, z, 0, 0))
@@ -346,26 +343,24 @@
     targets, red_out = pl.pallas_call(
         kernel,
         grid=(nz,),
-        in_specs=[big, big, big] + [red_in_spec] * pieces + [mixs, cell, par, edge, big_t, big_t],
+        in_specs=[big, big, big] + [red_in_spec] * pieces + [mixs, cell, par, edge, big_t, big_t, big_t],
         out_specs=[big_t, red],
         out_shape=[out, jax.ShapeDtypeStruct((nv, nz, 3, 2, na), it.dtype)],
         scratch_shapes=[pltpu.VMEM((3, 2 * pieces, nr), it.dtype)],
-    )(it, ia, ib, *red_in, mix_mid, cell_rad, visc_rad, edges, rad_a, rad_b)
+    )(it, ia, ib, *red_in, mix_mid, cell_rad, visc_rad, edges, rad_a, rad_b, sides)
     return targets, red_out
 
 
-def rad_solve(targets, cell_rad, visc_rad):
+def rad_solve(targets, sides):
     nv, nz, nr, na = targets.shape
     big_t = pl.BlockSpec((nv, 1, nr, na), lambda z: (0, z, 0, 0))
-    cell = pl.BlockSpec((1, na, nr), lambda z: (z, 0, 0))
-    par = pl.BlockSpec(visc_rad.shape, lambda z: (0, 0))
     return pl.pallas_call(
-        functools.partial(rad_solve_kernel, axis_name="rad"),
+        rad_solve_kernel,
         grid=(nz,),
-        in_specs=[big_t, cell, par],
+        in_specs=[big_t, big_t],
         out_specs=big_t,
         out_shape=jax.ShapeDtypeStruct(targets.shape, targets.dtype),
-    )(targets, cell_rad, visc_rad)
+    )(targets, sides)
 
 
 def out_sweep(it, ia, ib, red_in, mix_out):
@@ -427,12 +422,12 @@
 ):
     rad_cells = flow_state.shape[3]
     nb = neighbour_planes(flow_state, "ax")
-    rad_a, rad_b, rad_edges = rad_pre(cell_rad, visc_rad, flow_state.shape[0])
+    rad_a, rad_b, sides, rad_edges = rad_pre(cell_rad, visc_rad, flow_state.shape[0])
     it, ia, ib, red = az_sweep(flow_state, nb, source, cell_az, visc_az, beta_az, axial_diff, mix_in, rad_edges)
     red = gathered(red, "az")
-    targets, red = rad_sweep(it, ia, ib, red, mix_mid, cell_rad, visc_rad, rad_edges, rad_a, rad_b)
+    targets, red = rad_sweep(it, ia, ib, red, mix_mid, cell_rad, visc_rad, rad_edges, rad_a, rad_b, sides)
     red = gathered(red, "rad")
-    it = rad_solve(targets, cell_rad, visc_rad)
+    it = rad_solve(targets, sides)
     ia, ib = rad_a, rad_b
     return out_sweep(it, ia, ib, red, mix_out)
 

time: 49.4 us -> 49 us (level)
  transfers between devices with their start and end apart: 7 -> 7, of which waited for: 4 -> 4; matrix products, arithmetic and copies ran while one was open for 0% -> 0% of each run, Pallas kernels for 39% -> 38%
where the time goes in v14:
time: 49 us; the launch traced here: 48.8 us
  Pallas kernels  30.6 us (62%)
  starting transfers between devices  11.7 us (24%)
  waiting for transfers between devices  3.78 us (8%)
  local copies, waits for them, and re-layouts  2.62 us (5%)
    ppermute x6, starting transfers between devices, gathered(): received.append(lax.ppermute(block, axis_name, pairs))  8.74 us
    pallas_call x1, Pallas kernels, az_sweep(): pl.pallas_call(az_local_kernel, grid=grid, in_specs=[big, big, cell, par,...  6.86 us
    pallas_call x1, Pallas kernels, rad_pre(): pl.pallas_call(functools.partial(rad_pre_kernel, axis_name='rad'), grid=(...  6.09 us
    pallas_call x1, Pallas kernels, rad_solve(): pl.pallas_call(rad_solve_kernel, grid=(nz,), in_specs=[big_t, big_t], out...  5.65 us
    pallas_call x1, Pallas kernels, az_sweep(): pl.pallas_call(az_plane_kernel, grid=grid, in_specs=[big, cell, par, par,...  5.47 us
    pallas_call x1, Pallas kernels, rad_sweep(): pl.pallas_call(kernel, grid=(nz,), in_specs=[big, big, big] + [red_in_spe...  3.76 us
    ppermute x1, starting transfers between devices, neighbour_planes(): return lax.ppermute(block, axis_name, [(0, 1), (1, 0)])  2.97 us
    pallas_call x1, Pallas kernels, out_sweep(): pl.pallas_call(functools.partial(out_kernel, pieces=pieces), grid=(nz,),...  2.79 us
  transfers between devices with their start and end apart: 7, of which 4 were waited for; matrix products, arithmetic and copies ran while one was open for 0% of the time, Pallas kernels for 38%

profile of v14, /device:TPU:0, one launch (start us, length us, event | category | flops | bytes accessed | tf_op | source)
XLA Modules:
  0.0 48.8 jit_solution(12225992453631888133)
XLA Ops:
  0.0 3.0 %collective-permute-start = (f32[5,1,128,256]{3,2,1,0:T(8,128)}, f32[5,1,128,256]{3,2,1,0:T(8,128)S(1)}, u32[]{:S(2)}, u32[]{:S(2)}) collective-permute-start(f32[5,1,128,256]{3,2,1,0:T(8,128)} %fs_ref.1), channel_id=1, source_target_pairs={{0,1},{1,0},{2,3},{3,2},{4,5},{5,4},{6,7},{7,6},{8,9},{9,8},{10,11... | collective-permute-start | bytes 1966088 | tf_op jit(solution)/shard_map/ppermute | solution.py:395
  3.0 6.1 %shard_map.110 = (f32[5,1,256,128]{3,2,1,0:T(8,128)}, f32[5,1,256,128]{3,2,1,0:T(8,128)}, f32[5,1,256,128]{3,2,1,0:T(8,128)}, f32[5,1,4,128]{3,2,1,0:T(4,128)}) custom-call(f32[1,128,256]{2,1,0:T(8,128)} %refs_8_.1, f32[5,1024]{1,0:T(8,128)} %refs_9_.1), custom_call_target="tpu_custom_call" | custom-call | tf_op jit(solution)/shard_map/pallas_call | solution.py:321
  9.1 6.9 %shard_map.109 = (f32[5,1,128,256]{3,2,1,0:T(8,128)}, f32[5,1,128,256]{3,2,1,0:T(8,128)}, f32[5,1,128,256]{3,2,1,0:T(8,128)}, f32[5,1,6,256]{3,2,1,0:T(8,128)}) custom-call(f32[5,1,128,256]{3,2,1,0:T(8,128)} %fs_ref.1, f32[5,1,128,256]{3,2,1,0:T(8,128)} %src_ref.1, f32[1,128,256]{2,1,0:T(8,128)} %cell_ref.5, f32[5,256]{1,0:T(8,128)} %visc_ref.5, ...), custom_call_target="tpu_custom_call" | custom-call | tf_op jit(solution)/shard_map/pallas_call | solution.py:296
  15.9 2.0 %collective-permute-done.nb_ref = f32[5,1,128,256]{3,2,1,0:T(8,128)S(1)} collective-permute-done((f32[5,1,128,256]{3,2,1,0:T(8,128)}, f32[5,1,128,256]{3,2,1,0:T(8,128)S(1)}, u32[]{:S(2)}, u32[]{:S(2)}) %collective-permute-start) | collective-permute-done | bytes 655392 | tf_op jit(solution)/shard_map/ppermute | solution.py:395
  17.9 0.0 copy-start
  17.9 0.8 %copy-done = f32[5,1,128,256]{3,2,1,0:T(8,128)} copy-done((f32[5,1,128,256]{3,2,1,0:T(8,128)}, f32[5,1,128,256]{3,2,1,0:T(8,128)S(1)}, u32[]{:S(2)}) %copy-start) | copy-done | bytes 655384
  18.7 5.5 %shard_map.111 = (f32[5,1,128,256]{3,2,1,0:T(8,128)}, f32[5,1,3,2,256]{4,3,2,1,0:T(2,128)}) custom-call(f32[5,1,128,256]{3,2,1,0:T(8,128)} %copy-done, f32[1,128,256]{2,1,0:T(8,128)} %cell_ref.5, f32[5,256]{1,0:T(8,128)} %visc_ref.5, f32[5,256]{1,0:T(8,128)} %beta_ref.3, f32[5,256]{1,0:T(8,128)} %diff_ref.3, ...), custom_call_target="tpu_custom_call", output_to_operand_aliasing={{0}: (6, {})} | custom-call | tf_op jit(solution)/shard_map/pallas_call | solution.py:303
  24.2 0.0 collective-permute-start.3
  24.3 1.8 %collective-permute-start.2 = (f32[5,1,3,2,256]{4,3,2,1,0:T(2,128)}, f32[5,1,3,2,256]{4,3,2,1,0:T(2,128)S(1)}, u32[]{:S(2)}, u32[]{:S(2)}) collective-permute-start(f32[5,1,3,2,256]{4,3,2,1,0:T(2,128)} %get-tuple-element.23.refs_3_), channel_id=1, source_target_pairs={{16,0},{24,8},{0,16},{8,24},{17,1},{25,9},{1,17},{9,25},{18,2},{26... | collective-permute-start | bytes 92168 | tf_op jit(solution)/shard_map/ppermute | solution.py:388
  26.0 1.4 %collective-permute-start.1 = (f32[5,1,3,2,256]{4,3,2,1,0:T(2,128)}, f32[5,1,3,2,256]{4,3,2,1,0:T(2,128)S(1)}, u32[]{:S(2)}, u32[]{:S(2)}) collective-permute-start(f32[5,1,3,2,256]{4,3,2,1,0:T(2,128)} %get-tuple-element.23.refs_3_), channel_id=1, source_target_pairs={{8,0},{16,8},{24,16},{0,24},{9,1},{17,9},{25,17},{1,25},{10,2},{18... | collective-permute-start | bytes 92168 | tf_op jit(solution)/shard_map/ppermute | solution.py:388
  27.4 0.3 collective-permute-done.3.refs_6_
  27.8 0.0 copy-start.1
  27.8 0.7 %collective-permute-done.2.refs_5_ = f32[5,1,3,2,256]{4,3,2,1,0:T(2,128)S(1)} collective-permute-done((f32[5,1,3,2,256]{4,3,2,1,0:T(2,128)}, f32[5,1,3,2,256]{4,3,2,1,0:T(2,128)S(1)}, u32[]{:S(2)}, u32[]{:S(2)}) %collective-permute-start.2) | collective-permute-done | bytes 30752 | tf_op jit(solution)/shard_map/ppermute | solution.py:388
  28.4 0.0 copy-start.2
  28.4 0.8 %collective-permute-done.1.refs_4_ = f32[5,1,3,2,256]{4,3,2,1,0:T(2,128)S(1)} collective-permute-done((f32[5,1,3,2,256]{4,3,2,1,0:T(2,128)}, f32[5,1,3,2,256]{4,3,2,1,0:T(2,128)S(1)}, u32[]{:S(2)}, u32[]{:S(2)}) %collective-permute-start.1) | collective-permute-done | bytes 30752 | tf_op jit(solution)/shard_map/ppermute | solution.py:388
  29.2 0.0 copy-start.3
  29.2 0.0 copy-done.1
  29.2 0.0 copy-done.2
  29.2 0.6 %copy-done.3 = f32[5,1,3,2,256]{4,3,2,1,0:T(2,128)} copy-done((f32[5,1,3,2,256]{4,3,2,1,0:T(2,128)}, f32[5,1,3,2,256]{4,3,2,1,0:T(2,128)S(1)}, u32[]{:S(2)}) %copy-start.3) | copy-done | bytes 30744
  29.8 3.8 %shard_map.112 = (f32[5,1,256,128]{3,2,1,0:T(8,128)}, f32[5,1,3,2,128]{4,3,2,1,0:T(2,128)}) custom-call(f32[5,1,128,256]{3,2,1,0:T(8,128)} %get-tuple-element.20.refs_0_, f32[5,1,128,256]{3,2,1,0:T(8,128)} %get-tuple-element.21.refs_1_, f32[5,1,128,256]{3,2,1,0:T(8,128)} %get-tuple-element.22.refs_2_, f32[5,1,3,2,256]{4,3,2,1,0:T(2,128)} %get-tuple-element.23.refs_3_, ...), custom_call_target="tpu_custom_call" | custom-call | tf_op jit(solution)/shard_map/pallas_call | solution.py:343
  33.6 1.6 %collective-permute-start.6 = (f32[5,1,3,2,128]{4,3,2,1,0:T(2,128)}, f32[5,1,3,2,128]{4,3,2,1,0:T(2,128)S(1)}, u32[]{:S(2)}, u32[]{:S(2)}) collective-permute-start(f32[5,1,3,2,128]{4,3,2,1,0:T(2,128)} %get-tuple-element.28.refs_3_), channel_id=1, source_target_pairs={{6,0},{0,2},{2,4},{4,6},{7,1},{1,3},{3,5},{5,7},{14,8},{8,10},{10,... | collective-permute-start | bytes 46088 | tf_op jit(solution)/shard_map/ppermute | solution.py:388
  35.2 2.6 %collective-permute-start.5 = (f32[5,1,3,2,128]{4,3,2,1,0:T(2,128)}, f32[5,1,3,2,128]{4,3,2,1,0:T(2,128)S(1)}, u32[]{:S(2)}, u32[]{:S(2)}) collective-permute-start(f32[5,1,3,2,128]{4,3,2,1,0:T(2,128)} %get-tuple-element.28.refs_3_), channel_id=1, source_target_pairs={{4,0},{6,2},{0,4},{2,6},{5,1},{7,3},{1,5},{3,7},{12,8},{14,10},{8,... | collective-permute-start | bytes 46088 | tf_op jit(solution)/shard_map/ppermute | solution.py:388
  37.8 1.4 %collective-permute-start.4 = (f32[5,1,3,2,128]{4,3,2,1,0:T(2,128)}, f32[5,1,3,2,128]{4,3,2,1,0:T(2,128)S(1)}, u32[]{:S(2)}, u32[]{:S(2)}) collective-permute-start(f32[5,1,3,2,128]{4,3,2,1,0:T(2,128)} %get-tuple-element.28.refs_3_), channel_id=1, source_target_pairs={{2,0},{4,2},{6,4},{0,6},{3,1},{5,3},{7,5},{1,7},{10,8},{12,10},{14... | collective-permute-start | bytes 46088 | tf_op jit(solution)/shard_map/ppermute | solution.py:388
  39.1 5.6 %shard_map.113.refs_0_ = f32[5,1,256,128]{3,2,1,0:T(8,128)} custom-call(f32[5,1,256,128]{3,2,1,0:T(8,128)} %get-tuple-element.27.tt_ref, f32[5,1,256,128]{3,2,1,0:T(8,128)} %get-tuple-element.26.refs_13_.side_ref), custom_call_target="tpu_custom_call" | custom-call | tf_op jit(solution)/shard_map/pallas_call | solution.py:357
  44.8 0.0 collective-permute-done.6.refs_6_
  44.8 0.0 copy-start.4
  44.8 0.0 collective-permute-done.5.refs_5_
  44.8 0.0 copy-start.5
  44.8 0.0 collective-permute-done.4.refs_4_
  44.8 0.6 %copy-done.4 = f32[5,1,3,2,128]{4,3,2,1,0:T(2,128)} copy-done((f32[5,1,3,2,128]{4,3,2,1,0:T(2,128)}, f32[5,1,3,2,128]{4,3,2,1,0:T(2,128)S(1)}, u32[]{:S(2)}) %copy-start.4) | copy-done | bytes 15384
  45.4 0.0 copy-done.5
  45.4 0.0 copy-start.6
  45.4 0.6 %copy-done.6 = f32[5,1,3,2,128]{4,3,2,1,0:T(2,128)} copy-done((f32[5,1,3,2,128]{4,3,2,1,0:T(2,128)}, f32[5,1,3,2,128]{4,3,2,1,0:T(2,128)S(1)}, u32[]{:S(2)}) %copy-start.6) | copy-done | bytes 15384
  46.0 2.8 %shard_map.114 = f32[5,1,128,256]{3,2,1,0:T(8,128)} custom-call(f32[5,1,256,128]{3,2,1,0:T(8,128)} %shard_map.113.refs_0_, f32[5,1,256,128]{3,2,1,0:T(8,128)} %get-tuple-element.24.refs_11_.refs_1_, f32[5,1,256,128]{3,2,1,0:T(8,128)} %get-tuple-element.25.refs_12_.refs_2_, f32[5,1,3,2,128]{4,3,2,1,0:T(2,128)} %get-tuple-element.28.refs_3_, ...), custom_call_target="tpu_custom_call" | custom-call | tf_op jit(solution)/shard_map/pallas_call | solution.py:373
Async XLA Ops:
  0.0 17.9 %collective-permute-start = (f32[5,1,128,256]{3,2,1,0:T(8,128)}, f32[5,1,128,256]{3,2,1,0:T(8,128)S(1)}, u32[]{:S(2)}, u32[]{:S(2)}) collective-permute-start(f32[5,1,128,256]{3,2,1,0:T(8,128)} %fs_ref.1), channel_id=1, source_target_pairs={{0,1},{1,0},{2,3},{3,2},{4,5},{5,4},{6,7},{7,6},{8,9},{9,8},{10,11... | collective-permute-start | bytes 1966088 | tf_op jit(solution)/shard_map/ppermute | solution.py:395
  17.9 0.8 %copy-start = (f32[5,1,128,256]{3,2,1,0:T(8,128)}, f32[5,1,128,256]{3,2,1,0:T(8,128)S(1)}, u32[]{:S(2)}) copy-start(f32[5,1,128,256]{3,2,1,0:T(8,128)S(1)} %collective-permute-done.nb_ref) | copy-start | bytes 1966084
  24.2 3.6 %collective-permute-start.3 = (f32[5,1,3,2,256]{4,3,2,1,0:T(2,128)}, f32[5,1,3,2,256]{4,3,2,1,0:T(2,128)S(1)}, u32[]{:S(2)}, u32[]{:S(2)}) collective-permute-start(f32[5,1,3,2,256]{4,3,2,1,0:T(2,128)} %get-tuple-element.23.refs_3_), channel_id=1, source_target_pairs={{24,0},{0,8},{8,16},{16,24},{25,1},{1,9},{9,17},{17,25},{26,2},{2,... | collective-permute-start | bytes 92168 | tf_op jit(solution)/shard_map/ppermute | solution.py:388
  24.3 4.2 %collective-permute-start.2 = (f32[5,1,3,2,256]{4,3,2,1,0:T(2,128)}, f32[5,1,3,2,256]{4,3,2,1,0:T(2,128)S(1)}, u32[]{:S(2)}, u32[]{:S(2)}) collective-permute-start(f32[5,1,3,2,256]{4,3,2,1,0:T(2,128)} %get-tuple-element.23.refs_3_), channel_id=1, source_target_pairs={{16,0},{24,8},{0,16},{8,24},{17,1},{25,9},{1,17},{9,25},{18,2},{26... | collective-permute-start | bytes 92168 | tf_op jit(solution)/shard_map/ppermute | solution.py:388
  26.0 3.2 %collective-permute-start.1 = (f32[5,1,3,2,256]{4,3,2,1,0:T(2,128)}, f32[5,1,3,2,256]{4,3,2,1,0:T(2,128)S(1)}, u32[]{:S(2)}, u32[]{:S(2)}) collective-permute-start(f32[5,1,3,2,256]{4,3,2,1,0:T(2,128)} %get-tuple-element.23.refs_3_), channel_id=1, source_target_pairs={{8,0},{16,8},{24,16},{0,24},{9,1},{17,9},{25,17},{1,25},{10,2},{18... | collective-permute-start | bytes 92168 | tf_op jit(solution)/shard_map/ppermute | solution.py:388
  27.8 1.4 %copy-start.1 = (f32[5,1,3,2,256]{4,3,2,1,0:T(2,128)}, f32[5,1,3,2,256]{4,3,2,1,0:T(2,128)S(1)}, u32[]{:S(2)}) copy-start(f32[5,1,3,2,256]{4,3,2,1,0:T(2,128)S(1)} %collective-permute-done.3.refs_6_) | copy-start | bytes 92164
  28.4 0.8 %copy-start.2 = (f32[5,1,3,2,256]{4,3,2,1,0:T(2,128)}, f32[5,1,3,2,256]{4,3,2,1,0:T(2,128)S(1)}, u32[]{:S(2)}) copy-start(f32[5,1,3,2,256]{4,3,2,1,0:T(2,128)S(1)} %collective-permute-done.2.refs_5_) | copy-start | bytes 92164
  29.2 0.6 %copy-start.3 = (f32[5,1,3,2,256]{4,3,2,1,0:T(2,128)}, f32[5,1,3,2,256]{4,3,2,1,0:T(2,128)S(1)}, u32[]{:S(2)}) copy-start(f32[5,1,3,2,256]{4,3,2,1,0:T(2,128)S(1)} %collective-permute-done.1.refs_4_) | copy-start | bytes 92164
  33.6 11.2 %collective-permute-start.6 = (f32[5,1,3,2,128]{4,3,2,1,0:T(2,128)}, f32[5,1,3,2,128]{4,3,2,1,0:T(2,128)S(1)}, u32[]{:S(2)}, u32[]{:S(2)}) collective-permute-start(f32[5,1,3,2,128]{4,3,2,1,0:T(2,128)} %get-tuple-element.28.refs_3_), channel_id=1, source_target_pairs={{6,0},{0,2},{2,4},{4,6},{7,1},{1,3},{3,5},{5,7},{14,8},{8,10},{10,... | collective-permute-start | bytes 46088 | tf_op jit(solution)/shard_map/ppermute | solution.py:388
  35.2 9.6 %collective-permute-start.5 = (f32[5,1,3,2,128]{4,3,2,1,0:T(2,128)}, f32[5,1,3,2,128]{4,3,2,1,0:T(2,128)S(1)}, u32[]{:S(2)}, u32[]{:S(2)}) collective-permute-start(f32[5,1,3,2,128]{4,3,2,1,0:T(2,128)} %get-tuple-element.28.refs_3_), channel_id=1, source_target_pairs={{4,0},{6,2},{0,4},{2,6},{5,1},{7,3},{1,5},{3,7},{12,8},{14,10},{8,... | collective-permute-start | bytes 46088 | tf_op jit(solution)/shard_map/ppermute | solution.py:388
  37.8 7.0 %collective-permute-start.4 = (f32[5,1,3,2,128]{4,3,2,1,0:T(2,128)}, f32[5,1,3,2,128]{4,3,2,1,0:T(2,128)S(1)}, u32[]{:S(2)}, u32[]{:S(2)}) collective-permute-start(f32[5,1,3,2,128]{4,3,2,1,0:T(2,128)} %get-tuple-element.28.refs_3_), channel_id=1, source_target_pairs={{2,0},{4,2},{6,4},{0,6},{3,1},{5,3},{7,5},{1,7},{10,8},{12,10},{14... | collective-permute-start | bytes 46088 | tf_op jit(solution)/shard_map/ppermute | solution.py:388
  44.8 0.6 %copy-start.4 = (f32[5,1,3,2,128]{4,3,2,1,0:T(2,128)}, f32[5,1,3,2,128]{4,3,2,1,0:T(2,128)S(1)}, u32[]{:S(2)}) copy-start(f32[5,1,3,2,128]{4,3,2,1,0:T(2,128)S(1)} %collective-permute-done.6.refs_6_) | copy-start | bytes 46084
  44.8 0.6 %copy-start.5 = (f32[5,1,3,2,128]{4,3,2,1,0:T(2,128)}, f32[5,1,3,2,128]{4,3,2,1,0:T(2,128)S(1)}, u32[]{:S(2)}) copy-start(f32[5,1,3,2,128]{4,3,2,1,0:T(2,128)S(1)} %collective-permute-done.5.refs_5_) | copy-start | bytes 46084
  45.4 0.6 %copy-start.6 = (f32[5,1,3,2,128]{4,3,2,1,0:T(2,128)}, f32[5,1,3,2,128]{4,3,2,1,0:T(2,128)S(1)}, u32[]{:S(2)}) copy-start(f32[5,1,3,2,128]{4,3,2,1,0:T(2,128)S(1)} %collective-permute-done.4.refs_4_) | copy-start | bytes 46084

commit v15 on v11

--- a/solution.py
+++ b/solution.py
@@ -127,9 +127,9 @@
     return ends[0:1], ends[1:2]
 
 
-def back_substitute(it, ia, ib, first, last):
-    length = it.shape[0]
-    idx = lax.broadcasted_iota(jnp.int32, it.shape, 0)
+def back_substitute(it, ia, ib, first, last, offset=0, length=None):
+    length = it.shape[0] if length is None else length
+    idx = lax.broadcasted_iota(jnp.int32, it.shape, 0) + offset
     inner = it - ia * first - ib * last
     return jnp.where(idx == 0, first, jnp.where(idx == length - 1, last, inner))
 
@@ -258,15 +258,16 @@
         ot_ref[v, 0] = it
 
 
-def out_kernel(*refs, pieces):
+def out_kernel(*refs, pieces, length):
     it_ref, ia_ref, ib_ref = refs[:3]
     red_in = refs[3 : 3 + pieces]
     mix_ref, out_ref, rows_ref = refs[3 + pieces :]
     count = it_ref.shape[0]
+    offset = pl.program_id(1) * it_ref.shape[2]
     solved = []
     for w in range(count):
         first, last = reduced_ends(red_in, rows_ref, w)
-        solved.append(back_substitute(it_ref[w, 0], ia_ref[w, 0], ib_ref[w, 0], first, last).T)
+        solved.append(back_substitute(it_ref[w, 0], ia_ref[w, 0], ib_ref[w, 0], first, last, offset, length).T)
     for v, value in enumerate(mixed(mix_ref, solved)):
         out_ref[v, 0] = value
 
@@ -341,14 +342,15 @@
 
 def out_sweep(it, ia, ib, red_in, mix_out):
     nv, nz, nr, na = it.shape
-    big_t = pl.BlockSpec((nv, 1, nr, na), lambda z: (0, z, 0, 0))
-    big = pl.BlockSpec((nv, 1, na, nr), lambda z: (0, z, 0, 0))
-    red_in_spec = pl.BlockSpec((nv, 1) + red_in[0].shape[2:], lambda z: (0, z, 0, 0, 0))
-    mixs = pl.BlockSpec((nv, nv, nr), lambda z: (0, 0, 0))
+    chunk = 128 if nr % 128 == 0 else nr
+    big_t = pl.BlockSpec((nv, 1, chunk, na), lambda z, c: (0, z, c, 0))
+    big = pl.BlockSpec((nv, 1, na, chunk), lambda z, c: (0, z, 0, c))
+    red_in_spec = pl.BlockSpec((nv, 1) + red_in[0].shape[2:], lambda z, c: (0, z, 0, 0, 0))
+    mixs = pl.BlockSpec((nv, nv, chunk), lambda z, c: (0, 0, c))
     pieces = len(red_in)
     return pl.pallas_call(
-        functools.partial(out_kernel, pieces=pieces),
-        grid=(nz,),
+        functools.partial(out_kernel, pieces=pieces, length=nr),
+        grid=(nz, nr // chunk),
         in_specs=[big_t, big_t, big_t] + [red_in_spec] * pieces + [mixs],
         out_specs=big,
         out_shape=jax.ShapeDtypeStruct((nv, nz, na, nr), it.dtype),

time: 48 us -> 47.8 us (level)
  no operation moved by 1% of the time
where the time goes in v15:
time: 47.8 us; the launch traced here: 47.5 us
  Pallas kernels  27.4 us (57%)
  starting transfers between devices  11.7 us (24%)
  waiting for transfers between devices  6.41 us (13%)
  local copies, waits for them, and re-layouts  2.05 us (4%)
    ppermute x6, starting transfers between devices, gathered(): received.append(lax.ppermute(block, axis_name, pairs))  8.75 us
    pallas_call x1, Pallas kernels, az_sweep(): pl.pallas_call(az_local_kernel, grid=grid, in_specs=[big, big, cell, par,...  6.86 us
    pallas_call x1, Pallas kernels, rad_sweep(): pl.pallas_call(kernel, grid=(nz,), in_specs=[big, big, big] + [red_in_spe...  6.43 us
    pallas_call x1, Pallas kernels, rad_pre(): pl.pallas_call(functools.partial(rad_pre_kernel, axis_name='rad'), grid=(...  6.04 us
    pallas_call x1, Pallas kernels, az_sweep(): pl.pallas_call(az_plane_kernel, grid=grid, in_specs=[big, cell, par, par,...  5.45 us
    ppermute x6, waiting for transfers between devices, gathered(): received.append(lax.ppermute(block, axis_name, pairs))  4.37 us
    ppermute x1, starting transfers between devices, neighbour_planes(): return lax.ppermute(block, axis_name, [(0, 1), (1, 0)])  2.97 us
    pallas_call x1, Pallas kernels, out_sweep(): pl.pallas_call(functools.partial(out_kernel, pieces=pieces, length=nr), g...  2.57 us
  transfers between devices with their start and end apart: 7, of which 7 were waited for; matrix products, arithmetic and copies ran while one was open for 0% of the time, Pallas kernels for 27%

profile of v15, /device:TPU:0, one launch (start us, length us, event | category | flops | bytes accessed | tf_op | source)
XLA Modules:
  0.0 47.5 jit_solution(9282111817366081779)
XLA Ops:
  0.0 3.0 %collective-permute-start = (f32[5,1,128,256]{3,2,1,0:T(8,128)}, f32[5,1,128,256]{3,2,1,0:T(8,128)S(1)}, u32[]{:S(2)}, u32[]{:S(2)}) collective-permute-start(f32[5,1,128,256]{3,2,1,0:T(8,128)} %fs_ref.1), channel_id=1, source_target_pairs={{0,1},{1,0},{2,3},{3,2},{4,5},{5,4},{6,7},{7,6},{8,9},{9,8},{10,11... | collective-permute-start | bytes 1966088 | tf_op jit(solution)/shard_map/ppermute | solution.py:373
  3.0 6.0 %shard_map.110 = (f32[5,1,256,128]{3,2,1,0:T(8,128)}, f32[5,1,256,128]{3,2,1,0:T(8,128)}, f32[5,1,4,128]{3,2,1,0:T(4,128)}) custom-call(f32[1,128,256]{2,1,0:T(8,128)} %refs_8_.1, f32[5,1024]{1,0:T(8,128)} %refs_9_.1), custom_call_target="tpu_custom_call" | custom-call | tf_op jit(solution)/shard_map/pallas_call | solution.py:311
  9.0 6.9 %shard_map.109 = (f32[5,1,128,256]{3,2,1,0:T(8,128)}, f32[5,1,128,256]{3,2,1,0:T(8,128)}, f32[5,1,128,256]{3,2,1,0:T(8,128)}, f32[5,1,6,256]{3,2,1,0:T(8,128)}) custom-call(f32[5,1,128,256]{3,2,1,0:T(8,128)} %fs_ref.1, f32[5,1,128,256]{3,2,1,0:T(8,128)} %src_ref.1, f32[1,128,256]{2,1,0:T(8,128)} %cell_ref.5, f32[5,256]{1,0:T(8,128)} %visc_ref.5, ...), custom_call_target="tpu_custom_call" | custom-call | tf_op jit(solution)/shard_map/pallas_call | solution.py:286
  15.9 2.0 %collective-permute-done.nb_ref = f32[5,1,128,256]{3,2,1,0:T(8,128)S(1)} collective-permute-done((f32[5,1,128,256]{3,2,1,0:T(8,128)}, f32[5,1,128,256]{3,2,1,0:T(8,128)S(1)}, u32[]{:S(2)}, u32[]{:S(2)}) %collective-permute-start) | collective-permute-done | bytes 655392 | tf_op jit(solution)/shard_map/ppermute | solution.py:373
  17.9 0.0 copy-start
  17.9 0.8 %copy-done = f32[5,1,128,256]{3,2,1,0:T(8,128)} copy-done((f32[5,1,128,256]{3,2,1,0:T(8,128)}, f32[5,1,128,256]{3,2,1,0:T(8,128)S(1)}, u32[]{:S(2)}) %copy-start) | copy-done | bytes 655384
  18.7 5.5 %shard_map.111 = (f32[5,1,128,256]{3,2,1,0:T(8,128)}, f32[5,1,3,2,256]{4,3,2,1,0:T(2,128)}) custom-call(f32[5,1,128,256]{3,2,1,0:T(8,128)} %copy-done, f32[1,128,256]{2,1,0:T(8,128)} %cell_ref.5, f32[5,256]{1,0:T(8,128)} %visc_ref.5, f32[5,256]{1,0:T(8,128)} %beta_ref.3, f32[5,256]{1,0:T(8,128)} %diff_ref.3, ...), custom_call_target="tpu_custom_call", output_to_operand_aliasing={{0}: (6, {})} | custom-call | tf_op jit(solution)/shard_map/pallas_call | solution.py:293
  24.2 0.1 collective-permute-start.3
  24.3 1.8 %collective-permute-start.2 = (f32[5,1,3,2,256]{4,3,2,1,0:T(2,128)}, f32[5,1,3,2,256]{4,3,2,1,0:T(2,128)S(1)}, u32[]{:S(2)}, u32[]{:S(2)}) collective-permute-start(f32[5,1,3,2,256]{4,3,2,1,0:T(2,128)} %get-tuple-element.22.refs_3_), channel_id=1, source_target_pairs={{16,0},{24,8},{0,16},{8,24},{17,1},{25,9},{1,17},{9,25},{18,2},{26... | collective-permute-start | bytes 92168 | tf_op jit(solution)/shard_map/ppermute | solution.py:366
  26.0 1.4 %collective-permute-start.1 = (f32[5,1,3,2,256]{4,3,2,1,0:T(2,128)}, f32[5,1,3,2,256]{4,3,2,1,0:T(2,128)S(1)}, u32[]{:S(2)}, u32[]{:S(2)}) collective-permute-start(f32[5,1,3,2,256]{4,3,2,1,0:T(2,128)} %get-tuple-element.22.refs_3_), channel_id=1, source_target_pairs={{8,0},{16,8},{24,16},{0,24},{9,1},{17,9},{25,17},{1,25},{10,2},{18... | collective-permute-start | bytes 92168 | tf_op jit(solution)/shard_map/ppermute | solution.py:366
  27.4 0.3 collective-permute-done.3.refs_6_
  27.8 0.0 copy-start.1
  27.8 0.7 %collective-permute-done.2.refs_5_ = f32[5,1,3,2,256]{4,3,2,1,0:T(2,128)S(1)} collective-permute-done((f32[5,1,3,2,256]{4,3,2,1,0:T(2,128)}, f32[5,1,3,2,256]{4,3,2,1,0:T(2,128)S(1)}, u32[]{:S(2)}, u32[]{:S(2)}) %collective-permute-start.2) | collective-permute-done | bytes 30752 | tf_op jit(solution)/shard_map/ppermute | solution.py:366
  28.4 0.0 copy-start.2
  28.4 0.8 %collective-permute-done.1.refs_4_ = f32[5,1,3,2,256]{4,3,2,1,0:T(2,128)S(1)} collective-permute-done((f32[5,1,3,2,256]{4,3,2,1,0:T(2,128)}, f32[5,1,3,2,256]{4,3,2,1,0:T(2,128)S(1)}, u32[]{:S(2)}, u32[]{:S(2)}) %collective-permute-start.1) | collective-permute-done | bytes 30752 | tf_op jit(solution)/shard_map/ppermute | solution.py:366
  29.2 0.0 copy-start.3
  29.2 0.0 copy-done.1
  29.2 0.0 copy-done.2
  29.2 0.6 %copy-done.3 = f32[5,1,3,2,256]{4,3,2,1,0:T(2,128)} copy-done((f32[5,1,3,2,256]{4,3,2,1,0:T(2,128)}, f32[5,1,3,2,256]{4,3,2,1,0:T(2,128)S(1)}, u32[]{:S(2)}) %copy-start.3) | copy-done | bytes 30744
  29.8 6.4 %shard_map.112 = (f32[5,1,256,128]{3,2,1,0:T(8,128)}, f32[5,1,3,2,128]{4,3,2,1,0:T(2,128)}) custom-call(f32[5,1,128,256]{3,2,1,0:T(8,128)} %get-tuple-element.19.refs_0_, f32[5,1,128,256]{3,2,1,0:T(8,128)} %get-tuple-element.20.refs_1_, f32[5,1,128,256]{3,2,1,0:T(8,128)} %get-tuple-element.21.refs_2_, f32[5,1,3,2,256]{4,3,2,1,0:T(2,128)} %get-tuple-element.22.refs_3_, ...), custom_call_target="tpu_custom_call" | custom-call | tf_op jit(solution)/shard_map/pallas_call | solution.py:333
  36.3 1.6 %collective-permute-start.6 = (f32[5,1,3,2,128]{4,3,2,1,0:T(2,128)}, f32[5,1,3,2,128]{4,3,2,1,0:T(2,128)S(1)}, u32[]{:S(2)}, u32[]{:S(2)}) collective-permute-start(f32[5,1,3,2,128]{4,3,2,1,0:T(2,128)} %get-tuple-element.26.refs_3_), channel_id=1, source_target_pairs={{6,0},{0,2},{2,4},{4,6},{7,1},{1,3},{3,5},{5,7},{14,8},{8,10},{10,... | collective-permute-start | bytes 46088 | tf_op jit(solution)/shard_map/ppermute | solution.py:366
  37.8 2.6 %collective-permute-start.5 = (f32[5,1,3,2,128]{4,3,2,1,0:T(2,128)}, f32[5,1,3,2,128]{4,3,2,1,0:T(2,128)S(1)}, u32[]{:S(2)}, u32[]{:S(2)}) collective-permute-start(f32[5,1,3,2,128]{4,3,2,1,0:T(2,128)} %get-tuple-element.26.refs_3_), channel_id=1, source_target_pairs={{4,0},{6,2},{0,4},{2,6},{5,1},{7,3},{1,5},{3,7},{12,8},{14,10},{8,... | collective-permute-start | bytes 46088 | tf_op jit(solution)/shard_map/ppermute | solution.py:366
  40.4 1.4 %collective-permute-start.4 = (f32[5,1,3,2,128]{4,3,2,1,0:T(2,128)}, f32[5,1,3,2,128]{4,3,2,1,0:T(2,128)S(1)}, u32[]{:S(2)}, u32[]{:S(2)}) collective-permute-start(f32[5,1,3,2,128]{4,3,2,1,0:T(2,128)} %get-tuple-element.26.refs_3_), channel_id=1, source_target_pairs={{2,0},{4,2},{6,4},{0,6},{3,1},{5,3},{7,5},{1,7},{10,8},{12,10},{14... | collective-permute-start | bytes 46088 | tf_op jit(solution)/shard_map/ppermute | solution.py:366
  41.8 0.2 collective-permute-done.6.refs_6_
  42.0 0.0 copy-start.4
  42.0 0.7 %collective-permute-done.5.refs_5_ = f32[5,1,3,2,128]{4,3,2,1,0:T(2,128)S(1)} collective-permute-done((f32[5,1,3,2,128]{4,3,2,1,0:T(2,128)}, f32[5,1,3,2,128]{4,3,2,1,0:T(2,128)S(1)}, u32[]{:S(2)}, u32[]{:S(2)}) %collective-permute-start.5) | collective-permute-done | bytes 15392 | tf_op jit(solution)/shard_map/ppermute | solution.py:366
  42.7 0.0 copy-start.5
  42.7 1.7 %collective-permute-done.4.refs_4_ = f32[5,1,3,2,128]{4,3,2,1,0:T(2,128)S(1)} collective-permute-done((f32[5,1,3,2,128]{4,3,2,1,0:T(2,128)}, f32[5,1,3,2,128]{4,3,2,1,0:T(2,128)S(1)}, u32[]{:S(2)}, u32[]{:S(2)}) %collective-permute-start.4) | collective-permute-done | bytes 15392 | tf_op jit(solution)/shard_map/ppermute | solution.py:366
  44.4 0.0 copy-start.6
  44.4 0.0 copy-done.4
  44.4 0.0 copy-done.5
  44.4 0.6 %copy-done.6 = f32[5,1,3,2,128]{4,3,2,1,0:T(2,128)} copy-done((f32[5,1,3,2,128]{4,3,2,1,0:T(2,128)}, f32[5,1,3,2,128]{4,3,2,1,0:T(2,128)S(1)}, u32[]{:S(2)}) %copy-start.6) | copy-done | bytes 15384
  45.0 2.6 %shard_map.113 = f32[5,1,128,256]{3,2,1,0:T(8,128)} custom-call(f32[5,1,256,128]{3,2,1,0:T(8,128)} %get-tuple-element.23.refs_0_, f32[5,1,256,128]{3,2,1,0:T(8,128)} %get-tuple-element.24.refs_1_, f32[5,1,256,128]{3,2,1,0:T(8,128)} %get-tuple-element.25.refs_2_, f32[5,1,3,2,128]{4,3,2,1,0:T(2,128)} %get-tuple-element.26.refs_3_, ...), custom_call_target="tpu_custom_call" | custom-call | tf_op jit(solution)/shard_map/pallas_call | solution.py:351
Async XLA Ops:
  0.0 17.9 %collective-permute-start = (f32[5,1,128,256]{3,2,1,0:T(8,128)}, f32[5,1,128,256]{3,2,1,0:T(8,128)S(1)}, u32[]{:S(2)}, u32[]{:S(2)}) collective-permute-start(f32[5,1,128,256]{3,2,1,0:T(8,128)} %fs_ref.1), channel_id=1, source_target_pairs={{0,1},{1,0},{2,3},{3,2},{4,5},{5,4},{6,7},{7,6},{8,9},{9,8},{10,11... | collective-permute-start | bytes 1966088 | tf_op jit(solution)/shard_map/ppermute | solution.py:373
  17.9 0.8 %copy-start = (f32[5,1,128,256]{3,2,1,0:T(8,128)}, f32[5,1,128,256]{3,2,1,0:T(8,128)S(1)}, u32[]{:S(2)}) copy-start(f32[5,1,128,256]{3,2,1,0:T(8,128)S(1)} %collective-permute-done.nb_ref) | copy-start | bytes 1966084
  24.2 3.6 %collective-permute-start.3 = (f32[5,1,3,2,256]{4,3,2,1,0:T(2,128)}, f32[5,1,3,2,256]{4,3,2,1,0:T(2,128)S(1)}, u32[]{:S(2)}, u32[]{:S(2)}) collective-permute-start(f32[5,1,3,2,256]{4,3,2,1,0:T(2,128)} %get-tuple-element.22.refs_3_), channel_id=1, source_target_pairs={{24,0},{0,8},{8,16},{16,24},{25,1},{1,9},{9,17},{17,25},{26,2},{2,... | collective-permute-start | bytes 92168 | tf_op jit(solution)/shard_map/ppermute | solution.py:366
  24.3 4.2 %collective-permute-start.2 = (f32[5,1,3,2,256]{4,3,2,1,0:T(2,128)}, f32[5,1,3,2,256]{4,3,2,1,0:T(2,128)S(1)}, u32[]{:S(2)}, u32[]{:S(2)}) collective-permute-start(f32[5,1,3,2,256]{4,3,2,1,0:T(2,128)} %get-tuple-element.22.refs_3_), channel_id=1, source_target_pairs={{16,0},{24,8},{0,16},{8,24},{17,1},{25,9},{1,17},{9,25},{18,2},{26... | collective-permute-start | bytes 92168 | tf_op jit(solution)/shard_map/ppermute | solution.py:366
  26.0 3.2 %collective-permute-start.1 = (f32[5,1,3,2,256]{4,3,2,1,0:T(2,128)}, f32[5,1,3,2,256]{4,3,2,1,0:T(2,128)S(1)}, u32[]{:S(2)}, u32[]{:S(2)}) collective-permute-start(f32[5,1,3,2,256]{4,3,2,1,0:T(2,128)} %get-tuple-element.22.refs_3_), channel_id=1, source_target_pairs={{8,0},{16,8},{24,16},{0,24},{9,1},{17,9},{25,17},{1,25},{10,2},{18... | collective-permute-start | bytes 92168 | tf_op jit(solution)/shard_map/ppermute | solution.py:366
  27.8 1.4 %copy-start.1 = (f32[5,1,3,2,256]{4,3,2,1,0:T(2,128)}, f32[5,1,3,2,256]{4,3,2,1,0:T(2,128)S(1)}, u32[]{:S(2)}) copy-start(f32[5,1,3,2,256]{4,3,2,1,0:T(2,128)S(1)} %collective-permute-done.3.refs_6_) | copy-start | bytes 92164
  28.4 0.8 %copy-start.2 = (f32[5,1,3,2,256]{4,3,2,1,0:T(2,128)}, f32[5,1,3,2,256]{4,3,2,1,0:T(2,128)S(1)}, u32[]{:S(2)}) copy-start(f32[5,1,3,2,256]{4,3,2,1,0:T(2,128)S(1)} %collective-permute-done.2.refs_5_) | copy-start | bytes 92164
  29.2 0.6 %copy-start.3 = (f32[5,1,3,2,256]{4,3,2,1,0:T(2,128)}, f32[5,1,3,2,256]{4,3,2,1,0:T(2,128)S(1)}, u32[]{:S(2)}) copy-start(f32[5,1,3,2,256]{4,3,2,1,0:T(2,128)S(1)} %collective-permute-done.1.refs_4_) | copy-start | bytes 92164
  36.3 5.7 %collective-permute-start.6 = (f32[5,1,3,2,128]{4,3,2,1,0:T(2,128)}, f32[5,1,3,2,128]{4,3,2,1,0:T(2,128)S(1)}, u32[]{:S(2)}, u32[]{:S(2)}) collective-permute-start(f32[5,1,3,2,128]{4,3,2,1,0:T(2,128)} %get-tuple-element.26.refs_3_), channel_id=1, source_target_pairs={{6,0},{0,2},{2,4},{4,6},{7,1},{1,3},{3,5},{5,7},{14,8},{8,10},{10,... | collective-permute-start | bytes 46088 | tf_op jit(solution)/shard_map/ppermute | solution.py:366
  37.8 4.9 %collective-permute-start.5 = (f32[5,1,3,2,128]{4,3,2,1,0:T(2,128)}, f32[5,1,3,2,128]{4,3,2,1,0:T(2,128)S(1)}, u32[]{:S(2)}, u32[]{:S(2)}) collective-permute-start(f32[5,1,3,2,128]{4,3,2,1,0:T(2,128)} %get-tuple-element.26.refs_3_), channel_id=1, source_target_pairs={{4,0},{6,2},{0,4},{2,6},{5,1},{7,3},{1,5},{3,7},{12,8},{14,10},{8,... | collective-permute-start | bytes 46088 | tf_op jit(solution)/shard_map/ppermute | solution.py:366
  40.4 3.9 %collective-permute-start.4 = (f32[5,1,3,2,128]{4,3,2,1,0:T(2,128)}, f32[5,1,3,2,128]{4,3,2,1,0:T(2,128)S(1)}, u32[]{:S(2)}, u32[]{:S(2)}) collective-permute-start(f32[5,1,3,2,128]{4,3,2,1,0:T(2,128)} %get-tuple-element.26.refs_3_), channel_id=1, source_target_pairs={{2,0},{4,2},{6,4},{0,6},{3,1},{5,3},{7,5},{1,7},{10,8},{12,10},{14... | collective-permute-start | bytes 46088 | tf_op jit(solution)/shard_map/ppermute | solution.py:366
  42.0 2.4 %copy-start.4 = (f32[5,1,3,2,128]{4,3,2,1,0:T(2,128)}, f32[5,1,3,2,128]{4,3,2,1,0:T(2,128)S(1)}, u32[]{:S(2)}) copy-start(f32[5,1,3,2,128]{4,3,2,1,0:T(2,128)S(1)} %collective-permute-done.6.refs_6_) | copy-start | bytes 46084
  42.7 1.7 %copy-start.5 = (f32[5,1,3,2,128]{4,3,2,1,0:T(2,128)}, f32[5,1,3,2,128]{4,3,2,1,0:T(2,128)S(1)}, u32[]{:S(2)}) copy-start(f32[5,1,3,2,128]{4,3,2,1,0:T(2,128)S(1)} %collective-permute-done.5.refs_5_) | copy-start | bytes 46084
  44.4 0.6 %copy-start.6 = (f32[5,1,3,2,128]{4,3,2,1,0:T(2,128)}, f32[5,1,3,2,128]{4,3,2,1,0:T(2,128)S(1)}, u32[]{:S(2)}) copy-start(f32[5,1,3,2,128]{4,3,2,1,0:T(2,128)S(1)} %collective-permute-done.4.refs_4_) | copy-start | bytes 46084

commit v16 on v15

--- a/solution.py
+++ b/solution.py
@@ -112,6 +112,7 @@
 def reduced_ends(red_refs, rows_ref, v):
     for k, ref in enumerate(red_refs):
         rows_ref[:, 2 * k : 2 * k + 2, :] = ref[v, 0]
+
     lower, upper, target = rows_ref[0], rows_ref[1], rows_ref[2]
     length = lower.shape[0]
     stride = 1
@@ -228,16 +229,32 @@
 def rad_kernel(*refs, axis_name, devices, pieces):
     it_ref, ia_ref, ib_ref = refs[:3]
     red_in = refs[3 : 3 + pieces]
-    mix_ref, cell_ref, visc_ref, edge_ref, ot_ref, red_ref, rows_ref = refs[3 + pieces :]
-    count = it_ref.shape[0]
+    mix_ref, cell_ref, visc_ref, edge_ref, ot_ref, red_ref, rows_ref, acc_ref = refs[3 + pieces :]
+    count = mix_ref.shape[0]
     cells = it_ref.shape[3]
+    w = pl.program_id(1)
+    first, last = reduced_ends(red_in, rows_ref, w)
+    solved = back_substitute(it_ref[0, 0], ia_ref[0, 0], ib_ref[0, 0], first, last)
+
+    @pl.when(w == 0)
+    def _():
+        acc_ref[...] = jnp.zeros_like(acc_ref)
+
+    for v in range(count):
+        acc_ref[v] = acc_ref[v] + mix_ref[v, pl.ds(w, 1), :] * solved
+    acc_ref[w] = acc_ref[w] + solved
+
+    @pl.when(w == count - 1)
+    def _():
+        rad_finish(acc_ref, cell_ref, visc_ref, edge_ref, ot_ref, red_ref, axis_name, devices)
+
+
+def rad_finish(acc_ref, cell_ref, visc_ref, edge_ref, ot_ref, red_ref, axis_name, devices):
+    count = acc_ref.shape[0]
+    cells = acc_ref.shape[2]
     place = lax.axis_index(axis_name)
     visc = local_visc(visc_ref, axis_name, cells)
-    solved = []
-    for w in range(count):
-        first, last = reduced_ends(red_in, rows_ref, w)
-        solved.append(back_substitute(it_ref[w, 0], ia_ref[w, 0], ib_ref[w, 0], first, last))
-    section_three = mixed(mix_ref, solved)
+    section_three = [acc_ref[v] for v in range(count)]
     cell = cell_ref[0]
     for v in range(count):
         side, scale = rad_side(cell, visc, v)
@@ -319,24 +336,24 @@
 
 def rad_sweep(it, ia, ib, red_in, mix_mid, cell_rad, visc_rad, edges):
     nv, nz, na, nr = it.shape
-    big = pl.BlockSpec((nv, 1, na, nr), lambda z: (0, z, 0, 0))
-    big_t = pl.BlockSpec((nv, 1, nr, na), lambda z: (0, z, 0, 0))
-    red_in_spec = pl.BlockSpec((nv, 1) + red_in[0].shape[2:], lambda z: (0, z, 0, 0, 0))
-    mixs = pl.BlockSpec((nv, nv, nr), lambda z: (0, 0, 0))
-    cell = pl.BlockSpec((1, na, nr), lambda z: (z, 0, 0))
-    par = pl.BlockSpec(visc_rad.shape, lambda z: (0, 0))
-    edge = pl.BlockSpec((nv, 1, 4, na), lambda z: (0, z, 0, 0))
-    red = pl.BlockSpec((nv, 1, 3, 2, na), lambda z: (0, z, 0, 0, 0))
+    one = pl.BlockSpec((1, 1, na, nr), lambda z, w: (w, z, 0, 0))
+    big_t = pl.BlockSpec((nv, 1, nr, na), lambda z, w: (0, z, 0, 0))
+    red_in_spec = pl.BlockSpec((nv, 1) + red_in[0].shape[2:], lambda z, w: (0, z, 0, 0, 0))
+    mixs = pl.BlockSpec((nv, nv, nr), lambda z, w: (0, 0, 0))
+    cell = pl.BlockSpec((1, na, nr), lambda z, w: (z, 0, 0))
+    par = pl.BlockSpec(visc_rad.shape, lambda z, w: (0, 0))
+    edge = pl.BlockSpec((nv, 1, 4, na), lambda z, w: (0, z, 0, 0))
+    red = pl.BlockSpec((nv, 1, 3, 2, na), lambda z, w: (0, z, 0, 0, 0))
     out = jax.ShapeDtypeStruct((nv, nz, nr, na), it.dtype)
     pieces = len(red_in)
     kernel = functools.partial(rad_kernel, axis_name="rad", devices=lax.axis_size("rad"), pieces=pieces)
     return pl.pallas_call(
         kernel,
-        grid=(nz,),
-        in_specs=[big, big, big] + [red_in_spec] * pieces + [mixs, cell, par, edge],
+        grid=(nz, nv),
+        in_specs=[one, one, one] + [red_in_spec] * pieces + [mixs, cell, par, edge],
         out_specs=[big_t, red],
         out_shape=[out, jax.ShapeDtypeStruct((nv, nz, 3, 2, na), it.dtype)],
-        scratch_shapes=[pltpu.VMEM((3, 2 * pieces, nr), it.dtype)],
+        scratch_shapes=[pltpu.VMEM((3, 2 * pieces, nr), it.dtype), pltpu.VMEM((nv, na, nr), it.dtype)],
     )(it, ia, ib, *red_in, mix_mid, cell_rad, visc_rad, edges)
 
 

time: 47.8 us -> 49.6 us (1.038)
  Pallas kernels: 27.4 us -> 29.2 us
    pallas_call x1, Pallas kernels: 6.43 us -> 8.25 us  [rad_sweep(): pl.pallas_call(kernel, grid=(nz, nv), in_specs=[one, one, one] + [red_in_...]
  transfers between devices with their start and end apart: 7 -> 7, of which waited for: 7 -> 7; matrix products, arithmetic and copies ran while one was open for 0% -> 0% of each run, Pallas kernels for 27% -> 26%
where the time goes in v16:
time: 49.6 us; the launch traced here: 49.4 us
  Pallas kernels  29.2 us (59%)
  starting transfers between devices  11.7 us (24%)
  waiting for transfers between devices  6.41 us (13%)
  local copies, waits for them, and re-layouts  2.05 us (4%)
    ppermute x6, starting transfers between devices, gathered(): received.append(lax.ppermute(block, axis_name, pairs))  8.75 us
    pallas_call x1, Pallas kernels, rad_sweep(): pl.pallas_call(kernel, grid=(nz, nv), in_specs=[one, one, one] + [red_in_...  8.25 us
    pallas_call x1, Pallas kernels, az_sweep(): pl.pallas_call(az_local_kernel, grid=grid, in_specs=[big, big, cell, par,...  6.86 us
    pallas_call x1, Pallas kernels, rad_pre(): pl.pallas_call(functools.partial(rad_pre_kernel, axis_name='rad'), grid=(...  6.04 us
    pallas_call x1, Pallas kernels, az_sweep(): pl.pallas_call(az_plane_kernel, grid=grid, in_specs=[big, cell, par, par,...  5.45 us
    ppermute x6, waiting for transfers between devices, gathered(): received.append(lax.ppermute(block, axis_name, pairs))  4.36 us
    ppermute x1, starting transfers between devices, neighbour_planes(): return lax.ppermute(block, axis_name, [(0, 1), (1, 0)])  2.97 us
    pallas_call x1, Pallas kernels, out_sweep(): pl.pallas_call(functools.partial(out_kernel, pieces=pieces, length=nr), g...  2.57 us
  transfers between devices with their start and end apart: 7, of which 7 were waited for; matrix products, arithmetic and copies ran while one was open for 0% of the time, Pallas kernels for 26%

profile of v16, /device:TPU:0, one launch (start us, length us, event | category | flops | bytes accessed | tf_op | source)
XLA Modules:
  0.0 49.4 jit_solution(10088044480448103481)
XLA Ops:
  0.0 3.0 %collective-permute-start = (f32[5,1,128,256]{3,2,1,0:T(8,128)}, f32[5,1,128,256]{3,2,1,0:T(8,128)S(1)}, u32[]{:S(2)}, u32[]{:S(2)}) collective-permute-start(f32[5,1,128,256]{3,2,1,0:T(8,128)} %fs_ref.1), channel_id=1, source_target_pairs={{0,1},{1,0},{2,3},{3,2},{4,5},{5,4},{6,7},{7,6},{8,9},{9,8},{10,11... | collective-permute-start | bytes 1966088 | tf_op jit(solution)/shard_map/ppermute | solution.py:390
  3.0 6.0 %shard_map.110 = (f32[5,1,256,128]{3,2,1,0:T(8,128)}, f32[5,1,256,128]{3,2,1,0:T(8,128)}, f32[5,1,4,128]{3,2,1,0:T(4,128)}) custom-call(f32[1,128,256]{2,1,0:T(8,128)} %refs_8_.1, f32[5,1024]{1,0:T(8,128)} %refs_9_.1), custom_call_target="tpu_custom_call" | custom-call | tf_op jit(solution)/shard_map/pallas_call | solution.py:328
  9.0 6.9 %shard_map.109 = (f32[5,1,128,256]{3,2,1,0:T(8,128)}, f32[5,1,128,256]{3,2,1,0:T(8,128)}, f32[5,1,128,256]{3,2,1,0:T(8,128)}, f32[5,1,6,256]{3,2,1,0:T(8,128)}) custom-call(f32[5,1,128,256]{3,2,1,0:T(8,128)} %fs_ref.1, f32[5,1,128,256]{3,2,1,0:T(8,128)} %src_ref.1, f32[1,128,256]{2,1,0:T(8,128)} %cell_ref.5, f32[5,256]{1,0:T(8,128)} %visc_ref.5, ...), custom_call_target="tpu_custom_call" | custom-call | tf_op jit(solution)/shard_map/pallas_call | solution.py:303
  15.9 2.0 %collective-permute-done.nb_ref = f32[5,1,128,256]{3,2,1,0:T(8,128)S(1)} collective-permute-done((f32[5,1,128,256]{3,2,1,0:T(8,128)}, f32[5,1,128,256]{3,2,1,0:T(8,128)S(1)}, u32[]{:S(2)}, u32[]{:S(2)}) %collective-permute-start) | collective-permute-done | bytes 655392 | tf_op jit(solution)/shard_map/ppermute | solution.py:390
  17.9 0.0 copy-start
  17.9 0.8 %copy-done = f32[5,1,128,256]{3,2,1,0:T(8,128)} copy-done((f32[5,1,128,256]{3,2,1,0:T(8,128)}, f32[5,1,128,256]{3,2,1,0:T(8,128)S(1)}, u32[]{:S(2)}) %copy-start) | copy-done | bytes 655384
  18.7 5.5 %shard_map.111 = (f32[5,1,128,256]{3,2,1,0:T(8,128)}, f32[5,1,3,2,256]{4,3,2,1,0:T(2,128)}) custom-call(f32[5,1,128,256]{3,2,1,0:T(8,128)} %copy-done, f32[1,128,256]{2,1,0:T(8,128)} %cell_ref.5, f32[5,256]{1,0:T(8,128)} %visc_ref.5, f32[5,256]{1,0:T(8,128)} %beta_ref.3, f32[5,256]{1,0:T(8,128)} %diff_ref.3, ...), custom_call_target="tpu_custom_call", output_to_operand_aliasing={{0}: (6, {})} | custom-call | tf_op jit(solution)/shard_map/pallas_call | solution.py:310
  24.2 0.1 collective-permute-start.3
  24.3 1.8 %collective-permute-start.2 = (f32[5,1,3,2,256]{4,3,2,1,0:T(2,128)}, f32[5,1,3,2,256]{4,3,2,1,0:T(2,128)S(1)}, u32[]{:S(2)}, u32[]{:S(2)}) collective-permute-start(f32[5,1,3,2,256]{4,3,2,1,0:T(2,128)} %get-tuple-element.22.refs_3_), channel_id=1, source_target_pairs={{16,0},{24,8},{0,16},{8,24},{17,1},{25,9},{1,17},{9,25},{18,2},{26... | collective-permute-start | bytes 92168 | tf_op jit(solution)/shard_map/ppermute | solution.py:383
  26.0 1.4 %collective-permute-start.1 = (f32[5,1,3,2,256]{4,3,2,1,0:T(2,128)}, f32[5,1,3,2,256]{4,3,2,1,0:T(2,128)S(1)}, u32[]{:S(2)}, u32[]{:S(2)}) collective-permute-start(f32[5,1,3,2,256]{4,3,2,1,0:T(2,128)} %get-tuple-element.22.refs_3_), channel_id=1, source_target_pairs={{8,0},{16,8},{24,16},{0,24},{9,1},{17,9},{25,17},{1,25},{10,2},{18... | collective-permute-start | bytes 92168 | tf_op jit(solution)/shard_map/ppermute | solution.py:383
  27.4 0.3 collective-permute-done.3.refs_6_
  27.8 0.0 copy-start.1
  27.8 0.7 %collective-permute-done.2.refs_5_ = f32[5,1,3,2,256]{4,3,2,1,0:T(2,128)S(1)} collective-permute-done((f32[5,1,3,2,256]{4,3,2,1,0:T(2,128)}, f32[5,1,3,2,256]{4,3,2,1,0:T(2,128)S(1)}, u32[]{:S(2)}, u32[]{:S(2)}) %collective-permute-start.2) | collective-permute-done | bytes 30752 | tf_op jit(solution)/shard_map/ppermute | solution.py:383
  28.4 0.0 copy-start.2
  28.4 0.8 %collective-permute-done.1.refs_4_ = f32[5,1,3,2,256]{4,3,2,1,0:T(2,128)S(1)} collective-permute-done((f32[5,1,3,2,256]{4,3,2,1,0:T(2,128)}, f32[5,1,3,2,256]{4,3,2,1,0:T(2,128)S(1)}, u32[]{:S(2)}, u32[]{:S(2)}) %collective-permute-start.1) | collective-permute-done | bytes 30752 | tf_op jit(solution)/shard_map/ppermute | solution.py:383
  29.2 0.0 copy-start.3
  29.2 0.0 copy-done.1
  29.2 0.0 copy-done.2
  29.2 0.6 %copy-done.3 = f32[5,1,3,2,256]{4,3,2,1,0:T(2,128)} copy-done((f32[5,1,3,2,256]{4,3,2,1,0:T(2,128)}, f32[5,1,3,2,256]{4,3,2,1,0:T(2,128)S(1)}, u32[]{:S(2)}) %copy-start.3) | copy-done | bytes 30744
  29.8 8.2 %shard_map.112 = (f32[5,1,256,128]{3,2,1,0:T(8,128)}, f32[5,1,3,2,128]{4,3,2,1,0:T(2,128)}) custom-call(f32[5,1,128,256]{3,2,1,0:T(8,128)} %get-tuple-element.19.refs_0_, f32[5,1,128,256]{3,2,1,0:T(8,128)} %get-tuple-element.20.refs_1_, f32[5,1,128,256]{3,2,1,0:T(8,128)} %get-tuple-element.21.refs_2_, f32[5,1,3,2,256]{4,3,2,1,0:T(2,128)} %get-tuple-element.22.refs_3_, ...), custom_call_target="tpu_custom_call" | custom-call | tf_op jit(solution)/shard_map/pallas_call | solution.py:350
  38.1 1.6 %collective-permute-start.6 = (f32[5,1,3,2,128]{4,3,2,1,0:T(2,128)}, f32[5,1,3,2,128]{4,3,2,1,0:T(2,128)S(1)}, u32[]{:S(2)}, u32[]{:S(2)}) collective-permute-start(f32[5,1,3,2,128]{4,3,2,1,0:T(2,128)} %get-tuple-element.26.refs_3_), channel_id=1, source_target_pairs={{6,0},{0,2},{2,4},{4,6},{7,1},{1,3},{3,5},{5,7},{14,8},{8,10},{10,... | collective-permute-start | bytes 46088 | tf_op jit(solution)/shard_map/ppermute | solution.py:383
  39.7 2.6 %collective-permute-start.5 = (f32[5,1,3,2,128]{4,3,2,1,0:T(2,128)}, f32[5,1,3,2,128]{4,3,2,1,0:T(2,128)S(1)}, u32[]{:S(2)}, u32[]{:S(2)}) collective-permute-start(f32[5,1,3,2,128]{4,3,2,1,0:T(2,128)} %get-tuple-element.26.refs_3_), channel_id=1, source_target_pairs={{4,0},{6,2},{0,4},{2,6},{5,1},{7,3},{1,5},{3,7},{12,8},{14,10},{8,... | collective-permute-start | bytes 46088 | tf_op jit(solution)/shard_map/ppermute | solution.py:383
  42.3 1.4 %collective-permute-start.4 = (f32[5,1,3,2,128]{4,3,2,1,0:T(2,128)}, f32[5,1,3,2,128]{4,3,2,1,0:T(2,128)S(1)}, u32[]{:S(2)}, u32[]{:S(2)}) collective-permute-start(f32[5,1,3,2,128]{4,3,2,1,0:T(2,128)} %get-tuple-element.26.refs_3_), channel_id=1, source_target_pairs={{2,0},{4,2},{6,4},{0,6},{3,1},{5,3},{7,5},{1,7},{10,8},{12,10},{14... | collective-permute-start | bytes 46088 | tf_op jit(solution)/shard_map/ppermute | solution.py:383
  43.6 0.2 collective-permute-done.6.refs_6_
  43.8 0.0 copy-start.4
  43.8 0.7 %collective-permute-done.5.refs_5_ = f32[5,1,3,2,128]{4,3,2,1,0:T(2,128)S(1)} collective-permute-done((f32[5,1,3,2,128]{4,3,2,1,0:T(2,128)}, f32[5,1,3,2,128]{4,3,2,1,0:T(2,128)S(1)}, u32[]{:S(2)}, u32[]{:S(2)}) %collective-permute-start.5) | collective-permute-done | bytes 15392 | tf_op jit(solution)/shard_map/ppermute | solution.py:383
  44.5 0.0 copy-start.5
  44.5 1.7 %collective-permute-done.4.refs_4_ = f32[5,1,3,2,128]{4,3,2,1,0:T(2,128)S(1)} collective-permute-done((f32[5,1,3,2,128]{4,3,2,1,0:T(2,128)}, f32[5,1,3,2,128]{4,3,2,1,0:T(2,128)S(1)}, u32[]{:S(2)}, u32[]{:S(2)}) %collective-permute-start.4) | collective-permute-done | bytes 15392 | tf_op jit(solution)/shard_map/ppermute | solution.py:383
  46.2 0.0 copy-start.6
  46.2 0.0 copy-done.4
  46.2 0.0 copy-done.5
  46.2 0.6 %copy-done.6 = f32[5,1,3,2,128]{4,3,2,1,0:T(2,128)} copy-done((f32[5,1,3,2,128]{4,3,2,1,0:T(2,128)}, f32[5,1,3,2,128]{4,3,2,1,0:T(2,128)S(1)}, u32[]{:S(2)}) %copy-start.6) | copy-done | bytes 15384
  46.8 2.6 %shard_map.113 = f32[5,1,128,256]{3,2,1,0:T(8,128)} custom-call(f32[5,1,256,128]{3,2,1,0:T(8,128)} %get-tuple-element.23.refs_0_, f32[5,1,256,128]{3,2,1,0:T(8,128)} %get-tuple-element.24.refs_1_, f32[5,1,256,128]{3,2,1,0:T(8,128)} %get-tuple-element.25.refs_2_, f32[5,1,3,2,128]{4,3,2,1,0:T(2,128)} %get-tuple-element.26.refs_3_, ...), custom_call_target="tpu_custom_call" | custom-call | tf_op jit(solution)/shard_map/pallas_call | solution.py:368
Async XLA Ops:
  0.0 17.9 %collective-permute-start = (f32[5,1,128,256]{3,2,1,0:T(8,128)}, f32[5,1,128,256]{3,2,1,0:T(8,128)S(1)}, u32[]{:S(2)}, u32[]{:S(2)}) collective-permute-start(f32[5,1,128,256]{3,2,1,0:T(8,128)} %fs_ref.1), channel_id=1, source_target_pairs={{0,1},{1,0},{2,3},{3,2},{4,5},{5,4},{6,7},{7,6},{8,9},{9,8},{10,11... | collective-permute-start | bytes 1966088 | tf_op jit(solution)/shard_map/ppermute | solution.py:390
  17.9 0.8 %copy-start = (f32[5,1,128,256]{3,2,1,0:T(8,128)}, f32[5,1,128,256]{3,2,1,0:T(8,128)S(1)}, u32[]{:S(2)}) copy-start(f32[5,1,128,256]{3,2,1,0:T(8,128)S(1)} %collective-permute-done.nb_ref) | copy-start | bytes 1966084
  24.2 3.6 %collective-permute-start.3 = (f32[5,1,3,2,256]{4,3,2,1,0:T(2,128)}, f32[5,1,3,2,256]{4,3,2,1,0:T(2,128)S(1)}, u32[]{:S(2)}, u32[]{:S(2)}) collective-permute-start(f32[5,1,3,2,256]{4,3,2,1,0:T(2,128)} %get-tuple-element.22.refs_3_), channel_id=1, source_target_pairs={{24,0},{0,8},{8,16},{16,24},{25,1},{1,9},{9,17},{17,25},{26,2},{2,... | collective-permute-start | bytes 92168 | tf_op jit(solution)/shard_map/ppermute | solution.py:383
  24.3 4.2 %collective-permute-start.2 = (f32[5,1,3,2,256]{4,3,2,1,0:T(2,128)}, f32[5,1,3,2,256]{4,3,2,1,0:T(2,128)S(1)}, u32[]{:S(2)}, u32[]{:S(2)}) collective-permute-start(f32[5,1,3,2,256]{4,3,2,1,0:T(2,128)} %get-tuple-element.22.refs_3_), channel_id=1, source_target_pairs={{16,0},{24,8},{0,16},{8,24},{17,1},{25,9},{1,17},{9,25},{18,2},{26... | collective-permute-start | bytes 92168 | tf_op jit(solution)/shard_map/ppermute | solution.py:383
  26.0 3.2 %collective-permute-start.1 = (f32[5,1,3,2,256]{4,3,2,1,0:T(2,128)}, f32[5,1,3,2,256]{4,3,2,1,0:T(2,128)S(1)}, u32[]{:S(2)}, u32[]{:S(2)}) collective-permute-start(f32[5,1,3,2,256]{4,3,2,1,0:T(2,128)} %get-tuple-element.22.refs_3_), channel_id=1, source_target_pairs={{8,0},{16,8},{24,16},{0,24},{9,1},{17,9},{25,17},{1,25},{10,2},{18... | collective-permute-start | bytes 92168 | tf_op jit(solution)/shard_map/ppermute | solution.py:383
  27.8 1.4 %copy-start.1 = (f32[5,1,3,2,256]{4,3,2,1,0:T(2,128)}, f32[5,1,3,2,256]{4,3,2,1,0:T(2,128)S(1)}, u32[]{:S(2)}) copy-start(f32[5,1,3,2,256]{4,3,2,1,0:T(2,128)S(1)} %collective-permute-done.3.refs_6_) | copy-start | bytes 92164
  28.4 0.8 %copy-start.2 = (f32[5,1,3,2,256]{4,3,2,1,0:T(2,128)}, f32[5,1,3,2,256]{4,3,2,1,0:T(2,128)S(1)}, u32[]{:S(2)}) copy-start(f32[5,1,3,2,256]{4,3,2,1,0:T(2,128)S(1)} %collective-permute-done.2.refs_5_) | copy-start | bytes 92164
  29.2 0.6 %copy-start.3 = (f32[5,1,3,2,256]{4,3,2,1,0:T(2,128)}, f32[5,1,3,2,256]{4,3,2,1,0:T(2,128)S(1)}, u32[]{:S(2)}) copy-start(f32[5,1,3,2,256]{4,3,2,1,0:T(2,128)S(1)} %collective-permute-done.1.refs_4_) | copy-start | bytes 92164
  38.1 5.7 %collective-permute-start.6 = (f32[5,1,3,2,128]{4,3,2,1,0:T(2,128)}, f32[5,1,3,2,128]{4,3,2,1,0:T(2,128)S(1)}, u32[]{:S(2)}, u32[]{:S(2)}) collective-permute-start(f32[5,1,3,2,128]{4,3,2,1,0:T(2,128)} %get-tuple-element.26.refs_3_), channel_id=1, source_target_pairs={{6,0},{0,2},{2,4},{4,6},{7,1},{1,3},{3,5},{5,7},{14,8},{8,10},{10,... | collective-permute-start | bytes 46088 | tf_op jit(solution)/shard_map/ppermute | solution.py:383
  39.7 4.9 %collective-permute-start.5 = (f32[5,1,3,2,128]{4,3,2,1,0:T(2,128)}, f32[5,1,3,2,128]{4,3,2,1,0:T(2,128)S(1)}, u32[]{:S(2)}, u32[]{:S(2)}) collective-permute-start(f32[5,1,3,2,128]{4,3,2,1,0:T(2,128)} %get-tuple-element.26.refs_3_), channel_id=1, source_target_pairs={{4,0},{6,2},{0,4},{2,6},{5,1},{7,3},{1,5},{3,7},{12,8},{14,10},{8,... | collective-permute-start | bytes 46088 | tf_op jit(solution)/shard_map/ppermute | solution.py:383
  42.3 3.9 %collective-permute-start.4 = (f32[5,1,3,2,128]{4,3,2,1,0:T(2,128)}, f32[5,1,3,2,128]{4,3,2,1,0:T(2,128)S(1)}, u32[]{:S(2)}, u32[]{:S(2)}) collective-permute-start(f32[5,1,3,2,128]{4,3,2,1,0:T(2,128)} %get-tuple-element.26.refs_3_), channel_id=1, source_target_pairs={{2,0},{4,2},{6,4},{0,6},{3,1},{5,3},{7,5},{1,7},{10,8},{12,10},{14... | collective-permute-start | bytes 46088 | tf_op jit(solution)/shard_map/ppermute | solution.py:383
  43.8 2.4 %copy-start.4 = (f32[5,1,3,2,128]{4,3,2,1,0:T(2,128)}, f32[5,1,3,2,128]{4,3,2,1,0:T(2,128)S(1)}, u32[]{:S(2)}) copy-start(f32[5,1,3,2,128]{4,3,2,1,0:T(2,128)S(1)} %collective-permute-done.6.refs_6_) | copy-start | bytes 46084
  44.5 1.7 %copy-start.5 = (f32[5,1,3,2,128]{4,3,2,1,0:T(2,128)}, f32[5,1,3,2,128]{4,3,2,1,0:T(2,128)S(1)}, u32[]{:S(2)}) copy-start(f32[5,1,3,2,128]{4,3,2,1,0:T(2,128)S(1)} %collective-permute-done.5.refs_5_) | copy-start | bytes 46084
  46.2 0.6 %copy-start.6 = (f32[5,1,3,2,128]{4,3,2,1,0:T(2,128)}, f32[5,1,3,2,128]{4,3,2,1,0:T(2,128)S(1)}, u32[]{:S(2)}) copy-start(f32[5,1,3,2,128]{4,3,2,1,0:T(2,128)S(1)} %collective-permute-done.4.refs_4_) | copy-start | bytes 46084

commit v17 on v15

--- a/solution.py
+++ b/solution.py
@@ -153,7 +153,7 @@
     return lower, upper, scale
 
 
-def az_local_kernel(fs_ref, src_ref, cell_ref, visc_ref, beta_ref, diff_ref, mix_ref, ot_ref, oa_ref, ob_ref, edge_ref):
+def az_local_kernel(fs_ref, src_ref, cell_ref, visc_ref, beta_ref, diff_ref, mix_ref, ot_ref, oa_ref, ob_ref, ol_ref, ou_ref, os_ref, edge_ref):
     count = fs_ref.shape[0]
     explicit = [src_ref[w, 0] + diff_ref[w : w + 1, :] * (-2.0 * fs_ref[w, 0]) for w in range(count)]
     section_one = mixed(mix_ref, explicit)
@@ -163,34 +163,37 @@
         target = section_one[v] * -scale
         length = lower.shape[0]
         il, iu, keep, a_init, b_init = interior(lower, upper)
+        ol_ref[v, 0] = il
+        ou_ref[v, 0] = iu
+        os_ref[v, 0] = -scale
         it, ia, ib = pcr_levels(il, iu, [target * keep, a_init, b_init])
         ot_ref[v, 0] = it
         oa_ref[v, 0] = ia
         ob_ref[v, 0] = ib
         n2 = length - 2
         for k, value in enumerate(
-            (target[0:1], target[length - 1 :], ia[1:2], ib[1:2], ia[n2 : n2 + 1], ib[n2 : n2 + 1])
+            (target[0:1], target[length - 1 :], ia[1:2], ib[1:2], ia[n2 : n2 + 1], ib[n2 : n2 + 1],
+             lower[0:1], lower[length - 1 :], upper[0:1], upper[length - 1 :])
         ):
             edge_ref[v, 0, k : k + 1, :] = value
 
 
-def az_plane_kernel(nb_ref, cell_ref, visc_ref, beta_ref, diff_ref, mix_ref, it_in_ref, edge_ref, order_ref, ot_ref, red_ref):
+def az_plane_kernel(nb_ref, il_ref, iu_ref, sc_ref, diff_ref, mix_ref, it_in_ref, edge_ref, order_ref, ot_ref, red_ref):
     count = nb_ref.shape[0]
     explicit = [diff_ref[w : w + 1, :] * nb_ref[w, 0] for w in range(count)]
     section_one = mixed(mix_ref, explicit)
-    cell = cell_ref[0]
     for v in range(count):
-        lower, upper, scale = az_coefficients(cell, visc_ref, beta_ref, v)
-        target = section_one[v] * -scale
-        length = lower.shape[0]
-        il, iu, keep, _, _ = interior(lower, upper)
+        il, iu = il_ref[v, 0], iu_ref[v, 0]
+        target = section_one[v] * sc_ref[v, 0]
+        length = il.shape[0]
+        _, _, keep, _, _ = interior(il, iu)
         (it,) = pcr_levels(il, iu, [target * keep])
         it = it_in_ref[v, 0] + it
         ot_ref[v, 0] = it
         edge = edge_ref[v, 0]
         n2 = length - 2
         rows = interface_rows(
-            lower, upper, edge[0:1] + target[0:1], edge[1:2] + target[length - 1 :], it[1:2], it[n2 : n2 + 1],
+            edge[6:8], edge[8:10], edge[0:1] + target[0:1], edge[1:2] + target[length - 1 :], it[1:2], it[n2 : n2 + 1],
             edge[2:3], edge[3:4], edge[4:5], edge[5:6],
         )
         store_rows(red_ref, v, rows)
@@ -280,24 +283,24 @@
     cell = pl.BlockSpec((1, na, chunk), lambda z, c: (z, 0, c))
     par = pl.BlockSpec((nv, chunk), lambda z, c: (0, c))
     mixs = pl.BlockSpec((nv, nv, chunk), lambda z, c: (0, 0, c))
-    edge = pl.BlockSpec((nv, 1, 6, chunk), lambda z, c: (0, z, 0, c))
+    edge = pl.BlockSpec((nv, 1, 10, chunk), lambda z, c: (0, z, 0, c))
     red = pl.BlockSpec((nv, 1, 3, 2, chunk), lambda z, c: (0, z, 0, 0, c))
     out = jax.ShapeDtypeStruct(flow_state.shape, flow_state.dtype)
-    it, ia, ib, edges = pl.pallas_call(
+    it, ia, ib, il, iu, scale, edges = pl.pallas_call(
         az_local_kernel,
         grid=grid,
         in_specs=[big, big, cell, par, par, par, mixs],
-        out_specs=[big, big, big, edge],
-        out_shape=[out, out, out, jax.ShapeDtypeStruct((nv, nz, 6, nr), flow_state.dtype)],
+        out_specs=[big] * 6 + [edge],
+        out_shape=[out] * 6 + [jax.ShapeDtypeStruct((nv, nz, 10, nr), flow_state.dtype)],
     )(flow_state, source, cell_az, visc_az, beta_az, axial_diff, mix_in)
     it, red = pl.pallas_call(
         az_plane_kernel,
         grid=grid,
-        in_specs=[big, cell, par, par, par, mixs, big, edge, pl.BlockSpec(memory_space=pl.ANY)],
+        in_specs=[big, big, big, big, par, mixs, big, edge, pl.BlockSpec(memory_space=pl.ANY)],
         out_specs=[big, red],
         out_shape=[out, jax.ShapeDtypeStruct((nv, nz, 3, 2, nr), flow_state.dtype)],
         input_output_aliases={6: 0},
-    )(nb, cell_az, visc_az, beta_az, axial_diff, mix_in, it, edges, order)
+    )(nb, il, iu, scale, axial_diff, mix_in, it, edges, order)
     return it, ia, ib, red
 
 

time: 47.8 us -> 47.8 us (level)
  transfers between devices with their start and end apart: 7 -> 7, of which waited for: 7 -> 7; matrix products, arithmetic and copies ran while one was open for 0% -> 0% of each run, Pallas kernels for 27% -> 28%
where the time goes in v17:
time: 47.8 us; the launch traced here: 47.6 us
  Pallas kernels  27.8 us (58%)
  starting transfers between devices  11.7 us (24%)
  waiting for transfers between devices  5.99 us (13%)
  local copies, waits for them, and re-layouts  2.05 us (4%)
    ppermute x6, starting transfers between devices, gathered(): received.append(lax.ppermute(block, axis_name, pairs))  8.74 us
    pallas_call x1, Pallas kernels, az_sweep(): pl.pallas_call(az_local_kernel, grid=grid, in_specs=[big, big, cell, par,...  7.27 us
    pallas_call x1, Pallas kernels, rad_sweep(): pl.pallas_call(kernel, grid=(nz,), in_specs=[big, big, big] + [red_in_spe...  6.43 us
    pallas_call x1, Pallas kernels, rad_pre(): pl.pallas_call(functools.partial(rad_pre_kernel, axis_name='rad'), grid=(...  6.04 us
    pallas_call x1, Pallas kernels, az_sweep(): pl.pallas_call(az_plane_kernel, grid=grid, in_specs=[big, big, big, big,...  5.49 us
    ppermute x6, waiting for transfers between devices, gathered(): received.append(lax.ppermute(block, axis_name, pairs))  4.37 us
    ppermute x1, starting transfers between devices, neighbour_planes(): return lax.ppermute(block, axis_name, [(0, 1), (1, 0)])  2.97 us
    pallas_call x1, Pallas kernels, out_sweep(): pl.pallas_call(functools.partial(out_kernel, pieces=pieces, length=nr), g...  2.57 us
  transfers between devices with their start and end apart: 7, of which 7 were waited for; matrix products, arithmetic and copies ran while one was open for 0% of the time, Pallas kernels for 28%

profile of v17, /device:TPU:0, one launch (start us, length us, event | category | flops | bytes accessed | tf_op | source)
XLA Modules:
  0.0 47.6 jit_solution(3959281585067755925)
XLA Ops:
  0.0 3.0 %collective-permute-start = (f32[5,1,128,256]{3,2,1,0:T(8,128)}, f32[5,1,128,256]{3,2,1,0:T(8,128)S(1)}, u32[]{:S(2)}, u32[]{:S(2)}) collective-permute-start(f32[5,1,128,256]{3,2,1,0:T(8,128)} %fs_ref.1), channel_id=1, source_target_pairs={{0,1},{1,0},{2,3},{3,2},{4,5},{5,4},{6,7},{7,6},{8,9},{9,8},{10,11... | collective-permute-start | bytes 1966088 | tf_op jit(solution)/shard_map/ppermute | solution.py:376
  3.0 6.0 %shard_map.110 = (f32[5,1,256,128]{3,2,1,0:T(8,128)}, f32[5,1,256,128]{3,2,1,0:T(8,128)}, f32[5,1,4,128]{3,2,1,0:T(4,128)}) custom-call(f32[1,128,256]{2,1,0:T(8,128)} %refs_8_.1, f32[5,1024]{1,0:T(8,128)} %refs_9_.1), custom_call_target="tpu_custom_call" | custom-call | tf_op jit(solution)/shard_map/pallas_call | solution.py:314
  9.0 7.3 %shard_map.109 = (f32[5,1,128,256]{3,2,1,0:T(8,128)}, f32[5,1,128,256]{3,2,1,0:T(8,128)}, f32[5,1,128,256]{3,2,1,0:T(8,128)}, f32[5,1,128,256]{3,2,1,0:T(8,128)}...) custom-call(f32[5,1,128,256]{3,2,1,0:T(8,128)} %fs_ref.1, ...), custom_call_target="tpu_custom_call" | custom-call | tf_op jit(solution)/shard_map/pallas_call | solution.py:289
  16.3 1.6 %collective-permute-done.nb_ref = f32[5,1,128,256]{3,2,1,0:T(8,128)S(1)} collective-permute-done((f32[5,1,128,256]{3,2,1,0:T(8,128)}, f32[5,1,128,256]{3,2,1,0:T(8,128)S(1)}, u32[]{:S(2)}, u32[]{:S(2)}) %collective-permute-start) | collective-permute-done | bytes 655392 | tf_op jit(solution)/shard_map/ppermute | solution.py:376
  17.9 0.0 copy-start
  17.9 0.8 %copy-done = f32[5,1,128,256]{3,2,1,0:T(8,128)} copy-done((f32[5,1,128,256]{3,2,1,0:T(8,128)}, f32[5,1,128,256]{3,2,1,0:T(8,128)S(1)}, u32[]{:S(2)}) %copy-start) | copy-done | bytes 655384
  18.7 5.5 %shard_map.111 = (f32[5,1,128,256]{3,2,1,0:T(8,128)}, f32[5,1,3,2,256]{4,3,2,1,0:T(2,128)}) custom-call(f32[5,1,128,256]{3,2,1,0:T(8,128)} %copy-done, f32[5,1,128,256]{3,2,1,0:T(8,128)} %get-tuple-element.19.il_ref, f32[5,1,128,256]{3,2,1,0:T(8,128)} %get-tuple-element.20.iu_ref, ...), custom_call_target="tpu_custom_call", output_to_operand_aliasing={{0}: (6, {})} | custom-call | tf_op jit(solution)/shard_map/pallas_call | solution.py:296
  24.2 0.0 collective-permute-start.3
  24.3 1.8 %collective-permute-start.2 = (f32[5,1,3,2,256]{4,3,2,1,0:T(2,128)}, f32[5,1,3,2,256]{4,3,2,1,0:T(2,128)S(1)}, u32[]{:S(2)}, u32[]{:S(2)}) collective-permute-start(f32[5,1,3,2,256]{4,3,2,1,0:T(2,128)} %get-tuple-element.28.refs_3_), channel_id=1, source_target_pairs={{16,0},{24,8},{0,16},{8,24},{17,1},{25,9},{1,17},{9,25},{18,2},{26... | collective-permute-start | bytes 92168 | tf_op jit(solution)/shard_map/ppermute | solution.py:369
  26.1 1.4 %collective-permute-start.1 = (f32[5,1,3,2,256]{4,3,2,1,0:T(2,128)}, f32[5,1,3,2,256]{4,3,2,1,0:T(2,128)S(1)}, u32[]{:S(2)}, u32[]{:S(2)}) collective-permute-start(f32[5,1,3,2,256]{4,3,2,1,0:T(2,128)} %get-tuple-element.28.refs_3_), channel_id=1, source_target_pairs={{8,0},{16,8},{24,16},{0,24},{9,1},{17,9},{25,17},{1,25},{10,2},{18... | collective-permute-start | bytes 92168 | tf_op jit(solution)/shard_map/ppermute | solution.py:369
  27.5 0.3 collective-permute-done.3.refs_6_
  27.8 0.0 copy-start.1
  27.8 0.7 %collective-permute-done.2.refs_5_ = f32[5,1,3,2,256]{4,3,2,1,0:T(2,128)S(1)} collective-permute-done((f32[5,1,3,2,256]{4,3,2,1,0:T(2,128)}, f32[5,1,3,2,256]{4,3,2,1,0:T(2,128)S(1)}, u32[]{:S(2)}, u32[]{:S(2)}) %collective-permute-start.2) | collective-permute-done | bytes 30752 | tf_op jit(solution)/shard_map/ppermute | solution.py:369
  28.5 0.0 copy-start.2
  28.5 0.8 %collective-permute-done.1.refs_4_ = f32[5,1,3,2,256]{4,3,2,1,0:T(2,128)S(1)} collective-permute-done((f32[5,1,3,2,256]{4,3,2,1,0:T(2,128)}, f32[5,1,3,2,256]{4,3,2,1,0:T(2,128)S(1)}, u32[]{:S(2)}, u32[]{:S(2)}) %collective-permute-start.1) | collective-permute-done | bytes 30752 | tf_op jit(solution)/shard_map/ppermute | solution.py:369
  29.2 0.0 copy-start.3
  29.2 0.0 copy-done.1
  29.2 0.0 copy-done.2
  29.2 0.6 %copy-done.3 = f32[5,1,3,2,256]{4,3,2,1,0:T(2,128)} copy-done((f32[5,1,3,2,256]{4,3,2,1,0:T(2,128)}, f32[5,1,3,2,256]{4,3,2,1,0:T(2,128)S(1)}, u32[]{:S(2)}) %copy-start.3) | copy-done | bytes 30744
  29.9 6.4 %shard_map.112 = (f32[5,1,256,128]{3,2,1,0:T(8,128)}, f32[5,1,3,2,128]{4,3,2,1,0:T(2,128)}) custom-call(f32[5,1,128,256]{3,2,1,0:T(8,128)} %get-tuple-element.25.refs_0_, f32[5,1,128,256]{3,2,1,0:T(8,128)} %get-tuple-element.26.refs_1_, f32[5,1,128,256]{3,2,1,0:T(8,128)} %get-tuple-element.27.refs_2_, f32[5,1,3,2,256]{4,3,2,1,0:T(2,128)} %get-tuple-element.28.refs_3_, ...), custom_call_target="tpu_custom_call" | custom-call | tf_op jit(solution)/shard_map/pallas_call | solution.py:336
  36.3 1.6 %collective-permute-start.6 = (f32[5,1,3,2,128]{4,3,2,1,0:T(2,128)}, f32[5,1,3,2,128]{4,3,2,1,0:T(2,128)S(1)}, u32[]{:S(2)}, u32[]{:S(2)}) collective-permute-start(f32[5,1,3,2,128]{4,3,2,1,0:T(2,128)} %get-tuple-element.32.refs_3_), channel_id=1, source_target_pairs={{6,0},{0,2},{2,4},{4,6},{7,1},{1,3},{3,5},{5,7},{14,8},{8,10},{10,... | collective-permute-start | bytes 46088 | tf_op jit(solution)/shard_map/ppermute | solution.py:369
  37.9 2.6 %collective-permute-start.5 = (f32[5,1,3,2,128]{4,3,2,1,0:T(2,128)}, f32[5,1,3,2,128]{4,3,2,1,0:T(2,128)S(1)}, u32[]{:S(2)}, u32[]{:S(2)}) collective-permute-start(f32[5,1,3,2,128]{4,3,2,1,0:T(2,128)} %get-tuple-element.32.refs_3_), channel_id=1, source_target_pairs={{4,0},{6,2},{0,4},{2,6},{5,1},{7,3},{1,5},{3,7},{12,8},{14,10},{8,... | collective-permute-start | bytes 46088 | tf_op jit(solution)/shard_map/ppermute | solution.py:369
  40.5 1.4 %collective-permute-start.4 = (f32[5,1,3,2,128]{4,3,2,1,0:T(2,128)}, f32[5,1,3,2,128]{4,3,2,1,0:T(2,128)S(1)}, u32[]{:S(2)}, u32[]{:S(2)}) collective-permute-start(f32[5,1,3,2,128]{4,3,2,1,0:T(2,128)} %get-tuple-element.32.refs_3_), channel_id=1, source_target_pairs={{2,0},{4,2},{6,4},{0,6},{3,1},{5,3},{7,5},{1,7},{10,8},{12,10},{14... | collective-permute-start | bytes 46088 | tf_op jit(solution)/shard_map/ppermute | solution.py:369
  41.8 0.2 collective-permute-done.6.refs_6_
  42.0 0.0 copy-start.4
  42.0 0.7 %collective-permute-done.5.refs_5_ = f32[5,1,3,2,128]{4,3,2,1,0:T(2,128)S(1)} collective-permute-done((f32[5,1,3,2,128]{4,3,2,1,0:T(2,128)}, f32[5,1,3,2,128]{4,3,2,1,0:T(2,128)S(1)}, u32[]{:S(2)}, u32[]{:S(2)}) %collective-permute-start.5) | collective-permute-done | bytes 15392 | tf_op jit(solution)/shard_map/ppermute | solution.py:369
  42.7 0.0 copy-start.5
  42.7 1.7 %collective-permute-done.4.refs_4_ = f32[5,1,3,2,128]{4,3,2,1,0:T(2,128)S(1)} collective-permute-done((f32[5,1,3,2,128]{4,3,2,1,0:T(2,128)}, f32[5,1,3,2,128]{4,3,2,1,0:T(2,128)S(1)}, u32[]{:S(2)}, u32[]{:S(2)}) %collective-permute-start.4) | collective-permute-done | bytes 15392 | tf_op jit(solution)/shard_map/ppermute | solution.py:369
  44.4 0.0 copy-start.6
  44.4 0.0 copy-done.4
  44.4 0.0 copy-done.5
  44.4 0.6 %copy-done.6 = f32[5,1,3,2,128]{4,3,2,1,0:T(2,128)} copy-done((f32[5,1,3,2,128]{4,3,2,1,0:T(2,128)}, f32[5,1,3,2,128]{4,3,2,1,0:T(2,128)S(1)}, u32[]{:S(2)}) %copy-start.6) | copy-done | bytes 15384
  45.0 2.6 %shard_map.113 = f32[5,1,128,256]{3,2,1,0:T(8,128)} custom-call(f32[5,1,256,128]{3,2,1,0:T(8,128)} %get-tuple-element.29.refs_0_, f32[5,1,256,128]{3,2,1,0:T(8,128)} %get-tuple-element.30.refs_1_, f32[5,1,256,128]{3,2,1,0:T(8,128)} %get-tuple-element.31.refs_2_, f32[5,1,3,2,128]{4,3,2,1,0:T(2,128)} %get-tuple-element.32.refs_3_, ...), custom_call_target="tpu_custom_call" | custom-call | tf_op jit(solution)/shard_map/pallas_call | solution.py:354
Async XLA Ops:
  0.0 17.9 %collective-permute-start = (f32[5,1,128,256]{3,2,1,0:T(8,128)}, f32[5,1,128,256]{3,2,1,0:T(8,128)S(1)}, u32[]{:S(2)}, u32[]{:S(2)}) collective-permute-start(f32[5,1,128,256]{3,2,1,0:T(8,128)} %fs_ref.1), channel_id=1, source_target_pairs={{0,1},{1,0},{2,3},{3,2},{4,5},{5,4},{6,7},{7,6},{8,9},{9,8},{10,11... | collective-permute-start | bytes 1966088 | tf_op jit(solution)/shard_map/ppermute | solution.py:376
  17.9 0.8 %copy-start = (f32[5,1,128,256]{3,2,1,0:T(8,128)}, f32[5,1,128,256]{3,2,1,0:T(8,128)S(1)}, u32[]{:S(2)}) copy-start(f32[5,1,128,256]{3,2,1,0:T(8,128)S(1)} %collective-permute-done.nb_ref) | copy-start | bytes 1966084
  24.2 3.6 %collective-permute-start.3 = (f32[5,1,3,2,256]{4,3,2,1,0:T(2,128)}, f32[5,1,3,2,256]{4,3,2,1,0:T(2,128)S(1)}, u32[]{:S(2)}, u32[]{:S(2)}) collective-permute-start(f32[5,1,3,2,256]{4,3,2,1,0:T(2,128)} %get-tuple-element.28.refs_3_), channel_id=1, source_target_pairs={{24,0},{0,8},{8,16},{16,24},{25,1},{1,9},{9,17},{17,25},{26,2},{2,... | collective-permute-start | bytes 92168 | tf_op jit(solution)/shard_map/ppermute | solution.py:369
  24.3 4.2 %collective-permute-start.2 = (f32[5,1,3,2,256]{4,3,2,1,0:T(2,128)}, f32[5,1,3,2,256]{4,3,2,1,0:T(2,128)S(1)}, u32[]{:S(2)}, u32[]{:S(2)}) collective-permute-start(f32[5,1,3,2,256]{4,3,2,1,0:T(2,128)} %get-tuple-element.28.refs_3_), channel_id=1, source_target_pairs={{16,0},{24,8},{0,16},{8,24},{17,1},{25,9},{1,17},{9,25},{18,2},{26... | collective-permute-start | bytes 92168 | tf_op jit(solution)/shard_map/ppermute | solution.py:369
  26.1 3.2 %collective-permute-start.1 = (f32[5,1,3,2,256]{4,3,2,1,0:T(2,128)}, f32[5,1,3,2,256]{4,3,2,1,0:T(2,128)S(1)}, u32[]{:S(2)}, u32[]{:S(2)}) collective-permute-start(f32[5,1,3,2,256]{4,3,2,1,0:T(2,128)} %get-tuple-element.28.refs_3_), channel_id=1, source_target_pairs={{8,0},{16,8},{24,16},{0,24},{9,1},{17,9},{25,17},{1,25},{10,2},{18... | collective-permute-start | bytes 92168 | tf_op jit(solution)/shard_map/ppermute | solution.py:369
  27.8 1.4 %copy-start.1 = (f32[5,1,3,2,256]{4,3,2,1,0:T(2,128)}, f32[5,1,3,2,256]{4,3,2,1,0:T(2,128)S(1)}, u32[]{:S(2)}) copy-start(f32[5,1,3,2,256]{4,3,2,1,0:T(2,128)S(1)} %collective-permute-done.3.refs_6_) | copy-start | bytes 92164
  28.5 0.8 %copy-start.2 = (f32[5,1,3,2,256]{4,3,2,1,0:T(2,128)}, f32[5,1,3,2,256]{4,3,2,1,0:T(2,128)S(1)}, u32[]{:S(2)}) copy-start(f32[5,1,3,2,256]{4,3,2,1,0:T(2,128)S(1)} %collective-permute-done.2.refs_5_) | copy-start | bytes 92164
  29.2 0.6 %copy-start.3 = (f32[5,1,3,2,256]{4,3,2,1,0:T(2,128)}, f32[5,1,3,2,256]{4,3,2,1,0:T(2,128)S(1)}, u32[]{:S(2)}) copy-start(f32[5,1,3,2,256]{4,3,2,1,0:T(2,128)S(1)} %collective-permute-done.1.refs_4_) | copy-start | bytes 92164
  36.3 5.7 %collective-permute-start.6 = (f32[5,1,3,2,128]{4,3,2,1,0:T(2,128)}, f32[5,1,3,2,128]{4,3,2,1,0:T(2,128)S(1)}, u32[]{:S(2)}, u32[]{:S(2)}) collective-permute-start(f32[5,1,3,2,128]{4,3,2,1,0:T(2,128)} %get-tuple-element.32.refs_3_), channel_id=1, source_target_pairs={{6,0},{0,2},{2,4},{4,6},{7,1},{1,3},{3,5},{5,7},{14,8},{8,10},{10,... | collective-permute-start | bytes 46088 | tf_op jit(solution)/shard_map/ppermute | solution.py:369
  37.9 4.9 %collective-permute-start.5 = (f32[5,1,3,2,128]{4,3,2,1,0:T(2,128)}, f32[5,1,3,2,128]{4,3,2,1,0:T(2,128)S(1)}, u32[]{:S(2)}, u32[]{:S(2)}) collective-permute-start(f32[5,1,3,2,128]{4,3,2,1,0:T(2,128)} %get-tuple-element.32.refs_3_), channel_id=1, source_target_pairs={{4,0},{6,2},{0,4},{2,6},{5,1},{7,3},{1,5},{3,7},{12,8},{14,10},{8,... | collective-permute-start | bytes 46088 | tf_op jit(solution)/shard_map/ppermute | solution.py:369
  40.5 3.9 %collective-permute-start.4 = (f32[5,1,3,2,128]{4,3,2,1,0:T(2,128)}, f32[5,1,3,2,128]{4,3,2,1,0:T(2,128)S(1)}, u32[]{:S(2)}, u32[]{:S(2)}) collective-permute-start(f32[5,1,3,2,128]{4,3,2,1,0:T(2,128)} %get-tuple-element.32.refs_3_), channel_id=1, source_target_pairs={{2,0},{4,2},{6,4},{0,6},{3,1},{5,3},{7,5},{1,7},{10,8},{12,10},{14... | collective-permute-start | bytes 46088 | tf_op jit(solution)/shard_map/ppermute | solution.py:369
  42.0 2.4 %copy-start.4 = (f32[5,1,3,2,128]{4,3,2,1,0:T(2,128)}, f32[5,1,3,2,128]{4,3,2,1,0:T(2,128)S(1)}, u32[]{:S(2)}) copy-start(f32[5,1,3,2,128]{4,3,2,1,0:T(2,128)S(1)} %collective-permute-done.6.refs_6_) | copy-start | bytes 46084
  42.7 1.7 %copy-start.5 = (f32[5,1,3,2,128]{4,3,2,1,0:T(2,128)}, f32[5,1,3,2,128]{4,3,2,1,0:T(2,128)S(1)}, u32[]{:S(2)}) copy-start(f32[5,1,3,2,128]{4,3,2,1,0:T(2,128)S(1)} %collective-permute-done.5.refs_5_) | copy-start | bytes 46084
  44.4 0.6 %copy-start.6 = (f32[5,1,3,2,128]{4,3,2,1,0:T(2,128)}, f32[5,1,3,2,128]{4,3,2,1,0:T(2,128)S(1)}, u32[]{:S(2)}) copy-start(f32[5,1,3,2,128]{4,3,2,1,0:T(2,128)S(1)} %collective-permute-done.4.refs_4_) | copy-start | bytes 46084

commit v18 on v17

--- a/solution.py
+++ b/solution.py
@@ -231,16 +231,30 @@
 def rad_kernel(*refs, axis_name, devices, pieces):
     it_ref, ia_ref, ib_ref = refs[:3]
     red_in = refs[3 : 3 + pieces]
-    mix_ref, cell_ref, visc_ref, edge_ref, ot_ref, red_ref, rows_ref = refs[3 + pieces :]
+    mix_ref, cell_ref, visc_ref, edge_ref, ot_ref, red_ref, rows_ref, s3_ref = refs[3 + pieces :]
     count = it_ref.shape[0]
-    cells = it_ref.shape[3]
-    place = lax.axis_index(axis_name)
-    visc = local_visc(visc_ref, axis_name, cells)
+    half = it_ref.shape[2]
+    step = pl.program_id(1)
     solved = []
     for w in range(count):
         first, last = reduced_ends(red_in, rows_ref, w)
-        solved.append(back_substitute(it_ref[w, 0], ia_ref[w, 0], ib_ref[w, 0], first, last))
-    section_three = mixed(mix_ref, solved)
+        solved.append(
+            back_substitute(it_ref[w, 0], ia_ref[w, 0], ib_ref[w, 0], first, last, step * half, s3_ref.shape[1])
+        )
+    for v, value in enumerate(mixed(mix_ref, solved)):
+        s3_ref[v, pl.ds(pl.multiple_of(step * half, half), half), :] = value
+
+    @pl.when(step == pl.num_programs(1) - 1)
+    def _():
+        rad_finish(s3_ref, cell_ref, visc_ref, edge_ref, ot_ref, red_ref, axis_name, devices)
+
+
+def rad_finish(s3_ref, cell_ref, visc_ref, edge_ref, ot_ref, red_ref, axis_name, devices):
+    count = s3_ref.shape[0]
+    cells = s3_ref.shape[2]
+    place = lax.axis_index(axis_name)
+    visc = local_visc(visc_ref, axis_name, cells)
+    section_three = [s3_ref[v] for v in range(count)]
     cell = cell_ref[0]
     for v in range(count):
         side, scale = rad_side(cell, visc, v)
@@ -322,24 +336,25 @@
 
 def rad_sweep(it, ia, ib, red_in, mix_mid, cell_rad, visc_rad, edges):
     nv, nz, na, nr = it.shape
-    big = pl.BlockSpec((nv, 1, na, nr), lambda z: (0, z, 0, 0))
-    big_t = pl.BlockSpec((nv, 1, nr, na), lambda z: (0, z, 0, 0))
-    red_in_spec = pl.BlockSpec((nv, 1) + red_in[0].shape[2:], lambda z: (0, z, 0, 0, 0))
-    mixs = pl.BlockSpec((nv, nv, nr), lambda z: (0, 0, 0))
-    cell = pl.BlockSpec((1, na, nr), lambda z: (z, 0, 0))
-    par = pl.BlockSpec(visc_rad.shape, lambda z: (0, 0))
-    edge = pl.BlockSpec((nv, 1, 4, na), lambda z: (0, z, 0, 0))
-    red = pl.BlockSpec((nv, 1, 3, 2, na), lambda z: (0, z, 0, 0, 0))
+    halves = 2 if na % 16 == 0 else 1
+    big = pl.BlockSpec((nv, 1, na // halves, nr), lambda z, c: (0, z, c, 0))
+    big_t = pl.BlockSpec((nv, 1, nr, na), lambda z, c: (0, z, 0, 0))
+    red_in_spec = pl.BlockSpec((nv, 1) + red_in[0].shape[2:], lambda z, c: (0, z, 0, 0, 0))
+    mixs = pl.BlockSpec((nv, nv, nr), lambda z, c: (0, 0, 0))
+    cell = pl.BlockSpec((1, na, nr), lambda z, c: (z, 0, 0))
+    par = pl.BlockSpec(visc_rad.shape, lambda z, c: (0, 0))
+    edge = pl.BlockSpec((nv, 1, 4, na), lambda z, c: (0, z, 0, 0))
+    red = pl.BlockSpec((nv, 1, 3, 2, na), lambda z, c: (0, z, 0, 0, 0))
     out = jax.ShapeDtypeStruct((nv, nz, nr, na), it.dtype)
     pieces = len(red_in)
     kernel = functools.partial(rad_kernel, axis_name="rad", devices=lax.axis_size("rad"), pieces=pieces)
     return pl.pallas_call(
         kernel,
-        grid=(nz,),
+        grid=(nz, halves),
         in_specs=[big, big, big] + [red_in_spec] * pieces + [mixs, cell, par, edge],
         out_specs=[big_t, red],
         out_shape=[out, jax.ShapeDtypeStruct((nv, nz, 3, 2, na), it.dtype)],
-        scratch_shapes=[pltpu.VMEM((3, 2 * pieces, nr), it.dtype)],
+        scratch_shapes=[pltpu.VMEM((3, 2 * pieces, nr), it.dtype), pltpu.VMEM((nv, na, nr), it.dtype)],
     )(it, ia, ib, *red_in, mix_mid, cell_rad, visc_rad, edges)
 
 

time: 47.8 us -> 47.7 us (level)
  no operation moved by 1% of the time
where the time goes in v18:
time: 47.7 us; the launch traced here: 47.4 us
  Pallas kernels  27.7 us (58%)
  starting transfers between devices  11.7 us (25%)
  waiting for transfers between devices  5.99 us (13%)
  local copies, waits for them, and re-layouts  2.05 us (4%)
    ppermute x6, starting transfers between devices, gathered(): received.append(lax.ppermute(block, axis_name, pairs))  8.74 us
    pallas_call x1, Pallas kernels, az_sweep(): pl.pallas_call(az_local_kernel, grid=grid, in_specs=[big, big, cell, par,...  7.27 us
    pallas_call x1, Pallas kernels, rad_sweep(): pl.pallas_call(kernel, grid=(nz, halves), in_specs=[big, big, big] + [red...  6.31 us
    pallas_call x1, Pallas kernels, rad_pre(): pl.pallas_call(functools.partial(rad_pre_kernel, axis_name='rad'), grid=(...  6.04 us
    pallas_call x1, Pallas kernels, az_sweep(): pl.pallas_call(az_plane_kernel, grid=grid, in_specs=[big, big, big, big,...  5.49 us
    ppermute x6, waiting for transfers between devices, gathered(): received.append(lax.ppermute(block, axis_name, pairs))  4.36 us
    ppermute x1, starting transfers between devices, neighbour_planes(): return lax.ppermute(block, axis_name, [(0, 1), (1, 0)])  2.97 us
    pallas_call x1, Pallas kernels, out_sweep(): pl.pallas_call(functools.partial(out_kernel, pieces=pieces, length=nr), g...  2.57 us
  transfers between devices with their start and end apart: 7, of which 7 were waited for; matrix products, arithmetic and copies ran while one was open for 0% of the time, Pallas kernels for 28%

profile of v18, /device:TPU:0, one launch (start us, length us, event | category | flops | bytes accessed | tf_op | source)
XLA Modules:
  0.0 47.4 jit_solution(4584213868826067655)
XLA Ops:
  0.0 3.0 %collective-permute-start = (f32[5,1,128,256]{3,2,1,0:T(8,128)}, f32[5,1,128,256]{3,2,1,0:T(8,128)S(1)}, u32[]{:S(2)}, u32[]{:S(2)}) collective-permute-start(f32[5,1,128,256]{3,2,1,0:T(8,128)} %fs_ref.1), channel_id=1, source_target_pairs={{0,1},{1,0},{2,3},{3,2},{4,5},{5,4},{6,7},{7,6},{8,9},{9,8},{10,11... | collective-permute-start | bytes 1966088 | tf_op jit(solution)/shard_map/ppermute | solution.py:391
  3.0 6.0 %shard_map.110 = (f32[5,1,256,128]{3,2,1,0:T(8,128)}, f32[5,1,256,128]{3,2,1,0:T(8,128)}, f32[5,1,4,128]{3,2,1,0:T(4,128)}) custom-call(f32[1,128,256]{2,1,0:T(8,128)} %refs_8_.1, f32[5,1024]{1,0:T(8,128)} %refs_9_.1), custom_call_target="tpu_custom_call" | custom-call | tf_op jit(solution)/shard_map/pallas_call | solution.py:328
  9.0 7.3 %shard_map.109 = (f32[5,1,128,256]{3,2,1,0:T(8,128)}, f32[5,1,128,256]{3,2,1,0:T(8,128)}, f32[5,1,128,256]{3,2,1,0:T(8,128)}, f32[5,1,128,256]{3,2,1,0:T(8,128)}...) custom-call(f32[5,1,128,256]{3,2,1,0:T(8,128)} %fs_ref.1, ...), custom_call_target="tpu_custom_call" | custom-call | tf_op jit(solution)/shard_map/pallas_call | solution.py:303
  16.3 1.6 %collective-permute-done.nb_ref = f32[5,1,128,256]{3,2,1,0:T(8,128)S(1)} collective-permute-done((f32[5,1,128,256]{3,2,1,0:T(8,128)}, f32[5,1,128,256]{3,2,1,0:T(8,128)S(1)}, u32[]{:S(2)}, u32[]{:S(2)}) %collective-permute-start) | collective-permute-done | bytes 655392 | tf_op jit(solution)/shard_map/ppermute | solution.py:391
  17.9 0.0 copy-start
  17.9 0.8 %copy-done = f32[5,1,128,256]{3,2,1,0:T(8,128)} copy-done((f32[5,1,128,256]{3,2,1,0:T(8,128)}, f32[5,1,128,256]{3,2,1,0:T(8,128)S(1)}, u32[]{:S(2)}) %copy-start) | copy-done | bytes 655384
  18.7 5.5 %shard_map.111 = (f32[5,1,128,256]{3,2,1,0:T(8,128)}, f32[5,1,3,2,256]{4,3,2,1,0:T(2,128)}) custom-call(f32[5,1,128,256]{3,2,1,0:T(8,128)} %copy-done, f32[5,1,128,256]{3,2,1,0:T(8,128)} %get-tuple-element.19.il_ref, f32[5,1,128,256]{3,2,1,0:T(8,128)} %get-tuple-element.20.iu_ref, ...), custom_call_target="tpu_custom_call", output_to_operand_aliasing={{0}: (6, {})} | custom-call | tf_op jit(solution)/shard_map/pallas_call | solution.py:310
  24.2 0.0 collective-permute-start.3
  24.3 1.8 %collective-permute-start.2 = (f32[5,1,3,2,256]{4,3,2,1,0:T(2,128)}, f32[5,1,3,2,256]{4,3,2,1,0:T(2,128)S(1)}, u32[]{:S(2)}, u32[]{:S(2)}) collective-permute-start(f32[5,1,3,2,256]{4,3,2,1,0:T(2,128)} %get-tuple-element.28.refs_3_), channel_id=1, source_target_pairs={{16,0},{24,8},{0,16},{8,24},{17,1},{25,9},{1,17},{9,25},{18,2},{26... | collective-permute-start | bytes 92168 | tf_op jit(solution)/shard_map/ppermute | solution.py:384
  26.1 1.4 %collective-permute-start.1 = (f32[5,1,3,2,256]{4,3,2,1,0:T(2,128)}, f32[5,1,3,2,256]{4,3,2,1,0:T(2,128)S(1)}, u32[]{:S(2)}, u32[]{:S(2)}) collective-permute-start(f32[5,1,3,2,256]{4,3,2,1,0:T(2,128)} %get-tuple-element.28.refs_3_), channel_id=1, source_target_pairs={{8,0},{16,8},{24,16},{0,24},{9,1},{17,9},{25,17},{1,25},{10,2},{18... | collective-permute-start | bytes 92168 | tf_op jit(solution)/shard_map/ppermute | solution.py:384
  27.5 0.3 collective-permute-done.3.refs_6_
  27.8 0.0 copy-start.1
  27.8 0.7 %collective-permute-done.2.refs_5_ = f32[5,1,3,2,256]{4,3,2,1,0:T(2,128)S(1)} collective-permute-done((f32[5,1,3,2,256]{4,3,2,1,0:T(2,128)}, f32[5,1,3,2,256]{4,3,2,1,0:T(2,128)S(1)}, u32[]{:S(2)}, u32[]{:S(2)}) %collective-permute-start.2) | collective-permute-done | bytes 30752 | tf_op jit(solution)/shard_map/ppermute | solution.py:384
  28.5 0.0 copy-start.2
  28.5 0.8 %collective-permute-done.1.refs_4_ = f32[5,1,3,2,256]{4,3,2,1,0:T(2,128)S(1)} collective-permute-done((f32[5,1,3,2,256]{4,3,2,1,0:T(2,128)}, f32[5,1,3,2,256]{4,3,2,1,0:T(2,128)S(1)}, u32[]{:S(2)}, u32[]{:S(2)}) %collective-permute-start.1) | collective-permute-done | bytes 30752 | tf_op jit(solution)/shard_map/ppermute | solution.py:384
  29.2 0.0 copy-start.3
  29.2 0.0 copy-done.1
  29.2 0.0 copy-done.2
  29.2 0.6 %copy-done.3 = f32[5,1,3,2,256]{4,3,2,1,0:T(2,128)} copy-done((f32[5,1,3,2,256]{4,3,2,1,0:T(2,128)}, f32[5,1,3,2,256]{4,3,2,1,0:T(2,128)S(1)}, u32[]{:S(2)}) %copy-start.3) | copy-done | bytes 30744
  29.9 6.3 %shard_map.112 = (f32[5,1,256,128]{3,2,1,0:T(8,128)}, f32[5,1,3,2,128]{4,3,2,1,0:T(2,128)}) custom-call(f32[5,1,128,256]{3,2,1,0:T(8,128)} %get-tuple-element.25.refs_0_, f32[5,1,128,256]{3,2,1,0:T(8,128)} %get-tuple-element.26.refs_1_, f32[5,1,128,256]{3,2,1,0:T(8,128)} %get-tuple-element.27.refs_2_, f32[5,1,3,2,256]{4,3,2,1,0:T(2,128)} %get-tuple-element.28.refs_3_, ...), custom_call_target="tpu_custom_call" | custom-call | tf_op jit(solution)/shard_map/pallas_call | solution.py:351
  36.2 1.6 %collective-permute-start.6 = (f32[5,1,3,2,128]{4,3,2,1,0:T(2,128)}, f32[5,1,3,2,128]{4,3,2,1,0:T(2,128)S(1)}, u32[]{:S(2)}, u32[]{:S(2)}) collective-permute-start(f32[5,1,3,2,128]{4,3,2,1,0:T(2,128)} %get-tuple-element.32.refs_3_), channel_id=1, source_target_pairs={{6,0},{0,2},{2,4},{4,6},{7,1},{1,3},{3,5},{5,7},{14,8},{8,10},{10,... | collective-permute-start | bytes 46088 | tf_op jit(solution)/shard_map/ppermute | solution.py:384
  37.7 2.6 %collective-permute-start.5 = (f32[5,1,3,2,128]{4,3,2,1,0:T(2,128)}, f32[5,1,3,2,128]{4,3,2,1,0:T(2,128)S(1)}, u32[]{:S(2)}, u32[]{:S(2)}) collective-permute-start(f32[5,1,3,2,128]{4,3,2,1,0:T(2,128)} %get-tuple-element.32.refs_3_), channel_id=1, source_target_pairs={{4,0},{6,2},{0,4},{2,6},{5,1},{7,3},{1,5},{3,7},{12,8},{14,10},{8,... | collective-permute-start | bytes 46088 | tf_op jit(solution)/shard_map/ppermute | solution.py:384
  40.3 1.4 %collective-permute-start.4 = (f32[5,1,3,2,128]{4,3,2,1,0:T(2,128)}, f32[5,1,3,2,128]{4,3,2,1,0:T(2,128)S(1)}, u32[]{:S(2)}, u32[]{:S(2)}) collective-permute-start(f32[5,1,3,2,128]{4,3,2,1,0:T(2,128)} %get-tuple-element.32.refs_3_), channel_id=1, source_target_pairs={{2,0},{4,2},{6,4},{0,6},{3,1},{5,3},{7,5},{1,7},{10,8},{12,10},{14... | collective-permute-start | bytes 46088 | tf_op jit(solution)/shard_map/ppermute | solution.py:384
  41.7 0.2 collective-permute-done.6.refs_6_
  41.9 0.0 copy-start.4
  41.9 0.7 %collective-permute-done.5.refs_5_ = f32[5,1,3,2,128]{4,3,2,1,0:T(2,128)S(1)} collective-permute-done((f32[5,1,3,2,128]{4,3,2,1,0:T(2,128)}, f32[5,1,3,2,128]{4,3,2,1,0:T(2,128)S(1)}, u32[]{:S(2)}, u32[]{:S(2)}) %collective-permute-start.5) | collective-permute-done | bytes 15392 | tf_op jit(solution)/shard_map/ppermute | solution.py:384
  42.6 0.0 copy-start.5
  42.6 1.7 %collective-permute-done.4.refs_4_ = f32[5,1,3,2,128]{4,3,2,1,0:T(2,128)S(1)} collective-permute-done((f32[5,1,3,2,128]{4,3,2,1,0:T(2,128)}, f32[5,1,3,2,128]{4,3,2,1,0:T(2,128)S(1)}, u32[]{:S(2)}, u32[]{:S(2)}) %collective-permute-start.4) | collective-permute-done | bytes 15392 | tf_op jit(solution)/shard_map/ppermute | solution.py:384
  44.3 0.0 copy-start.6
  44.3 0.0 copy-done.4
  44.3 0.0 copy-done.5
  44.3 0.6 %copy-done.6 = f32[5,1,3,2,128]{4,3,2,1,0:T(2,128)} copy-done((f32[5,1,3,2,128]{4,3,2,1,0:T(2,128)}, f32[5,1,3,2,128]{4,3,2,1,0:T(2,128)S(1)}, u32[]{:S(2)}) %copy-start.6) | copy-done | bytes 15384
  44.9 2.6 %shard_map.113 = f32[5,1,128,256]{3,2,1,0:T(8,128)} custom-call(f32[5,1,256,128]{3,2,1,0:T(8,128)} %get-tuple-element.29.refs_0_, f32[5,1,256,128]{3,2,1,0:T(8,128)} %get-tuple-element.30.refs_1_, f32[5,1,256,128]{3,2,1,0:T(8,128)} %get-tuple-element.31.refs_2_, f32[5,1,3,2,128]{4,3,2,1,0:T(2,128)} %get-tuple-element.32.refs_3_, ...), custom_call_target="tpu_custom_call" | custom-call | tf_op jit(solution)/shard_map/pallas_call | solution.py:369
Async XLA Ops:
  0.0 17.9 %collective-permute-start = (f32[5,1,128,256]{3,2,1,0:T(8,128)}, f32[5,1,128,256]{3,2,1,0:T(8,128)S(1)}, u32[]{:S(2)}, u32[]{:S(2)}) collective-permute-start(f32[5,1,128,256]{3,2,1,0:T(8,128)} %fs_ref.1), channel_id=1, source_target_pairs={{0,1},{1,0},{2,3},{3,2},{4,5},{5,4},{6,7},{7,6},{8,9},{9,8},{10,11... | collective-permute-start | bytes 1966088 | tf_op jit(solution)/shard_map/ppermute | solution.py:391
  17.9 0.8 %copy-start = (f32[5,1,128,256]{3,2,1,0:T(8,128)}, f32[5,1,128,256]{3,2,1,0:T(8,128)S(1)}, u32[]{:S(2)}) copy-start(f32[5,1,128,256]{3,2,1,0:T(8,128)S(1)} %collective-permute-done.nb_ref) | copy-start | bytes 1966084
  24.2 3.6 %collective-permute-start.3 = (f32[5,1,3,2,256]{4,3,2,1,0:T(2,128)}, f32[5,1,3,2,256]{4,3,2,1,0:T(2,128)S(1)}, u32[]{:S(2)}, u32[]{:S(2)}) collective-permute-start(f32[5,1,3,2,256]{4,3,2,1,0:T(2,128)} %get-tuple-element.28.refs_3_), channel_id=1, source_target_pairs={{24,0},{0,8},{8,16},{16,24},{25,1},{1,9},{9,17},{17,25},{26,2},{2,... | collective-permute-start | bytes 92168 | tf_op jit(solution)/shard_map/ppermute | solution.py:384
  24.3 4.2 %collective-permute-start.2 = (f32[5,1,3,2,256]{4,3,2,1,0:T(2,128)}, f32[5,1,3,2,256]{4,3,2,1,0:T(2,128)S(1)}, u32[]{:S(2)}, u32[]{:S(2)}) collective-permute-start(f32[5,1,3,2,256]{4,3,2,1,0:T(2,128)} %get-tuple-element.28.refs_3_), channel_id=1, source_target_pairs={{16,0},{24,8},{0,16},{8,24},{17,1},{25,9},{1,17},{9,25},{18,2},{26... | collective-permute-start | bytes 92168 | tf_op jit(solution)/shard_map/ppermute | solution.py:384
  26.1 3.2 %collective-permute-start.1 = (f32[5,1,3,2,256]{4,3,2,1,0:T(2,128)}, f32[5,1,3,2,256]{4,3,2,1,0:T(2,128)S(1)}, u32[]{:S(2)}, u32[]{:S(2)}) collective-permute-start(f32[5,1,3,2,256]{4,3,2,1,0:T(2,128)} %get-tuple-element.28.refs_3_), channel_id=1, source_target_pairs={{8,0},{16,8},{24,16},{0,24},{9,1},{17,9},{25,17},{1,25},{10,2},{18... | collective-permute-start | bytes 92168 | tf_op jit(solution)/shard_map/ppermute | solution.py:384
  27.8 1.4 %copy-start.1 = (f32[5,1,3,2,256]{4,3,2,1,0:T(2,128)}, f32[5,1,3,2,256]{4,3,2,1,0:T(2,128)S(1)}, u32[]{:S(2)}) copy-start(f32[5,1,3,2,256]{4,3,2,1,0:T(2,128)S(1)} %collective-permute-done.3.refs_6_) | copy-start | bytes 92164
  28.5 0.8 %copy-start.2 = (f32[5,1,3,2,256]{4,3,2,1,0:T(2,128)}, f32[5,1,3,2,256]{4,3,2,1,0:T(2,128)S(1)}, u32[]{:S(2)}) copy-start(f32[5,1,3,2,256]{4,3,2,1,0:T(2,128)S(1)} %collective-permute-done.2.refs_5_) | copy-start | bytes 92164
  29.2 0.6 %copy-start.3 = (f32[5,1,3,2,256]{4,3,2,1,0:T(2,128)}, f32[5,1,3,2,256]{4,3,2,1,0:T(2,128)S(1)}, u32[]{:S(2)}) copy-start(f32[5,1,3,2,256]{4,3,2,1,0:T(2,128)S(1)} %collective-permute-done.1.refs_4_) | copy-start | bytes 92164
  36.2 5.7 %collective-permute-start.6 = (f32[5,1,3,2,128]{4,3,2,1,0:T(2,128)}, f32[5,1,3,2,128]{4,3,2,1,0:T(2,128)S(1)}, u32[]{:S(2)}, u32[]{:S(2)}) collective-permute-start(f32[5,1,3,2,128]{4,3,2,1,0:T(2,128)} %get-tuple-element.32.refs_3_), channel_id=1, source_target_pairs={{6,0},{0,2},{2,4},{4,6},{7,1},{1,3},{3,5},{5,7},{14,8},{8,10},{10,... | collective-permute-start | bytes 46088 | tf_op jit(solution)/shard_map/ppermute | solution.py:384
  37.7 4.9 %collective-permute-start.5 = (f32[5,1,3,2,128]{4,3,2,1,0:T(2,128)}, f32[5,1,3,2,128]{4,3,2,1,0:T(2,128)S(1)}, u32[]{:S(2)}, u32[]{:S(2)}) collective-permute-start(f32[5,1,3,2,128]{4,3,2,1,0:T(2,128)} %get-tuple-element.32.refs_3_), channel_id=1, source_target_pairs={{4,0},{6,2},{0,4},{2,6},{5,1},{7,3},{1,5},{3,7},{12,8},{14,10},{8,... | collective-permute-start | bytes 46088 | tf_op jit(solution)/shard_map/ppermute | solution.py:384
  40.3 3.9 %collective-permute-start.4 = (f32[5,1,3,2,128]{4,3,2,1,0:T(2,128)}, f32[5,1,3,2,128]{4,3,2,1,0:T(2,128)S(1)}, u32[]{:S(2)}, u32[]{:S(2)}) collective-permute-start(f32[5,1,3,2,128]{4,3,2,1,0:T(2,128)} %get-tuple-element.32.refs_3_), channel_id=1, source_target_pairs={{2,0},{4,2},{6,4},{0,6},{3,1},{5,3},{7,5},{1,7},{10,8},{12,10},{14... | collective-permute-start | bytes 46088 | tf_op jit(solution)/shard_map/ppermute | solution.py:384
  41.9 2.4 %copy-start.4 = (f32[5,1,3,2,128]{4,3,2,1,0:T(2,128)}, f32[5,1,3,2,128]{4,3,2,1,0:T(2,128)S(1)}, u32[]{:S(2)}) copy-start(f32[5,1,3,2,128]{4,3,2,1,0:T(2,128)S(1)} %collective-permute-done.6.refs_6_) | copy-start | bytes 46084
  42.6 1.7 %copy-start.5 = (f32[5,1,3,2,128]{4,3,2,1,0:T(2,128)}, f32[5,1,3,2,128]{4,3,2,1,0:T(2,128)S(1)}, u32[]{:S(2)}) copy-start(f32[5,1,3,2,128]{4,3,2,1,0:T(2,128)S(1)} %collective-permute-done.5.refs_5_) | copy-start | bytes 46084
  44.3 0.6 %copy-start.6 = (f32[5,1,3,2,128]{4,3,2,1,0:T(2,128)}, f32[5,1,3,2,128]{4,3,2,1,0:T(2,128)S(1)}, u32[]{:S(2)}) copy-start(f32[5,1,3,2,128]{4,3,2,1,0:T(2,128)S(1)} %collective-permute-done.4.refs_4_) | copy-start | bytes 46084

commit v19 on v18

--- a/solution.py
+++ b/solution.py
@@ -336,7 +336,7 @@
 
 def rad_sweep(it, ia, ib, red_in, mix_mid, cell_rad, visc_rad, edges):
     nv, nz, na, nr = it.shape
-    halves = 2 if na % 16 == 0 else 1
+    halves = 4 if na % 32 == 0 else 1
     big = pl.BlockSpec((nv, 1, na // halves, nr), lambda z, c: (0, z, c, 0))
     big_t = pl.BlockSpec((nv, 1, nr, na), lambda z, c: (0, z, 0, 0))
     red_in_spec = pl.BlockSpec((nv, 1) + red_in[0].shape[2:], lambda z, c: (0, z, 0, 0, 0))

time: 47.7 us -> 48.8 us (1.023)
  Pallas kernels: 27.7 us -> 28.8 us
    pallas_call x1, Pallas kernels: 6.31 us -> 7.41 us  [rad_sweep(): pl.pallas_call(kernel, grid=(nz, halves), in_specs=[big, big, big] + [red...]
  transfers between devices with their start and end apart: 7 -> 7, of which waited for: 7 -> 7; matrix products, arithmetic and copies ran while one was open for 0% -> 0% of each run, Pallas kernels for 28% -> 27%
where the time goes in v19:
time: 48.8 us; the launch traced here: 48.5 us
  Pallas kernels  28.8 us (59%)
  starting transfers between devices  11.7 us (24%)
  waiting for transfers between devices  5.99 us (12%)
  local copies, waits for them, and re-layouts  2.05 us (4%)
    ppermute x6, starting transfers between devices, gathered(): received.append(lax.ppermute(block, axis_name, pairs))  8.74 us
    pallas_call x1, Pallas kernels, rad_sweep(): pl.pallas_call(kernel, grid=(nz, halves), in_specs=[big, big, big] + [red...  7.41 us
    pallas_call x1, Pallas kernels, az_sweep(): pl.pallas_call(az_local_kernel, grid=grid, in_specs=[big, big, cell, par,...  7.27 us
    pallas_call x1, Pallas kernels, rad_pre(): pl.pallas_call(functools.partial(rad_pre_kernel, axis_name='rad'), grid=(...  6.04 us
    pallas_call x1, Pallas kernels, az_sweep(): pl.pallas_call(az_plane_kernel, grid=grid, in_specs=[big, big, big, big,...  5.49 us
    ppermute x6, waiting for transfers between devices, gathered(): received.append(lax.ppermute(block, axis_name, pairs))  4.37 us
    ppermute x1, starting transfers between devices, neighbour_planes(): return lax.ppermute(block, axis_name, [(0, 1), (1, 0)])  2.97 us
    pallas_call x1, Pallas kernels, out_sweep(): pl.pallas_call(functools.partial(out_kernel, pieces=pieces, length=nr), g...  2.57 us
  transfers between devices with their start and end apart: 7, of which 7 were waited for; matrix products, arithmetic and copies ran while one was open for 0% of the time, Pallas kernels for 27%

profile of v19, /device:TPU:0, one launch (start us, length us, event | category | flops | bytes accessed | tf_op | source)
XLA Modules:
  0.0 48.5 jit_solution(17909389841585218572)
XLA Ops:
  0.0 3.0 %collective-permute-start = (f32[5,1,128,256]{3,2,1,0:T(8,128)}, f32[5,1,128,256]{3,2,1,0:T(8,128)S(1)}, u32[]{:S(2)}, u32[]{:S(2)}) collective-permute-start(f32[5,1,128,256]{3,2,1,0:T(8,128)} %fs_ref.1), channel_id=1, source_target_pairs={{0,1},{1,0},{2,3},{3,2},{4,5},{5,4},{6,7},{7,6},{8,9},{9,8},{10,11... | collective-permute-start | bytes 1966088 | tf_op jit(solution)/shard_map/ppermute | solution.py:391
  3.0 6.0 %shard_map.110 = (f32[5,1,256,128]{3,2,1,0:T(8,128)}, f32[5,1,256,128]{3,2,1,0:T(8,128)}, f32[5,1,4,128]{3,2,1,0:T(4,128)}) custom-call(f32[1,128,256]{2,1,0:T(8,128)} %refs_8_.1, f32[5,1024]{1,0:T(8,128)} %refs_9_.1), custom_call_target="tpu_custom_call" | custom-call | tf_op jit(solution)/shard_map/pallas_call | solution.py:328
  9.0 7.3 %shard_map.109 = (f32[5,1,128,256]{3,2,1,0:T(8,128)}, f32[5,1,128,256]{3,2,1,0:T(8,128)}, f32[5,1,128,256]{3,2,1,0:T(8,128)}, f32[5,1,128,256]{3,2,1,0:T(8,128)}...) custom-call(f32[5,1,128,256]{3,2,1,0:T(8,128)} %fs_ref.1, ...), custom_call_target="tpu_custom_call" | custom-call | tf_op jit(solution)/shard_map/pallas_call | solution.py:303
  16.3 1.6 %collective-permute-done.nb_ref = f32[5,1,128,256]{3,2,1,0:T(8,128)S(1)} collective-permute-done((f32[5,1,128,256]{3,2,1,0:T(8,128)}, f32[5,1,128,256]{3,2,1,0:T(8,128)S(1)}, u32[]{:S(2)}, u32[]{:S(2)}) %collective-permute-start) | collective-permute-done | bytes 655392 | tf_op jit(solution)/shard_map/ppermute | solution.py:391
  17.9 0.0 copy-start
  17.9 0.8 %copy-done = f32[5,1,128,256]{3,2,1,0:T(8,128)} copy-done((f32[5,1,128,256]{3,2,1,0:T(8,128)}, f32[5,1,128,256]{3,2,1,0:T(8,128)S(1)}, u32[]{:S(2)}) %copy-start) | copy-done | bytes 655384
  18.7 5.5 %shard_map.111 = (f32[5,1,128,256]{3,2,1,0:T(8,128)}, f32[5,1,3,2,256]{4,3,2,1,0:T(2,128)}) custom-call(f32[5,1,128,256]{3,2,1,0:T(8,128)} %copy-done, f32[5,1,128,256]{3,2,1,0:T(8,128)} %get-tuple-element.19.il_ref, f32[5,1,128,256]{3,2,1,0:T(8,128)} %get-tuple-element.20.iu_ref, ...), custom_call_target="tpu_custom_call", output_to_operand_aliasing={{0}: (6, {})} | custom-call | tf_op jit(solution)/shard_map/pallas_call | solution.py:310
  24.2 0.0 collective-permute-start.3
  24.3 1.8 %collective-permute-start.2 = (f32[5,1,3,2,256]{4,3,2,1,0:T(2,128)}, f32[5,1,3,2,256]{4,3,2,1,0:T(2,128)S(1)}, u32[]{:S(2)}, u32[]{:S(2)}) collective-permute-start(f32[5,1,3,2,256]{4,3,2,1,0:T(2,128)} %get-tuple-element.28.refs_3_), channel_id=1, source_target_pairs={{16,0},{24,8},{0,16},{8,24},{17,1},{25,9},{1,17},{9,25},{18,2},{26... | collective-permute-start | bytes 92168 | tf_op jit(solution)/shard_map/ppermute | solution.py:384
  26.1 1.4 %collective-permute-start.1 = (f32[5,1,3,2,256]{4,3,2,1,0:T(2,128)}, f32[5,1,3,2,256]{4,3,2,1,0:T(2,128)S(1)}, u32[]{:S(2)}, u32[]{:S(2)}) collective-permute-start(f32[5,1,3,2,256]{4,3,2,1,0:T(2,128)} %get-tuple-element.28.refs_3_), channel_id=1, source_target_pairs={{8,0},{16,8},{24,16},{0,24},{9,1},{17,9},{25,17},{1,25},{10,2},{18... | collective-permute-start | bytes 92168 | tf_op jit(solution)/shard_map/ppermute | solution.py:384
  27.5 0.3 collective-permute-done.3.refs_6_
  27.8 0.0 copy-start.1
  27.8 0.7 %collective-permute-done.2.refs_5_ = f32[5,1,3,2,256]{4,3,2,1,0:T(2,128)S(1)} collective-permute-done((f32[5,1,3,2,256]{4,3,2,1,0:T(2,128)}, f32[5,1,3,2,256]{4,3,2,1,0:T(2,128)S(1)}, u32[]{:S(2)}, u32[]{:S(2)}) %collective-permute-start.2) | collective-permute-done | bytes 30752 | tf_op jit(solution)/shard_map/ppermute | solution.py:384
  28.5 0.0 copy-start.2
  28.5 0.8 %collective-permute-done.1.refs_4_ = f32[5,1,3,2,256]{4,3,2,1,0:T(2,128)S(1)} collective-permute-done((f32[5,1,3,2,256]{4,3,2,1,0:T(2,128)}, f32[5,1,3,2,256]{4,3,2,1,0:T(2,128)S(1)}, u32[]{:S(2)}, u32[]{:S(2)}) %collective-permute-start.1) | collective-permute-done | bytes 30752 | tf_op jit(solution)/shard_map/ppermute | solution.py:384
  29.2 0.0 copy-start.3
  29.2 0.0 copy-done.1
  29.2 0.0 copy-done.2
  29.2 0.6 %copy-done.3 = f32[5,1,3,2,256]{4,3,2,1,0:T(2,128)} copy-done((f32[5,1,3,2,256]{4,3,2,1,0:T(2,128)}, f32[5,1,3,2,256]{4,3,2,1,0:T(2,128)S(1)}, u32[]{:S(2)}) %copy-start.3) | copy-done | bytes 30744
  29.9 7.4 %shard_map.112 = (f32[5,1,256,128]{3,2,1,0:T(8,128)}, f32[5,1,3,2,128]{4,3,2,1,0:T(2,128)}) custom-call(f32[5,1,128,256]{3,2,1,0:T(8,128)} %get-tuple-element.25.refs_0_, f32[5,1,128,256]{3,2,1,0:T(8,128)} %get-tuple-element.26.refs_1_, f32[5,1,128,256]{3,2,1,0:T(8,128)} %get-tuple-element.27.refs_2_, f32[5,1,3,2,256]{4,3,2,1,0:T(2,128)} %get-tuple-element.28.refs_3_, ...), custom_call_target="tpu_custom_call" | custom-call | tf_op jit(solution)/shard_map/pallas_call | solution.py:351
  37.3 1.6 %collective-permute-start.6 = (f32[5,1,3,2,128]{4,3,2,1,0:T(2,128)}, f32[5,1,3,2,128]{4,3,2,1,0:T(2,128)S(1)}, u32[]{:S(2)}, u32[]{:S(2)}) collective-permute-start(f32[5,1,3,2,128]{4,3,2,1,0:T(2,128)} %get-tuple-element.32.refs_3_), channel_id=1, source_target_pairs={{6,0},{0,2},{2,4},{4,6},{7,1},{1,3},{3,5},{5,7},{14,8},{8,10},{10,... | collective-permute-start | bytes 46088 | tf_op jit(solution)/shard_map/ppermute | solution.py:384
  38.8 2.6 %collective-permute-start.5 = (f32[5,1,3,2,128]{4,3,2,1,0:T(2,128)}, f32[5,1,3,2,128]{4,3,2,1,0:T(2,128)S(1)}, u32[]{:S(2)}, u32[]{:S(2)}) collective-permute-start(f32[5,1,3,2,128]{4,3,2,1,0:T(2,128)} %get-tuple-element.32.refs_3_), channel_id=1, source_target_pairs={{4,0},{6,2},{0,4},{2,6},{5,1},{7,3},{1,5},{3,7},{12,8},{14,10},{8,... | collective-permute-start | bytes 46088 | tf_op jit(solution)/shard_map/ppermute | solution.py:384
  41.4 1.4 %collective-permute-start.4 = (f32[5,1,3,2,128]{4,3,2,1,0:T(2,128)}, f32[5,1,3,2,128]{4,3,2,1,0:T(2,128)S(1)}, u32[]{:S(2)}, u32[]{:S(2)}) collective-permute-start(f32[5,1,3,2,128]{4,3,2,1,0:T(2,128)} %get-tuple-element.32.refs_3_), channel_id=1, source_target_pairs={{2,0},{4,2},{6,4},{0,6},{3,1},{5,3},{7,5},{1,7},{10,8},{12,10},{14... | collective-permute-start | bytes 46088 | tf_op jit(solution)/shard_map/ppermute | solution.py:384
  42.8 0.2 collective-permute-done.6.refs_6_
  43.0 0.0 copy-start.4
  43.0 0.7 %collective-permute-done.5.refs_5_ = f32[5,1,3,2,128]{4,3,2,1,0:T(2,128)S(1)} collective-permute-done((f32[5,1,3,2,128]{4,3,2,1,0:T(2,128)}, f32[5,1,3,2,128]{4,3,2,1,0:T(2,128)S(1)}, u32[]{:S(2)}, u32[]{:S(2)}) %collective-permute-start.5) | collective-permute-done | bytes 15392 | tf_op jit(solution)/shard_map/ppermute | solution.py:384
  43.7 0.0 copy-start.5
  43.7 1.7 %collective-permute-done.4.refs_4_ = f32[5,1,3,2,128]{4,3,2,1,0:T(2,128)S(1)} collective-permute-done((f32[5,1,3,2,128]{4,3,2,1,0:T(2,128)}, f32[5,1,3,2,128]{4,3,2,1,0:T(2,128)S(1)}, u32[]{:S(2)}, u32[]{:S(2)}) %collective-permute-start.4) | collective-permute-done | bytes 15392 | tf_op jit(solution)/shard_map/ppermute | solution.py:384
  45.4 0.0 copy-start.6
  45.4 0.0 copy-done.4
  45.4 0.0 copy-done.5
  45.4 0.6 %copy-done.6 = f32[5,1,3,2,128]{4,3,2,1,0:T(2,128)} copy-done((f32[5,1,3,2,128]{4,3,2,1,0:T(2,128)}, f32[5,1,3,2,128]{4,3,2,1,0:T(2,128)S(1)}, u32[]{:S(2)}) %copy-start.6) | copy-done | bytes 15384
  46.0 2.6 %shard_map.113 = f32[5,1,128,256]{3,2,1,0:T(8,128)} custom-call(f32[5,1,256,128]{3,2,1,0:T(8,128)} %get-tuple-element.29.refs_0_, f32[5,1,256,128]{3,2,1,0:T(8,128)} %get-tuple-element.30.refs_1_, f32[5,1,256,128]{3,2,1,0:T(8,128)} %get-tuple-element.31.refs_2_, f32[5,1,3,2,128]{4,3,2,1,0:T(2,128)} %get-tuple-element.32.refs_3_, ...), custom_call_target="tpu_custom_call" | custom-call | tf_op jit(solution)/shard_map/pallas_call | solution.py:369
Async XLA Ops:
  0.0 17.9 %collective-permute-start = (f32[5,1,128,256]{3,2,1,0:T(8,128)}, f32[5,1,128,256]{3,2,1,0:T(8,128)S(1)}, u32[]{:S(2)}, u32[]{:S(2)}) collective-permute-start(f32[5,1,128,256]{3,2,1,0:T(8,128)} %fs_ref.1), channel_id=1, source_target_pairs={{0,1},{1,0},{2,3},{3,2},{4,5},{5,4},{6,7},{7,6},{8,9},{9,8},{10,11... | collective-permute-start | bytes 1966088 | tf_op jit(solution)/shard_map/ppermute | solution.py:391
  17.9 0.8 %copy-start = (f32[5,1,128,256]{3,2,1,0:T(8,128)}, f32[5,1,128,256]{3,2,1,0:T(8,128)S(1)}, u32[]{:S(2)}) copy-start(f32[5,1,128,256]{3,2,1,0:T(8,128)S(1)} %collective-permute-done.nb_ref) | copy-start | bytes 1966084
  24.2 3.6 %collective-permute-start.3 = (f32[5,1,3,2,256]{4,3,2,1,0:T(2,128)}, f32[5,1,3,2,256]{4,3,2,1,0:T(2,128)S(1)}, u32[]{:S(2)}, u32[]{:S(2)}) collective-permute-start(f32[5,1,3,2,256]{4,3,2,1,0:T(2,128)} %get-tuple-element.28.refs_3_), channel_id=1, source_target_pairs={{24,0},{0,8},{8,16},{16,24},{25,1},{1,9},{9,17},{17,25},{26,2},{2,... | collective-permute-start | bytes 92168 | tf_op jit(solution)/shard_map/ppermute | solution.py:384
  24.3 4.2 %collective-permute-start.2 = (f32[5,1,3,2,256]{4,3,2,1,0:T(2,128)}, f32[5,1,3,2,256]{4,3,2,1,0:T(2,128)S(1)}, u32[]{:S(2)}, u32[]{:S(2)}) collective-permute-start(f32[5,1,3,2,256]{4,3,2,1,0:T(2,128)} %get-tuple-element.28.refs_3_), channel_id=1, source_target_pairs={{16,0},{24,8},{0,16},{8,24},{17,1},{25,9},{1,17},{9,25},{18,2},{26... | collective-permute-start | bytes 92168 | tf_op jit(solution)/shard_map/ppermute | solution.py:384
  26.1 3.2 %collective-permute-start.1 = (f32[5,1,3,2,256]{4,3,2,1,0:T(2,128)}, f32[5,1,3,2,256]{4,3,2,1,0:T(2,128)S(1)}, u32[]{:S(2)}, u32[]{:S(2)}) collective-permute-start(f32[5,1,3,2,256]{4,3,2,1,0:T(2,128)} %get-tuple-element.28.refs_3_), channel_id=1, source_target_pairs={{8,0},{16,8},{24,16},{0,24},{9,1},{17,9},{25,17},{1,25},{10,2},{18... | collective-permute-start | bytes 92168 | tf_op jit(solution)/shard_map/ppermute | solution.py:384
  27.8 1.4 %copy-start.1 = (f32[5,1,3,2,256]{4,3,2,1,0:T(2,128)}, f32[5,1,3,2,256]{4,3,2,1,0:T(2,128)S(1)}, u32[]{:S(2)}) copy-start(f32[5,1,3,2,256]{4,3,2,1,0:T(2,128)S(1)} %collective-permute-done.3.refs_6_) | copy-start | bytes 92164
  28.5 0.8 %copy-start.2 = (f32[5,1,3,2,256]{4,3,2,1,0:T(2,128)}, f32[5,1,3,2,256]{4,3,2,1,0:T(2,128)S(1)}, u32[]{:S(2)}) copy-start(f32[5,1,3,2,256]{4,3,2,1,0:T(2,128)S(1)} %collective-permute-done.2.refs_5_) | copy-start | bytes 92164
  29.2 0.6 %copy-start.3 = (f32[5,1,3,2,256]{4,3,2,1,0:T(2,128)}, f32[5,1,3,2,256]{4,3,2,1,0:T(2,128)S(1)}, u32[]{:S(2)}) copy-start(f32[5,1,3,2,256]{4,3,2,1,0:T(2,128)S(1)} %collective-permute-done.1.refs_4_) | copy-start | bytes 92164
  37.3 5.7 %collective-permute-start.6 = (f32[5,1,3,2,128]{4,3,2,1,0:T(2,128)}, f32[5,1,3,2,128]{4,3,2,1,0:T(2,128)S(1)}, u32[]{:S(2)}, u32[]{:S(2)}) collective-permute-start(f32[5,1,3,2,128]{4,3,2,1,0:T(2,128)} %get-tuple-element.32.refs_3_), channel_id=1, source_target_pairs={{6,0},{0,2},{2,4},{4,6},{7,1},{1,3},{3,5},{5,7},{14,8},{8,10},{10,... | collective-permute-start | bytes 46088 | tf_op jit(solution)/shard_map/ppermute | solution.py:384
  38.8 4.9 %collective-permute-start.5 = (f32[5,1,3,2,128]{4,3,2,1,0:T(2,128)}, f32[5,1,3,2,128]{4,3,2,1,0:T(2,128)S(1)}, u32[]{:S(2)}, u32[]{:S(2)}) collective-permute-start(f32[5,1,3,2,128]{4,3,2,1,0:T(2,128)} %get-tuple-element.32.refs_3_), channel_id=1, source_target_pairs={{4,0},{6,2},{0,4},{2,6},{5,1},{7,3},{1,5},{3,7},{12,8},{14,10},{8,... | collective-permute-start | bytes 46088 | tf_op jit(solution)/shard_map/ppermute | solution.py:384
  41.4 3.9 %collective-permute-start.4 = (f32[5,1,3,2,128]{4,3,2,1,0:T(2,128)}, f32[5,1,3,2,128]{4,3,2,1,0:T(2,128)S(1)}, u32[]{:S(2)}, u32[]{:S(2)}) collective-permute-start(f32[5,1,3,2,128]{4,3,2,1,0:T(2,128)} %get-tuple-element.32.refs_3_), channel_id=1, source_target_pairs={{2,0},{4,2},{6,4},{0,6},{3,1},{5,3},{7,5},{1,7},{10,8},{12,10},{14... | collective-permute-start | bytes 46088 | tf_op jit(solution)/shard_map/ppermute | solution.py:384
  43.0 2.4 %copy-start.4 = (f32[5,1,3,2,128]{4,3,2,1,0:T(2,128)}, f32[5,1,3,2,128]{4,3,2,1,0:T(2,128)S(1)}, u32[]{:S(2)}) copy-start(f32[5,1,3,2,128]{4,3,2,1,0:T(2,128)S(1)} %collective-permute-done.6.refs_6_) | copy-start | bytes 46084
  43.7 1.7 %copy-start.5 = (f32[5,1,3,2,128]{4,3,2,1,0:T(2,128)}, f32[5,1,3,2,128]{4,3,2,1,0:T(2,128)S(1)}, u32[]{:S(2)}) copy-start(f32[5,1,3,2,128]{4,3,2,1,0:T(2,128)S(1)} %collective-permute-done.5.refs_5_) | copy-start | bytes 46084
  45.4 0.6 %copy-start.6 = (f32[5,1,3,2,128]{4,3,2,1,0:T(2,128)}, f32[5,1,3,2,128]{4,3,2,1,0:T(2,128)S(1)}, u32[]{:S(2)}) copy-start(f32[5,1,3,2,128]{4,3,2,1,0:T(2,128)S(1)} %collective-permute-done.4.refs_4_) | copy-start | bytes 46084

commit v20 on v18

--- a/solution.py
+++ b/solution.py
@@ -125,6 +125,16 @@
         stride = stride * 2
     ends = target / (1.0 + lower + upper)
     return ends[0:1], ends[1:2]
+
+
+def cached_ends(red_refs, rows_ref, ends_ref, w):
+    @pl.when(pl.program_id(1) == 0)
+    def _():
+        first, last = reduced_ends(red_refs, rows_ref, w)
+        ends_ref[w, 0:1, :] = first
+        ends_ref[w, 1:2, :] = last
+
+    return ends_ref[w, 0:1, :], ends_ref[w, 1:2, :]
 
 
 def back_substitute(it, ia, ib, first, last, offset=0, length=None):
@@ -231,13 +241,13 @@
 def rad_kernel(*refs, axis_name, devices, pieces):
     it_ref, ia_ref, ib_ref = refs[:3]
     red_in = refs[3 : 3 + pieces]
-    mix_ref, cell_ref, visc_ref, edge_ref, ot_ref, red_ref, rows_ref, s3_ref = refs[3 + pieces :]
+    mix_ref, cell_ref, visc_ref, edge_ref, ot_ref, red_ref, rows_ref, s3_ref, ends_ref = refs[3 + pieces :]
     count = it_ref.shape[0]
     half = it_ref.shape[2]
     step = pl.program_id(1)
     solved = []
     for w in range(count):
-        first, last = reduced_ends(red_in, rows_ref, w)
+        first, last = cached_ends(red_in, rows_ref, ends_ref, w)
         solved.append(
             back_substitute(it_ref[w, 0], ia_ref[w, 0], ib_ref[w, 0], first, last, step * half, s3_ref.shape[1])
         )
@@ -278,12 +288,12 @@
 def out_kernel(*refs, pieces, length):
     it_ref, ia_ref, ib_ref = refs[:3]
     red_in = refs[3 : 3 + pieces]
-    mix_ref, out_ref, rows_ref = refs[3 + pieces :]
+    mix_ref, out_ref, rows_ref, ends_ref = refs[3 + pieces :]
     count = it_ref.shape[0]
     offset = pl.program_id(1) * it_ref.shape[2]
     solved = []
     for w in range(count):
-        first, last = reduced_ends(red_in, rows_ref, w)
+        first, last = cached_ends(red_in, rows_ref, ends_ref, w)
         solved.append(back_substitute(it_ref[w, 0], ia_ref[w, 0], ib_ref[w, 0], first, last, offset, length).T)
     for v, value in enumerate(mixed(mix_ref, solved)):
         out_ref[v, 0] = value
@@ -354,7 +364,9 @@
         in_specs=[big, big, big] + [red_in_spec] * pieces + [mixs, cell, par, edge],
         out_specs=[big_t, red],
         out_shape=[out, jax.ShapeDtypeStruct((nv, nz, 3, 2, na), it.dtype)],
-        scratch_shapes=[pltpu.VMEM((3, 2 * pieces, nr), it.dtype), pltpu.VMEM((nv, na, nr), it.dtype)],
+        scratch_shapes=[
+            pltpu.VMEM((3, 2 * pieces, nr), it.dtype), pltpu.VMEM((nv, na, nr), it.dtype), pltpu.VMEM((nv, 2, nr), it.dtype)
+        ],
     )(it, ia, ib, *red_in, mix_mid, cell_rad, visc_rad, edges)
 
 
@@ -372,7 +384,7 @@
         in_specs=[big_t, big_t, big_t] + [red_in_spec] * pieces + [mixs],
         out_specs=big,
         out_shape=jax.ShapeDtypeStruct((nv, nz, na, nr), it.dtype),
-        scratch_shapes=[pltpu.VMEM((3, 2 * pieces, na), it.dtype)],
+        scratch_shapes=[pltpu.VMEM((3, 2 * pieces, na), it.dtype), pltpu.VMEM((nv, 2, na), it.dtype)],
     )(it, ia, ib, *red_in, mix_out)
 
 

time: 47.7 us -> 48.4 us (1.015)
  Pallas kernels: 27.7 us -> 28.4 us
    pallas_call x1, Pallas kernels: 2.57 us -> 3.24 us  [out_sweep(): pl.pallas_call(functools.partial(out_kernel, pieces=pieces, length=nr), g...]
where the time goes in v20:
time: 48.4 us; the launch traced here: 48.2 us
  Pallas kernels  28.4 us (59%)
  starting transfers between devices  11.7 us (24%)
  waiting for transfers between devices  5.99 us (12%)
  local copies, waits for them, and re-layouts  2.05 us (4%)
    ppermute x6, starting transfers between devices, gathered(): received.append(lax.ppermute(block, axis_name, pairs))  8.74 us
    pallas_call x1, Pallas kernels, az_sweep(): pl.pallas_call(az_local_kernel, grid=grid, in_specs=[big, big, cell, par,...  7.27 us
    pallas_call x1, Pallas kernels, rad_sweep(): pl.pallas_call(kernel, grid=(nz, halves), in_specs=[big, big, big] + [red...  6.38 us
    pallas_call x1, Pallas kernels, rad_pre(): pl.pallas_call(functools.partial(rad_pre_kernel, axis_name='rad'), grid=(...  6.04 us
    pallas_call x1, Pallas kernels, az_sweep(): pl.pallas_call(az_plane_kernel, grid=grid, in_specs=[big, big, big, big,...  5.49 us
    ppermute x6, waiting for transfers between devices, gathered(): received.append(lax.ppermute(block, axis_name, pairs))  4.37 us
    pallas_call x1, Pallas kernels, out_sweep(): pl.pallas_call(functools.partial(out_kernel, pieces=pieces, length=nr), g...  3.24 us
    ppermute x1, starting transfers between devices, neighbour_planes(): return lax.ppermute(block, axis_name, [(0, 1), (1, 0)])  2.97 us
  transfers between devices with their start and end apart: 7, of which 7 were waited for; matrix products, arithmetic and copies ran while one was open for 0% of the time, Pallas kernels for 28%

profile of v20, /device:TPU:0, one launch (start us, length us, event | category | flops | bytes accessed | tf_op | source)
XLA Modules:
  0.0 48.2 jit_solution(9821587195892975224)
XLA Ops:
  0.0 3.0 %collective-permute-start = (f32[5,1,128,256]{3,2,1,0:T(8,128)}, f32[5,1,128,256]{3,2,1,0:T(8,128)S(1)}, u32[]{:S(2)}, u32[]{:S(2)}) collective-permute-start(f32[5,1,128,256]{3,2,1,0:T(8,128)} %fs_ref.1), channel_id=1, source_target_pairs={{0,1},{1,0},{2,3},{3,2},{4,5},{5,4},{6,7},{7,6},{8,9},{9,8},{10,11... | collective-permute-start | bytes 1966088 | tf_op jit(solution)/shard_map/ppermute | solution.py:403
  3.0 6.0 %shard_map.110 = (f32[5,1,256,128]{3,2,1,0:T(8,128)}, f32[5,1,256,128]{3,2,1,0:T(8,128)}, f32[5,1,4,128]{3,2,1,0:T(4,128)}) custom-call(f32[1,128,256]{2,1,0:T(8,128)} %refs_8_.1, f32[5,1024]{1,0:T(8,128)} %refs_9_.1), custom_call_target="tpu_custom_call" | custom-call | tf_op jit(solution)/shard_map/pallas_call | solution.py:338
  9.0 7.3 %shard_map.109 = (f32[5,1,128,256]{3,2,1,0:T(8,128)}, f32[5,1,128,256]{3,2,1,0:T(8,128)}, f32[5,1,128,256]{3,2,1,0:T(8,128)}, f32[5,1,128,256]{3,2,1,0:T(8,128)}...) custom-call(f32[5,1,128,256]{3,2,1,0:T(8,128)} %fs_ref.1, ...), custom_call_target="tpu_custom_call" | custom-call | tf_op jit(solution)/shard_map/pallas_call | solution.py:313
  16.3 1.6 %collective-permute-done.nb_ref = f32[5,1,128,256]{3,2,1,0:T(8,128)S(1)} collective-permute-done((f32[5,1,128,256]{3,2,1,0:T(8,128)}, f32[5,1,128,256]{3,2,1,0:T(8,128)S(1)}, u32[]{:S(2)}, u32[]{:S(2)}) %collective-permute-start) | collective-permute-done | bytes 655392 | tf_op jit(solution)/shard_map/ppermute | solution.py:403
  17.9 0.0 copy-start
  17.9 0.8 %copy-done = f32[5,1,128,256]{3,2,1,0:T(8,128)} copy-done((f32[5,1,128,256]{3,2,1,0:T(8,128)}, f32[5,1,128,256]{3,2,1,0:T(8,128)S(1)}, u32[]{:S(2)}) %copy-start) | copy-done | bytes 655384
  18.7 5.5 %shard_map.111 = (f32[5,1,128,256]{3,2,1,0:T(8,128)}, f32[5,1,3,2,256]{4,3,2,1,0:T(2,128)}) custom-call(f32[5,1,128,256]{3,2,1,0:T(8,128)} %copy-done, f32[5,1,128,256]{3,2,1,0:T(8,128)} %get-tuple-element.19.il_ref, f32[5,1,128,256]{3,2,1,0:T(8,128)} %get-tuple-element.20.iu_ref, ...), custom_call_target="tpu_custom_call", output_to_operand_aliasing={{0}: (6, {})} | custom-call | tf_op jit(solution)/shard_map/pallas_call | solution.py:320
  24.2 0.0 collective-permute-start.3
  24.3 1.8 %collective-permute-start.2 = (f32[5,1,3,2,256]{4,3,2,1,0:T(2,128)}, f32[5,1,3,2,256]{4,3,2,1,0:T(2,128)S(1)}, u32[]{:S(2)}, u32[]{:S(2)}) collective-permute-start(f32[5,1,3,2,256]{4,3,2,1,0:T(2,128)} %get-tuple-element.28.refs_3_), channel_id=1, source_target_pairs={{16,0},{24,8},{0,16},{8,24},{17,1},{25,9},{1,17},{9,25},{18,2},{26... | collective-permute-start | bytes 92168 | tf_op jit(solution)/shard_map/ppermute | solution.py:396
  26.1 1.4 %collective-permute-start.1 = (f32[5,1,3,2,256]{4,3,2,1,0:T(2,128)}, f32[5,1,3,2,256]{4,3,2,1,0:T(2,128)S(1)}, u32[]{:S(2)}, u32[]{:S(2)}) collective-permute-start(f32[5,1,3,2,256]{4,3,2,1,0:T(2,128)} %get-tuple-element.28.refs_3_), channel_id=1, source_target_pairs={{8,0},{16,8},{24,16},{0,24},{9,1},{17,9},{25,17},{1,25},{10,2},{18... | collective-permute-start | bytes 92168 | tf_op jit(solution)/shard_map/ppermute | solution.py:396
  27.5 0.3 collective-permute-done.3.refs_6_
  27.8 0.0 copy-start.1
  27.8 0.7 %collective-permute-done.2.refs_5_ = f32[5,1,3,2,256]{4,3,2,1,0:T(2,128)S(1)} collective-permute-done((f32[5,1,3,2,256]{4,3,2,1,0:T(2,128)}, f32[5,1,3,2,256]{4,3,2,1,0:T(2,128)S(1)}, u32[]{:S(2)}, u32[]{:S(2)}) %collective-permute-start.2) | collective-permute-done | bytes 30752 | tf_op jit(solution)/shard_map/ppermute | solution.py:396
  28.5 0.0 copy-start.2
  28.5 0.8 %collective-permute-done.1.refs_4_ = f32[5,1,3,2,256]{4,3,2,1,0:T(2,128)S(1)} collective-permute-done((f32[5,1,3,2,256]{4,3,2,1,0:T(2,128)}, f32[5,1,3,2,256]{4,3,2,1,0:T(2,128)S(1)}, u32[]{:S(2)}, u32[]{:S(2)}) %collective-permute-start.1) | collective-permute-done | bytes 30752 | tf_op jit(solution)/shard_map/ppermute | solution.py:396
  29.2 0.0 copy-start.3
  29.2 0.0 copy-done.1
  29.2 0.0 copy-done.2
  29.2 0.6 %copy-done.3 = f32[5,1,3,2,256]{4,3,2,1,0:T(2,128)} copy-done((f32[5,1,3,2,256]{4,3,2,1,0:T(2,128)}, f32[5,1,3,2,256]{4,3,2,1,0:T(2,128)S(1)}, u32[]{:S(2)}) %copy-start.3) | copy-done | bytes 30744
  29.9 6.4 %shard_map.112 = (f32[5,1,256,128]{3,2,1,0:T(8,128)}, f32[5,1,3,2,128]{4,3,2,1,0:T(2,128)}) custom-call(f32[5,1,128,256]{3,2,1,0:T(8,128)} %get-tuple-element.25.refs_0_, f32[5,1,128,256]{3,2,1,0:T(8,128)} %get-tuple-element.26.refs_1_, f32[5,1,128,256]{3,2,1,0:T(8,128)} %get-tuple-element.27.refs_2_, f32[5,1,3,2,256]{4,3,2,1,0:T(2,128)} %get-tuple-element.28.refs_3_, ...), custom_call_target="tpu_custom_call" | custom-call | tf_op jit(solution)/shard_map/pallas_call | solution.py:361
  36.2 1.6 %collective-permute-start.6 = (f32[5,1,3,2,128]{4,3,2,1,0:T(2,128)}, f32[5,1,3,2,128]{4,3,2,1,0:T(2,128)S(1)}, u32[]{:S(2)}, u32[]{:S(2)}) collective-permute-start(f32[5,1,3,2,128]{4,3,2,1,0:T(2,128)} %get-tuple-element.32.refs_3_), channel_id=1, source_target_pairs={{6,0},{0,2},{2,4},{4,6},{7,1},{1,3},{3,5},{5,7},{14,8},{8,10},{10,... | collective-permute-start | bytes 46088 | tf_op jit(solution)/shard_map/ppermute | solution.py:396
  37.8 2.6 %collective-permute-start.5 = (f32[5,1,3,2,128]{4,3,2,1,0:T(2,128)}, f32[5,1,3,2,128]{4,3,2,1,0:T(2,128)S(1)}, u32[]{:S(2)}, u32[]{:S(2)}) collective-permute-start(f32[5,1,3,2,128]{4,3,2,1,0:T(2,128)} %get-tuple-element.32.refs_3_), channel_id=1, source_target_pairs={{4,0},{6,2},{0,4},{2,6},{5,1},{7,3},{1,5},{3,7},{12,8},{14,10},{8,... | collective-permute-start | bytes 46088 | tf_op jit(solution)/shard_map/ppermute | solution.py:396
  40.4 1.3 %collective-permute-start.4 = (f32[5,1,3,2,128]{4,3,2,1,0:T(2,128)}, f32[5,1,3,2,128]{4,3,2,1,0:T(2,128)S(1)}, u32[]{:S(2)}, u32[]{:S(2)}) collective-permute-start(f32[5,1,3,2,128]{4,3,2,1,0:T(2,128)} %get-tuple-element.32.refs_3_), channel_id=1, source_target_pairs={{2,0},{4,2},{6,4},{0,6},{3,1},{5,3},{7,5},{1,7},{10,8},{12,10},{14... | collective-permute-start | bytes 46088 | tf_op jit(solution)/shard_map/ppermute | solution.py:396
  41.8 0.2 collective-permute-done.6.refs_6_
  42.0 0.0 copy-start.4
  42.0 0.7 %collective-permute-done.5.refs_5_ = f32[5,1,3,2,128]{4,3,2,1,0:T(2,128)S(1)} collective-permute-done((f32[5,1,3,2,128]{4,3,2,1,0:T(2,128)}, f32[5,1,3,2,128]{4,3,2,1,0:T(2,128)S(1)}, u32[]{:S(2)}, u32[]{:S(2)}) %collective-permute-start.5) | collective-permute-done | bytes 15392 | tf_op jit(solution)/shard_map/ppermute | solution.py:396
  42.7 0.0 copy-start.5
  42.7 1.7 %collective-permute-done.4.refs_4_ = f32[5,1,3,2,128]{4,3,2,1,0:T(2,128)S(1)} collective-permute-done((f32[5,1,3,2,128]{4,3,2,1,0:T(2,128)}, f32[5,1,3,2,128]{4,3,2,1,0:T(2,128)S(1)}, u32[]{:S(2)}, u32[]{:S(2)}) %collective-permute-start.4) | collective-permute-done | bytes 15392 | tf_op jit(solution)/shard_map/ppermute | solution.py:396
  44.4 0.0 copy-start.6
  44.4 0.0 copy-done.4
  44.4 0.0 copy-done.5
  44.4 0.6 %copy-done.6 = f32[5,1,3,2,128]{4,3,2,1,0:T(2,128)} copy-done((f32[5,1,3,2,128]{4,3,2,1,0:T(2,128)}, f32[5,1,3,2,128]{4,3,2,1,0:T(2,128)S(1)}, u32[]{:S(2)}) %copy-start.6) | copy-done | bytes 15384
  44.9 3.2 %shard_map.113 = f32[5,1,128,256]{3,2,1,0:T(8,128)} custom-call(f32[5,1,256,128]{3,2,1,0:T(8,128)} %get-tuple-element.29.refs_0_, f32[5,1,256,128]{3,2,1,0:T(8,128)} %get-tuple-element.30.refs_1_, f32[5,1,256,128]{3,2,1,0:T(8,128)} %get-tuple-element.31.refs_2_, f32[5,1,3,2,128]{4,3,2,1,0:T(2,128)} %get-tuple-element.32.refs_3_, ...), custom_call_target="tpu_custom_call" | custom-call | tf_op jit(solution)/shard_map/pallas_call | solution.py:381
Async XLA Ops:
  0.0 17.9 %collective-permute-start = (f32[5,1,128,256]{3,2,1,0:T(8,128)}, f32[5,1,128,256]{3,2,1,0:T(8,128)S(1)}, u32[]{:S(2)}, u32[]{:S(2)}) collective-permute-start(f32[5,1,128,256]{3,2,1,0:T(8,128)} %fs_ref.1), channel_id=1, source_target_pairs={{0,1},{1,0},{2,3},{3,2},{4,5},{5,4},{6,7},{7,6},{8,9},{9,8},{10,11... | collective-permute-start | bytes 1966088 | tf_op jit(solution)/shard_map/ppermute | solution.py:403
  17.9 0.8 %copy-start = (f32[5,1,128,256]{3,2,1,0:T(8,128)}, f32[5,1,128,256]{3,2,1,0:T(8,128)S(1)}, u32[]{:S(2)}) copy-start(f32[5,1,128,256]{3,2,1,0:T(8,128)S(1)} %collective-permute-done.nb_ref) | copy-start | bytes 1966084
  24.2 3.6 %collective-permute-start.3 = (f32[5,1,3,2,256]{4,3,2,1,0:T(2,128)}, f32[5,1,3,2,256]{4,3,2,1,0:T(2,128)S(1)}, u32[]{:S(2)}, u32[]{:S(2)}) collective-permute-start(f32[5,1,3,2,256]{4,3,2,1,0:T(2,128)} %get-tuple-element.28.refs_3_), channel_id=1, source_target_pairs={{24,0},{0,8},{8,16},{16,24},{25,1},{1,9},{9,17},{17,25},{26,2},{2,... | collective-permute-start | bytes 92168 | tf_op jit(solution)/shard_map/ppermute | solution.py:396
  24.3 4.2 %collective-permute-start.2 = (f32[5,1,3,2,256]{4,3,2,1,0:T(2,128)}, f32[5,1,3,2,256]{4,3,2,1,0:T(2,128)S(1)}, u32[]{:S(2)}, u32[]{:S(2)}) collective-permute-start(f32[5,1,3,2,256]{4,3,2,1,0:T(2,128)} %get-tuple-element.28.refs_3_), channel_id=1, source_target_pairs={{16,0},{24,8},{0,16},{8,24},{17,1},{25,9},{1,17},{9,25},{18,2},{26... | collective-permute-start | bytes 92168 | tf_op jit(solution)/shard_map/ppermute | solution.py:396
  26.1 3.2 %collective-permute-start.1 = (f32[5,1,3,2,256]{4,3,2,1,0:T(2,128)}, f32[5,1,3,2,256]{4,3,2,1,0:T(2,128)S(1)}, u32[]{:S(2)}, u32[]{:S(2)}) collective-permute-start(f32[5,1,3,2,256]{4,3,2,1,0:T(2,128)} %get-tuple-element.28.refs_3_), channel_id=1, source_target_pairs={{8,0},{16,8},{24,16},{0,24},{9,1},{17,9},{25,17},{1,25},{10,2},{18... | collective-permute-start | bytes 92168 | tf_op jit(solution)/shard_map/ppermute | solution.py:396
  27.8 1.4 %copy-start.1 = (f32[5,1,3,2,256]{4,3,2,1,0:T(2,128)}, f32[5,1,3,2,256]{4,3,2,1,0:T(2,128)S(1)}, u32[]{:S(2)}) copy-start(f32[5,1,3,2,256]{4,3,2,1,0:T(2,128)S(1)} %collective-permute-done.3.refs_6_) | copy-start | bytes 92164
  28.5 0.8 %copy-start.2 = (f32[5,1,3,2,256]{4,3,2,1,0:T(2,128)}, f32[5,1,3,2,256]{4,3,2,1,0:T(2,128)S(1)}, u32[]{:S(2)}) copy-start(f32[5,1,3,2,256]{4,3,2,1,0:T(2,128)S(1)} %collective-permute-done.2.refs_5_) | copy-start | bytes 92164
  29.2 0.6 %copy-start.3 = (f32[5,1,3,2,256]{4,3,2,1,0:T(2,128)}, f32[5,1,3,2,256]{4,3,2,1,0:T(2,128)S(1)}, u32[]{:S(2)}) copy-start(f32[5,1,3,2,256]{4,3,2,1,0:T(2,128)S(1)} %collective-permute-done.1.refs_4_) | copy-start | bytes 92164
  36.2 5.7 %collective-permute-start.6 = (f32[5,1,3,2,128]{4,3,2,1,0:T(2,128)}, f32[5,1,3,2,128]{4,3,2,1,0:T(2,128)S(1)}, u32[]{:S(2)}, u32[]{:S(2)}) collective-permute-start(f32[5,1,3,2,128]{4,3,2,1,0:T(2,128)} %get-tuple-element.32.refs_3_), channel_id=1, source_target_pairs={{6,0},{0,2},{2,4},{4,6},{7,1},{1,3},{3,5},{5,7},{14,8},{8,10},{10,... | collective-permute-start | bytes 46088 | tf_op jit(solution)/shard_map/ppermute | solution.py:396
  37.8 4.9 %collective-permute-start.5 = (f32[5,1,3,2,128]{4,3,2,1,0:T(2,128)}, f32[5,1,3,2,128]{4,3,2,1,0:T(2,128)S(1)}, u32[]{:S(2)}, u32[]{:S(2)}) collective-permute-start(f32[5,1,3,2,128]{4,3,2,1,0:T(2,128)} %get-tuple-element.32.refs_3_), channel_id=1, source_target_pairs={{4,0},{6,2},{0,4},{2,6},{5,1},{7,3},{1,5},{3,7},{12,8},{14,10},{8,... | collective-permute-start | bytes 46088 | tf_op jit(solution)/shard_map/ppermute | solution.py:396
  40.4 3.9 %collective-permute-start.4 = (f32[5,1,3,2,128]{4,3,2,1,0:T(2,128)}, f32[5,1,3,2,128]{4,3,2,1,0:T(2,128)S(1)}, u32[]{:S(2)}, u32[]{:S(2)}) collective-permute-start(f32[5,1,3,2,128]{4,3,2,1,0:T(2,128)} %get-tuple-element.32.refs_3_), channel_id=1, source_target_pairs={{2,0},{4,2},{6,4},{0,6},{3,1},{5,3},{7,5},{1,7},{10,8},{12,10},{14... | collective-permute-start | bytes 46088 | tf_op jit(solution)/shard_map/ppermute | solution.py:396
  42.0 2.4 %copy-start.4 = (f32[5,1,3,2,128]{4,3,2,1,0:T(2,128)}, f32[5,1,3,2,128]{4,3,2,1,0:T(2,128)S(1)}, u32[]{:S(2)}) copy-start(f32[5,1,3,2,128]{4,3,2,1,0:T(2,128)S(1)} %collective-permute-done.6.refs_6_) | copy-start | bytes 46084
  42.7 1.7 %copy-start.5 = (f32[5,1,3,2,128]{4,3,2,1,0:T(2,128)}, f32[5,1,3,2,128]{4,3,2,1,0:T(2,128)S(1)}, u32[]{:S(2)}) copy-start(f32[5,1,3,2,128]{4,3,2,1,0:T(2,128)S(1)} %collective-permute-done.5.refs_5_) | copy-start | bytes 46084
  44.4 0.6 %copy-start.6 = (f32[5,1,3,2,128]{4,3,2,1,0:T(2,128)}, f32[5,1,3,2,128]{4,3,2,1,0:T(2,128)S(1)}, u32[]{:S(2)}) copy-start(f32[5,1,3,2,128]{4,3,2,1,0:T(2,128)S(1)} %collective-permute-done.4.refs_4_) | copy-start | bytes 46084

commit v21 on v18

--- a/solution.py
+++ b/solution.py
@@ -291,7 +291,7 @@
 
 def az_sweep(flow_state, nb, source, cell_az, visc_az, beta_az, axial_diff, mix_in, order):
     nv, nz, na, nr = flow_state.shape
-    chunk = 128 if nr % 128 == 0 else nr
+    chunk = nr
     grid = (nz, nr // chunk)
     big = pl.BlockSpec((nv, 1, na, chunk), lambda z, c: (0, z, 0, c))
     cell = pl.BlockSpec((1, na, chunk), lambda z, c: (z, 0, c))

time: 47.7 us -> 48.4 us (1.015)
  Pallas kernels: 27.7 us -> 28.7 us
    pallas_call x1, Pallas kernels: 5.49 us -> 6.29 us  [az_sweep(): pl.pallas_call(az_plane_kernel, grid=grid, in_specs=[big, big, big, big,...]
where the time goes in v21:
time: 48.4 us; the launch traced here: 48.2 us
  Pallas kernels  28.7 us (59%)
  starting transfers between devices  11.7 us (24%)
  waiting for transfers between devices  5.8 us (12%)
  local copies, waits for them, and re-layouts  2.05 us (4%)
    ppermute x6, starting transfers between devices, gathered(): received.append(lax.ppermute(block, axis_name, pairs))  8.71 us
    pallas_call x1, Pallas kernels, az_sweep(): pl.pallas_call(az_local_kernel, grid=grid, in_specs=[big, big, cell, par,...  7.47 us
    pallas_call x1, Pallas kernels, rad_sweep(): pl.pallas_call(kernel, grid=(nz, halves), in_specs=[big, big, big] + [red...  6.31 us
    pallas_call x1, Pallas kernels, az_sweep(): pl.pallas_call(az_plane_kernel, grid=grid, in_specs=[big, big, big, big,...  6.29 us
    pallas_call x1, Pallas kernels, rad_pre(): pl.pallas_call(functools.partial(rad_pre_kernel, axis_name='rad'), grid=(...  6.04 us
    ppermute x6, waiting for transfers between devices, gathered(): received.append(lax.ppermute(block, axis_name, pairs))  4.36 us
    ppermute x1, starting transfers between devices, neighbour_planes(): return lax.ppermute(block, axis_name, [(0, 1), (1, 0)])  2.97 us
    pallas_call x1, Pallas kernels, out_sweep(): pl.pallas_call(functools.partial(out_kernel, pieces=pieces, length=nr), g...  2.57 us
  transfers between devices with their start and end apart: 7, of which 7 were waited for; matrix products, arithmetic and copies ran while one was open for 0% of the time, Pallas kernels for 28%

profile of v21, /device:TPU:0, one launch (start us, length us, event | category | flops | bytes accessed | tf_op | source)
XLA Modules:
  0.0 48.2 jit_solution(15176059254752582559)
XLA Ops:
  0.0 3.0 %collective-permute-start = (f32[5,1,128,256]{3,2,1,0:T(8,128)}, f32[5,1,128,256]{3,2,1,0:T(8,128)S(1)}, u32[]{:S(2)}, u32[]{:S(2)}) collective-permute-start(f32[5,1,128,256]{3,2,1,0:T(8,128)} %fs_ref.1), channel_id=1, source_target_pairs={{0,1},{1,0},{2,3},{3,2},{4,5},{5,4},{6,7},{7,6},{8,9},{9,8},{10,11... | collective-permute-start | bytes 1966088 | tf_op jit(solution)/shard_map/ppermute | solution.py:391
  3.0 6.0 %shard_map.110 = (f32[5,1,256,128]{3,2,1,0:T(8,128)}, f32[5,1,256,128]{3,2,1,0:T(8,128)}, f32[5,1,4,128]{3,2,1,0:T(4,128)}) custom-call(f32[1,128,256]{2,1,0:T(8,128)} %refs_8_.1, f32[5,1024]{1,0:T(8,128)} %refs_9_.1), custom_call_target="tpu_custom_call" | custom-call | tf_op jit(solution)/shard_map/pallas_call | solution.py:328
  9.0 7.5 %shard_map.109 = (f32[5,1,128,256]{3,2,1,0:T(8,128)}, f32[5,1,128,256]{3,2,1,0:T(8,128)}, f32[5,1,128,256]{3,2,1,0:T(8,128)}, f32[5,1,128,256]{3,2,1,0:T(8,128)}...) custom-call(f32[5,1,128,256]{3,2,1,0:T(8,128)} %fs_ref.1, ...), custom_call_target="tpu_custom_call" | custom-call | tf_op jit(solution)/shard_map/pallas_call | solution.py:303
  16.5 1.4 %collective-permute-done.nb_ref = f32[5,1,128,256]{3,2,1,0:T(8,128)S(1)} collective-permute-done((f32[5,1,128,256]{3,2,1,0:T(8,128)}, f32[5,1,128,256]{3,2,1,0:T(8,128)S(1)}, u32[]{:S(2)}, u32[]{:S(2)}) %collective-permute-start) | collective-permute-done | bytes 655392 | tf_op jit(solution)/shard_map/ppermute | solution.py:391
  17.9 0.0 copy-start
  17.9 0.8 %copy-done = f32[5,1,128,256]{3,2,1,0:T(8,128)} copy-done((f32[5,1,128,256]{3,2,1,0:T(8,128)}, f32[5,1,128,256]{3,2,1,0:T(8,128)S(1)}, u32[]{:S(2)}) %copy-start) | copy-done | bytes 655384
  18.7 6.3 %shard_map.111 = (f32[5,1,128,256]{3,2,1,0:T(8,128)}, f32[5,1,3,2,256]{4,3,2,1,0:T(2,128)}) custom-call(f32[5,1,128,256]{3,2,1,0:T(8,128)} %copy-done, f32[5,1,128,256]{3,2,1,0:T(8,128)} %get-tuple-element.19.il_ref, f32[5,1,128,256]{3,2,1,0:T(8,128)} %get-tuple-element.20.iu_ref, ...), custom_call_target="tpu_custom_call", output_to_operand_aliasing={{0}: (6, {})} | custom-call | tf_op jit(solution)/shard_map/pallas_call | solution.py:310
  25.0 0.0 collective-permute-start.3
  25.0 1.7 %collective-permute-start.2 = (f32[5,1,3,2,256]{4,3,2,1,0:T(2,128)}, f32[5,1,3,2,256]{4,3,2,1,0:T(2,128)S(1)}, u32[]{:S(2)}, u32[]{:S(2)}) collective-permute-start(f32[5,1,3,2,256]{4,3,2,1,0:T(2,128)} %get-tuple-element.28.refs_3_), channel_id=1, source_target_pairs={{16,0},{24,8},{0,16},{8,24},{17,1},{25,9},{1,17},{9,25},{18,2},{26... | collective-permute-start | bytes 92168 | tf_op jit(solution)/shard_map/ppermute | solution.py:384
  26.8 1.4 %collective-permute-start.1 = (f32[5,1,3,2,256]{4,3,2,1,0:T(2,128)}, f32[5,1,3,2,256]{4,3,2,1,0:T(2,128)S(1)}, u32[]{:S(2)}, u32[]{:S(2)}) collective-permute-start(f32[5,1,3,2,256]{4,3,2,1,0:T(2,128)} %get-tuple-element.28.refs_3_), channel_id=1, source_target_pairs={{8,0},{16,8},{24,16},{0,24},{9,1},{17,9},{25,17},{1,25},{10,2},{18... | collective-permute-start | bytes 92168 | tf_op jit(solution)/shard_map/ppermute | solution.py:384
  28.2 0.3 collective-permute-done.3.refs_6_
  28.6 0.0 copy-start.1
  28.6 0.6 %collective-permute-done.2.refs_5_ = f32[5,1,3,2,256]{4,3,2,1,0:T(2,128)S(1)} collective-permute-done((f32[5,1,3,2,256]{4,3,2,1,0:T(2,128)}, f32[5,1,3,2,256]{4,3,2,1,0:T(2,128)S(1)}, u32[]{:S(2)}, u32[]{:S(2)}) %collective-permute-start.2) | collective-permute-done | bytes 30752 | tf_op jit(solution)/shard_map/ppermute | solution.py:384
  29.2 0.0 copy-start.2
  29.2 0.8 %collective-permute-done.1.refs_4_ = f32[5,1,3,2,256]{4,3,2,1,0:T(2,128)S(1)} collective-permute-done((f32[5,1,3,2,256]{4,3,2,1,0:T(2,128)}, f32[5,1,3,2,256]{4,3,2,1,0:T(2,128)S(1)}, u32[]{:S(2)}, u32[]{:S(2)}) %collective-permute-start.1) | collective-permute-done | bytes 30752 | tf_op jit(solution)/shard_map/ppermute | solution.py:384
  30.0 0.0 copy-start.3
  30.0 0.0 copy-done.1
  30.0 0.0 copy-done.2
  30.0 0.6 %copy-done.3 = f32[5,1,3,2,256]{4,3,2,1,0:T(2,128)} copy-done((f32[5,1,3,2,256]{4,3,2,1,0:T(2,128)}, f32[5,1,3,2,256]{4,3,2,1,0:T(2,128)S(1)}, u32[]{:S(2)}) %copy-start.3) | copy-done | bytes 30744
  30.6 6.3 %shard_map.112 = (f32[5,1,256,128]{3,2,1,0:T(8,128)}, f32[5,1,3,2,128]{4,3,2,1,0:T(2,128)}) custom-call(f32[5,1,128,256]{3,2,1,0:T(8,128)} %get-tuple-element.25.refs_0_, f32[5,1,128,256]{3,2,1,0:T(8,128)} %get-tuple-element.26.refs_1_, f32[5,1,128,256]{3,2,1,0:T(8,128)} %get-tuple-element.27.refs_2_, f32[5,1,3,2,256]{4,3,2,1,0:T(2,128)} %get-tuple-element.28.refs_3_, ...), custom_call_target="tpu_custom_call" | custom-call | tf_op jit(solution)/shard_map/pallas_call | solution.py:351
  36.9 1.6 %collective-permute-start.6 = (f32[5,1,3,2,128]{4,3,2,1,0:T(2,128)}, f32[5,1,3,2,128]{4,3,2,1,0:T(2,128)S(1)}, u32[]{:S(2)}, u32[]{:S(2)}) collective-permute-start(f32[5,1,3,2,128]{4,3,2,1,0:T(2,128)} %get-tuple-element.32.refs_3_), channel_id=1, source_target_pairs={{6,0},{0,2},{2,4},{4,6},{7,1},{1,3},{3,5},{5,7},{14,8},{8,10},{10,... | collective-permute-start | bytes 46088 | tf_op jit(solution)/shard_map/ppermute | solution.py:384
  38.5 2.6 %collective-permute-start.5 = (f32[5,1,3,2,128]{4,3,2,1,0:T(2,128)}, f32[5,1,3,2,128]{4,3,2,1,0:T(2,128)S(1)}, u32[]{:S(2)}, u32[]{:S(2)}) collective-permute-start(f32[5,1,3,2,128]{4,3,2,1,0:T(2,128)} %get-tuple-element.32.refs_3_), channel_id=1, source_target_pairs={{4,0},{6,2},{0,4},{2,6},{5,1},{7,3},{1,5},{3,7},{12,8},{14,10},{8,... | collective-permute-start | bytes 46088 | tf_op jit(solution)/shard_map/ppermute | solution.py:384
  41.1 1.4 %collective-permute-start.4 = (f32[5,1,3,2,128]{4,3,2,1,0:T(2,128)}, f32[5,1,3,2,128]{4,3,2,1,0:T(2,128)S(1)}, u32[]{:S(2)}, u32[]{:S(2)}) collective-permute-start(f32[5,1,3,2,128]{4,3,2,1,0:T(2,128)} %get-tuple-element.32.refs_3_), channel_id=1, source_target_pairs={{2,0},{4,2},{6,4},{0,6},{3,1},{5,3},{7,5},{1,7},{10,8},{12,10},{14... | collective-permute-start | bytes 46088 | tf_op jit(solution)/shard_map/ppermute | solution.py:384
  42.5 0.2 collective-permute-done.6.refs_6_
  42.7 0.0 copy-start.4
  42.7 0.7 %collective-permute-done.5.refs_5_ = f32[5,1,3,2,128]{4,3,2,1,0:T(2,128)S(1)} collective-permute-done((f32[5,1,3,2,128]{4,3,2,1,0:T(2,128)}, f32[5,1,3,2,128]{4,3,2,1,0:T(2,128)S(1)}, u32[]{:S(2)}, u32[]{:S(2)}) %collective-permute-start.5) | collective-permute-done | bytes 15392 | tf_op jit(solution)/shard_map/ppermute | solution.py:384
  43.4 0.0 copy-start.5
  43.4 1.7 %collective-permute-done.4.refs_4_ = f32[5,1,3,2,128]{4,3,2,1,0:T(2,128)S(1)} collective-permute-done((f32[5,1,3,2,128]{4,3,2,1,0:T(2,128)}, f32[5,1,3,2,128]{4,3,2,1,0:T(2,128)S(1)}, u32[]{:S(2)}, u32[]{:S(2)}) %collective-permute-start.4) | collective-permute-done | bytes 15392 | tf_op jit(solution)/shard_map/ppermute | solution.py:384
  45.0 0.0 copy-start.6
  45.0 0.0 copy-done.4
  45.0 0.0 copy-done.5
  45.0 0.6 %copy-done.6 = f32[5,1,3,2,128]{4,3,2,1,0:T(2,128)} copy-done((f32[5,1,3,2,128]{4,3,2,1,0:T(2,128)}, f32[5,1,3,2,128]{4,3,2,1,0:T(2,128)S(1)}, u32[]{:S(2)}) %copy-start.6) | copy-done | bytes 15384
  45.6 2.6 %shard_map.113 = f32[5,1,128,256]{3,2,1,0:T(8,128)} custom-call(f32[5,1,256,128]{3,2,1,0:T(8,128)} %get-tuple-element.29.refs_0_, f32[5,1,256,128]{3,2,1,0:T(8,128)} %get-tuple-element.30.refs_1_, f32[5,1,256,128]{3,2,1,0:T(8,128)} %get-tuple-element.31.refs_2_, f32[5,1,3,2,128]{4,3,2,1,0:T(2,128)} %get-tuple-element.32.refs_3_, ...), custom_call_target="tpu_custom_call" | custom-call | tf_op jit(solution)/shard_map/pallas_call | solution.py:369
Async XLA Ops:
  0.0 17.9 %collective-permute-start = (f32[5,1,128,256]{3,2,1,0:T(8,128)}, f32[5,1,128,256]{3,2,1,0:T(8,128)S(1)}, u32[]{:S(2)}, u32[]{:S(2)}) collective-permute-start(f32[5,1,128,256]{3,2,1,0:T(8,128)} %fs_ref.1), channel_id=1, source_target_pairs={{0,1},{1,0},{2,3},{3,2},{4,5},{5,4},{6,7},{7,6},{8,9},{9,8},{10,11... | collective-permute-start | bytes 1966088 | tf_op jit(solution)/shard_map/ppermute | solution.py:391
  17.9 0.8 %copy-start = (f32[5,1,128,256]{3,2,1,0:T(8,128)}, f32[5,1,128,256]{3,2,1,0:T(8,128)S(1)}, u32[]{:S(2)}) copy-start(f32[5,1,128,256]{3,2,1,0:T(8,128)S(1)} %collective-permute-done.nb_ref) | copy-start | bytes 1966084
  25.0 3.5 %collective-permute-start.3 = (f32[5,1,3,2,256]{4,3,2,1,0:T(2,128)}, f32[5,1,3,2,256]{4,3,2,1,0:T(2,128)S(1)}, u32[]{:S(2)}, u32[]{:S(2)}) collective-permute-start(f32[5,1,3,2,256]{4,3,2,1,0:T(2,128)} %get-tuple-element.28.refs_3_), channel_id=1, source_target_pairs={{24,0},{0,8},{8,16},{16,24},{25,1},{1,9},{9,17},{17,25},{26,2},{2,... | collective-permute-start | bytes 92168 | tf_op jit(solution)/shard_map/ppermute | solution.py:384
  25.0 4.1 %collective-permute-start.2 = (f32[5,1,3,2,256]{4,3,2,1,0:T(2,128)}, f32[5,1,3,2,256]{4,3,2,1,0:T(2,128)S(1)}, u32[]{:S(2)}, u32[]{:S(2)}) collective-permute-start(f32[5,1,3,2,256]{4,3,2,1,0:T(2,128)} %get-tuple-element.28.refs_3_), channel_id=1, source_target_pairs={{16,0},{24,8},{0,16},{8,24},{17,1},{25,9},{1,17},{9,25},{18,2},{26... | collective-permute-start | bytes 92168 | tf_op jit(solution)/shard_map/ppermute | solution.py:384
  26.8 3.2 %collective-permute-start.1 = (f32[5,1,3,2,256]{4,3,2,1,0:T(2,128)}, f32[5,1,3,2,256]{4,3,2,1,0:T(2,128)S(1)}, u32[]{:S(2)}, u32[]{:S(2)}) collective-permute-start(f32[5,1,3,2,256]{4,3,2,1,0:T(2,128)} %get-tuple-element.28.refs_3_), channel_id=1, source_target_pairs={{8,0},{16,8},{24,16},{0,24},{9,1},{17,9},{25,17},{1,25},{10,2},{18... | collective-permute-start | bytes 92168 | tf_op jit(solution)/shard_map/ppermute | solution.py:384
  28.6 1.4 %copy-start.1 = (f32[5,1,3,2,256]{4,3,2,1,0:T(2,128)}, f32[5,1,3,2,256]{4,3,2,1,0:T(2,128)S(1)}, u32[]{:S(2)}) copy-start(f32[5,1,3,2,256]{4,3,2,1,0:T(2,128)S(1)} %collective-permute-done.3.refs_6_) | copy-start | bytes 92164
  29.2 0.8 %copy-start.2 = (f32[5,1,3,2,256]{4,3,2,1,0:T(2,128)}, f32[5,1,3,2,256]{4,3,2,1,0:T(2,128)S(1)}, u32[]{:S(2)}) copy-start(f32[5,1,3,2,256]{4,3,2,1,0:T(2,128)S(1)} %collective-permute-done.2.refs_5_) | copy-start | bytes 92164
  30.0 0.6 %copy-start.3 = (f32[5,1,3,2,256]{4,3,2,1,0:T(2,128)}, f32[5,1,3,2,256]{4,3,2,1,0:T(2,128)S(1)}, u32[]{:S(2)}) copy-start(f32[5,1,3,2,256]{4,3,2,1,0:T(2,128)S(1)} %collective-permute-done.1.refs_4_) | copy-start | bytes 92164
  36.9 5.7 %collective-permute-start.6 = (f32[5,1,3,2,128]{4,3,2,1,0:T(2,128)}, f32[5,1,3,2,128]{4,3,2,1,0:T(2,128)S(1)}, u32[]{:S(2)}, u32[]{:S(2)}) collective-permute-start(f32[5,1,3,2,128]{4,3,2,1,0:T(2,128)} %get-tuple-element.32.refs_3_), channel_id=1, source_target_pairs={{6,0},{0,2},{2,4},{4,6},{7,1},{1,3},{3,5},{5,7},{14,8},{8,10},{10,... | collective-permute-start | bytes 46088 | tf_op jit(solution)/shard_map/ppermute | solution.py:384
  38.5 4.9 %collective-permute-start.5 = (f32[5,1,3,2,128]{4,3,2,1,0:T(2,128)}, f32[5,1,3,2,128]{4,3,2,1,0:T(2,128)S(1)}, u32[]{:S(2)}, u32[]{:S(2)}) collective-permute-start(f32[5,1,3,2,128]{4,3,2,1,0:T(2,128)} %get-tuple-element.32.refs_3_), channel_id=1, source_target_pairs={{4,0},{6,2},{0,4},{2,6},{5,1},{7,3},{1,5},{3,7},{12,8},{14,10},{8,... | collective-permute-start | bytes 46088 | tf_op jit(solution)/shard_map/ppermute | solution.py:384
  41.1 3.9 %collective-permute-start.4 = (f32[5,1,3,2,128]{4,3,2,1,0:T(2,128)}, f32[5,1,3,2,128]{4,3,2,1,0:T(2,128)S(1)}, u32[]{:S(2)}, u32[]{:S(2)}) collective-permute-start(f32[5,1,3,2,128]{4,3,2,1,0:T(2,128)} %get-tuple-element.32.refs_3_), channel_id=1, source_target_pairs={{2,0},{4,2},{6,4},{0,6},{3,1},{5,3},{7,5},{1,7},{10,8},{12,10},{14... | collective-permute-start | bytes 46088 | tf_op jit(solution)/shard_map/ppermute | solution.py:384
  42.7 2.4 %copy-start.4 = (f32[5,1,3,2,128]{4,3,2,1,0:T(2,128)}, f32[5,1,3,2,128]{4,3,2,1,0:T(2,128)S(1)}, u32[]{:S(2)}) copy-start(f32[5,1,3,2,128]{4,3,2,1,0:T(2,128)S(1)} %collective-permute-done.6.refs_6_) | copy-start | bytes 46084
  43.4 1.7 %copy-start.5 = (f32[5,1,3,2,128]{4,3,2,1,0:T(2,128)}, f32[5,1,3,2,128]{4,3,2,1,0:T(2,128)S(1)}, u32[]{:S(2)}) copy-start(f32[5,1,3,2,128]{4,3,2,1,0:T(2,128)S(1)} %collective-permute-done.5.refs_5_) | copy-start | bytes 46084
  45.0 0.6 %copy-start.6 = (f32[5,1,3,2,128]{4,3,2,1,0:T(2,128)}, f32[5,1,3,2,128]{4,3,2,1,0:T(2,128)S(1)}, u32[]{:S(2)}) copy-start(f32[5,1,3,2,128]{4,3,2,1,0:T(2,128)S(1)} %collective-permute-done.4.refs_4_) | copy-start | bytes 46084
